TPU v7x, 32 devices: a whole 2x2x4 slice. The times are simulated.
32 devices in a mesh: row: 4 (over y, core), col: 8 (over z, x).
Axes of the slice: x: 2, y: 2, z: 4, core: 2. Of those that a mesh axis runs over, the one named last changes fastest.
Arguments:
- bands: float32 [2, 12, 32, 1024], P(None, None, 'row', 'col'), may hold values from -500 to 500
- directions: float32 [2, 12, 32, 1024], P(None, None, 'row', 'col'), may hold values from -500 to 500
- materials: int32 [32, 1024], P('row', 'col'), may hold values from 0 to 7
- permittivity: float32 [8], replicated, may hold values from 1 to 12
- wavevector: int32 [2], replicated, may hold values from 0 to 15
Outputs:
- basis: float32 [2, 36, 32, 1024], P(None, None, 'row', 'col')
- reduced: float32 [2, 36, 36], replicated
All inputs are finite; a program needn't handle non-finite values.
Results may differ from a plain program's by a relative error of at most 0.00018.
Values sent between devices are 32-bit elements; how exact they have to be, the bound alone decides.
No kernel may reach another device: no remote copies, remote signals or barrier semaphores. Data moves between devices by JAX's collectives and lax.ppermute only.
A program may use at most 64 MiB of HBM per device.

v0:
```python
import math

import jax
import jax.numpy as jnp
from jax import lax
from jax.sharding import PartitionSpec as P

KDEN = 16
NS_STEPS = 5


def with_halo(cells, sides, width):
    for axis, dim in sides:
        count = lax.axis_size(axis)
        head = lax.slice_in_dim(cells, 0, width, axis=dim)
        tail = lax.slice_in_dim(cells, cells.shape[dim] - width, cells.shape[dim], axis=dim)
        cells = jnp.concatenate(
            [
                lax.ppermute(tail, axis, [(i, (i + 1) % count) for i in range(count)]),
                cells,
                lax.ppermute(head, axis, [((i + 1) % count, i) for i in range(count)]),
            ],
            axis=dim,
        )
    return cells


def rotate(values, phase_angle):
    cosine = jnp.cos(phase_angle)
    sine_part = jnp.sin(phase_angle)
    return jnp.stack(
        [values[0] * cosine - values[1] * sine_part, values[0] * sine_part + values[1] * cosine]
    )


def bloch_rims(padded, edges, rim_layers):
    low_row, high_row, low_col, high_col = edges
    padded = padded.at[:, :, :rim_layers].set(rotate(padded[:, :, :rim_layers], low_row))
    padded = padded.at[:, :, -rim_layers:].set(rotate(padded[:, :, -rim_layers:], high_row))
    padded = padded.at[:, :, :, :rim_layers].set(rotate(padded[:, :, :, :rim_layers], low_col))
    padded = padded.at[:, :, :, -rim_layers:].set(rotate(padded[:, :, :, -rim_layers:], high_col))
    return padded


def stencil(padded, stiff_pad):
    centre = stiff_pad[1:-1, 1:-1]
    upward = 0.5 * (centre + stiff_pad[:-2, 1:-1])
    downward = 0.5 * (centre + stiff_pad[2:, 1:-1])
    leftward = 0.5 * (centre + stiff_pad[1:-1, :-2])
    rightward = 0.5 * (centre + stiff_pad[1:-1, 2:])
    diagonal = upward + downward + leftward + rightward
    inner_cells = padded[:, :, 1:-1, 1:-1]
    neighbours = (
        upward * padded[:, :, :-2, 1:-1]
        + downward * padded[:, :, 2:, 1:-1]
        + leftward * padded[:, :, 1:-1, :-2]
        + rightward * padded[:, :, 1:-1, 2:]
    )
    return (diagonal * inner_cells - neighbours, diagonal)


def complex_gram(first_block, second_block):
    highest = lax.Precision.HIGHEST
    first_flat = first_block.reshape(first_block.shape[0], first_block.shape[1], -1)
    second_flat = second_block.reshape(second_block.shape[0], second_block.shape[1], -1)
    real_part = jnp.einsum("pjc,pkc->jk", first_flat, second_flat, precision=highest)
    imag_part = jnp.einsum(
        "jc,kc->jk", first_flat[0], second_flat[1], precision=highest
    ) - jnp.einsum("jc,kc->jk", first_flat[1], second_flat[0], precision=highest)
    return (real_part, imag_part)


def inverse_root(gram_real, gram_imag):
    highest = lax.Precision.HIGHEST
    order_size = gram_real.shape[0]
    upper_half = jnp.concatenate([gram_real, -gram_imag], axis=1)
    lower_half = jnp.concatenate([gram_imag, gram_real], axis=1)
    embedded = jnp.concatenate([upper_half, lower_half], axis=0)
    magnitude = jnp.sqrt(jnp.sum(embedded * embedded))
    identity = jnp.eye(2 * order_size, dtype=embedded.dtype)

    def newton(turn_index, carried):
        current, inverse = carried
        factor = 1.5 * identity - 0.5 * jnp.dot(inverse, current, precision=highest)
        return (
            jnp.dot(current, factor, precision=highest),
            jnp.dot(factor, inverse, precision=highest),
        )

    current, inverse = lax.fori_loop(0, NS_STEPS, newton, (embedded / magnitude, identity))
    root_full = inverse / jnp.sqrt(magnitude)
    return (root_full[:order_size, :order_size], root_full[order_size:, :order_size])


def reduce_matrix(root_real, root_imag, ham_real, ham_imag):
    highest = lax.Precision.HIGHEST
    prod_real = jnp.dot(ham_real, root_real, precision=highest) - jnp.dot(
        ham_imag, root_imag, precision=highest
    )
    prod_imag = jnp.dot(ham_real, root_imag, precision=highest) + jnp.dot(
        ham_imag, root_real, precision=highest
    )
    red_real = jnp.dot(root_real.T, prod_real, precision=highest) + jnp.dot(
        root_imag.T, prod_imag, precision=highest
    )
    red_imag = jnp.dot(root_real.T, prod_imag, precision=highest) - jnp.dot(
        root_imag.T, prod_real, precision=highest
    )
    return jnp.stack([red_real, red_imag])


def rotate_basis(raw_basis, root_real, root_imag, scale_factor):
    highest = lax.Precision.HIGHEST
    basis_real = jnp.einsum("jrc,jk->krc", raw_basis[0], root_real, precision=highest) - jnp.einsum(
        "jrc,jk->krc", raw_basis[1], root_imag, precision=highest
    )
    basis_imag = jnp.einsum("jrc,jk->krc", raw_basis[0], root_imag, precision=highest) + jnp.einsum(
        "jrc,jk->krc", raw_basis[1], root_real, precision=highest
    )
    return scale_factor * jnp.stack([basis_real, basis_imag])


def project_mixing(mixing, matrix):
    highest = lax.Precision.HIGHEST
    return jnp.dot(mixing.T, jnp.dot(matrix, mixing, precision=highest), precision=highest)


def body(bands, directions, materials, permittivity, wavevector):
    band_count = bands.shape[1]
    height = bands.shape[2]
    breadth = bands.shape[3]
    levels = jnp.arange(permittivity.shape[0], dtype=jnp.int32)
    stiffness = jnp.sum(
        jnp.where(
            materials[None] == levels[:, None, None], (1.0 / permittivity)[:, None, None], 0.0
        ),
        axis=0,
    )
    angle_row = 2.0 * math.pi * wavevector[0].astype(jnp.float32) / KDEN
    angle_col = 2.0 * math.pi * wavevector[1].astype(jnp.float32) / KDEN
    row_index = lax.axis_index("row")
    col_index = lax.axis_index("col")
    edges = (
        jnp.where(row_index == 0, -angle_row, 0.0),
        jnp.where(row_index == lax.axis_size("row") - 1, angle_row, 0.0),
        jnp.where(col_index == 0, -angle_col, 0.0),
        jnp.where(col_index == lax.axis_size("col") - 1, angle_col, 0.0),
    )
    packed = jnp.concatenate(
        [bands.reshape(2 * band_count, height, breadth), stiffness[None]], axis=0
    )
    padded = with_halo(packed, (("row", 1), ("col", 2)), 1)
    stiff_cycle = padded[-1]
    band_pad = bloch_rims(padded[:-1].reshape(2, band_count, height + 2, breadth + 2), edges, 1)
    applied_cycle, diagonal_cycle = stencil(band_pad, stiff_cycle)
    scaled_cycle = jnp.concatenate([applied_cycle / diagonal_cycle, bands / diagonal_cycle], axis=1)
    stacked = jnp.concatenate([scaled_cycle, directions], axis=1)
    columns_now = stacked.shape[1]
    field_pad = with_halo(
        stacked.reshape(2 * columns_now, height, breadth), (("row", 1), ("col", 2)), 1
    )
    field_pad = bloch_rims(field_pad.reshape(2, columns_now, height + 2, breadth + 2), edges, 1)
    extra_applied = stencil(field_pad, stiff_cycle)[0]
    scaled_image = scaled_cycle[:, :band_count]
    scaled_bands = scaled_cycle[:, band_count:]
    extra = jnp.concatenate([scaled_image, scaled_bands, directions], axis=1)
    extended = jnp.concatenate([bands, extra], axis=1)
    extended_applied = jnp.concatenate([applied_cycle, extra_applied], axis=1)
    local_gram = complex_gram(extended, extended)
    local_ham = complex_gram(extended, extended_applied)
    gram_whole, gram_imag_whole, ham_whole, ham_imag_whole = lax.psum(
        (local_gram[0], local_gram[1], local_ham[0], local_ham[1]), ("row", "col")
    )
    quotient = jnp.diagonal(ham_whole)[:band_count] / jnp.diagonal(gram_whole)[:band_count]
    identity = jnp.eye(band_count, dtype=jnp.float32)
    zeros_block = jnp.zeros((band_count, band_count), jnp.float32)
    mixing = jnp.concatenate(
        [
            jnp.concatenate([identity, zeros_block, zeros_block], axis=1),
            jnp.concatenate([zeros_block, identity, zeros_block], axis=1),
            jnp.concatenate([zeros_block, -jnp.diag(quotient), zeros_block], axis=1),
            jnp.concatenate([zeros_block, zeros_block, identity], axis=1),
        ],
        axis=0,
    )
    gram_real = project_mixing(mixing, gram_whole)
    gram_imag = project_mixing(mixing, gram_imag_whole)
    ham_real = project_mixing(mixing, ham_whole)
    ham_imag = project_mixing(mixing, ham_imag_whole)
    precond = scaled_image - quotient[None, :, None, None] * scaled_bands
    raw_basis = jnp.concatenate([bands, precond, directions], axis=1)
    root_real, root_imag = inverse_root(gram_real, gram_imag)
    scale_factor = math.sqrt(height * breadth * lax.axis_size("row") * lax.axis_size("col"))
    basis = rotate_basis(raw_basis, root_real, root_imag, scale_factor)
    reduced = reduce_matrix(root_real, root_imag, ham_real, ham_imag)
    return (basis, reduced)


def solution(mesh):
    placed = (P(None, None, "row", "col"), P(None, None, "row", "col"), P("row", "col"), P(), P())
    return jax.shard_map(
        body,
        mesh=mesh,
        in_specs=placed,
        out_specs=(P(None, None, "row", "col"), P()),
        check_vma=False,
    )
```

profile of v0, /device:TPU:0, one launch (start us, length us, event | category | flops | bytes accessed | tf_op | source)
XLA Modules:
  0.0 113.8 jit_solution(13991296870753142769)
XLA Ops:
  3.6 2.0 %collective-permute-start.1 = (f32[25,1,128]{2,0,1:T(8,128)S(1)}, f32[25,1,128]{2,0,1:T(8,128)S(1)}, u32[]{:S(2)}, u32[]{:S(2)}) collective-permute-start(f32[25,1,128]{2,0,1:T(8,128)S(1)} %get-tuple-element.209), channel_id=1, source_target_pairs={{8,0},{16,8},{24,16},{0,24},{9,1},{17,9},{25,17},{1,25},{10,2},{18... | collective-permute-start | bytes 38408 | tf_op jit(solution)/shard_map/ppermute | solution.py:21
  5.6 1.3 %fusion.70 = (s32[1]{0:T(128)}, s32[1]{0:T(128)}) fusion(s32[2]{0:T(128)} %param.27), kind=kLoop, calls=%fused_computation.163 | loop fusion | bytes 16 | tf_op jit(solution)/shard_map/slice | solution.py:140
  7.9 2.3 %collective-permute-start.2 = (f32[25,10,1]{2,0,1:T(8,128)S(1)}, f32[25,10,1]{2,0,1:T(8,128)S(1)}, u32[]{:S(2)}, u32[]{:S(2)}) collective-permute-start(f32[25,10,1]{2,0,1:T(8,128)S(1)} %get-tuple-element.206), channel_id=1, source_target_pairs={{0,1},{1,2},{2,3},{3,4},{4,5},{5,6},{6,7},{7,0},{8,9},{9,10},{10,1... | collective-permute-start | bytes 3008 | tf_op jit(solution)/shard_map/ppermute | solution.py:19
  10.2 3.1 %collective-permute-start.3 = (f32[25,10,1]{2,0,1:T(8,128)S(1)}, f32[25,10,1]{2,0,1:T(8,128)S(1)}, u32[]{:S(2)}, u32[]{:S(2)}) collective-permute-start(f32[25,10,1]{2,0,1:T(8,128)S(1)} %get-tuple-element.207), channel_id=1, source_target_pairs={{1,0},{2,1},{3,2},{4,3},{5,4},{6,5},{7,6},{0,7},{9,8},{10,9},{11,1... | collective-permute-start | bytes 3008 | tf_op jit(solution)/shard_map/ppermute | solution.py:21
  14.4 1.3 %copy.212 = f32[2,12,8,128]{1,3,2,0:T(8,128)} copy(f32[2,12,8,128]{3,2,1,0:T(8,128)S(1)} %copy-done.6) | data formatting | bytes 196608 | tf_op args[0]
  15.7 2.6 %collective-permute-done.2 = f32[25,10,1]{2,0,1:T(8,128)S(1)} collective-permute-done((f32[25,10,1]{2,0,1:T(8,128)S(1)}, f32[25,10,1]{2,0,1:T(8,128)S(1)}, u32[]{:S(2)}, u32[]{:S(2)}) %collective-permute-start.2) | collective-permute-done | bytes 1032 | tf_op jit(solution)/shard_map/ppermute | solution.py:19
  18.3 2.1 %collective-permute-done.3 = f32[25,10,1]{2,0,1:T(8,128)S(1)} collective-permute-done((f32[25,10,1]{2,0,1:T(8,128)S(1)}, f32[25,10,1]{2,0,1:T(8,128)S(1)}, u32[]{:S(2)}, u32[]{:S(2)}) %collective-permute-start.3) | collective-permute-done | bytes 1032 | tf_op jit(solution)/shard_map/ppermute | solution.py:21
  21.6 2.8 %broadcast_divide_fusion.1 = (f32[2,12,8,128]{1,3,2,0:T(8,128)S(1)}, f32[2,12,8,128]{1,3,2,0:T(8,128)}, f32[2,12,8,128]{1,3,2,0:T(8,128)S(1)}) fusion(f32[8,128]{1,0:T(8,128)S(1)} %get-tuple-element.181, f32[2,12,10,130]{1,3,2,0:T(8,128)S(1)} %scatter.31, f32[8,128]{1,0:T(8,128)S(1)} %get-tuple-element.185, f32[8,128]{1,0:T(8,128)S(1)} %get-tuple-element.184, ...), kind=kLoop, calls=%fused_computation.62 | loop fusion | flops 270336 | bytes 905216 | tf_op jit(solution)/shard_map/div | solution.py:156
  25.4 1.7 %collective-permute-start.5 = (f32[72,1,128]{2,1,0:T(1,128)S(1)}, f32[72,1,128]{2,1,0:T(1,128)S(1)}, u32[]{:S(2)}, u32[]{:S(2)}) collective-permute-start(f32[72,1,128]{2,1,0:T(1,128)S(1)} %get-tuple-element.205), channel_id=1, source_target_pairs={{8,0},{16,8},{24,16},{0,24},{9,1},{17,9},{25,17},{1,25},{10,2},{18... | collective-permute-start | bytes 110600 | tf_op jit(solution)/shard_map/ppermute | solution.py:21
  30.0 1.3 %copy.216 = f32[72,10,1]{0,2,1:T(1,128)S(1)} copy(f32[72,10,1]{2,1,0:T(8,128)} %get-tuple-element.202) | data formatting | bytes 5760 | tf_op jit(solution)/shard_map/slice | solution.py:16
  31.8 4.5 %collective-permute-start.7 = (f32[72,10,1]{0,2,1:T(1,128)S(1)}, f32[72,10,1]{0,2,1:T(1,128)S(1)}, u32[]{:S(2)}, u32[]{:S(2)}) collective-permute-start(f32[72,10,1]{0,2,1:T(1,128)S(1)} %copy.217), channel_id=1, source_target_pairs={{1,0},{2,1},{3,2},{4,3},{5,4},{6,5},{7,6},{0,7},{9,8},{10,9},{11,1... | collective-permute-start | bytes 8648 | tf_op jit(solution)/shard_map/ppermute | solution.py:21
  36.2 1.4 %copy.213 = f32[2,12,8,128]{1,3,2,0:T(8,128)} copy(f32[2,12,8,128]{3,2,1,0:T(8,128)S(1)} %copy-done.5) | data formatting | bytes 196608 | tf_op args[1]
  37.9 1.1 copy.219
  39.0 3.0 %pad_maximum_fusion = f32[72,10,130]{2,1,0:T(8,128)} fusion(f32[72,10,1]{2,1,0:T(8,128)} %copy.219, f32[72,1,128]{2,1,0:T(1,128)S(1)} %collective-permute-done.5, f32[72,8,128]{2,1,0:T(8,128)S(1)} %bitcast.123, f32[72,1,128]{2,1,0:T(1,128)S(1)} %collective-permute-done.4, f32[72,10,1]{2,1,0:T(8,128)S(1)} %copy.218), kind=kLoop, calls=%fused_computation.7 | loop fusion | flops 374400 | bytes 748800 | tf_op jit(solution)/shard_map/concatenate | solution.py:17
  42.0 1.8 %copy.223 = f32[2,36,10,130]{1,3,2,0:T(8,128)S(1)} copy(f32[2,36,10,130]{3,2,1,0:T(8,128)} %bitcast.119) | data formatting | bytes 748800 | tf_op jit(solution)/shard_map/reshape | solution.py:162
  44.3 1.8 %fusion.10 = f32[2,36,8,128]{1,3,2,0:T(8,128)S(1)} fusion(f32[2,36,10,130]{1,3,2,0:T(8,128)S(1)} %scatter.39, f32[8,128]{1,0:T(8,128)} %copy-done.8, f32[8,128]{1,0:T(8,128)} %copy-done.7, f32[8,128]{1,0:T(8,128)S(1)} %get-tuple-element.183, f32[8,128]{1,0:T(8,128)S(1)} %get-tuple-element.182, f32[8,128]{1,0:T(8,128)S(1)} %get-tuple-element.181), kind=kLoop, calls=%fused_computation.28 | loop fusion | flops 663552 | bytes 1789952 | tf_op jit(solution)/shard_map/sub | solution.py:59
  46.2 1.1 %pad_maximum_fusion.1 = (f32[2,48,8,128]{1,3,2,0:T(8,128)S(1)}, f32[2,48,8,128]{1,3,2,0:T(8,128)S(1)}) fusion(f32[2,12,8,128]{1,3,2,0:T(8,128)S(1)} %copy-done.3, f32[2,12,8,128]{1,3,2,0:T(8,128)S(1)} %get-tuple-element.210, f32[2,12,8,128]{1,3,2,0:T(8,128)S(1)} %get-tuple-element.179, f32[2,12,8,128]{1,3,2,0:T(8,128)S(1)} %copy-done, ...), kind=kLoop, calls=%fused_computation.44 | loop fusion | flops 393216 | bytes 1572864 | tf_op jit(solution)/shard_map/concatenate | solution.py:167
  47.3 1.1 convolution_bitcast_fusion.2
  49.5 1.1 fusion.5
  51.6 1.8 %convolution_bitcast_fusion.5 = f32[48,48]{1,0:T(8,128)S(1)} fusion(f32[2,48,1024]{1,2,0:T(8,128)S(1)} %bitcast.117), kind=kOutput, calls=%fused_computation.18 | convolution fusion | flops 56623104 | bytes 402432 | tf_op jit(solution)/shard_map/pjc,pkc->jk/dot_general | solution.py:66
  53.4 1.8 %convolution_bitcast_fusion.6 = f32[48,48]{1,0:T(8,128)S(1)} fusion(f32[2,48,1024]{1,2,0:T(8,128)S(1)} %bitcast.118, f32[2,48,1024]{1,2,0:T(8,128)S(1)} %bitcast.120), kind=kOutput, calls=%fused_computation.19 | convolution fusion | flops 56623104 | bytes 795648 | tf_op jit(solution)/shard_map/pjc,pkc->jk/dot_general | solution.py:66
  55.2 40.8 %all-reduce.2 = (f32[48,48]{1,0:T(8,128)S(1)}, f32[48,48]{1,0:T(8,128)S(1)}, f32[48,48]{1,0:T(8,128)S(1)}, f32[48,48]{1,0:T(8,128)S(1)}) all-reduce(f32[48,48]{1,0:T(8,128)S(1)} %convolution_bitcast_fusion.5, f32[48,48]{1,0:T(8,128)S(1)} %convolution_bitcast_fusion.6, ...), channel_id=1, replica_groups=mesh['row'=4,'col'=8] {'row','col'}, use_global_device_ids=true, to_apply=%region_2.3 | all-reduce | flops 9216 | bytes 73728 | tf_op jit(solution)/shard_map/psum | solution.py:171
  101.5 3.7 %while.21 = (s32[]{:T(128)}, f32[72,72]{0,1:T(8,128)S(1)}, f32[72,72]{1,0:T(8,128)S(1)}, s32[]{:T(128)}) while((s32[]{:T(128)}, f32[72,72]{0,1:T(8,128)S(1)}, f32[72,72]{1,0:T(8,128)S(1)}, s32[]{:T(128)}) %tuple.94), condition=%wide.region_6.7_spmd.clone, body=%wide.region_5.6_spmd.clone.sunk | while | flops 13457666 | bytes 269621 | solution.py:90
  105.9 1.1 copy-done.1
  (134 shorter events, 26.8 us)
Async XLA Ops:
  0.6 13.7 %copy-start.6 = (f32[2,12,8,128]{3,2,1,0:T(8,128)S(1)}, f32[2,12,8,128]{3,2,1,0:T(8,128)}, u32[]{:S(2)}) copy-start(f32[2,12,8,128]{3,2,1,0:T(8,128)} %param.23) | copy-start | bytes 294916
  3.1 4.7 %collective-permute-start = (f32[25,1,128]{2,0,1:T(8,128)S(1)}, f32[25,1,128]{2,0,1:T(8,128)S(1)}, u32[]{:S(2)}, u32[]{:S(2)}) collective-permute-start(f32[25,1,128]{2,0,1:T(8,128)S(1)} %get-tuple-element.208), channel_id=1, source_target_pairs={{0,8},{8,16},{16,24},{24,0},{1,9},{9,17},{17,25},{25,1},{2,10},{10... | collective-permute-start | bytes 38408 | tf_op jit(solution)/shard_map/ppermute | solution.py:19
  3.6 4.2 %collective-permute-start.1 = (f32[25,1,128]{2,0,1:T(8,128)S(1)}, f32[25,1,128]{2,0,1:T(8,128)S(1)}, u32[]{:S(2)}, u32[]{:S(2)}) collective-permute-start(f32[25,1,128]{2,0,1:T(8,128)S(1)} %get-tuple-element.209), channel_id=1, source_target_pairs={{8,0},{16,8},{24,16},{0,24},{9,1},{17,9},{25,17},{1,25},{10,2},{18... | collective-permute-start | bytes 38408 | tf_op jit(solution)/shard_map/ppermute | solution.py:21
  7.9 10.3 %collective-permute-start.2 = (f32[25,10,1]{2,0,1:T(8,128)S(1)}, f32[25,10,1]{2,0,1:T(8,128)S(1)}, u32[]{:S(2)}, u32[]{:S(2)}) collective-permute-start(f32[25,10,1]{2,0,1:T(8,128)S(1)} %get-tuple-element.206), channel_id=1, source_target_pairs={{0,1},{1,2},{2,3},{3,4},{4,5},{5,6},{6,7},{7,0},{8,9},{9,10},{10,1... | collective-permute-start | bytes 3008 | tf_op jit(solution)/shard_map/ppermute | solution.py:19
  10.2 10.1 %collective-permute-start.3 = (f32[25,10,1]{2,0,1:T(8,128)S(1)}, f32[25,10,1]{2,0,1:T(8,128)S(1)}, u32[]{:S(2)}, u32[]{:S(2)}) collective-permute-start(f32[25,10,1]{2,0,1:T(8,128)S(1)} %get-tuple-element.207), channel_id=1, source_target_pairs={{1,0},{2,1},{3,2},{4,3},{5,4},{6,5},{7,6},{0,7},{9,8},{10,9},{11,1... | collective-permute-start | bytes 3008 | tf_op jit(solution)/shard_map/ppermute | solution.py:21
  21.5 2.9 %copy-start.7 = (f32[8,128]{1,0:T(8,128)}, f32[8,128]{1,0:T(8,128)S(1)}, u32[]{:S(2)}) copy-start(f32[8,128]{1,0:T(8,128)S(1)} %get-tuple-element.184) | copy-start | bytes 12292
  21.5 2.9 %copy-start.8 = (f32[8,128]{1,0:T(8,128)}, f32[8,128]{1,0:T(8,128)S(1)}, u32[]{:S(2)}) copy-start(f32[8,128]{1,0:T(8,128)S(1)} %get-tuple-element.185) | copy-start | bytes 12292
  24.4 0.9 copy-start.5
  25.4 3.4 %collective-permute-start.4 = (f32[72,1,128]{2,1,0:T(1,128)S(1)}, f32[72,1,128]{2,1,0:T(1,128)S(1)}, u32[]{:S(2)}, u32[]{:S(2)}) collective-permute-start(f32[72,1,128]{2,1,0:T(1,128)S(1)} %get-tuple-element.204), channel_id=1, source_target_pairs={{0,8},{8,16},{16,24},{24,0},{1,9},{9,17},{17,25},{25,1},{2,10},{10... | collective-permute-start | bytes 110600 | tf_op jit(solution)/shard_map/ppermute | solution.py:19
  25.4 3.4 %collective-permute-start.5 = (f32[72,1,128]{2,1,0:T(1,128)S(1)}, f32[72,1,128]{2,1,0:T(1,128)S(1)}, u32[]{:S(2)}, u32[]{:S(2)}) collective-permute-start(f32[72,1,128]{2,1,0:T(1,128)S(1)} %get-tuple-element.205), channel_id=1, source_target_pairs={{8,0},{16,8},{24,16},{0,24},{9,1},{17,9},{25,17},{1,25},{10,2},{18... | collective-permute-start | bytes 110600 | tf_op jit(solution)/shard_map/ppermute | solution.py:21
  31.2 6.4 %collective-permute-start.6 = (f32[72,10,1]{0,2,1:T(1,128)S(1)}, f32[72,10,1]{0,2,1:T(1,128)S(1)}, u32[]{:S(2)}, u32[]{:S(2)}) collective-permute-start(f32[72,10,1]{0,2,1:T(1,128)S(1)} %copy.216), channel_id=1, source_target_pairs={{0,1},{1,2},{2,3},{3,4},{4,5},{5,6},{6,7},{7,0},{8,9},{9,10},{10,1... | collective-permute-start | bytes 8648 | tf_op jit(solution)/shard_map/ppermute | solution.py:19
  31.8 6.2 %collective-permute-start.7 = (f32[72,10,1]{0,2,1:T(1,128)S(1)}, f32[72,10,1]{0,2,1:T(1,128)S(1)}, u32[]{:S(2)}, u32[]{:S(2)}) collective-permute-start(f32[72,10,1]{0,2,1:T(1,128)S(1)} %copy.217), channel_id=1, source_target_pairs={{1,0},{2,1},{3,2},{4,3},{5,4},{6,5},{7,6},{0,7},{9,8},{10,9},{11,1... | collective-permute-start | bytes 8648 | tf_op jit(solution)/shard_map/ppermute | solution.py:21
  44.3 1.8 %copy-start = (f32[2,12,8,128]{1,3,2,0:T(8,128)S(1)}, f32[2,12,8,128]{1,3,2,0:T(8,128)}, u32[]{:S(2)}) copy-start(f32[2,12,8,128]{1,3,2,0:T(8,128)} %copy.212) | copy-start | bytes 294916
  44.3 1.8 %copy-start.2 = (f32[2,12,8,128]{1,3,2,0:T(8,128)S(1)}, f32[2,12,8,128]{1,3,2,0:T(8,128)}, u32[]{:S(2)}) copy-start(f32[2,12,8,128]{1,3,2,0:T(8,128)} %get-tuple-element.180) | copy-start | bytes 294916
  44.3 1.9 %copy-start.3 = (f32[2,12,8,128]{1,3,2,0:T(8,128)S(1)}, f32[2,12,8,128]{1,3,2,0:T(8,128)}, u32[]{:S(2)}) copy-start(f32[2,12,8,128]{1,3,2,0:T(8,128)} %copy.213) | copy-start | bytes 294916
  53.4 44.7 %copy-start.9 = (f32[12,12]{1,0:T(8,128)S(1)}, f32[12,12]{1,0:T(8,128)}, u32[]{:S(2)}) copy-start(f32[12,12]{1,0:T(8,128)} %fusion.47) | copy-start | bytes 1732
  105.7 1.2 %copy-start.1 = (f32[2,12,8,128]{1,3,2,0:T(8,128)S(1)}, f32[2,12,8,128]{1,3,2,0:T(8,128)}, u32[]{:S(2)}) copy-start(f32[2,12,8,128]{1,3,2,0:T(8,128)} %copy.212) | copy-start | bytes 294916
  105.7 1.5 %copy-start.4 = (f32[2,12,8,128]{1,3,2,0:T(8,128)S(1)}, f32[2,12,8,128]{1,3,2,0:T(8,128)}, u32[]{:S(2)}) copy-start(f32[2,12,8,128]{1,3,2,0:T(8,128)} %copy.213) | copy-start | bytes 294916
where the time goes:
time: 114 us
  blocking collectives  40.8 us (36%)
  local copies, waits for them, and re-layouts  17.8 us (16%)
  matrix products  17.8 us (16%)
  starting transfers between devices  14.4 us (13%)
  other arithmetic  13.1 us (11%)
  waiting for transfers between devices  5.71 us (5%)
  between operations  3.93 us (3%)
    psum x1, blocking collectives, body(): lax.psum((local_gram[0], local_gram[1], local_ham[0], local_ham[1]), ('ro...  40.8 us
    ppermute x4, starting transfers between devices, with_halo(): lax.ppermute(head, axis, [((i + 1) % count, i) for i in range(count)])  11.3 us
    unnamed x26, local copies, waits for them, and re-layouts  5.86 us
    ppermute x4, waiting for transfers between devices, with_halo(): lax.ppermute(tail, axis, [(i, (i + 1) % count) for i in range(count)])  3.62 us
    dot_general x2, matrix products, complex_gram(): jnp.einsum('pjc,pkc->jk', first_flat, second_flat, precision=highest)  3.6 us
    concatenate x4, other arithmetic, with_halo(): jnp.concatenate([lax.ppermute(tail, axis, [(i, (i + 1) % count) for i in...  3.24 us
    ppermute x4, starting transfers between devices, with_halo(): lax.ppermute(tail, axis, [(i, (i + 1) % count) for i in range(count)])  3.13 us
    div x1, other arithmetic, body(): applied_cycle / diagonal_cycle  2.78 us
  transfers between devices with their start and end apart: 8, of which 3 were waited for; matrix products, arithmetic and copies ran while one was open for 5% of the time, Pallas kernels for 0%

commit v1 on v0

--- a/solution.py
+++ b/solution.py
@@ -7,22 +7,6 @@
 
 KDEN = 16
 NS_STEPS = 5
-
-
-def with_halo(cells, sides, width):
-    for axis, dim in sides:
-        count = lax.axis_size(axis)
-        head = lax.slice_in_dim(cells, 0, width, axis=dim)
-        tail = lax.slice_in_dim(cells, cells.shape[dim] - width, cells.shape[dim], axis=dim)
-        cells = jnp.concatenate(
-            [
-                lax.ppermute(tail, axis, [(i, (i + 1) % count) for i in range(count)]),
-                cells,
-                lax.ppermute(head, axis, [((i + 1) % count, i) for i in range(count)]),
-            ],
-            axis=dim,
-        )
-    return cells
 
 
 def rotate(values, phase_angle):
@@ -31,15 +15,6 @@
     return jnp.stack(
         [values[0] * cosine - values[1] * sine_part, values[0] * sine_part + values[1] * cosine]
     )
-
-
-def bloch_rims(padded, edges, rim_layers):
-    low_row, high_row, low_col, high_col = edges
-    padded = padded.at[:, :, :rim_layers].set(rotate(padded[:, :, :rim_layers], low_row))
-    padded = padded.at[:, :, -rim_layers:].set(rotate(padded[:, :, -rim_layers:], high_row))
-    padded = padded.at[:, :, :, :rim_layers].set(rotate(padded[:, :, :, :rim_layers], low_col))
-    padded = padded.at[:, :, :, -rim_layers:].set(rotate(padded[:, :, :, -rim_layers:], high_col))
-    return padded
 
 
 def stencil(padded, stiff_pad):
@@ -125,6 +100,50 @@
     return jnp.dot(mixing.T, jnp.dot(matrix, mixing, precision=highest), precision=highest)
 
 
+def exchange_rim(cells, axis, dim, width, low_angle, high_angle):
+    count = lax.axis_size(axis)
+    head = lax.slice_in_dim(cells, 0, width, axis=dim)
+    tail = lax.slice_in_dim(cells, cells.shape[dim] - width, cells.shape[dim], axis=dim)
+    before = lax.ppermute(tail, axis, [(i, (i + 1) % count) for i in range(count)])
+    after = lax.ppermute(head, axis, [((i + 1) % count, i) for i in range(count)])
+    return jnp.concatenate(
+        [rotate_rim(before, low_angle), cells, rotate_rim(after, high_angle)], axis=dim
+    )
+
+
+def rotate_rim(rim, phase_angle):
+    field_part = rim[:-1].reshape((2, -1) + rim.shape[1:])
+    turned = rotate(field_part, phase_angle).reshape((-1,) + rim.shape[1:])
+    return jnp.concatenate([turned, rim[-1:]], axis=0)
+
+
+def tree_sum(value, axis):
+    count = lax.axis_size(axis)
+    if count & (count - 1):
+        return lax.psum(value, axis)
+    step = 1
+    while step < count:
+        value = value + lax.ppermute(value, axis, [(i, i ^ step) for i in range(count)])
+        step *= 2
+    return value
+
+
+def pack_hermitian(real_part, imag_part):
+    order_size = real_part.shape[0]
+    upper = jnp.arange(order_size)[:, None] <= jnp.arange(order_size)[None, :]
+    return jnp.where(upper, real_part, imag_part)
+
+
+def unpack_hermitian(packed):
+    order_size = packed.shape[0]
+    upper = jnp.arange(order_size)[:, None] <= jnp.arange(order_size)[None, :]
+    strict_upper = jnp.arange(order_size)[:, None] < jnp.arange(order_size)[None, :]
+    real_upper = jnp.where(upper, packed, 0.0)
+    real_part = real_upper + jnp.where(strict_upper, packed, 0.0).T
+    imag_lower = jnp.where(upper, 0.0, packed)
+    return (real_part, imag_lower - imag_lower.T)
+
+
 def body(bands, directions, materials, permittivity, wavevector):
     band_count = bands.shape[1]
     height = bands.shape[2]
@@ -140,37 +159,51 @@
     angle_col = 2.0 * math.pi * wavevector[1].astype(jnp.float32) / KDEN
     row_index = lax.axis_index("row")
     col_index = lax.axis_index("col")
-    edges = (
+    fields = jnp.concatenate([bands, directions], axis=1)
+    packed = jnp.concatenate(
+        [fields.reshape(4 * band_count, height, breadth), stiffness[None]], axis=0
+    )
+    padded = exchange_rim(
+        packed,
+        "row",
+        1,
+        2,
         jnp.where(row_index == 0, -angle_row, 0.0),
         jnp.where(row_index == lax.axis_size("row") - 1, angle_row, 0.0),
+    )
+    padded = exchange_rim(
+        padded,
+        "col",
+        2,
+        2,
         jnp.where(col_index == 0, -angle_col, 0.0),
         jnp.where(col_index == lax.axis_size("col") - 1, angle_col, 0.0),
     )
-    packed = jnp.concatenate(
-        [bands.reshape(2 * band_count, height, breadth), stiffness[None]], axis=0
-    )
-    padded = with_halo(packed, (("row", 1), ("col", 2)), 1)
-    stiff_cycle = padded[-1]
-    band_pad = bloch_rims(padded[:-1].reshape(2, band_count, height + 2, breadth + 2), edges, 1)
-    applied_cycle, diagonal_cycle = stencil(band_pad, stiff_cycle)
-    scaled_cycle = jnp.concatenate([applied_cycle / diagonal_cycle, bands / diagonal_cycle], axis=1)
-    stacked = jnp.concatenate([scaled_cycle, directions], axis=1)
-    columns_now = stacked.shape[1]
-    field_pad = with_halo(
-        stacked.reshape(2 * columns_now, height, breadth), (("row", 1), ("col", 2)), 1
-    )
-    field_pad = bloch_rims(field_pad.reshape(2, columns_now, height + 2, breadth + 2), edges, 1)
-    extra_applied = stencil(field_pad, stiff_cycle)[0]
-    scaled_image = scaled_cycle[:, :band_count]
-    scaled_bands = scaled_cycle[:, band_count:]
-    extra = jnp.concatenate([scaled_image, scaled_bands, directions], axis=1)
-    extended = jnp.concatenate([bands, extra], axis=1)
+    stiff_wide = padded[-1]
+    field_wide = padded[:-1].reshape(2, 2 * band_count, height + 4, breadth + 4)
+    band_wide = field_wide[:, :band_count]
+    applied_ring, diagonal_ring = stencil(band_wide, stiff_wide)
+    stiff_ring = stiff_wide[1:-1, 1:-1]
+    scaled_ring = jnp.concatenate(
+        [
+            applied_ring / diagonal_ring,
+            band_wide[:, :, 1:-1, 1:-1] / diagonal_ring,
+            field_wide[:, band_count:, 1:-1, 1:-1],
+        ],
+        axis=1,
+    )
+    extra_applied = stencil(scaled_ring, stiff_ring)[0]
+    applied_cycle = applied_ring[:, :, 1:-1, 1:-1]
+    scaled_image = scaled_ring[:, :band_count, 1:-1, 1:-1]
+    scaled_bands = scaled_ring[:, band_count : 2 * band_count, 1:-1, 1:-1]
+    extended = jnp.concatenate([bands, scaled_image, scaled_bands, directions], axis=1)
     extended_applied = jnp.concatenate([applied_cycle, extra_applied], axis=1)
     local_gram = complex_gram(extended, extended)
     local_ham = complex_gram(extended, extended_applied)
-    gram_whole, gram_imag_whole, ham_whole, ham_imag_whole = lax.psum(
-        (local_gram[0], local_gram[1], local_ham[0], local_ham[1]), ("row", "col")
-    )
+    summed = jnp.stack([pack_hermitian(*local_gram), pack_hermitian(*local_ham)])
+    summed = tree_sum(tree_sum(summed, "row"), "col")
+    gram_whole, gram_imag_whole = unpack_hermitian(summed[0])
+    ham_whole, ham_imag_whole = unpack_hermitian(summed[1])
     quotient = jnp.diagonal(ham_whole)[:band_count] / jnp.diagonal(gram_whole)[:band_count]
     identity = jnp.eye(band_count, dtype=jnp.float32)
     zeros_block = jnp.zeros((band_count, band_count), jnp.float32)

time: 114 us -> 65.9 us (0.58)
  blocking collectives: 40.8 us -> 0 us
  waiting for transfers between devices: 5.71 us -> 24.3 us
  local copies, waits for them, and re-layouts: 17.8 us -> 6.3 us
  other arithmetic: 13.1 us -> 4.43 us
  matrix products: 17.8 us -> 10.9 us
    psum x1 -> x0, blocking collectives: 40.8 us -> none  [body(): lax.psum((local_gram[0], local_gram[1], local_ham[0], local_ham[1]), ('ro...]
    ppermute x8 -> x9, waiting for transfers between devices: 5.71 us -> 24.3 us  [the longest x5 11.1 us: tree_sum(): lax.ppermute(value, axis, [(i, i ^ step) for i in range(count)])]
    unnamed x26 -> x14, local copies, waits for them, and re-layouts: 5.86 us -> 2.18 us
    reshape x4 -> x2, local copies, waits for them, and re-layouts: 3.34 us -> 0.04 us  [rotate_rim(): turned = rotate(field_part, phase_angle).reshape((-1,) + rim.shape[1:])]
    concatenate x6 -> x5, other arithmetic: 4.4 us -> 1.44 us  [the longest x1 0.96 us: body(): fields = jnp.concatenate([bands, directions], axis=1)]
    dot_general x2, matrix products: 3.6 us -> 0.98 us  [complex_gram(): jnp.einsum('pjc,pkc->jk', first_flat, second_flat, precision=highest)]
    div x1, other arithmetic: 2.78 us -> 0.23 us  [body(): applied_ring / diagonal_ring]
    slice x5 -> x9, local copies, waits for them, and re-layouts: 2.67 us -> 0.95 us  [the longest x1 0.49 us: stencil(): padded[:, :, :-2, 1:-1]]
  transfers between devices with their start and end apart: 8 -> 9, of which waited for: 3 -> 9; matrix products, arithmetic and copies ran while one was open for 5% -> 1% of each run, Pallas kernels for 0% -> 0%
where the time goes in v1:
time: 65.9 us; the launch traced here: 65.2 us
  waiting for transfers between devices  24.3 us (37%)
  starting transfers between devices  15.1 us (23%)
  matrix products  10.9 us (17%)
  local copies, waits for them, and re-layouts  6.3 us (10%)
  other arithmetic  4.43 us (7%)
  between operations  3.91 us (6%)
    ppermute x5, waiting for transfers between devices, tree_sum(): lax.ppermute(value, axis, [(i, i ^ step) for i in range(count)])  11.1 us
    ppermute x5, starting transfers between devices, tree_sum(): lax.ppermute(value, axis, [(i, i ^ step) for i in range(count)])  8 us
    ppermute x2, waiting for transfers between devices, exchange_rim(): lax.ppermute(tail, axis, [(i, (i + 1) % count) for i in range(count)])  7.36 us
    ppermute x2, starting transfers between devices, exchange_rim(): lax.ppermute(head, axis, [((i + 1) % count, i) for i in range(count)])  7.04 us
    ppermute x2, waiting for transfers between devices, exchange_rim(): lax.ppermute(head, axis, [((i + 1) % count, i) for i in range(count)])  5.92 us
    unnamed x14, local copies, waits for them, and re-layouts  2.18 us
  transfers between devices with their start and end apart: 9, of which 9 were waited for; matrix products, arithmetic and copies ran while one was open for 1% of the time, Pallas kernels for 0%

profile of v1, /device:TPU:0, one launch (start us, length us, event | category | flops | bytes accessed | tf_op | source)
XLA Modules:
  0.0 65.2 jit_solution(9856301800121756568)
XLA Ops:
  0.6 0.7 %broadcast_divide_fusion.3 = f32[8]{0:T(128)S(1)} fusion(f32[8]{0:T(128)} %param.10), kind=kLoop, calls=%fused_computation.172 | loop fusion | flops 8 | bytes 64 | tf_op jit(solution)/shard_map/div | solution.py:154
  1.3 1.0 %pad_maximum_fusion.11 = f32[2,24,8,128]{3,2,1,0:T(8,128)S(1)} fusion(f32[2,12,8,128]{3,2,1,0:T(8,128)} %param.8, f32[2,12,8,128]{3,2,1,0:T(8,128)} %param.7), kind=kLoop, calls=%fused_computation.81 | loop fusion | flops 49152 | bytes 393216 | tf_op jit(solution)/shard_map/concatenate | solution.py:162
  2.3 0.6 copy-done.2
  3.0 2.5 %collective-permute-start.1 = (f32[49,2,128]{2,0,1:T(8,128)S(1)}, f32[49,2,128]{2,0,1:T(8,128)S(1)}, u32[]{:S(2)}, u32[]{:S(2)}) collective-permute-start(f32[49,2,128]{2,0,1:T(8,128)S(1)} %get-tuple-element.90), channel_id=1, source_target_pairs={{8,0},{16,8},{24,16},{0,24},{9,1},{17,9},{25,17},{1,25},{10,2},{18... | collective-permute-start | bytes 150536 | tf_op jit(solution)/shard_map/ppermute | solution.py:108
  7.1 0.7 %collective-permute-done.1 = f32[49,2,128]{2,0,1:T(8,128)S(1)} collective-permute-done((f32[49,2,128]{2,0,1:T(8,128)S(1)}, f32[49,2,128]{2,0,1:T(8,128)S(1)}, u32[]{:S(2)}, u32[]{:S(2)}) %collective-permute-start.1) | collective-permute-done | bytes 50208 | tf_op jit(solution)/shard_map/ppermute | solution.py:108
  7.8 1.3 %collective-permute-done = f32[49,2,128]{2,0,1:T(8,128)S(1)} collective-permute-done((f32[49,2,128]{2,0,1:T(8,128)S(1)}, f32[49,2,128]{2,0,1:T(8,128)S(1)}, u32[]{:S(2)}, u32[]{:S(2)}) %collective-permute-start) | collective-permute-done | bytes 50208 | tf_op jit(solution)/shard_map/ppermute | solution.py:107
  9.4 4.6 %collective-permute-start.3 = (f32[49,12,2]{2,0,1:T(8,128)S(1)}, f32[49,12,2]{2,0,1:T(8,128)S(1)}, u32[]{:S(2)}, u32[]{:S(2)}) collective-permute-start(f32[49,12,2]{2,0,1:T(8,128)S(1)} %get-tuple-element.86), channel_id=1, source_target_pairs={{1,0},{2,1},{3,2},{4,3},{5,4},{6,5},{7,6},{0,7},{9,8},{10,9},{11,1... | collective-permute-start | bytes 14120 | tf_op jit(solution)/shard_map/ppermute | solution.py:108
  15.2 5.2 %collective-permute-done.3 = f32[49,12,2]{2,0,1:T(8,128)S(1)} collective-permute-done((f32[49,12,2]{2,0,1:T(8,128)S(1)}, f32[49,12,2]{2,0,1:T(8,128)S(1)}, u32[]{:S(2)}, u32[]{:S(2)}) %collective-permute-start.3) | collective-permute-done | bytes 4736 | tf_op jit(solution)/shard_map/ppermute | solution.py:108
  20.5 6.0 %collective-permute-done.2 = f32[49,12,2]{2,0,1:T(8,128)S(1)} collective-permute-done((f32[49,12,2]{2,0,1:T(8,128)S(1)}, f32[49,12,2]{2,0,1:T(8,128)S(1)}, u32[]{:S(2)}, u32[]{:S(2)}) %collective-permute-start.2) | collective-permute-done | bytes 4736 | tf_op jit(solution)/shard_map/ppermute | solution.py:107
  31.4 1.2 %collective-permute-done.4 = f32[2,48,48]{2,1,0:T(8,128)S(1)} collective-permute-done((f32[2,48,48]{2,1,0:T(8,128)S(1)}, f32[2,48,48]{2,1,0:T(8,128)S(1)}, u32[]{:S(2)}, u32[]{:S(2)}) %collective-permute-start.4) | collective-permute-done | bytes 18464 | tf_op jit(solution)/shard_map/ppermute | solution.py:126
  32.6 2.4 %collective-permute-start.5 = (f32[2,48,48]{2,1,0:T(8,128)S(1)}, f32[2,48,48]{2,1,0:T(8,128)S(1)}, u32[]{:S(2)}, u32[]{:S(2)}) collective-permute-start(f32[2,48,48]{2,1,0:T(8,128)S(1)} %fusion.75), channel_id=1, source_target_pairs={{0,16},{8,24},{16,0},{24,8},{1,17},{9,25},{17,1},{25,9},{2,18},{10... | collective-permute-start | bytes 55304 | tf_op jit(solution)/shard_map/ppermute | solution.py:126
  35.0 2.1 %collective-permute-done.5 = f32[2,48,48]{2,1,0:T(8,128)S(1)} collective-permute-done((f32[2,48,48]{2,1,0:T(8,128)S(1)}, f32[2,48,48]{2,1,0:T(8,128)S(1)}, u32[]{:S(2)}, u32[]{:S(2)}) %collective-permute-start.5) | collective-permute-done | bytes 18464 | tf_op jit(solution)/shard_map/ppermute | solution.py:126
  37.1 1.6 %collective-permute-start.6 = (f32[2,48,48]{2,1,0:T(8,128)S(1)}, f32[2,48,48]{2,1,0:T(8,128)S(1)}, u32[]{:S(2)}, u32[]{:S(2)}) collective-permute-start(f32[2,48,48]{2,1,0:T(8,128)S(1)} %fusion.116), channel_id=1, source_target_pairs={{0,1},{1,0},{2,3},{3,2},{4,5},{5,4},{6,7},{7,6},{8,9},{9,8},{10,11... | collective-permute-start | bytes 55304 | tf_op jit(solution)/shard_map/ppermute | solution.py:126
  38.7 2.5 %collective-permute-done.6 = f32[2,48,48]{2,1,0:T(8,128)S(1)} collective-permute-done((f32[2,48,48]{2,1,0:T(8,128)S(1)}, f32[2,48,48]{2,1,0:T(8,128)S(1)}, u32[]{:S(2)}, u32[]{:S(2)}) %collective-permute-start.6) | collective-permute-done | bytes 18464 | tf_op jit(solution)/shard_map/ppermute | solution.py:126
  41.2 1.2 %collective-permute-start.7 = (f32[2,48,48]{2,1,0:T(8,128)S(1)}, f32[2,48,48]{2,1,0:T(8,128)S(1)}, u32[]{:S(2)}, u32[]{:S(2)}) collective-permute-start(f32[2,48,48]{2,1,0:T(8,128)S(1)} %add.141), channel_id=1, source_target_pairs={{0,2},{1,3},{2,0},{3,1},{4,6},{5,7},{6,4},{7,5},{8,10},{9,11},{10,... | collective-permute-start | bytes 55304 | tf_op jit(solution)/shard_map/ppermute | solution.py:126
  42.4 3.0 %collective-permute-done.7 = f32[2,48,48]{2,1,0:T(8,128)S(1)} collective-permute-done((f32[2,48,48]{2,1,0:T(8,128)S(1)}, f32[2,48,48]{2,1,0:T(8,128)S(1)}, u32[]{:S(2)}, u32[]{:S(2)}) %collective-permute-start.7) | collective-permute-done | bytes 18464 | tf_op jit(solution)/shard_map/ppermute | solution.py:126
  45.4 2.7 %collective-permute-start.8 = (f32[2,48,48]{2,1,0:T(8,128)S(1)}, f32[2,48,48]{2,1,0:T(8,128)S(1)}, u32[]{:S(2)}, u32[]{:S(2)}) collective-permute-start(f32[2,48,48]{2,1,0:T(8,128)S(1)} %add.142), channel_id=1, source_target_pairs={{0,4},{1,5},{2,6},{3,7},{4,0},{5,1},{6,2},{7,3},{8,12},{9,13},{10,... | collective-permute-start | bytes 55304 | tf_op jit(solution)/shard_map/ppermute | solution.py:126
  48.1 2.3 %collective-permute-done.8 = f32[2,48,48]{2,1,0:T(8,128)S(1)} collective-permute-done((f32[2,48,48]{2,1,0:T(8,128)S(1)}, f32[2,48,48]{2,1,0:T(8,128)S(1)}, u32[]{:S(2)}, u32[]{:S(2)}) %collective-permute-start.8) | collective-permute-done | bytes 18464 | tf_op jit(solution)/shard_map/ppermute | solution.py:126
  50.6 1.0 %gather_fusion.1 = f32[48]{0:T(128)S(1)} fusion(f32[48,48]{0,1:T(8,128)S(1)} %get-tuple-element.98, s32[48]{0:T(128)S(1)} %or_bitcast_fusion), kind=kCustom, calls=%fused_computation.1 | custom fusion | bytes 768 | tf_op jit(solution)/shard_map/jit(diagonal)/cond/branch_0_fun/gather | solution.py:207
  51.6 1.0 %gather_fusion = f32[48]{0:T(128)S(1)} fusion(f32[48,48]{0,1:T(8,128)S(1)} %get-tuple-element.97, s32[48]{0:T(128)S(1)} %or_bitcast_fusion), kind=kCustom, calls=%fused_computation | custom fusion | bytes 768 | tf_op jit(solution)/shard_map/jit(diagonal)/cond/branch_0_fun/gather | solution.py:207
  54.1 0.7 %multiply_reduce_fusion = f32[]{:T(128)} fusion(f32[36,36]{1,0:T(8,128)S(1)} %fusion.80, f32[36,36]{1,0:T(8,128)S(1)} %get-tuple-element.104, f32[36,36]{1,0:T(8,128)S(1)} %get-tuple-element.103), kind=kLoop, calls=%fused_computation.100 | loop fusion | flops 25919 | bytes 15556 | tf_op jit(solution)/shard_map/reduce_sum | solution.py:54
  55.7 3.7 %while.13 = (s32[]{:T(128)}, f32[72,72]{0,1:T(8,128)S(1)}, f32[72,72]{1,0:T(8,128)S(1)}, s32[]{:T(128)}) while((s32[]{:T(128)}, f32[72,72]{0,1:T(8,128)S(1)}, f32[72,72]{1,0:T(8,128)S(1)}, s32[]{:T(128)}) %tuple.61), condition=%wide.region_3.4_spmd.clone, body=%wide.region_2.3_spmd.clone.sunk | while | flops 13457666 | bytes 269621 | solution.py:65
  61.9 0.8 %copy.172 = f32[2,36,8,128]{3,2,1,0:T(8,128)} copy(f32[2,36,8,128]{3,1,2,0:T(8,128)S(1)} %maximum_multiply_fusion) | data formatting | bytes 589824
  64.6 0.6 copy.173
  (128 shorter events, 15.5 us)
Async XLA Ops:
  2.2 0.7 %copy-start.2 = (s32[8,128]{1,0:T(8,128)S(1)}, s32[8,128]{1,0:T(8,128)}, u32[]{:S(2)}) copy-start(s32[8,128]{1,0:T(8,128)} %param.9) | copy-start | bytes 12292
  3.0 2.5 %copy-start.3 = (s32[2]{0:T(128)S(1)}, s32[2]{0:T(128)}, u32[]{:S(2)}) copy-start(s32[2]{0:T(128)} %param.11) | copy-start | bytes 28
  3.0 4.7 %collective-permute-start.1 = (f32[49,2,128]{2,0,1:T(8,128)S(1)}, f32[49,2,128]{2,0,1:T(8,128)S(1)}, u32[]{:S(2)}, u32[]{:S(2)}) collective-permute-start(f32[49,2,128]{2,0,1:T(8,128)S(1)} %get-tuple-element.90), channel_id=1, source_target_pairs={{8,0},{16,8},{24,16},{0,24},{9,1},{17,9},{25,17},{1,25},{10,2},{18... | collective-permute-start | bytes 150536 | tf_op jit(solution)/shard_map/ppermute | solution.py:108
  5.5 3.6 %collective-permute-start = (f32[49,2,128]{2,0,1:T(8,128)S(1)}, f32[49,2,128]{2,0,1:T(8,128)S(1)}, u32[]{:S(2)}, u32[]{:S(2)}) collective-permute-start(f32[49,2,128]{2,0,1:T(8,128)S(1)} %get-tuple-element.89), channel_id=1, source_target_pairs={{0,8},{8,16},{16,24},{24,0},{1,9},{9,17},{17,25},{25,1},{2,10},{10... | collective-permute-start | bytes 150536 | tf_op jit(solution)/shard_map/ppermute | solution.py:107
  9.2 4.8 %copy-start = (f32[2,12,8,128]{3,2,1,0:T(8,128)S(1)}, f32[2,12,8,128]{3,2,1,0:T(8,128)}, u32[]{:S(2)}) copy-start(f32[2,12,8,128]{3,2,1,0:T(8,128)} %param.8) | copy-start | bytes 294916
  9.4 11.1 %collective-permute-start.3 = (f32[49,12,2]{2,0,1:T(8,128)S(1)}, f32[49,12,2]{2,0,1:T(8,128)S(1)}, u32[]{:S(2)}, u32[]{:S(2)}) collective-permute-start(f32[49,12,2]{2,0,1:T(8,128)S(1)} %get-tuple-element.86), channel_id=1, source_target_pairs={{1,0},{2,1},{3,2},{4,3},{5,4},{6,5},{7,6},{0,7},{9,8},{10,9},{11,1... | collective-permute-start | bytes 14120 | tf_op jit(solution)/shard_map/ppermute | solution.py:108
  14.0 1.0 %copy-start.1 = (f32[2,12,8,128]{3,2,1,0:T(8,128)S(1)}, f32[2,12,8,128]{3,2,1,0:T(8,128)}, u32[]{:S(2)}) copy-start(f32[2,12,8,128]{3,2,1,0:T(8,128)} %param.7) | copy-start | bytes 294916
  15.2 11.4 %collective-permute-start.2 = (f32[49,12,2]{2,0,1:T(8,128)S(1)}, f32[49,12,2]{2,0,1:T(8,128)S(1)}, u32[]{:S(2)}, u32[]{:S(2)}) collective-permute-start(f32[49,12,2]{2,0,1:T(8,128)S(1)} %get-tuple-element.85), channel_id=1, source_target_pairs={{0,1},{1,2},{2,3},{3,4},{4,5},{5,6},{6,7},{7,0},{8,9},{9,10},{10,1... | collective-permute-start | bytes 14120 | tf_op jit(solution)/shard_map/ppermute | solution.py:107
  31.3 1.3 %collective-permute-start.4 = (f32[2,48,48]{2,1,0:T(8,128)S(1)}, f32[2,48,48]{2,1,0:T(8,128)S(1)}, u32[]{:S(2)}, u32[]{:S(2)}) collective-permute-start(f32[2,48,48]{2,1,0:T(8,128)S(1)} %pad_maximum_fusion.16), channel_id=1, source_target_pairs={{0,8},{8,0},{16,24},{24,16},{1,9},{9,1},{17,25},{25,17},{2,10},{10... | collective-permute-start | bytes 55304 | tf_op jit(solution)/shard_map/ppermute | solution.py:126
  32.6 4.5 %collective-permute-start.5 = (f32[2,48,48]{2,1,0:T(8,128)S(1)}, f32[2,48,48]{2,1,0:T(8,128)S(1)}, u32[]{:S(2)}, u32[]{:S(2)}) collective-permute-start(f32[2,48,48]{2,1,0:T(8,128)S(1)} %fusion.75), channel_id=1, source_target_pairs={{0,16},{8,24},{16,0},{24,8},{1,17},{9,25},{17,1},{25,9},{2,18},{10... | collective-permute-start | bytes 55304 | tf_op jit(solution)/shard_map/ppermute | solution.py:126
  37.1 4.2 %collective-permute-start.6 = (f32[2,48,48]{2,1,0:T(8,128)S(1)}, f32[2,48,48]{2,1,0:T(8,128)S(1)}, u32[]{:S(2)}, u32[]{:S(2)}) collective-permute-start(f32[2,48,48]{2,1,0:T(8,128)S(1)} %fusion.116), channel_id=1, source_target_pairs={{0,1},{1,0},{2,3},{3,2},{4,5},{5,4},{6,7},{7,6},{8,9},{9,8},{10,11... | collective-permute-start | bytes 55304 | tf_op jit(solution)/shard_map/ppermute | solution.py:126
  41.2 4.1 %collective-permute-start.7 = (f32[2,48,48]{2,1,0:T(8,128)S(1)}, f32[2,48,48]{2,1,0:T(8,128)S(1)}, u32[]{:S(2)}, u32[]{:S(2)}) collective-permute-start(f32[2,48,48]{2,1,0:T(8,128)S(1)} %add.141), channel_id=1, source_target_pairs={{0,2},{1,3},{2,0},{3,1},{4,6},{5,7},{6,4},{7,5},{8,10},{9,11},{10,... | collective-permute-start | bytes 55304 | tf_op jit(solution)/shard_map/ppermute | solution.py:126
  45.4 5.0 %collective-permute-start.8 = (f32[2,48,48]{2,1,0:T(8,128)S(1)}, f32[2,48,48]{2,1,0:T(8,128)S(1)}, u32[]{:S(2)}, u32[]{:S(2)}) collective-permute-start(f32[2,48,48]{2,1,0:T(8,128)S(1)} %add.142), channel_id=1, source_target_pairs={{0,4},{1,5},{2,6},{3,7},{4,0},{5,1},{6,2},{7,3},{8,12},{9,13},{10,... | collective-permute-start | bytes 55304 | tf_op jit(solution)/shard_map/ppermute | solution.py:126

commit v2 on v1

--- a/solution.py
+++ b/solution.py
@@ -104,8 +104,10 @@
     count = lax.axis_size(axis)
     head = lax.slice_in_dim(cells, 0, width, axis=dim)
     tail = lax.slice_in_dim(cells, cells.shape[dim] - width, cells.shape[dim], axis=dim)
-    before = lax.ppermute(tail, axis, [(i, (i + 1) % count) for i in range(count)])
-    after = lax.ppermute(head, axis, [((i + 1) % count, i) for i in range(count)])
+    before = lax.ppermute(tail.reshape(-1), axis, [(i, (i + 1) % count) for i in range(count)])
+    after = lax.ppermute(head.reshape(-1), axis, [((i + 1) % count, i) for i in range(count)])
+    before = before.reshape(tail.shape)
+    after = after.reshape(head.shape)
     return jnp.concatenate(
         [rotate_rim(before, low_angle), cells, rotate_rim(after, high_angle)], axis=dim
     )
@@ -201,7 +203,7 @@
     local_gram = complex_gram(extended, extended)
     local_ham = complex_gram(extended, extended_applied)
     summed = jnp.stack([pack_hermitian(*local_gram), pack_hermitian(*local_ham)])
-    summed = tree_sum(tree_sum(summed, "row"), "col")
+    summed = tree_sum(tree_sum(summed.reshape(-1), "row"), "col").reshape(summed.shape)
     gram_whole, gram_imag_whole = unpack_hermitian(summed[0])
     ham_whole, ham_imag_whole = unpack_hermitian(summed[1])
     quotient = jnp.diagonal(ham_whole)[:band_count] / jnp.diagonal(gram_whole)[:band_count]

time: 65.9 us -> 60.2 us (0.914)
  starting transfers between devices: 15.1 us -> 8.24 us
  local copies, waits for them, and re-layouts: 6.3 us -> 9.27 us
  waiting for transfers between devices: 24.3 us -> 22.6 us
    ppermute x5, starting transfers between devices: 8 us -> 1.09 us  [tree_sum(): lax.ppermute(value, axis, [(i, i ^ step) for i in range(count)])]
    ppermute x4, waiting for transfers between devices: 13.3 us -> 6.7 us  [the longest x2 6.7 us: exchange_rim(): lax.ppermute(tail.reshape(-1), axis, [(i, (i + 1) % count) for i in range...]
    ppermute x5, waiting for transfers between devices: 11.1 us -> 15.9 us  [tree_sum(): lax.ppermute(value, axis, [(i, i ^ step) for i in range(count)])]
  transfers between devices with their start and end apart: 9 -> 9, of which waited for: 9 -> 7; matrix products, arithmetic and copies ran while one was open for 1% -> 4% of each run, Pallas kernels for 0% -> 0%
where the time goes in v2:
time: 60.2 us; the launch traced here: 60 us
  waiting for transfers between devices  22.6 us (38%)
  matrix products  10.9 us (18%)
  local copies, waits for them, and re-layouts  9.27 us (15%)
  starting transfers between devices  8.24 us (14%)
  other arithmetic  4.75 us (8%)
  between operations  3.98 us (7%)
    ppermute x5, waiting for transfers between devices, tree_sum(): lax.ppermute(value, axis, [(i, i ^ step) for i in range(count)])  15.9 us
    ppermute x2, starting transfers between devices, exchange_rim(): lax.ppermute(head.reshape(-1), axis, [((i + 1) % count, i) for i in range...  7.04 us
    ppermute x2, waiting for transfers between devices, exchange_rim(): lax.ppermute(tail.reshape(-1), axis, [(i, (i + 1) % count) for i in range...  6.7 us
    unnamed x14, local copies, waits for them, and re-layouts  2.71 us
    dot_general x5, matrix products, newton(): jnp.dot(current, factor, precision=highest)  1.28 us
    dot_general x4, matrix products, project_mixing(): jnp.dot(mixing.T, jnp.dot(matrix, mixing, precision=highest), precision=h...  1.22 us
    dot_general x4, matrix products, project_mixing(): jnp.dot(matrix, mixing, precision=highest)  1.22 us
  transfers between devices with their start and end apart: 9, of which 7 were waited for; matrix products, arithmetic and copies ran while one was open for 4% of the time, Pallas kernels for 0%

profile of v2, /device:TPU:0, one launch (start us, length us, event | category | flops | bytes accessed | tf_op | source)
XLA Modules:
  0.0 60.0 jit_solution(4952995129342554636)
XLA Ops:
  0.6 0.7 %broadcast_divide_fusion.3 = f32[8]{0:T(128)S(1)} fusion(f32[8]{0:T(128)} %param.10), kind=kLoop, calls=%fused_computation.170 | loop fusion | flops 8 | bytes 64 | tf_op jit(solution)/shard_map/div | solution.py:156
  1.3 1.0 %pad_maximum_fusion.11 = f32[2,24,8,128]{3,2,1,0:T(8,128)S(1)} fusion(f32[2,12,8,128]{3,2,1,0:T(8,128)} %param.8, f32[2,12,8,128]{3,2,1,0:T(8,128)} %param.7), kind=kLoop, calls=%fused_computation.79 | loop fusion | flops 49152 | bytes 393216 | tf_op jit(solution)/shard_map/concatenate | solution.py:164
  2.3 0.6 %copy-done.2 = s32[8,128]{1,0:T(8,128)S(1)} copy-done((s32[8,128]{1,0:T(8,128)S(1)}, s32[8,128]{1,0:T(8,128)}, u32[]{:S(2)}) %copy-start.2) | copy-done | bytes 4120
  3.1 2.5 %collective-permute-start.1 = (f32[12544]{0:T(1024)S(1)}, f32[12544]{0:T(1024)S(1)}, u32[]{:S(2)}, u32[]{:S(2)}) collective-permute-start(f32[12544]{0:T(1024)S(1)} %reshape.377), channel_id=1, source_target_pairs={{8,0},{16,8},{24,16},{0,24},{9,1},{17,9},{25,17},{1,25},{10,2},{18... | collective-permute-start | bytes 150536 | tf_op jit(solution)/shard_map/ppermute | solution.py:108
  5.7 0.5 copy-done.3
  6.3 0.6 fusion.93
  7.9 1.4 %collective-permute-done = f32[12544]{0:T(1024)S(1)} collective-permute-done((f32[12544]{0:T(1024)S(1)}, f32[12544]{0:T(1024)S(1)}, u32[]{:S(2)}, u32[]{:S(2)}) %collective-permute-start) | collective-permute-done | bytes 50208 | tf_op jit(solution)/shard_map/ppermute | solution.py:107
  9.8 4.6 %collective-permute-start.3 = (f32[1176]{0:T(1024)S(1)}, f32[1176]{0:T(1024)S(1)}, u32[]{:S(2)}, u32[]{:S(2)}) collective-permute-start(f32[1176]{0:T(1024)S(1)} %reshape.381), channel_id=1, source_target_pairs={{1,0},{2,1},{3,2},{4,3},{5,4},{6,5},{7,6},{0,7},{9,8},{10,9},{11,1... | collective-permute-start | bytes 14120 | tf_op jit(solution)/shard_map/ppermute | solution.py:108
  16.8 5.3 %collective-permute-done.2 = f32[1176]{0:T(1024)S(1)} collective-permute-done((f32[1176]{0:T(1024)S(1)}, f32[1176]{0:T(1024)S(1)}, u32[]{:S(2)}, u32[]{:S(2)}) %collective-permute-start.2) | collective-permute-done | bytes 4736 | tf_op jit(solution)/shard_map/ppermute | solution.py:107
  23.7 0.5 fusion.90
  24.7 0.5 convolution_bitcast_fusion.2
  25.8 0.5 convolution_bitcast_fusion.1
  27.8 1.2 %collective-permute-done.4 = f32[4608]{0:T(1024)S(1)} collective-permute-done((f32[4608]{0:T(1024)S(1)}, f32[4608]{0:T(1024)S(1)}, u32[]{:S(2)}, u32[]{:S(2)}) %collective-permute-start.4) | collective-permute-done | bytes 18464 | tf_op jit(solution)/shard_map/ppermute | solution.py:128
  29.0 1.0 %collective-permute-start.5 = (f32[4608]{0:T(1024)S(1)}, f32[4608]{0:T(1024)S(1)}, u32[]{:S(2)}, u32[]{:S(2)}) collective-permute-start(f32[4608]{0:T(1024)S(1)} %add.163), channel_id=1, source_target_pairs={{0,16},{8,24},{16,0},{24,8},{1,17},{9,25},{17,1},{25,9},{2,18},{10... | collective-permute-start | bytes 55304 | tf_op jit(solution)/shard_map/ppermute | solution.py:128
  30.0 2.8 %collective-permute-done.5 = f32[4608]{0:T(1024)S(1)} collective-permute-done((f32[4608]{0:T(1024)S(1)}, f32[4608]{0:T(1024)S(1)}, u32[]{:S(2)}, u32[]{:S(2)}) %collective-permute-start.5) | collective-permute-done | bytes 18464 | tf_op jit(solution)/shard_map/ppermute | solution.py:128
  32.8 3.8 %collective-permute-done.6 = f32[4608]{0:T(1024)S(1)} collective-permute-done((f32[4608]{0:T(1024)S(1)}, f32[4608]{0:T(1024)S(1)}, u32[]{:S(2)}, u32[]{:S(2)}) %collective-permute-start.6) | collective-permute-done | bytes 18464 | tf_op jit(solution)/shard_map/ppermute | solution.py:128
  36.6 3.8 %collective-permute-done.7 = f32[4608]{0:T(1024)S(1)} collective-permute-done((f32[4608]{0:T(1024)S(1)}, f32[4608]{0:T(1024)S(1)}, u32[]{:S(2)}, u32[]{:S(2)}) %collective-permute-start.7) | collective-permute-done | bytes 18464 | tf_op jit(solution)/shard_map/ppermute | solution.py:128
  40.6 4.5 %collective-permute-done.8 = f32[4608]{0:T(1024)S(1)} collective-permute-done((f32[4608]{0:T(1024)S(1)}, f32[4608]{0:T(1024)S(1)}, u32[]{:S(2)}, u32[]{:S(2)}) %collective-permute-start.8) | collective-permute-done | bytes 18464 | tf_op jit(solution)/shard_map/ppermute | solution.py:128
  45.4 1.0 %gather_fusion.1 = f32[48]{0:T(128)S(1)} fusion(f32[48,48]{1,0:T(8,128)S(1)} %bitcast_add_fusion, s32[48]{0:T(128)S(1)} %or_bitcast_fusion), kind=kCustom, calls=%fused_computation.1 | custom fusion | bytes 768 | tf_op jit(solution)/shard_map/jit(diagonal)/cond/branch_0_fun/gather | solution.py:209
  46.4 1.0 %gather_fusion = f32[48]{0:T(128)S(1)} fusion(f32[48,48]{0,1:T(8,128)S(1)} %get-tuple-element.103, s32[48]{0:T(128)S(1)} %or_bitcast_fusion), kind=kCustom, calls=%fused_computation | custom fusion | bytes 768 | tf_op jit(solution)/shard_map/jit(diagonal)/cond/branch_0_fun/gather | solution.py:209
  48.9 0.7 %multiply_reduce_fusion = f32[]{:T(128)} fusion(f32[36,36]{1,0:T(8,128)S(1)} %fusion.79, f32[36,36]{1,0:T(8,128)S(1)} %get-tuple-element.107, f32[36,36]{1,0:T(8,128)S(1)} %get-tuple-element.106), kind=kLoop, calls=%fused_computation.94 | loop fusion | flops 25919 | bytes 15556 | tf_op jit(solution)/shard_map/reduce_sum | solution.py:54
  50.5 3.7 %while.13 = (s32[]{:T(128)}, f32[72,72]{0,1:T(8,128)S(1)}, f32[72,72]{1,0:T(8,128)S(1)}, s32[]{:T(128)}) while((s32[]{:T(128)}, f32[72,72]{0,1:T(8,128)S(1)}, f32[72,72]{1,0:T(8,128)S(1)}, s32[]{:T(128)}) %tuple.62), condition=%wide.region_3.4_spmd.clone, body=%wide.region_2.3_spmd.clone.sunk | while | flops 13457666 | bytes 269621 | solution.py:65
  56.6 0.8 %copy.223 = f32[2,36,8,128]{3,2,1,0:T(8,128)} copy(f32[2,36,8,128]{3,1,2,0:T(8,128)S(1)} %maximum_multiply_fusion) | data formatting | bytes 589824
  59.4 0.6 %copy.224 = f32[2,36,36]{2,0,1:T(2,128)} copy(f32[2,36,36]{2,1,0:T(8,128)S(1)} %pad_maximum_fusion.17) | data formatting | bytes 20736
  (151 shorter events, 16.3 us)
Async XLA Ops:
  2.2 0.7 %copy-start.2 = (s32[8,128]{1,0:T(8,128)S(1)}, s32[8,128]{1,0:T(8,128)}, u32[]{:S(2)}) copy-start(s32[8,128]{1,0:T(8,128)} %param.9) | copy-start | bytes 12292
  3.1 4.7 %collective-permute-start.1 = (f32[12544]{0:T(1024)S(1)}, f32[12544]{0:T(1024)S(1)}, u32[]{:S(2)}, u32[]{:S(2)}) collective-permute-start(f32[12544]{0:T(1024)S(1)} %reshape.377), channel_id=1, source_target_pairs={{8,0},{16,8},{24,16},{0,24},{9,1},{17,9},{25,17},{1,25},{10,2},{18... | collective-permute-start | bytes 150536 | tf_op jit(solution)/shard_map/ppermute | solution.py:108
  5.6 0.7 %copy-start.3 = (s32[2]{0:T(128)S(1)}, s32[2]{0:T(128)}, u32[]{:S(2)}) copy-start(s32[2]{0:T(128)} %param.11) | copy-start | bytes 28
  5.7 3.6 %collective-permute-start = (f32[12544]{0:T(1024)S(1)}, f32[12544]{0:T(1024)S(1)}, u32[]{:S(2)}, u32[]{:S(2)}) collective-permute-start(f32[12544]{0:T(1024)S(1)} %reshape.375), channel_id=1, source_target_pairs={{0,8},{8,16},{16,24},{24,0},{1,9},{9,17},{17,25},{25,1},{2,10},{10... | collective-permute-start | bytes 150536 | tf_op jit(solution)/shard_map/ppermute | solution.py:107
  9.6 4.8 %copy-start = (f32[2,12,8,128]{3,2,1,0:T(8,128)S(1)}, f32[2,12,8,128]{3,2,1,0:T(8,128)}, u32[]{:S(2)}) copy-start(f32[2,12,8,128]{3,2,1,0:T(8,128)} %param.8) | copy-start | bytes 294916
  9.8 5.6 %copy-start.1 = (f32[2,12,8,128]{3,2,1,0:T(8,128)S(1)}, f32[2,12,8,128]{3,2,1,0:T(8,128)}, u32[]{:S(2)}) copy-start(f32[2,12,8,128]{3,2,1,0:T(8,128)} %param.7) | copy-start | bytes 294916
  9.8 6.0 %collective-permute-start.3 = (f32[1176]{0:T(1024)S(1)}, f32[1176]{0:T(1024)S(1)}, u32[]{:S(2)}, u32[]{:S(2)}) collective-permute-start(f32[1176]{0:T(1024)S(1)} %reshape.381), channel_id=1, source_target_pairs={{1,0},{2,1},{3,2},{4,3},{5,4},{6,5},{7,6},{0,7},{9,8},{10,9},{11,1... | collective-permute-start | bytes 14120 | tf_op jit(solution)/shard_map/ppermute | solution.py:108
  15.7 6.4 %collective-permute-start.2 = (f32[1176]{0:T(1024)S(1)}, f32[1176]{0:T(1024)S(1)}, u32[]{:S(2)}, u32[]{:S(2)}) collective-permute-start(f32[1176]{0:T(1024)S(1)} %reshape.379), channel_id=1, source_target_pairs={{0,1},{1,2},{2,3},{3,4},{4,5},{5,6},{6,7},{7,0},{8,9},{9,10},{10,1... | collective-permute-start | bytes 14120 | tf_op jit(solution)/shard_map/ppermute | solution.py:107
  27.7 1.3 %collective-permute-start.4 = (f32[4608]{0:T(1024)S(1)}, f32[4608]{0:T(1024)S(1)}, u32[]{:S(2)}, u32[]{:S(2)}) collective-permute-start(f32[4608]{0:T(1024)S(1)} %reshape.390), channel_id=1, source_target_pairs={{0,8},{8,0},{16,24},{24,16},{1,9},{9,1},{17,25},{25,17},{2,10},{10... | collective-permute-start | bytes 55304 | tf_op jit(solution)/shard_map/ppermute | solution.py:128
  29.0 3.8 %collective-permute-start.5 = (f32[4608]{0:T(1024)S(1)}, f32[4608]{0:T(1024)S(1)}, u32[]{:S(2)}, u32[]{:S(2)}) collective-permute-start(f32[4608]{0:T(1024)S(1)} %add.163), channel_id=1, source_target_pairs={{0,16},{8,24},{16,0},{24,8},{1,17},{9,25},{17,1},{25,9},{2,18},{10... | collective-permute-start | bytes 55304 | tf_op jit(solution)/shard_map/ppermute | solution.py:128
  32.8 3.8 %collective-permute-start.6 = (f32[4608]{0:T(1024)S(1)}, f32[4608]{0:T(1024)S(1)}, u32[]{:S(2)}, u32[]{:S(2)}) collective-permute-start(f32[4608]{0:T(1024)S(1)} %add.164), channel_id=1, source_target_pairs={{0,1},{1,0},{2,3},{3,2},{4,5},{5,4},{6,7},{7,6},{8,9},{9,8},{10,11... | collective-permute-start | bytes 55304 | tf_op jit(solution)/shard_map/ppermute | solution.py:128
  36.6 3.8 %collective-permute-start.7 = (f32[4608]{0:T(1024)S(1)}, f32[4608]{0:T(1024)S(1)}, u32[]{:S(2)}, u32[]{:S(2)}) collective-permute-start(f32[4608]{0:T(1024)S(1)} %add.165), channel_id=1, source_target_pairs={{0,2},{1,3},{2,0},{3,1},{4,6},{5,7},{6,4},{7,5},{8,10},{9,11},{10,... | collective-permute-start | bytes 55304 | tf_op jit(solution)/shard_map/ppermute | solution.py:128
  40.4 4.7 %collective-permute-start.8 = (f32[4608]{0:T(1024)S(1)}, f32[4608]{0:T(1024)S(1)}, u32[]{:S(2)}, u32[]{:S(2)}) collective-permute-start(f32[4608]{0:T(1024)S(1)} %add.166), channel_id=1, source_target_pairs={{0,4},{1,5},{2,6},{3,7},{4,0},{5,1},{6,2},{7,3},{8,12},{9,13},{10,... | collective-permute-start | bytes 55304 | tf_op jit(solution)/shard_map/ppermute | solution.py:128

commit v3 on v2

--- a/solution.py
+++ b/solution.py
@@ -1,8 +1,11 @@
+import functools
 import math
 
 import jax
 import jax.numpy as jnp
 from jax import lax
+from jax.experimental import pallas as pl
+from jax.experimental.pallas import tpu as pltpu
 from jax.sharding import PartitionSpec as P
 
 KDEN = 16
@@ -146,6 +149,87 @@
     return (real_part, imag_lower - imag_lower.T)
 
 
+def matrix_kernel(packed_ref, mix_ref, red_ref, work_ref, *, band_count):
+    highest = lax.Precision.HIGHEST
+
+    def dot(first, second):
+        return jnp.dot(first, second, precision=highest, preferred_element_type=jnp.float32)
+
+    size = work_ref.shape[-1]
+    ext = packed_ref.shape[-1]
+    raw = 3 * band_count
+    half = size // 2
+    work_ref[...] = jnp.zeros(work_ref.shape, jnp.float32)
+    work_ref[0, :ext, :ext] = packed_ref[0]
+    work_ref[1, :ext, :ext] = packed_ref[1]
+    rows = lax.broadcasted_iota(jnp.int32, (size, size), 0)
+    cols = lax.broadcasted_iota(jnp.int32, (size, size), 1)
+    upper = rows <= cols
+    strict = rows < cols
+    eye = rows == cols
+
+    def unpack(packed):
+        real_part = jnp.where(upper, packed, 0.0) + jnp.where(strict, packed, 0.0).T
+        lower = jnp.where(upper, 0.0, packed)
+        return real_part, lower - lower.T
+
+    gram_re, gram_im = unpack(work_ref[0])
+    ham_re, ham_im = unpack(work_ref[1])
+    band_diag = eye & (rows < band_count)
+    quotient = jnp.where(band_diag, ham_re, 0.0) / jnp.where(band_diag, gram_re, 1.0)
+    to_row = ((rows == cols + 2 * band_count) & (cols < band_count)).astype(jnp.float32)
+    to_col = ((cols == rows + band_count) & (rows < band_count)).astype(jnp.float32)
+    shifted = dot(dot(to_row, quotient), to_col)
+    kept = (eye & (cols < 2 * band_count)) | (
+        (rows == cols + band_count) & (cols >= 2 * band_count) & (cols < raw)
+    )
+    mixing = kept.astype(jnp.float32) - shifted
+    mixing_t = mixing.T
+    proj_re = dot(mixing_t, dot(gram_re, mixing))
+    proj_im = dot(mixing_t, dot(gram_im, mixing))
+
+    def spread(value, axis):
+        return pltpu.roll(value, half, axis)
+
+    embedded = proj_re + spread(spread(proj_re, 0), 1) - spread(proj_im, 1) + spread(proj_im, 0)
+    active = (rows < raw) | ((rows >= half) & (rows < half + raw))
+    identity = (eye & active).astype(jnp.float32)
+    total = jnp.sum(jnp.sum(embedded * embedded, axis=0, keepdims=True), axis=1, keepdims=True)
+    magnitude = jnp.sqrt(total)
+    current = embedded / magnitude
+    inverse = identity
+    for _ in range(NS_STEPS):
+        factor = 1.5 * identity - 0.5 * dot(inverse, current)
+        current, inverse = dot(current, factor), dot(factor, inverse)
+    root = inverse / jnp.sqrt(magnitude)
+    corner = (rows < raw) & (cols < raw)
+    root_re = jnp.where(corner, root, 0.0)
+    root_im = jnp.where(corner, spread(root, 0), 0.0)
+    mix_re = dot(mixing, root_re)
+    mix_im = dot(mixing, root_im)
+    image_re = dot(ham_re, mix_re) - dot(ham_im, mix_im)
+    image_im = dot(ham_re, mix_im) + dot(ham_im, mix_re)
+    mix_re_t = mix_re.T
+    mix_im_t = mix_im.T
+    mix_ref[0] = mix_re
+    mix_ref[1] = mix_im
+    red_ref[0] = dot(mix_re_t, image_re) + dot(mix_im_t, image_im)
+    red_ref[1] = dot(mix_re_t, image_im) - dot(mix_im_t, image_re)
+
+
+def matrix_stage(packed, band_count):
+    size = 128
+    vmem = pl.BlockSpec(memory_space=pltpu.VMEM)
+    square = jax.ShapeDtypeStruct((2, size, size), jnp.float32)
+    return pl.pallas_call(
+        functools.partial(matrix_kernel, band_count=band_count),
+        out_shape=(square, square),
+        in_specs=[vmem],
+        out_specs=(vmem, vmem),
+        scratch_shapes=[pltpu.VMEM((2, size, size), jnp.float32)],
+    )(packed)
+
+
 def body(bands, directions, materials, permittivity, wavevector):
     band_count = bands.shape[1]
     height = bands.shape[2]
@@ -204,30 +288,13 @@
     local_ham = complex_gram(extended, extended_applied)
     summed = jnp.stack([pack_hermitian(*local_gram), pack_hermitian(*local_ham)])
     summed = tree_sum(tree_sum(summed.reshape(-1), "row"), "col").reshape(summed.shape)
-    gram_whole, gram_imag_whole = unpack_hermitian(summed[0])
-    ham_whole, ham_imag_whole = unpack_hermitian(summed[1])
-    quotient = jnp.diagonal(ham_whole)[:band_count] / jnp.diagonal(gram_whole)[:band_count]
-    identity = jnp.eye(band_count, dtype=jnp.float32)
-    zeros_block = jnp.zeros((band_count, band_count), jnp.float32)
-    mixing = jnp.concatenate(
-        [
-            jnp.concatenate([identity, zeros_block, zeros_block], axis=1),
-            jnp.concatenate([zeros_block, identity, zeros_block], axis=1),
-            jnp.concatenate([zeros_block, -jnp.diag(quotient), zeros_block], axis=1),
-            jnp.concatenate([zeros_block, zeros_block, identity], axis=1),
-        ],
-        axis=0,
-    )
-    gram_real = project_mixing(mixing, gram_whole)
-    gram_imag = project_mixing(mixing, gram_imag_whole)
-    ham_real = project_mixing(mixing, ham_whole)
-    ham_imag = project_mixing(mixing, ham_imag_whole)
-    precond = scaled_image - quotient[None, :, None, None] * scaled_bands
-    raw_basis = jnp.concatenate([bands, precond, directions], axis=1)
-    root_real, root_imag = inverse_root(gram_real, gram_imag)
+    mix, red = matrix_stage(summed, band_count)
+    raw_count = 3 * band_count
+    ext_count = 4 * band_count
+    mix = mix[:, :ext_count, :raw_count]
+    reduced = red[:, :raw_count, :raw_count]
     scale_factor = math.sqrt(height * breadth * lax.axis_size("row") * lax.axis_size("col"))
-    basis = rotate_basis(raw_basis, root_real, root_imag, scale_factor)
-    reduced = reduce_matrix(root_real, root_imag, ham_real, ham_imag)
+    basis = rotate_basis(extended, mix[0], mix[1], scale_factor)
     return (basis, reduced)
 
 

time: 60.2 us -> 56.6 us (0.940)
  matrix products: 10.9 us -> 4.42 us
  Pallas kernels: 0 us -> 6.05 us
  local copies, waits for them, and re-layouts: 9.27 us -> 8.01 us
  other arithmetic: 4.75 us -> 3.62 us
  between operations: 3.98 us -> 3.04 us
    dot_general x31 -> x0, matrix products: 7.41 us -> none  [the longest x5 1.28 us: newton(): jnp.dot(current, factor, precision=highest)]
    pallas_call x0 -> x1, Pallas kernels: none -> 6.05 us  [matrix_stage(): pl.pallas_call(functools.partial(matrix_kernel, band_count=band_count), o...]
    gather x2 -> x0, local copies, waits for them, and re-layouts: 1.92 us -> none  [the longest x1 0.96 us: body(): jnp.diagonal(gram_whole)[:band_count]]
    dot_general x1, matrix products: 0.35 us -> 1.15 us  [rotate_basis(): jnp.einsum('jrc,jk->krc', raw_basis[0], root_imag, precision=highest)]
    reshape x0 -> x1, local copies, waits for them, and re-layouts: none -> 0.7 us  [body(): tree_sum(tree_sum(summed.reshape(-1), 'row'), 'col').reshape(summed.shape)]
    reduce_sum x1 -> x0, other arithmetic: 0.68 us -> none  [inverse_root(): magnitude = jnp.sqrt(jnp.sum(embedded * embedded))]
    slice x6 -> x2, local copies, waits for them, and re-layouts: 0.8 us -> 1.27 us  [the longest x1 0.78 us: body(): reduced = red[:, :raw_count, :raw_count]]
    unnamed x14 -> x15, local copies, waits for them, and re-layouts: 2.71 us -> 2.64 us
where the time goes in v3:
time: 56.6 us; the launch traced here: 56.3 us
  waiting for transfers between devices  22.9 us (40%)
  starting transfers between devices  8.24 us (15%)
  local copies, waits for them, and re-layouts  8.01 us (14%)
  Pallas kernels  6.05 us (11%)
  matrix products  4.42 us (8%)
  other arithmetic  3.62 us (6%)
  between operations  3.04 us (5%)
    ppermute x5, waiting for transfers between devices, tree_sum(): lax.ppermute(value, axis, [(i, i ^ step) for i in range(count)])  16.2 us
    ppermute x2, starting transfers between devices, exchange_rim(): lax.ppermute(head.reshape(-1), axis, [((i + 1) % count, i) for i in range...  7.04 us
    ppermute x2, waiting for transfers between devices, exchange_rim(): lax.ppermute(tail.reshape(-1), axis, [(i, (i + 1) % count) for i in range...  6.7 us
    pallas_call x1, Pallas kernels, matrix_stage(): pl.pallas_call(functools.partial(matrix_kernel, band_count=band_count), o...  6.05 us
    unnamed x15, local copies, waits for them, and re-layouts  2.64 us
    dot_general x1, matrix products, rotate_basis(): jnp.einsum('jrc,jk->krc', raw_basis[0], root_imag, precision=highest)  1.15 us
  transfers between devices with their start and end apart: 9, of which 7 were waited for; matrix products, arithmetic and copies ran while one was open for 4% of the time, Pallas kernels for 0%

profile of v3, /device:TPU:0, one launch (start us, length us, event | category | flops | bytes accessed | tf_op | source)
XLA Modules:
  0.0 56.3 jit_solution(3176485198727526914)
XLA Ops:
  0.6 0.7 %broadcast_divide_fusion.1 = f32[8]{0:T(128)S(1)} fusion(f32[8]{0:T(128)} %param.8), kind=kLoop, calls=%fused_computation.115 | loop fusion | flops 8 | bytes 64 | tf_op jit(solution)/shard_map/div | solution.py:240
  1.3 1.0 %pad_maximum_fusion.10 = f32[2,24,8,128]{3,2,1,0:T(8,128)S(1)} fusion(f32[2,12,8,128]{3,2,1,0:T(8,128)} %param.6, f32[2,12,8,128]{3,2,1,0:T(8,128)} %param.5), kind=kLoop, calls=%fused_computation.65 | loop fusion | flops 49152 | bytes 393216 | tf_op jit(solution)/shard_map/concatenate | solution.py:248
  2.3 0.6 %copy-done.3 = s32[8,128]{1,0:T(8,128)S(1)} copy-done((s32[8,128]{1,0:T(8,128)S(1)}, s32[8,128]{1,0:T(8,128)}, u32[]{:S(2)}) %copy-start.3) | copy-done | bytes 4120
  3.1 2.5 %collective-permute-start.1 = (f32[12544]{0:T(1024)S(1)}, f32[12544]{0:T(1024)S(1)}, u32[]{:S(2)}, u32[]{:S(2)}) collective-permute-start(f32[12544]{0:T(1024)S(1)} %reshape.357), channel_id=1, source_target_pairs={{8,0},{16,8},{24,16},{0,24},{9,1},{17,9},{25,17},{1,25},{10,2},{18... | collective-permute-start | bytes 150536 | tf_op jit(solution)/shard_map/ppermute | solution.py:111
  5.7 0.5 copy-done.4
  6.3 0.6 %fusion.62 = (s32[1]{0:T(128)}, s32[1]{0:T(128)}) fusion(s32[2]{0:T(128)S(1)} %copy-done.4), kind=kLoop, calls=%fused_computation.120 | loop fusion | bytes 16 | tf_op jit(solution)/shard_map/slice | solution.py:245
  7.9 1.4 %collective-permute-done = f32[12544]{0:T(1024)S(1)} collective-permute-done((f32[12544]{0:T(1024)S(1)}, f32[12544]{0:T(1024)S(1)}, u32[]{:S(2)}, u32[]{:S(2)}) %collective-permute-start) | collective-permute-done | bytes 50208 | tf_op jit(solution)/shard_map/ppermute | solution.py:110
  9.8 4.6 %collective-permute-start.3 = (f32[1176]{0:T(1024)S(1)}, f32[1176]{0:T(1024)S(1)}, u32[]{:S(2)}, u32[]{:S(2)}) collective-permute-start(f32[1176]{0:T(1024)S(1)} %reshape.361), channel_id=1, source_target_pairs={{1,0},{2,1},{3,2},{4,3},{5,4},{6,5},{7,6},{0,7},{9,8},{10,9},{11,1... | collective-permute-start | bytes 14120 | tf_op jit(solution)/shard_map/ppermute | solution.py:111
  16.8 5.3 %collective-permute-done.2 = f32[1176]{0:T(1024)S(1)} collective-permute-done((f32[1176]{0:T(1024)S(1)}, f32[1176]{0:T(1024)S(1)}, u32[]{:S(2)}, u32[]{:S(2)}) %collective-permute-start.2) | collective-permute-done | bytes 4736 | tf_op jit(solution)/shard_map/ppermute | solution.py:110
  23.7 0.5 fusion.60
  24.7 0.5 convolution_bitcast_fusion.1
  25.8 0.5 convolution_bitcast_fusion
  27.8 1.2 %collective-permute-done.4 = f32[4608]{0:T(1024)S(1)} collective-permute-done((f32[4608]{0:T(1024)S(1)}, f32[4608]{0:T(1024)S(1)}, u32[]{:S(2)}, u32[]{:S(2)}) %collective-permute-start.4) | collective-permute-done | bytes 18464 | tf_op jit(solution)/shard_map/ppermute | solution.py:131
  29.0 1.0 %collective-permute-start.5 = (f32[4608]{0:T(1024)S(1)}, f32[4608]{0:T(1024)S(1)}, u32[]{:S(2)}, u32[]{:S(2)}) collective-permute-start(f32[4608]{0:T(1024)S(1)} %add.138), channel_id=1, source_target_pairs={{0,16},{8,24},{16,0},{24,8},{1,17},{9,25},{17,1},{25,9},{2,18},{10... | collective-permute-start | bytes 55304 | tf_op jit(solution)/shard_map/ppermute | solution.py:131
  30.0 2.8 %collective-permute-done.5 = f32[4608]{0:T(1024)S(1)} collective-permute-done((f32[4608]{0:T(1024)S(1)}, f32[4608]{0:T(1024)S(1)}, u32[]{:S(2)}, u32[]{:S(2)}) %collective-permute-start.5) | collective-permute-done | bytes 18464 | tf_op jit(solution)/shard_map/ppermute | solution.py:131
  32.8 3.8 %collective-permute-done.6 = f32[4608]{0:T(1024)S(1)} collective-permute-done((f32[4608]{0:T(1024)S(1)}, f32[4608]{0:T(1024)S(1)}, u32[]{:S(2)}, u32[]{:S(2)}) %collective-permute-start.6) | collective-permute-done | bytes 18464 | tf_op jit(solution)/shard_map/ppermute | solution.py:131
  36.6 3.8 %collective-permute-done.7 = f32[4608]{0:T(1024)S(1)} collective-permute-done((f32[4608]{0:T(1024)S(1)}, f32[4608]{0:T(1024)S(1)}, u32[]{:S(2)}, u32[]{:S(2)}) %collective-permute-start.7) | collective-permute-done | bytes 18464 | tf_op jit(solution)/shard_map/ppermute | solution.py:131
  40.4 4.7 %collective-permute-done.8 = f32[4608]{0:T(1024)S(1)} collective-permute-done((f32[4608]{0:T(1024)S(1)}, f32[4608]{0:T(1024)S(1)}, u32[]{:S(2)}, u32[]{:S(2)}) %collective-permute-start.8) | collective-permute-done | bytes 18464 | tf_op jit(solution)/shard_map/ppermute | solution.py:131
  45.1 0.7 %reshape.371.packed_ref = f32[2,48,48]{2,1,0:T(8,128)} reshape(f32[4608]{0:T(1024)S(1)} %add.142) | data formatting | bytes 36864 | tf_op jit(solution)/shard_map/reshape | solution.py:290
  45.8 6.0 %shard_map.68 = (f32[2,128,128]{2,1,0:T(8,128)}, f32[2,128,128]{2,1,0:T(8,128)}) custom-call(f32[2,48,48]{2,1,0:T(8,128)} %reshape.371.packed_ref), custom_call_target="tpu_custom_call" | custom-call | tf_op jit(solution)/shard_map/pallas_call | solution.py:224
  51.8 1.1 %fusion.31 = f32[36,8,128]{2,0,1:T(8,128)S(1)} fusion(f32[2,48,8,128]{3,1,2,0:T(8,128)S(1)} %pad_maximum_fusion.9, f32[2,128,128]{2,1,0:T(8,128)} %get-tuple-element.4), kind=kOutput, calls=%fused_computation.67 | convolution fusion | flops 21233664 | bytes 368640 | tf_op jit(solution)/shard_map/jrc,jk->krc/dot_general | solution.py:95
  54.1 0.8 %copy.158 = f32[2,36,8,128]{3,2,1,0:T(8,128)} copy(f32[2,36,8,128]{3,1,2,0:T(8,128)S(1)} %maximum_multiply_fusion) | data formatting | bytes 589824
  54.8 0.8 %slice.371 = f32[2,36,36]{2,1,0:T(8,128)S(1)} slice(f32[2,128,128]{2,1,0:T(8,128)} %get-tuple-element.5), slice={[0:2], [0:36], [0:36]} | slice | bytes 20736 | tf_op jit(solution)/shard_map/slice | solution.py:295
  55.6 0.6 %copy.159 = f32[2,36,36]{2,0,1:T(2,128)} copy(f32[2,36,36]{2,1,0:T(8,128)S(1)} %slice.371) | data formatting | bytes 20736
  (84 shorter events, 7.4 us)
Async XLA Ops:
  2.2 0.7 %copy-start.3 = (s32[8,128]{1,0:T(8,128)S(1)}, s32[8,128]{1,0:T(8,128)}, u32[]{:S(2)}) copy-start(s32[8,128]{1,0:T(8,128)} %param.7) | copy-start | bytes 12292
  3.1 4.7 %collective-permute-start.1 = (f32[12544]{0:T(1024)S(1)}, f32[12544]{0:T(1024)S(1)}, u32[]{:S(2)}, u32[]{:S(2)}) collective-permute-start(f32[12544]{0:T(1024)S(1)} %reshape.357), channel_id=1, source_target_pairs={{8,0},{16,8},{24,16},{0,24},{9,1},{17,9},{25,17},{1,25},{10,2},{18... | collective-permute-start | bytes 150536 | tf_op jit(solution)/shard_map/ppermute | solution.py:111
  5.6 0.7 %copy-start.4 = (s32[2]{0:T(128)S(1)}, s32[2]{0:T(128)}, u32[]{:S(2)}) copy-start(s32[2]{0:T(128)} %param.9) | copy-start | bytes 28
  5.7 3.6 %collective-permute-start = (f32[12544]{0:T(1024)S(1)}, f32[12544]{0:T(1024)S(1)}, u32[]{:S(2)}, u32[]{:S(2)}) collective-permute-start(f32[12544]{0:T(1024)S(1)} %reshape.355), channel_id=1, source_target_pairs={{0,8},{8,16},{16,24},{24,0},{1,9},{9,17},{17,25},{25,1},{2,10},{10... | collective-permute-start | bytes 150536 | tf_op jit(solution)/shard_map/ppermute | solution.py:110
  9.6 4.8 %copy-start = (f32[2,12,8,128]{3,2,1,0:T(8,128)S(1)}, f32[2,12,8,128]{3,2,1,0:T(8,128)}, u32[]{:S(2)}) copy-start(f32[2,12,8,128]{3,2,1,0:T(8,128)} %param.6) | copy-start | bytes 294916
  9.8 5.6 %copy-start.1 = (f32[2,12,8,128]{3,2,1,0:T(8,128)S(1)}, f32[2,12,8,128]{3,2,1,0:T(8,128)}, u32[]{:S(2)}) copy-start(f32[2,12,8,128]{3,2,1,0:T(8,128)} %param.5) | copy-start | bytes 294916
  9.8 6.0 %collective-permute-start.3 = (f32[1176]{0:T(1024)S(1)}, f32[1176]{0:T(1024)S(1)}, u32[]{:S(2)}, u32[]{:S(2)}) collective-permute-start(f32[1176]{0:T(1024)S(1)} %reshape.361), channel_id=1, source_target_pairs={{1,0},{2,1},{3,2},{4,3},{5,4},{6,5},{7,6},{0,7},{9,8},{10,9},{11,1... | collective-permute-start | bytes 14120 | tf_op jit(solution)/shard_map/ppermute | solution.py:111
  15.7 6.4 %collective-permute-start.2 = (f32[1176]{0:T(1024)S(1)}, f32[1176]{0:T(1024)S(1)}, u32[]{:S(2)}, u32[]{:S(2)}) collective-permute-start(f32[1176]{0:T(1024)S(1)} %reshape.359), channel_id=1, source_target_pairs={{0,1},{1,2},{2,3},{3,4},{4,5},{5,6},{6,7},{7,0},{8,9},{9,10},{10,1... | collective-permute-start | bytes 14120 | tf_op jit(solution)/shard_map/ppermute | solution.py:110
  27.7 1.3 %collective-permute-start.4 = (f32[4608]{0:T(1024)S(1)}, f32[4608]{0:T(1024)S(1)}, u32[]{:S(2)}, u32[]{:S(2)}) collective-permute-start(f32[4608]{0:T(1024)S(1)} %reshape.370), channel_id=1, source_target_pairs={{0,8},{8,0},{16,24},{24,16},{1,9},{9,1},{17,25},{25,17},{2,10},{10... | collective-permute-start | bytes 55304 | tf_op jit(solution)/shard_map/ppermute | solution.py:131
  29.0 3.8 %collective-permute-start.5 = (f32[4608]{0:T(1024)S(1)}, f32[4608]{0:T(1024)S(1)}, u32[]{:S(2)}, u32[]{:S(2)}) collective-permute-start(f32[4608]{0:T(1024)S(1)} %add.138), channel_id=1, source_target_pairs={{0,16},{8,24},{16,0},{24,8},{1,17},{9,25},{17,1},{25,9},{2,18},{10... | collective-permute-start | bytes 55304 | tf_op jit(solution)/shard_map/ppermute | solution.py:131
  32.8 3.8 %collective-permute-start.6 = (f32[4608]{0:T(1024)S(1)}, f32[4608]{0:T(1024)S(1)}, u32[]{:S(2)}, u32[]{:S(2)}) collective-permute-start(f32[4608]{0:T(1024)S(1)} %add.139), channel_id=1, source_target_pairs={{0,1},{1,0},{2,3},{3,2},{4,5},{5,4},{6,7},{7,6},{8,9},{9,8},{10,11... | collective-permute-start | bytes 55304 | tf_op jit(solution)/shard_map/ppermute | solution.py:131
  36.6 3.8 %collective-permute-start.7 = (f32[4608]{0:T(1024)S(1)}, f32[4608]{0:T(1024)S(1)}, u32[]{:S(2)}, u32[]{:S(2)}) collective-permute-start(f32[4608]{0:T(1024)S(1)} %add.140), channel_id=1, source_target_pairs={{0,2},{1,3},{2,0},{3,1},{4,6},{5,7},{6,4},{7,5},{8,10},{9,11},{10,... | collective-permute-start | bytes 55304 | tf_op jit(solution)/shard_map/ppermute | solution.py:131
  40.4 4.7 %collective-permute-start.8 = (f32[4608]{0:T(1024)S(1)}, f32[4608]{0:T(1024)S(1)}, u32[]{:S(2)}, u32[]{:S(2)}) collective-permute-start(f32[4608]{0:T(1024)S(1)} %add.141), channel_id=1, source_target_pairs={{0,4},{1,5},{2,6},{3,7},{4,0},{5,1},{6,2},{7,3},{8,12},{9,13},{10,... | collective-permute-start | bytes 55304 | tf_op jit(solution)/shard_map/ppermute | solution.py:131
  51.8 1.2 %copy-start.2 = (f32[2,128,128]{2,1,0:T(8,128)S(1)}, f32[2,128,128]{2,1,0:T(8,128)}, u32[]{:S(2)}) copy-start(f32[2,128,128]{2,1,0:T(8,128)} %get-tuple-element.4) | copy-start | bytes 393220

commit v4 on v3

--- a/solution.py
+++ b/solution.py
@@ -107,8 +107,21 @@
     count = lax.axis_size(axis)
     head = lax.slice_in_dim(cells, 0, width, axis=dim)
     tail = lax.slice_in_dim(cells, cells.shape[dim] - width, cells.shape[dim], axis=dim)
-    before = lax.ppermute(tail.reshape(-1), axis, [(i, (i + 1) % count) for i in range(count)])
-    after = lax.ppermute(head.reshape(-1), axis, [((i + 1) % count, i) for i in range(count)])
+    if count % 2:
+        before = lax.ppermute(tail.reshape(-1), axis, [(i, (i + 1) % count) for i in range(count)])
+        after = lax.ppermute(head.reshape(-1), axis, [((i + 1) % count, i) for i in range(count)])
+    else:
+        even = lax.axis_index(axis) % 2 == 0
+        first = lax.ppermute(
+            jnp.where(even, tail, head).reshape(-1), axis, [(i, i ^ 1) for i in range(count)]
+        )
+        second = lax.ppermute(
+            jnp.where(even, head, tail).reshape(-1),
+            axis,
+            [(i, (i + 1) % count if i % 2 else (i - 1) % count) for i in range(count)],
+        )
+        before = jnp.where(even, second, first)
+        after = jnp.where(even, first, second)
     before = before.reshape(tail.shape)
     after = after.reshape(head.shape)
     return jnp.concatenate(

time: 56.6 us -> 53.5 us (0.945)
  waiting for transfers between devices: 22.9 us -> 17.6 us
  starting transfers between devices: 8.24 us -> 10.2 us
    ppermute x4, waiting for transfers between devices: 6.7 us -> 2.01 us  [the longest x2 2 us: exchange_rim(): lax.ppermute(jnp.where(even, tail, head).reshape(-1), axis, [(i, i ^ 1) f...]
    ppermute x4, starting transfers between devices: 7.16 us -> 8.54 us  [the longest x2 7.73 us: exchange_rim(): lax.ppermute(jnp.where(even, head, tail).reshape(-1), axis, [(i, (i + 1)...]
    unnamed x15 -> x17, local copies, waits for them, and re-layouts: 2.64 us -> 3.35 us
    div x1, other arithmetic: 0.66 us -> 0.01 us  [body(): 1.0 / permittivity]
    ppermute x5, starting transfers between devices: 1.09 us -> 1.66 us  [tree_sum(): lax.ppermute(value, axis, [(i, i ^ step) for i in range(count)])]
    ppermute x5, waiting for transfers between devices: 16.2 us -> 15.6 us  [tree_sum(): lax.ppermute(value, axis, [(i, i ^ step) for i in range(count)])]
  transfers between devices with their start and end apart: 9 -> 9, of which waited for: 7 -> 6; matrix products, arithmetic and copies ran while one was open for 4% -> 2% of each run, Pallas kernels for 0% -> 0%
where the time goes in v4:
time: 53.5 us; the launch traced here: 53.1 us
  waiting for transfers between devices  17.6 us (33%)
  starting transfers between devices  10.2 us (19%)
  local copies, waits for them, and re-layouts  8.57 us (16%)
  Pallas kernels  6.04 us (11%)
  matrix products  4.43 us (8%)
  other arithmetic  3.15 us (6%)
  between operations  3.09 us (6%)
    ppermute x5, waiting for transfers between devices, tree_sum(): lax.ppermute(value, axis, [(i, i ^ step) for i in range(count)])  15.6 us
    ppermute x2, starting transfers between devices, exchange_rim(): lax.ppermute(jnp.where(even, head, tail).reshape(-1), axis, [(i, (i + 1)...  7.73 us
    pallas_call x1, Pallas kernels, matrix_stage(): pl.pallas_call(functools.partial(matrix_kernel, band_count=band_count), o...  6.04 us
    unnamed x17, local copies, waits for them, and re-layouts  3.35 us
    ppermute x2, waiting for transfers between devices, exchange_rim(): lax.ppermute(jnp.where(even, tail, head).reshape(-1), axis, [(i, i ^ 1) f...  2 us
    ppermute x5, starting transfers between devices, tree_sum(): lax.ppermute(value, axis, [(i, i ^ step) for i in range(count)])  1.66 us
    dot_general x1, matrix products, rotate_basis(): jnp.einsum('jrc,jk->krc', raw_basis[0], root_imag, precision=highest)  1.15 us
  transfers between devices with their start and end apart: 9, of which 6 were waited for; matrix products, arithmetic and copies ran while one was open for 2% of the time, Pallas kernels for 0%

profile of v4, /device:TPU:0, one launch (start us, length us, event | category | flops | bytes accessed | tf_op | source)
XLA Modules:
  0.0 53.1 jit_solution(965348596141303063)
XLA Ops:
  0.7 0.6 %copy-done.5 = f32[8]{0:T(128)S(1)} copy-done((f32[8]{0:T(128)S(1)}, f32[8]{0:T(128)}, u32[]{:S(2)}) %copy-start.5) | copy-done | bytes 56
  1.3 1.0 %pad_maximum_fusion.10 = f32[2,24,8,128]{3,2,1,0:T(8,128)S(1)} fusion(f32[2,12,8,128]{3,2,1,0:T(8,128)} %param.6, f32[2,12,8,128]{3,2,1,0:T(8,128)} %param.5), kind=kLoop, calls=%fused_computation.67 | loop fusion | flops 49152 | bytes 393216 | tf_op jit(solution)/shard_map/concatenate | solution.py:261
  2.3 0.6 %copy-done.3 = s32[8,128]{1,0:T(8,128)S(1)} copy-done((s32[8,128]{1,0:T(8,128)S(1)}, s32[8,128]{1,0:T(8,128)}, u32[]{:S(2)}) %copy-start.3) | copy-done | bytes 4120
  3.1 2.5 %collective-permute-start = (f32[12544]{0:T(1024)S(1)}, f32[12544]{0:T(1024)S(1)}, u32[]{:S(2)}, u32[]{:S(2)}) collective-permute-start(f32[12544]{0:T(1024)S(1)} %reshape.271), channel_id=1, source_target_pairs={{0,24},{8,16},{16,8},{24,0},{1,25},{9,17},{17,9},{25,1},{2,26},{10... | collective-permute-start | bytes 150536 | tf_op jit(solution)/shard_map/ppermute | solution.py:118
  5.7 0.7 %collective-permute-start.1 = (f32[12544]{0:T(1024)S(1)}, f32[12544]{0:T(1024)S(1)}, u32[]{:S(2)}, u32[]{:S(2)}) collective-permute-start(f32[12544]{0:T(1024)S(1)} %reshape.272), channel_id=1, source_target_pairs={{0,8},{8,0},{16,24},{24,16},{1,9},{9,1},{17,25},{25,17},{2,10},{10... | collective-permute-start | bytes 150536 | tf_op jit(solution)/shard_map/ppermute | solution.py:115
  6.5 0.6 %fusion.61 = (s32[1]{0:T(128)}, s32[1]{0:T(128)}) fusion(s32[2]{0:T(128)S(1)} %copy-done.4), kind=kLoop, calls=%fused_computation.127 | loop fusion | bytes 16 | tf_op jit(solution)/shard_map/slice | solution.py:258
  8.7 5.3 %collective-permute-start.2 = (f32[1176]{0:T(1024)S(1)}, f32[1176]{0:T(1024)S(1)}, u32[]{:S(2)}, u32[]{:S(2)}) collective-permute-start(f32[1176]{0:T(1024)S(1)} %reshape.275), channel_id=1, source_target_pairs={{0,7},{1,2},{2,1},{3,4},{4,3},{5,6},{6,5},{7,0},{8,15},{9,10},{10,... | collective-permute-start | bytes 14120 | tf_op jit(solution)/shard_map/ppermute | solution.py:118
  14.3 0.6 %copy-done = f32[2,12,8,128]{3,2,1,0:T(8,128)S(1)} copy-done((f32[2,12,8,128]{3,2,1,0:T(8,128)S(1)}, f32[2,12,8,128]{3,2,1,0:T(8,128)}, u32[]{:S(2)}) %copy-start) | copy-done | bytes 98328
  15.9 2.0 %collective-permute-done.3 = f32[1176]{0:T(1024)S(1)} collective-permute-done((f32[1176]{0:T(1024)S(1)}, f32[1176]{0:T(1024)S(1)}, u32[]{:S(2)}, u32[]{:S(2)}) %collective-permute-start.3) | collective-permute-done | bytes 4736 | tf_op jit(solution)/shard_map/ppermute | solution.py:115
  20.6 0.5 fusion.60
  21.6 0.5 convolution_bitcast_fusion.1
  22.7 0.5 convolution_bitcast_fusion
  24.7 1.2 %collective-permute-done.4 = f32[4608]{0:T(1024)S(1)} collective-permute-done((f32[4608]{0:T(1024)S(1)}, f32[4608]{0:T(1024)S(1)}, u32[]{:S(2)}, u32[]{:S(2)}) %collective-permute-start.4) | collective-permute-done | bytes 18464 | tf_op jit(solution)/shard_map/ppermute | solution.py:144
  25.8 1.6 %collective-permute-start.5 = (f32[4608]{0:T(1024)S(1)}, f32[4608]{0:T(1024)S(1)}, u32[]{:S(2)}, u32[]{:S(2)}) collective-permute-start(f32[4608]{0:T(1024)S(1)} %add.127), channel_id=1, source_target_pairs={{0,16},{8,24},{16,0},{24,8},{1,17},{9,25},{17,1},{25,9},{2,18},{10... | collective-permute-start | bytes 55304 | tf_op jit(solution)/shard_map/ppermute | solution.py:144
  27.4 2.2 %collective-permute-done.5 = f32[4608]{0:T(1024)S(1)} collective-permute-done((f32[4608]{0:T(1024)S(1)}, f32[4608]{0:T(1024)S(1)}, u32[]{:S(2)}, u32[]{:S(2)}) %collective-permute-start.5) | collective-permute-done | bytes 18464 | tf_op jit(solution)/shard_map/ppermute | solution.py:144
  29.6 3.8 %collective-permute-done.6 = f32[4608]{0:T(1024)S(1)} collective-permute-done((f32[4608]{0:T(1024)S(1)}, f32[4608]{0:T(1024)S(1)}, u32[]{:S(2)}, u32[]{:S(2)}) %collective-permute-start.6) | collective-permute-done | bytes 18464 | tf_op jit(solution)/shard_map/ppermute | solution.py:144
  33.4 3.8 %collective-permute-done.7 = f32[4608]{0:T(1024)S(1)} collective-permute-done((f32[4608]{0:T(1024)S(1)}, f32[4608]{0:T(1024)S(1)}, u32[]{:S(2)}, u32[]{:S(2)}) %collective-permute-start.7) | collective-permute-done | bytes 18464 | tf_op jit(solution)/shard_map/ppermute | solution.py:144
  37.2 4.7 %collective-permute-done.8 = f32[4608]{0:T(1024)S(1)} collective-permute-done((f32[4608]{0:T(1024)S(1)}, f32[4608]{0:T(1024)S(1)}, u32[]{:S(2)}, u32[]{:S(2)}) %collective-permute-start.8) | collective-permute-done | bytes 18464 | tf_op jit(solution)/shard_map/ppermute | solution.py:144
  41.9 0.7 %reshape.287.packed_ref = f32[2,48,48]{2,1,0:T(8,128)} reshape(f32[4608]{0:T(1024)S(1)} %add.131) | data formatting | bytes 36864 | tf_op jit(solution)/shard_map/reshape | solution.py:303
  42.6 6.0 %shard_map.68 = (f32[2,128,128]{2,1,0:T(8,128)}, f32[2,128,128]{2,1,0:T(8,128)}) custom-call(f32[2,48,48]{2,1,0:T(8,128)} %reshape.287.packed_ref), custom_call_target="tpu_custom_call" | custom-call | tf_op jit(solution)/shard_map/pallas_call | solution.py:237
  48.6 1.2 %fusion.31 = f32[36,8,128]{2,0,1:T(8,128)S(1)} fusion(f32[2,48,8,128]{3,1,2,0:T(8,128)S(1)} %pad_maximum_fusion.9, f32[2,128,128]{2,1,0:T(8,128)} %get-tuple-element.4), kind=kOutput, calls=%fused_computation.69 | convolution fusion | flops 21233664 | bytes 368640 | tf_op jit(solution)/shard_map/jrc,jk->krc/dot_general | solution.py:95
  50.9 0.8 %copy.158 = f32[2,36,8,128]{3,2,1,0:T(8,128)} copy(f32[2,36,8,128]{3,1,2,0:T(8,128)S(1)} %maximum_multiply_fusion) | data formatting | bytes 589824
  51.7 0.8 %slice.375 = f32[2,36,36]{2,1,0:T(8,128)S(1)} slice(f32[2,128,128]{2,1,0:T(8,128)} %get-tuple-element.5), slice={[0:2], [0:36], [0:36]} | slice | bytes 20736 | tf_op jit(solution)/shard_map/slice | solution.py:308
  52.5 0.6 %copy.159 = f32[2,36,36]{2,0,1:T(2,128)} copy(f32[2,36,36]{2,1,0:T(8,128)S(1)} %slice.375) | data formatting | bytes 20736
  (88 shorter events, 7.4 us)
Async XLA Ops:
  0.6 0.7 %copy-start.5 = (f32[8]{0:T(128)S(1)}, f32[8]{0:T(128)}, u32[]{:S(2)}) copy-start(f32[8]{0:T(128)} %param.8) | copy-start | bytes 100
  2.3 0.7 %copy-start.3 = (s32[8,128]{1,0:T(8,128)S(1)}, s32[8,128]{1,0:T(8,128)}, u32[]{:S(2)}) copy-start(s32[8,128]{1,0:T(8,128)} %param.7) | copy-start | bytes 12292
  3.1 4.9 %collective-permute-start = (f32[12544]{0:T(1024)S(1)}, f32[12544]{0:T(1024)S(1)}, u32[]{:S(2)}, u32[]{:S(2)}) collective-permute-start(f32[12544]{0:T(1024)S(1)} %reshape.271), channel_id=1, source_target_pairs={{0,24},{8,16},{16,8},{24,0},{1,25},{9,17},{17,9},{25,1},{2,26},{10... | collective-permute-start | bytes 150536 | tf_op jit(solution)/shard_map/ppermute | solution.py:118
  5.7 0.8 %copy-start.4 = (s32[2]{0:T(128)S(1)}, s32[2]{0:T(128)}, u32[]{:S(2)}) copy-start(s32[2]{0:T(128)} %param.9) | copy-start | bytes 28
  5.7 2.3 %collective-permute-start.1 = (f32[12544]{0:T(1024)S(1)}, f32[12544]{0:T(1024)S(1)}, u32[]{:S(2)}, u32[]{:S(2)}) collective-permute-start(f32[12544]{0:T(1024)S(1)} %reshape.272), channel_id=1, source_target_pairs={{0,8},{8,0},{16,24},{24,16},{1,9},{9,1},{17,25},{25,17},{2,10},{10... | collective-permute-start | bytes 150536 | tf_op jit(solution)/shard_map/ppermute | solution.py:115
  8.7 7.2 %collective-permute-start.2 = (f32[1176]{0:T(1024)S(1)}, f32[1176]{0:T(1024)S(1)}, u32[]{:S(2)}, u32[]{:S(2)}) collective-permute-start(f32[1176]{0:T(1024)S(1)} %reshape.275), channel_id=1, source_target_pairs={{0,7},{1,2},{2,1},{3,4},{4,3},{5,6},{6,5},{7,0},{8,15},{9,10},{10,... | collective-permute-start | bytes 14120 | tf_op jit(solution)/shard_map/ppermute | solution.py:118
  14.0 0.9 %copy-start = (f32[2,12,8,128]{3,2,1,0:T(8,128)S(1)}, f32[2,12,8,128]{3,2,1,0:T(8,128)}, u32[]{:S(2)}) copy-start(f32[2,12,8,128]{3,2,1,0:T(8,128)} %param.6) | copy-start | bytes 294916
  14.2 1.7 %copy-start.1 = (f32[2,12,8,128]{3,2,1,0:T(8,128)S(1)}, f32[2,12,8,128]{3,2,1,0:T(8,128)}, u32[]{:S(2)}) copy-start(f32[2,12,8,128]{3,2,1,0:T(8,128)} %param.5) | copy-start | bytes 294916
  14.2 3.7 %collective-permute-start.3 = (f32[1176]{0:T(1024)S(1)}, f32[1176]{0:T(1024)S(1)}, u32[]{:S(2)}, u32[]{:S(2)}) collective-permute-start(f32[1176]{0:T(1024)S(1)} %reshape.276), channel_id=1, source_target_pairs={{0,1},{1,0},{2,3},{3,2},{4,5},{5,4},{6,7},{7,6},{8,9},{9,8},{10,11... | collective-permute-start | bytes 14120 | tf_op jit(solution)/shard_map/ppermute | solution.py:115
  24.6 1.3 %collective-permute-start.4 = (f32[4608]{0:T(1024)S(1)}, f32[4608]{0:T(1024)S(1)}, u32[]{:S(2)}, u32[]{:S(2)}) collective-permute-start(f32[4608]{0:T(1024)S(1)} %reshape.286), channel_id=1, source_target_pairs={{0,8},{8,0},{16,24},{24,16},{1,9},{9,1},{17,25},{25,17},{2,10},{10... | collective-permute-start | bytes 55304 | tf_op jit(solution)/shard_map/ppermute | solution.py:144
  25.8 3.8 %collective-permute-start.5 = (f32[4608]{0:T(1024)S(1)}, f32[4608]{0:T(1024)S(1)}, u32[]{:S(2)}, u32[]{:S(2)}) collective-permute-start(f32[4608]{0:T(1024)S(1)} %add.127), channel_id=1, source_target_pairs={{0,16},{8,24},{16,0},{24,8},{1,17},{9,25},{17,1},{25,9},{2,18},{10... | collective-permute-start | bytes 55304 | tf_op jit(solution)/shard_map/ppermute | solution.py:144
  29.6 3.8 %collective-permute-start.6 = (f32[4608]{0:T(1024)S(1)}, f32[4608]{0:T(1024)S(1)}, u32[]{:S(2)}, u32[]{:S(2)}) collective-permute-start(f32[4608]{0:T(1024)S(1)} %add.128), channel_id=1, source_target_pairs={{0,1},{1,0},{2,3},{3,2},{4,5},{5,4},{6,7},{7,6},{8,9},{9,8},{10,11... | collective-permute-start | bytes 55304 | tf_op jit(solution)/shard_map/ppermute | solution.py:144
  33.4 3.8 %collective-permute-start.7 = (f32[4608]{0:T(1024)S(1)}, f32[4608]{0:T(1024)S(1)}, u32[]{:S(2)}, u32[]{:S(2)}) collective-permute-start(f32[4608]{0:T(1024)S(1)} %add.129), channel_id=1, source_target_pairs={{0,2},{1,3},{2,0},{3,1},{4,6},{5,7},{6,4},{7,5},{8,10},{9,11},{10,... | collective-permute-start | bytes 55304 | tf_op jit(solution)/shard_map/ppermute | solution.py:144
  37.2 4.7 %collective-permute-start.8 = (f32[4608]{0:T(1024)S(1)}, f32[4608]{0:T(1024)S(1)}, u32[]{:S(2)}, u32[]{:S(2)}) collective-permute-start(f32[4608]{0:T(1024)S(1)} %add.130), channel_id=1, source_target_pairs={{0,4},{1,5},{2,6},{3,7},{4,0},{5,1},{6,2},{7,3},{8,12},{9,13},{10,... | collective-permute-start | bytes 55304 | tf_op jit(solution)/shard_map/ppermute | solution.py:144
  48.6 1.2 %copy-start.2 = (f32[2,128,128]{2,1,0:T(8,128)S(1)}, f32[2,128,128]{2,1,0:T(8,128)}, u32[]{:S(2)}) copy-start(f32[2,128,128]{2,1,0:T(8,128)} %get-tuple-element.4) | copy-start | bytes 393220

commit v5 on v4

--- a/solution.py
+++ b/solution.py
@@ -162,7 +162,7 @@
     return (real_part, imag_lower - imag_lower.T)
 
 
-def matrix_kernel(packed_ref, mix_ref, red_ref, work_ref, *, band_count):
+def matrix_kernel(packed_ref, basis_ref, red_ref, work_ref, *, band_count, scale):
     highest = lax.Precision.HIGHEST
 
     def dot(first, second):
@@ -180,6 +180,13 @@
     upper = rows <= cols
     strict = rows < cols
     eye = rows == cols
+    corner = (rows < half) & (cols < half)
+
+    def spread(value, axis):
+        return pltpu.roll(value, half, axis)
+
+    def embed(real_part, imag_part):
+        return real_part + spread(spread(real_part, 0), 1) - spread(imag_part, 1) + spread(imag_part, 0)
 
     def unpack(packed):
         real_part = jnp.where(upper, packed, 0.0) + jnp.where(strict, packed, 0.0).T
@@ -197,14 +204,8 @@
         (rows == cols + band_count) & (cols >= 2 * band_count) & (cols < raw)
     )
     mixing = kept.astype(jnp.float32) - shifted
-    mixing_t = mixing.T
-    proj_re = dot(mixing_t, dot(gram_re, mixing))
-    proj_im = dot(mixing_t, dot(gram_im, mixing))
-
-    def spread(value, axis):
-        return pltpu.roll(value, half, axis)
-
-    embedded = proj_re + spread(spread(proj_re, 0), 1) - spread(proj_im, 1) + spread(proj_im, 0)
+    mixing = mixing + spread(spread(mixing, 0), 1)
+    embedded = dot(mixing.T, dot(embed(gram_re, gram_im), mixing))
     active = (rows < raw) | ((rows >= half) & (rows < half + raw))
     identity = (eye & active).astype(jnp.float32)
     total = jnp.sum(jnp.sum(embedded * embedded, axis=0, keepdims=True), axis=1, keepdims=True)
@@ -215,27 +216,26 @@
         factor = 1.5 * identity - 0.5 * dot(inverse, current)
         current, inverse = dot(current, factor), dot(factor, inverse)
     root = inverse / jnp.sqrt(magnitude)
-    corner = (rows < raw) & (cols < raw)
-    root_re = jnp.where(corner, root, 0.0)
-    root_im = jnp.where(corner, spread(root, 0), 0.0)
-    mix_re = dot(mixing, root_re)
-    mix_im = dot(mixing, root_im)
-    image_re = dot(ham_re, mix_re) - dot(ham_im, mix_im)
-    image_im = dot(ham_re, mix_im) + dot(ham_im, mix_re)
-    mix_re_t = mix_re.T
-    mix_im_t = mix_im.T
-    mix_ref[0] = mix_re
-    mix_ref[1] = mix_im
-    red_ref[0] = dot(mix_re_t, image_re) + dot(mix_im_t, image_im)
-    red_ref[1] = dot(mix_re_t, image_im) - dot(mix_im_t, image_re)
-
-
-def matrix_stage(packed, band_count):
+    root = embed(jnp.where(corner, root, 0.0), jnp.where(corner, spread(root, 0), 0.0))
+    rotation = dot(mixing, root)
+    red_ref[...] = dot(rotation.T, dot(embed(ham_re, ham_im), rotation))
+    rotation = jnp.where(corner | ~((rows < half) | (cols < half)), rotation, -rotation)
+    pick_rows = ((rows < ext) & (cols == rows)) | (
+        (rows >= ext) & (rows < 2 * ext) & (cols == rows - ext + half)
+    )
+    pick_cols = ((rows < raw) & (cols == rows)) | (
+        (rows >= half) & (rows < half + raw) & (cols == rows - half + raw)
+    )
+    packed_rotation = dot(pick_rows.astype(jnp.float32), dot(rotation, pick_cols.astype(jnp.float32)))
+    basis_ref[...] = scale * packed_rotation
+
+
+def matrix_stage(packed, band_count, scale):
     size = 128
     vmem = pl.BlockSpec(memory_space=pltpu.VMEM)
-    square = jax.ShapeDtypeStruct((2, size, size), jnp.float32)
+    square = jax.ShapeDtypeStruct((size, size), jnp.float32)
     return pl.pallas_call(
-        functools.partial(matrix_kernel, band_count=band_count),
+        functools.partial(matrix_kernel, band_count=band_count, scale=scale),
         out_shape=(square, square),
         in_specs=[vmem],
         out_specs=(vmem, vmem),
@@ -301,13 +301,18 @@
     local_ham = complex_gram(extended, extended_applied)
     summed = jnp.stack([pack_hermitian(*local_gram), pack_hermitian(*local_ham)])
     summed = tree_sum(tree_sum(summed.reshape(-1), "row"), "col").reshape(summed.shape)
-    mix, red = matrix_stage(summed, band_count)
     raw_count = 3 * band_count
     ext_count = 4 * band_count
-    mix = mix[:, :ext_count, :raw_count]
-    reduced = red[:, :raw_count, :raw_count]
     scale_factor = math.sqrt(height * breadth * lax.axis_size("row") * lax.axis_size("col"))
-    basis = rotate_basis(extended, mix[0], mix[1], scale_factor)
+    mix, red = matrix_stage(summed, band_count, scale_factor)
+    half = red.shape[0] // 2
+    reduced = jnp.stack([red[:raw_count, :raw_count], red[half : half + raw_count, :raw_count]])
+    basis = jnp.einsum(
+        "jrc,jk->krc",
+        extended.reshape(2 * ext_count, height, breadth),
+        mix[: 2 * ext_count, : 2 * raw_count],
+        precision=lax.Precision.HIGHEST,
+    ).reshape(2, raw_count, height, breadth)
     return (basis, reduced)
 
 

time: 53.5 us -> 51.1 us (0.955)
  matrix products: 4.43 us -> 2.71 us
  starting transfers between devices: 10.2 us -> 9.55 us
    dot_general x4 -> x1, matrix products: 2.19 us -> 0.48 us  [body(): jnp.einsum('jrc,jk->krc', extended.reshape(2 * ext_count, height, breadth...]
    dot_general x0 -> x3, local copies, waits for them, and re-layouts: none -> 0.88 us  [body(): jnp.einsum('jrc,jk->krc', extended.reshape(2 * ext_count, height, breadth...]
    slice x1 -> x0, local copies, waits for them, and re-layouts: 0.78 us -> none  [body(): reduced = red[:, :raw_count, :raw_count]]
    ppermute x2, starting transfers between devices: 7.73 us -> 7.04 us  [exchange_rim(): lax.ppermute(jnp.where(even, head, tail).reshape(-1), axis, [(i, (i + 1)...]
    ppermute x2, waiting for transfers between devices: 0.01 us -> 0.62 us  [exchange_rim(): lax.ppermute(jnp.where(even, head, tail).reshape(-1), axis, [(i, (i + 1)...]
  transfers between devices with their start and end apart: 9 -> 9, of which waited for: 6 -> 7; matrix products, arithmetic and copies ran while one was open for 2% -> 2% of each run, Pallas kernels for 0% -> 0%
where the time goes in v5:
time: 51.1 us; the launch traced here: 50.7 us
  waiting for transfers between devices  17.6 us (34%)
  starting transfers between devices  9.55 us (19%)
  local copies, waits for them, and re-layouts  9.09 us (18%)
  Pallas kernels  5.62 us (11%)
  other arithmetic  3.14 us (6%)
  between operations  3.05 us (6%)
  matrix products  2.71 us (5%)
    ppermute x5, waiting for transfers between devices, tree_sum(): lax.ppermute(value, axis, [(i, i ^ step) for i in range(count)])  15.2 us
    ppermute x2, starting transfers between devices, exchange_rim(): lax.ppermute(jnp.where(even, head, tail).reshape(-1), axis, [(i, (i + 1)...  7.04 us
    pallas_call x1, Pallas kernels, matrix_stage(): pl.pallas_call(functools.partial(matrix_kernel, band_count=band_count, sc...  5.62 us
    unnamed x17, local copies, waits for them, and re-layouts  3.67 us
    ppermute x5, starting transfers between devices, tree_sum(): lax.ppermute(value, axis, [(i, i ^ step) for i in range(count)])  1.92 us
    ppermute x2, waiting for transfers between devices, exchange_rim(): lax.ppermute(jnp.where(even, tail, head).reshape(-1), axis, [(i, i ^ 1) f...  1.73 us
  transfers between devices with their start and end apart: 9, of which 7 were waited for; matrix products, arithmetic and copies ran while one was open for 2% of the time, Pallas kernels for 0%

profile of v5, /device:TPU:0, one launch (start us, length us, event | category | flops | bytes accessed | tf_op | source)
XLA Modules:
  0.0 50.7 jit_solution(15783794850010880617)
XLA Ops:
  0.7 0.6 %copy-done.5 = f32[8]{0:T(128)S(1)} copy-done((f32[8]{0:T(128)S(1)}, f32[8]{0:T(128)}, u32[]{:S(2)}) %copy-start.5) | copy-done | bytes 56
  1.3 1.0 %pad_maximum_fusion.10 = f32[2,24,8,128]{3,2,1,0:T(8,128)S(1)} fusion(f32[2,12,8,128]{3,2,1,0:T(8,128)} %param.6, f32[2,12,8,128]{3,2,1,0:T(8,128)} %param.5), kind=kLoop, calls=%fused_computation.65 | loop fusion | flops 49152 | bytes 393216 | tf_op jit(solution)/shard_map/concatenate | solution.py:261
  2.3 0.6 %copy-done.3 = s32[8,128]{1,0:T(8,128)S(1)} copy-done((s32[8,128]{1,0:T(8,128)S(1)}, s32[8,128]{1,0:T(8,128)}, u32[]{:S(2)}) %copy-start.3) | copy-done | bytes 4120
  3.1 0.5 %collective-permute-start.1 = (f32[12544]{0:T(1024)S(1)}, f32[12544]{0:T(1024)S(1)}, u32[]{:S(2)}, u32[]{:S(2)}) collective-permute-start(f32[12544]{0:T(1024)S(1)} %reshape.277), channel_id=1, source_target_pairs={{0,8},{8,0},{16,24},{24,16},{1,9},{9,1},{17,25},{25,17},{2,10},{10... | collective-permute-start | bytes 150536 | tf_op jit(solution)/shard_map/ppermute | solution.py:115
  3.8 2.7 %collective-permute-start = (f32[12544]{0:T(1024)S(1)}, f32[12544]{0:T(1024)S(1)}, u32[]{:S(2)}, u32[]{:S(2)}) collective-permute-start(f32[12544]{0:T(1024)S(1)} %reshape.276), channel_id=1, source_target_pairs={{0,24},{8,16},{16,8},{24,0},{1,25},{9,17},{17,9},{25,1},{2,26},{10... | collective-permute-start | bytes 150536 | tf_op jit(solution)/shard_map/ppermute | solution.py:118
  6.5 0.6 %fusion.53 = (s32[1]{0:T(128)}, s32[1]{0:T(128)}) fusion(s32[2]{0:T(128)S(1)} %copy-done.4), kind=kLoop, calls=%fused_computation.120 | loop fusion | bytes 16 | tf_op jit(solution)/shard_map/slice | solution.py:258
  8.0 0.6 %collective-permute-done = f32[12544]{0:T(1024)S(1)} collective-permute-done((f32[12544]{0:T(1024)S(1)}, f32[12544]{0:T(1024)S(1)}, u32[]{:S(2)}, u32[]{:S(2)}) %collective-permute-start) | collective-permute-done | bytes 50208 | tf_op jit(solution)/shard_map/ppermute | solution.py:118
  9.3 4.3 %collective-permute-start.2 = (f32[1176]{0:T(1024)S(1)}, f32[1176]{0:T(1024)S(1)}, u32[]{:S(2)}, u32[]{:S(2)}) collective-permute-start(f32[1176]{0:T(1024)S(1)} %reshape.280), channel_id=1, source_target_pairs={{0,7},{1,2},{2,1},{3,4},{4,3},{5,6},{6,5},{7,0},{8,15},{9,10},{10,... | collective-permute-start | bytes 14120 | tf_op jit(solution)/shard_map/ppermute | solution.py:118
  15.0 0.9 %copy-done.1 = f32[2,12,8,128]{3,2,1,0:T(8,128)S(1)} copy-done((f32[2,12,8,128]{3,2,1,0:T(8,128)S(1)}, f32[2,12,8,128]{3,2,1,0:T(8,128)}, u32[]{:S(2)}) %copy-start.1) | copy-done | bytes 98328
  15.9 1.7 %collective-permute-done.3 = f32[1176]{0:T(1024)S(1)} collective-permute-done((f32[1176]{0:T(1024)S(1)}, f32[1176]{0:T(1024)S(1)}, u32[]{:S(2)}, u32[]{:S(2)}) %collective-permute-start.3) | collective-permute-done | bytes 4736 | tf_op jit(solution)/shard_map/ppermute | solution.py:115
  20.3 0.5 fusion.52
  22.7 0.5 %convolution_bitcast_fusion = f32[48,48]{1,0:T(8,128)S(1)} fusion(f32[2,36,8,128]{3,1,2,0:T(8,128)S(1)} %fusion.19, f32[2,12,8,128]{3,1,2,0:T(8,128)S(1)} %slice.399, f32[2,12,8,128]{3,1,2,0:T(8,128)S(1)} %copy.143, f32[2,12,8,128]{3,1,2,0:T(8,128)S(1)} %slice.396, f32[2,12,8,128]{3,1,2,0:T(8,128)S(1)} %slice.395, f32[2,12,8,128]{3,1,2,0:T(8,128)S(1)} %copy.142), kind=kOutput, calls=%fused_computation | convolution fusion | flops 57016320 | bytes 795648 | tf_op jit(solution)/shard_map/pjc,pkc->jk/dot_general | solution.py:44
  24.3 1.2 %collective-permute-done.4 = f32[4608]{0:T(1024)S(1)} collective-permute-done((f32[4608]{0:T(1024)S(1)}, f32[4608]{0:T(1024)S(1)}, u32[]{:S(2)}, u32[]{:S(2)}) %collective-permute-start.4) | collective-permute-done | bytes 18464 | tf_op jit(solution)/shard_map/ppermute | solution.py:144
  25.5 1.5 %collective-permute-start.5 = (f32[4608]{0:T(1024)S(1)}, f32[4608]{0:T(1024)S(1)}, u32[]{:S(2)}, u32[]{:S(2)}) collective-permute-start(f32[4608]{0:T(1024)S(1)} %add.124), channel_id=1, source_target_pairs={{0,16},{8,24},{16,0},{24,8},{1,17},{9,25},{17,1},{25,9},{2,18},{10... | collective-permute-start | bytes 55304 | tf_op jit(solution)/shard_map/ppermute | solution.py:144
  27.0 2.2 %collective-permute-done.5 = f32[4608]{0:T(1024)S(1)} collective-permute-done((f32[4608]{0:T(1024)S(1)}, f32[4608]{0:T(1024)S(1)}, u32[]{:S(2)}, u32[]{:S(2)}) %collective-permute-start.5) | collective-permute-done | bytes 18464 | tf_op jit(solution)/shard_map/ppermute | solution.py:144
  29.6 3.5 %collective-permute-done.6 = f32[4608]{0:T(1024)S(1)} collective-permute-done((f32[4608]{0:T(1024)S(1)}, f32[4608]{0:T(1024)S(1)}, u32[]{:S(2)}, u32[]{:S(2)}) %collective-permute-start.6) | collective-permute-done | bytes 18464 | tf_op jit(solution)/shard_map/ppermute | solution.py:144
  33.1 3.8 %collective-permute-done.7 = f32[4608]{0:T(1024)S(1)} collective-permute-done((f32[4608]{0:T(1024)S(1)}, f32[4608]{0:T(1024)S(1)}, u32[]{:S(2)}, u32[]{:S(2)}) %collective-permute-start.7) | collective-permute-done | bytes 18464 | tf_op jit(solution)/shard_map/ppermute | solution.py:144
  37.0 4.5 %collective-permute-done.8 = f32[4608]{0:T(1024)S(1)} collective-permute-done((f32[4608]{0:T(1024)S(1)}, f32[4608]{0:T(1024)S(1)}, u32[]{:S(2)}, u32[]{:S(2)}) %collective-permute-start.8) | collective-permute-done | bytes 18464 | tf_op jit(solution)/shard_map/ppermute | solution.py:144
  41.6 0.7 %reshape.292.packed_ref = f32[2,48,48]{2,1,0:T(8,128)} reshape(f32[4608]{0:T(1024)S(1)} %add.128) | data formatting | bytes 36864 | tf_op jit(solution)/shard_map/reshape | solution.py:303
  42.3 5.6 %shard_map.68 = (f32[128,128]{1,0:T(8,128)}, f32[128,128]{1,0:T(8,128)}) custom-call(f32[2,48,48]{2,1,0:T(8,128)} %reshape.292.packed_ref), custom_call_target="tpu_custom_call" | custom-call | tf_op jit(solution)/shard_map/pallas_call | solution.py:237
  47.9 0.8 %slice_bitcast_fusion.8 = f32[72,96]{0,1:T(8,128)S(1)} fusion(f32[128,128]{1,0:T(8,128)} %get-tuple-element.4), kind=kLoop, calls=%fused_computation.72 | loop fusion | bytes 55296 | tf_op jit(solution)/shard_map/jrc,jk->krc/dot_general | solution.py:310
  48.8 0.5 fusion.13
  49.3 0.8 %copy.150 = f32[2,36,8,128]{3,2,1,0:T(8,128)} copy(f32[2,36,8,128]{3,1,2,0:T(8,128)S(1)} %fusion.13) | data formatting | bytes 589824
  50.1 0.6 %copy.151 = f32[2,36,36]{2,0,1:T(2,128)} copy(f32[2,36,36]{2,1,0:T(8,128)S(1)} %pad_maximum_fusion.16) | data formatting | bytes 20736
  (89 shorter events, 7.3 us)
Async XLA Ops:
  0.6 0.7 %copy-start.5 = (f32[8]{0:T(128)S(1)}, f32[8]{0:T(128)}, u32[]{:S(2)}) copy-start(f32[8]{0:T(128)} %param.8) | copy-start | bytes 100
  2.3 0.7 %copy-start.3 = (s32[8,128]{1,0:T(8,128)S(1)}, s32[8,128]{1,0:T(8,128)}, u32[]{:S(2)}) copy-start(s32[8,128]{1,0:T(8,128)} %param.7) | copy-start | bytes 12292
  3.1 4.9 %collective-permute-start.1 = (f32[12544]{0:T(1024)S(1)}, f32[12544]{0:T(1024)S(1)}, u32[]{:S(2)}, u32[]{:S(2)}) collective-permute-start(f32[12544]{0:T(1024)S(1)} %reshape.277), channel_id=1, source_target_pairs={{0,8},{8,0},{16,24},{24,16},{1,9},{9,1},{17,25},{25,17},{2,10},{10... | collective-permute-start | bytes 150536 | tf_op jit(solution)/shard_map/ppermute | solution.py:115
  3.7 2.8 %copy-start.4 = (s32[2]{0:T(128)S(1)}, s32[2]{0:T(128)}, u32[]{:S(2)}) copy-start(s32[2]{0:T(128)} %param.9) | copy-start | bytes 28
  3.8 4.9 %collective-permute-start = (f32[12544]{0:T(1024)S(1)}, f32[12544]{0:T(1024)S(1)}, u32[]{:S(2)}, u32[]{:S(2)}) collective-permute-start(f32[12544]{0:T(1024)S(1)} %reshape.276), channel_id=1, source_target_pairs={{0,24},{8,16},{16,8},{24,0},{1,25},{9,17},{17,9},{25,1},{2,26},{10... | collective-permute-start | bytes 150536 | tf_op jit(solution)/shard_map/ppermute | solution.py:118
  9.3 6.6 %collective-permute-start.2 = (f32[1176]{0:T(1024)S(1)}, f32[1176]{0:T(1024)S(1)}, u32[]{:S(2)}, u32[]{:S(2)}) collective-permute-start(f32[1176]{0:T(1024)S(1)} %reshape.280), channel_id=1, source_target_pairs={{0,7},{1,2},{2,1},{3,4},{4,3},{5,6},{6,5},{7,0},{8,15},{9,10},{10,... | collective-permute-start | bytes 14120 | tf_op jit(solution)/shard_map/ppermute | solution.py:118
  13.7 1.3 %copy-start = (f32[2,12,8,128]{3,2,1,0:T(8,128)S(1)}, f32[2,12,8,128]{3,2,1,0:T(8,128)}, u32[]{:S(2)}) copy-start(f32[2,12,8,128]{3,2,1,0:T(8,128)} %param.5) | copy-start | bytes 294916
  13.9 3.7 %collective-permute-start.3 = (f32[1176]{0:T(1024)S(1)}, f32[1176]{0:T(1024)S(1)}, u32[]{:S(2)}, u32[]{:S(2)}) collective-permute-start(f32[1176]{0:T(1024)S(1)} %reshape.281), channel_id=1, source_target_pairs={{0,1},{1,0},{2,3},{3,2},{4,5},{5,4},{6,7},{7,6},{8,9},{9,8},{10,11... | collective-permute-start | bytes 14120 | tf_op jit(solution)/shard_map/ppermute | solution.py:115
  14.9 0.9 %copy-start.1 = (f32[2,12,8,128]{3,2,1,0:T(8,128)S(1)}, f32[2,12,8,128]{3,2,1,0:T(8,128)}, u32[]{:S(2)}) copy-start(f32[2,12,8,128]{3,2,1,0:T(8,128)} %param.6) | copy-start | bytes 294916
  24.2 1.3 %collective-permute-start.4 = (f32[4608]{0:T(1024)S(1)}, f32[4608]{0:T(1024)S(1)}, u32[]{:S(2)}, u32[]{:S(2)}) collective-permute-start(f32[4608]{0:T(1024)S(1)} %reshape.291), channel_id=1, source_target_pairs={{0,8},{8,0},{16,24},{24,16},{1,9},{9,1},{17,25},{25,17},{2,10},{10... | collective-permute-start | bytes 55304 | tf_op jit(solution)/shard_map/ppermute | solution.py:144
  25.5 3.8 %collective-permute-start.5 = (f32[4608]{0:T(1024)S(1)}, f32[4608]{0:T(1024)S(1)}, u32[]{:S(2)}, u32[]{:S(2)}) collective-permute-start(f32[4608]{0:T(1024)S(1)} %add.124), channel_id=1, source_target_pairs={{0,16},{8,24},{16,0},{24,8},{1,17},{9,25},{17,1},{25,9},{2,18},{10... | collective-permute-start | bytes 55304 | tf_op jit(solution)/shard_map/ppermute | solution.py:144
  29.3 3.8 %collective-permute-start.6 = (f32[4608]{0:T(1024)S(1)}, f32[4608]{0:T(1024)S(1)}, u32[]{:S(2)}, u32[]{:S(2)}) collective-permute-start(f32[4608]{0:T(1024)S(1)} %add.125), channel_id=1, source_target_pairs={{0,1},{1,0},{2,3},{3,2},{4,5},{5,4},{6,7},{7,6},{8,9},{9,8},{10,11... | collective-permute-start | bytes 55304 | tf_op jit(solution)/shard_map/ppermute | solution.py:144
  33.1 3.8 %collective-permute-start.7 = (f32[4608]{0:T(1024)S(1)}, f32[4608]{0:T(1024)S(1)}, u32[]{:S(2)}, u32[]{:S(2)}) collective-permute-start(f32[4608]{0:T(1024)S(1)} %add.126), channel_id=1, source_target_pairs={{0,2},{1,3},{2,0},{3,1},{4,6},{5,7},{6,4},{7,5},{8,10},{9,11},{10,... | collective-permute-start | bytes 55304 | tf_op jit(solution)/shard_map/ppermute | solution.py:144
  36.9 4.7 %collective-permute-start.8 = (f32[4608]{0:T(1024)S(1)}, f32[4608]{0:T(1024)S(1)}, u32[]{:S(2)}, u32[]{:S(2)}) collective-permute-start(f32[4608]{0:T(1024)S(1)} %add.127), channel_id=1, source_target_pairs={{0,4},{1,5},{2,6},{3,7},{4,0},{5,1},{6,2},{7,3},{8,12},{9,13},{10,... | collective-permute-start | bytes 55304 | tf_op jit(solution)/shard_map/ppermute | solution.py:144
  49.2 0.8 %copy-start.2 = (f32[128,128]{1,0:T(8,128)S(1)}, f32[128,128]{1,0:T(8,128)}, u32[]{:S(2)}) copy-start(f32[128,128]{1,0:T(8,128)} %get-tuple-element.5) | copy-start | bytes 196612

commit v6 on v5

--- a/solution.py
+++ b/solution.py
@@ -48,70 +48,18 @@
     return (real_part, imag_part)
 
 
-def inverse_root(gram_real, gram_imag):
-    highest = lax.Precision.HIGHEST
-    order_size = gram_real.shape[0]
-    upper_half = jnp.concatenate([gram_real, -gram_imag], axis=1)
-    lower_half = jnp.concatenate([gram_imag, gram_real], axis=1)
-    embedded = jnp.concatenate([upper_half, lower_half], axis=0)
-    magnitude = jnp.sqrt(jnp.sum(embedded * embedded))
-    identity = jnp.eye(2 * order_size, dtype=embedded.dtype)
-
-    def newton(turn_index, carried):
-        current, inverse = carried
-        factor = 1.5 * identity - 0.5 * jnp.dot(inverse, current, precision=highest)
-        return (
-            jnp.dot(current, factor, precision=highest),
-            jnp.dot(factor, inverse, precision=highest),
-        )
-
-    current, inverse = lax.fori_loop(0, NS_STEPS, newton, (embedded / magnitude, identity))
-    root_full = inverse / jnp.sqrt(magnitude)
-    return (root_full[:order_size, :order_size], root_full[order_size:, :order_size])
-
-
-def reduce_matrix(root_real, root_imag, ham_real, ham_imag):
-    highest = lax.Precision.HIGHEST
-    prod_real = jnp.dot(ham_real, root_real, precision=highest) - jnp.dot(
-        ham_imag, root_imag, precision=highest
-    )
-    prod_imag = jnp.dot(ham_real, root_imag, precision=highest) + jnp.dot(
-        ham_imag, root_real, precision=highest
-    )
-    red_real = jnp.dot(root_real.T, prod_real, precision=highest) + jnp.dot(
-        root_imag.T, prod_imag, precision=highest
-    )
-    red_imag = jnp.dot(root_real.T, prod_imag, precision=highest) - jnp.dot(
-        root_imag.T, prod_real, precision=highest
-    )
-    return jnp.stack([red_real, red_imag])
-
-
-def rotate_basis(raw_basis, root_real, root_imag, scale_factor):
-    highest = lax.Precision.HIGHEST
-    basis_real = jnp.einsum("jrc,jk->krc", raw_basis[0], root_real, precision=highest) - jnp.einsum(
-        "jrc,jk->krc", raw_basis[1], root_imag, precision=highest
-    )
-    basis_imag = jnp.einsum("jrc,jk->krc", raw_basis[0], root_imag, precision=highest) + jnp.einsum(
-        "jrc,jk->krc", raw_basis[1], root_real, precision=highest
-    )
-    return scale_factor * jnp.stack([basis_real, basis_imag])
-
-
-def project_mixing(mixing, matrix):
-    highest = lax.Precision.HIGHEST
-    return jnp.dot(mixing.T, jnp.dot(matrix, mixing, precision=highest), precision=highest)
-
-
-def exchange_rim(cells, axis, dim, width, low_angle, high_angle):
+def exchange_rim(cells, axis, dim, width, angle):
     count = lax.axis_size(axis)
+    index = lax.axis_index(axis)
     head = lax.slice_in_dim(cells, 0, width, axis=dim)
     tail = lax.slice_in_dim(cells, cells.shape[dim] - width, cells.shape[dim], axis=dim)
+    head = rotate_rim(head, jnp.where(index == 0, angle, 0.0))
+    tail = rotate_rim(tail, jnp.where(index == count - 1, -angle, 0.0))
     if count % 2:
         before = lax.ppermute(tail.reshape(-1), axis, [(i, (i + 1) % count) for i in range(count)])
         after = lax.ppermute(head.reshape(-1), axis, [((i + 1) % count, i) for i in range(count)])
     else:
-        even = lax.axis_index(axis) % 2 == 0
+        even = index % 2 == 0
         first = lax.ppermute(
             jnp.where(even, tail, head).reshape(-1), axis, [(i, i ^ 1) for i in range(count)]
         )
@@ -124,9 +72,7 @@
         after = jnp.where(even, first, second)
     before = before.reshape(tail.shape)
     after = after.reshape(head.shape)
-    return jnp.concatenate(
-        [rotate_rim(before, low_angle), cells, rotate_rim(after, high_angle)], axis=dim
-    )
+    return jnp.concatenate([before, cells, after], axis=dim)
 
 
 def rotate_rim(rim, phase_angle):
@@ -152,16 +98,6 @@
     return jnp.where(upper, real_part, imag_part)
 
 
-def unpack_hermitian(packed):
-    order_size = packed.shape[0]
-    upper = jnp.arange(order_size)[:, None] <= jnp.arange(order_size)[None, :]
-    strict_upper = jnp.arange(order_size)[:, None] < jnp.arange(order_size)[None, :]
-    real_upper = jnp.where(upper, packed, 0.0)
-    real_part = real_upper + jnp.where(strict_upper, packed, 0.0).T
-    imag_lower = jnp.where(upper, 0.0, packed)
-    return (real_part, imag_lower - imag_lower.T)
-
-
 def matrix_kernel(packed_ref, basis_ref, red_ref, work_ref, *, band_count, scale):
     highest = lax.Precision.HIGHEST
 
@@ -169,12 +105,11 @@
         return jnp.dot(first, second, precision=highest, preferred_element_type=jnp.float32)
 
     size = work_ref.shape[-1]
-    ext = packed_ref.shape[-1]
     raw = 3 * band_count
     half = size // 2
+    ext = packed_ref.shape[0]
     work_ref[...] = jnp.zeros(work_ref.shape, jnp.float32)
-    work_ref[0, :ext, :ext] = packed_ref[0]
-    work_ref[1, :ext, :ext] = packed_ref[1]
+    work_ref[0, :ext, :] = packed_ref[...]
     rows = lax.broadcasted_iota(jnp.int32, (size, size), 0)
     cols = lax.broadcasted_iota(jnp.int32, (size, size), 1)
     upper = rows <= cols
@@ -193,8 +128,10 @@
         lower = jnp.where(upper, 0.0, packed)
         return real_part, lower - lower.T
 
-    gram_re, gram_im = unpack(work_ref[0])
-    ham_re, ham_im = unpack(work_ref[1])
+    stacked = work_ref[0]
+    left = cols < half
+    gram_re, gram_im = unpack(jnp.where(left, stacked, 0.0))
+    ham_re, ham_im = unpack(jnp.where(left, spread(stacked, 1), 0.0))
     band_diag = eye & (rows < band_count)
     quotient = jnp.where(band_diag, ham_re, 0.0) / jnp.where(band_diag, gram_re, 1.0)
     to_row = ((rows == cols + 2 * band_count) & (cols < band_count)).astype(jnp.float32)
@@ -218,7 +155,9 @@
     root = inverse / jnp.sqrt(magnitude)
     root = embed(jnp.where(corner, root, 0.0), jnp.where(corner, spread(root, 0), 0.0))
     rotation = dot(mixing, root)
-    red_ref[...] = dot(rotation.T, dot(embed(ham_re, ham_im), rotation))
+    work_ref[1] = dot(rotation.T, dot(embed(ham_re, ham_im), rotation))
+    red_ref[0] = work_ref[1, :raw, :raw]
+    red_ref[1] = work_ref[1, half : half + raw, :raw]
     rotation = jnp.where(corner | ~((rows < half) | (cols < half)), rotation, -rotation)
     pick_rows = ((rows < ext) & (cols == rows)) | (
         (rows >= ext) & (rows < 2 * ext) & (cols == rows - ext + half)
@@ -227,16 +166,20 @@
         (rows >= half) & (rows < half + raw) & (cols == rows - half + raw)
     )
     packed_rotation = dot(pick_rows.astype(jnp.float32), dot(rotation, pick_cols.astype(jnp.float32)))
-    basis_ref[...] = scale * packed_rotation
+    work_ref[0] = scale * packed_rotation.T
+    basis_ref[...] = work_ref[0, : 2 * raw, : 2 * ext]
 
 
 def matrix_stage(packed, band_count, scale):
     size = 128
+    raw = 3 * band_count
     vmem = pl.BlockSpec(memory_space=pltpu.VMEM)
-    square = jax.ShapeDtypeStruct((size, size), jnp.float32)
     return pl.pallas_call(
         functools.partial(matrix_kernel, band_count=band_count, scale=scale),
-        out_shape=(square, square),
+        out_shape=(
+            jax.ShapeDtypeStruct((2 * raw, 2 * packed.shape[0]), jnp.float32),
+            jax.ShapeDtypeStruct((2, raw, raw), jnp.float32),
+        ),
         in_specs=[vmem],
         out_specs=(vmem, vmem),
         scratch_shapes=[pltpu.VMEM((2, size, size), jnp.float32)],
@@ -256,28 +199,12 @@
     )
     angle_row = 2.0 * math.pi * wavevector[0].astype(jnp.float32) / KDEN
     angle_col = 2.0 * math.pi * wavevector[1].astype(jnp.float32) / KDEN
-    row_index = lax.axis_index("row")
-    col_index = lax.axis_index("col")
     fields = jnp.concatenate([bands, directions], axis=1)
     packed = jnp.concatenate(
         [fields.reshape(4 * band_count, height, breadth), stiffness[None]], axis=0
     )
-    padded = exchange_rim(
-        packed,
-        "row",
-        1,
-        2,
-        jnp.where(row_index == 0, -angle_row, 0.0),
-        jnp.where(row_index == lax.axis_size("row") - 1, angle_row, 0.0),
-    )
-    padded = exchange_rim(
-        padded,
-        "col",
-        2,
-        2,
-        jnp.where(col_index == 0, -angle_col, 0.0),
-        jnp.where(col_index == lax.axis_size("col") - 1, angle_col, 0.0),
-    )
+    padded = exchange_rim(packed, "row", 1, 2, angle_row)
+    padded = exchange_rim(padded, "col", 2, 2, angle_col)
     stiff_wide = padded[-1]
     field_wide = padded[:-1].reshape(2, 2 * band_count, height + 4, breadth + 4)
     band_wide = field_wide[:, :band_count]
@@ -299,18 +226,19 @@
     extended_applied = jnp.concatenate([applied_cycle, extra_applied], axis=1)
     local_gram = complex_gram(extended, extended)
     local_ham = complex_gram(extended, extended_applied)
-    summed = jnp.stack([pack_hermitian(*local_gram), pack_hermitian(*local_ham)])
-    summed = tree_sum(tree_sum(summed.reshape(-1), "row"), "col").reshape(summed.shape)
+    ext_count = 4 * band_count
+    gap = jnp.zeros((ext_count, 64 - ext_count), jnp.float32)
+    summed = jnp.concatenate(
+        [pack_hermitian(*local_gram), gap, pack_hermitian(*local_ham), gap], axis=1
+    )
+    summed = tree_sum(tree_sum(summed, "row"), "col")
     raw_count = 3 * band_count
-    ext_count = 4 * band_count
     scale_factor = math.sqrt(height * breadth * lax.axis_size("row") * lax.axis_size("col"))
-    mix, red = matrix_stage(summed, band_count, scale_factor)
-    half = red.shape[0] // 2
-    reduced = jnp.stack([red[:raw_count, :raw_count], red[half : half + raw_count, :raw_count]])
+    mix, reduced = matrix_stage(summed, band_count, scale_factor)
     basis = jnp.einsum(
-        "jrc,jk->krc",
+        "kj,jrc->krc",
+        mix,
         extended.reshape(2 * ext_count, height, breadth),
-        mix[: 2 * ext_count, : 2 * raw_count],
         precision=lax.Precision.HIGHEST,
     ).reshape(2, raw_count, height, breadth)
     return (basis, reduced)

time: 51.1 us -> 53.1 us (1.039)
  waiting for transfers between devices: 17.6 us -> 19.7 us
    ppermute x2, waiting for transfers between devices: 0.62 us -> 1.84 us  [exchange_rim(): lax.ppermute(jnp.where(even, head, tail).reshape(-1), axis, [(i, (i + 1)...]
    add x5, other arithmetic: 0.02 us -> 0.71 us  [tree_sum(): value + lax.ppermute(value, axis, [(i, i ^ step) for i in range(count)])]
    reshape x6 -> x8, local copies, waits for them, and re-layouts: 1.24 us -> 0.67 us  [the longest x4 0.34 us: exchange_rim(): before = before.reshape(tail.shape)]
  transfers between devices with their start and end apart: 9 -> 9, of which waited for: 7 -> 8; matrix products, arithmetic and copies ran while one was open for 2% -> 1% of each run, Pallas kernels for 0% -> 0%
where the time goes in v6:
time: 53.1 us; the launch traced here: 52.7 us
  waiting for transfers between devices  19.7 us (37%)
  starting transfers between devices  9.29 us (17%)
  local copies, waits for them, and re-layouts  8.56 us (16%)
  Pallas kernels  5.68 us (11%)
  other arithmetic  3.64 us (7%)
  between operations  3.03 us (6%)
  matrix products  2.72 us (5%)
    ppermute x5, waiting for transfers between devices, tree_sum(): lax.ppermute(value, axis, [(i, i ^ step) for i in range(count)])  15.7 us
    ppermute x2, starting transfers between devices, exchange_rim(): lax.ppermute(jnp.where(even, head, tail).reshape(-1), axis, [(i, (i + 1)...  7.04 us
    pallas_call x1, Pallas kernels, matrix_stage(): pl.pallas_call(functools.partial(matrix_kernel, band_count=band_count, sc...  5.68 us
    unnamed x17, local copies, waits for them, and re-layouts  3.57 us
    ppermute x2, waiting for transfers between devices, exchange_rim(): lax.ppermute(jnp.where(even, tail, head).reshape(-1), axis, [(i, i ^ 1) f...  2.16 us
    ppermute x2, waiting for transfers between devices, exchange_rim(): lax.ppermute(jnp.where(even, head, tail).reshape(-1), axis, [(i, (i + 1)...  1.84 us
    ppermute x5, starting transfers between devices, tree_sum(): lax.ppermute(value, axis, [(i, i ^ step) for i in range(count)])  1.66 us
  transfers between devices with their start and end apart: 9, of which 8 were waited for; matrix products, arithmetic and copies ran while one was open for 1% of the time, Pallas kernels for 0%

profile of v6, /device:TPU:0, one launch (start us, length us, event | category | flops | bytes accessed | tf_op | source)
XLA Modules:
  0.0 52.7 jit_solution(10662605043979478077)
XLA Ops:
  0.7 0.6 %copy-done.4 = s32[2]{0:T(128)S(1)} copy-done((s32[2]{0:T(128)S(1)}, s32[2]{0:T(128)}, u32[]{:S(2)}) %copy-start.4) | copy-done | bytes 32
  1.3 0.6 %fusion.52 = (s32[1]{0:T(128)}, s32[1]{0:T(128)}) fusion(s32[2]{0:T(128)S(1)} %copy-done.4), kind=kLoop, calls=%fused_computation.115 | loop fusion | bytes 16 | tf_op jit(solution)/shard_map/slice | solution.py:201
  2.9 0.6 %copy-done.5 = f32[8]{0:T(128)S(1)} copy-done((f32[8]{0:T(128)S(1)}, f32[8]{0:T(128)}, u32[]{:S(2)}) %copy-start.5) | copy-done | bytes 56
  3.6 1.0 %pad_maximum_fusion.11 = f32[2,24,8,128]{3,2,1,0:T(8,128)S(1)} fusion(f32[2,12,8,128]{3,2,1,0:T(8,128)} %param.6, f32[2,12,8,128]{3,2,1,0:T(8,128)} %param.5), kind=kLoop, calls=%fused_computation.59 | loop fusion | flops 49152 | bytes 393216 | tf_op jit(solution)/shard_map/concatenate | solution.py:202
  4.8 0.5 collective-permute-start.1
  5.4 2.7 %collective-permute-start = (f32[12544]{0:T(1024)S(1)}, f32[12544]{0:T(1024)S(1)}, u32[]{:S(2)}, u32[]{:S(2)}) collective-permute-start(f32[12544]{0:T(1024)S(1)} %select_n.109), channel_id=1, source_target_pairs={{0,24},{8,16},{16,8},{24,0},{1,25},{9,17},{17,9},{25,1},{2,26},{10... | collective-permute-start | bytes 150536 | tf_op jit(solution)/shard_map/ppermute | solution.py:66
  9.1 1.2 %collective-permute-done = f32[12544]{0:T(1024)S(1)} collective-permute-done((f32[12544]{0:T(1024)S(1)}, f32[12544]{0:T(1024)S(1)}, u32[]{:S(2)}, u32[]{:S(2)}) %collective-permute-start) | collective-permute-done | bytes 50208 | tf_op jit(solution)/shard_map/ppermute | solution.py:66
  12.2 4.3 %collective-permute-start.2 = (f32[1176]{0:T(1024)S(1)}, f32[1176]{0:T(1024)S(1)}, u32[]{:S(2)}, u32[]{:S(2)}) collective-permute-start(f32[1176]{0:T(1024)S(1)} %select_n.117), channel_id=1, source_target_pairs={{0,7},{1,2},{2,1},{3,4},{4,3},{5,6},{6,5},{7,0},{8,15},{9,10},{10,... | collective-permute-start | bytes 14120 | tf_op jit(solution)/shard_map/ppermute | solution.py:66
  17.2 0.6 %copy-done = f32[2,12,8,128]{3,2,1,0:T(8,128)S(1)} copy-done((f32[2,12,8,128]{3,2,1,0:T(8,128)S(1)}, f32[2,12,8,128]{3,2,1,0:T(8,128)}, u32[]{:S(2)}) %copy-start) | copy-done | bytes 98328
  18.0 0.6 %collective-permute-done.2 = f32[1176]{0:T(1024)S(1)} collective-permute-done((f32[1176]{0:T(1024)S(1)}, f32[1176]{0:T(1024)S(1)}, u32[]{:S(2)}, u32[]{:S(2)}) %collective-permute-start.2) | collective-permute-done | bytes 4736 | tf_op jit(solution)/shard_map/ppermute | solution.py:66
  18.7 2.2 %collective-permute-done.3 = f32[1176]{0:T(1024)S(1)} collective-permute-done((f32[1176]{0:T(1024)S(1)}, f32[1176]{0:T(1024)S(1)}, u32[]{:S(2)}, u32[]{:S(2)}) %collective-permute-start.3) | collective-permute-done | bytes 4736 | tf_op jit(solution)/shard_map/ppermute | solution.py:63
  22.0 0.5 fusion.50
  24.5 0.5 convolution_bitcast_fusion
  26.1 1.2 %collective-permute-done.4 = f32[48,128]{1,0:T(8,128)S(1)} collective-permute-done((f32[48,128]{1,0:T(8,128)S(1)}, f32[48,128]{1,0:T(8,128)S(1)}, u32[]{:S(2)}, u32[]{:S(2)}) %collective-permute-start.4) | collective-permute-done | bytes 24608 | tf_op jit(solution)/shard_map/ppermute | solution.py:90
  27.4 1.6 %collective-permute-start.5 = (f32[48,128]{1,0:T(8,128)S(1)}, f32[48,128]{1,0:T(8,128)S(1)}, u32[]{:S(2)}, u32[]{:S(2)}) collective-permute-start(f32[48,128]{1,0:T(8,128)S(1)} %fusion.53), channel_id=1, source_target_pairs={{0,16},{8,24},{16,0},{24,8},{1,17},{9,25},{17,1},{25,9},{2,18},{10... | collective-permute-start | bytes 73736 | tf_op jit(solution)/shard_map/ppermute | solution.py:90
  29.0 2.3 %collective-permute-done.5 = f32[48,128]{1,0:T(8,128)S(1)} collective-permute-done((f32[48,128]{1,0:T(8,128)S(1)}, f32[48,128]{1,0:T(8,128)S(1)}, u32[]{:S(2)}, u32[]{:S(2)}) %collective-permute-start.5) | collective-permute-done | bytes 24608 | tf_op jit(solution)/shard_map/ppermute | solution.py:90
  31.3 3.8 %collective-permute-done.6 = f32[48,128]{1,0:T(8,128)S(1)} collective-permute-done((f32[48,128]{1,0:T(8,128)S(1)}, f32[48,128]{1,0:T(8,128)S(1)}, u32[]{:S(2)}, u32[]{:S(2)}) %collective-permute-start.6) | collective-permute-done | bytes 24608 | tf_op jit(solution)/shard_map/ppermute | solution.py:90
  35.1 3.8 %collective-permute-done.7 = f32[48,128]{1,0:T(8,128)S(1)} collective-permute-done((f32[48,128]{1,0:T(8,128)S(1)}, f32[48,128]{1,0:T(8,128)S(1)}, u32[]{:S(2)}, u32[]{:S(2)}) %collective-permute-start.7) | collective-permute-done | bytes 24608 | tf_op jit(solution)/shard_map/ppermute | solution.py:90
  39.1 4.6 %collective-permute-done.8 = f32[48,128]{1,0:T(8,128)S(1)} collective-permute-done((f32[48,128]{1,0:T(8,128)S(1)}, f32[48,128]{1,0:T(8,128)S(1)}, u32[]{:S(2)}, u32[]{:S(2)}) %collective-permute-start.8) | collective-permute-done | bytes 24608 | tf_op jit(solution)/shard_map/ppermute | solution.py:90
  43.7 0.6 %add.124.packed_ref = f32[48,128]{1,0:T(8,128)} add(f32[48,128]{1,0:T(8,128)S(1)} %add.123, f32[48,128]{1,0:T(8,128)S(1)} %collective-permute-done.8) | non-fusion elementwise | flops 6144 | bytes 73728 | tf_op jit(solution)/shard_map/add | solution.py:90
  44.3 5.7 %shard_map.68 = (f32[72,96]{1,0:T(8,128)}, f32[2,36,36]{2,1,0:T(8,128)}) custom-call(f32[48,128]{1,0:T(8,128)} %add.124.packed_ref), custom_call_target="tpu_custom_call" | custom-call | tf_op jit(solution)/shard_map/pallas_call | solution.py:177
  50.0 0.8 %reshape.152 = f32[2,36,96,1]{2,1,0,3:T(8,128)S(1)} reshape(f32[72,96]{1,0:T(8,128)} %get-tuple-element.4) | data formatting | bytes 55296 | tf_op jit(solution)/shard_map/kj,jrc->krc/dot_general | solution.py:238
  51.3 0.8 %copy.152 = f32[2,36,8,128]{3,2,1,0:T(8,128)} copy(f32[2,36,8,128]{3,1,2,0:T(8,128)S(1)} %fusion.9) | data formatting | bytes 589824
  52.0 0.6 %copy.153 = f32[2,36,36]{2,0,1:T(2,128)} copy(f32[2,36,36]{2,1,0:T(8,128)S(1)} %copy-done.2) | data formatting | bytes 20736
  (80 shorter events, 7.9 us)
Async XLA Ops:
  0.6 0.7 %copy-start.4 = (s32[2]{0:T(128)S(1)}, s32[2]{0:T(128)}, u32[]{:S(2)}) copy-start(s32[2]{0:T(128)} %param.9) | copy-start | bytes 28
  2.9 0.7 %copy-start.3 = (s32[8,128]{1,0:T(8,128)S(1)}, s32[8,128]{1,0:T(8,128)}, u32[]{:S(2)}) copy-start(s32[8,128]{1,0:T(8,128)} %param.7) | copy-start | bytes 12292
  2.9 0.7 %copy-start.5 = (f32[8]{0:T(128)S(1)}, f32[8]{0:T(128)}, u32[]{:S(2)}) copy-start(f32[8]{0:T(128)} %param.8) | copy-start | bytes 100
  4.8 4.3 %collective-permute-start.1 = (f32[12544]{0:T(1024)S(1)}, f32[12544]{0:T(1024)S(1)}, u32[]{:S(2)}, u32[]{:S(2)}) collective-permute-start(f32[12544]{0:T(1024)S(1)} %select_n.111), channel_id=1, source_target_pairs={{0,8},{8,0},{16,24},{24,16},{1,9},{9,1},{17,25},{25,17},{2,10},{10... | collective-permute-start | bytes 150536 | tf_op jit(solution)/shard_map/ppermute | solution.py:63
  5.4 4.9 %collective-permute-start = (f32[12544]{0:T(1024)S(1)}, f32[12544]{0:T(1024)S(1)}, u32[]{:S(2)}, u32[]{:S(2)}) collective-permute-start(f32[12544]{0:T(1024)S(1)} %select_n.109), channel_id=1, source_target_pairs={{0,24},{8,16},{16,8},{24,0},{1,25},{9,17},{17,9},{25,1},{2,26},{10... | collective-permute-start | bytes 150536 | tf_op jit(solution)/shard_map/ppermute | solution.py:66
  12.2 6.4 %collective-permute-start.2 = (f32[1176]{0:T(1024)S(1)}, f32[1176]{0:T(1024)S(1)}, u32[]{:S(2)}, u32[]{:S(2)}) collective-permute-start(f32[1176]{0:T(1024)S(1)} %select_n.117), channel_id=1, source_target_pairs={{0,7},{1,2},{2,1},{3,4},{4,3},{5,6},{6,5},{7,0},{8,15},{9,10},{10,... | collective-permute-start | bytes 14120 | tf_op jit(solution)/shard_map/ppermute | solution.py:66
  16.9 0.9 %copy-start = (f32[2,12,8,128]{3,2,1,0:T(8,128)S(1)}, f32[2,12,8,128]{3,2,1,0:T(8,128)}, u32[]{:S(2)}) copy-start(f32[2,12,8,128]{3,2,1,0:T(8,128)} %param.5) | copy-start | bytes 294916
  17.1 0.9 %copy-start.1 = (f32[2,12,8,128]{3,2,1,0:T(8,128)S(1)}, f32[2,12,8,128]{3,2,1,0:T(8,128)}, u32[]{:S(2)}) copy-start(f32[2,12,8,128]{3,2,1,0:T(8,128)} %param.6) | copy-start | bytes 294916
  17.1 3.7 %collective-permute-start.3 = (f32[1176]{0:T(1024)S(1)}, f32[1176]{0:T(1024)S(1)}, u32[]{:S(2)}, u32[]{:S(2)}) collective-permute-start(f32[1176]{0:T(1024)S(1)} %select_n.119), channel_id=1, source_target_pairs={{0,1},{1,0},{2,3},{3,2},{4,5},{5,4},{6,7},{7,6},{8,9},{9,8},{10,11... | collective-permute-start | bytes 14120 | tf_op jit(solution)/shard_map/ppermute | solution.py:63
  26.0 1.3 %collective-permute-start.4 = (f32[48,128]{1,0:T(8,128)S(1)}, f32[48,128]{1,0:T(8,128)S(1)}, u32[]{:S(2)}, u32[]{:S(2)}) collective-permute-start(f32[48,128]{1,0:T(8,128)S(1)} %pad_maximum_fusion.16), channel_id=1, source_target_pairs={{0,8},{8,0},{16,24},{24,16},{1,9},{9,1},{17,25},{25,17},{2,10},{10... | collective-permute-start | bytes 73736 | tf_op jit(solution)/shard_map/ppermute | solution.py:90
  27.4 3.9 %collective-permute-start.5 = (f32[48,128]{1,0:T(8,128)S(1)}, f32[48,128]{1,0:T(8,128)S(1)}, u32[]{:S(2)}, u32[]{:S(2)}) collective-permute-start(f32[48,128]{1,0:T(8,128)S(1)} %fusion.53), channel_id=1, source_target_pairs={{0,16},{8,24},{16,0},{24,8},{1,17},{9,25},{17,1},{25,9},{2,18},{10... | collective-permute-start | bytes 73736 | tf_op jit(solution)/shard_map/ppermute | solution.py:90
  31.3 3.8 %collective-permute-start.6 = (f32[48,128]{1,0:T(8,128)S(1)}, f32[48,128]{1,0:T(8,128)S(1)}, u32[]{:S(2)}, u32[]{:S(2)}) collective-permute-start(f32[48,128]{1,0:T(8,128)S(1)} %add.121), channel_id=1, source_target_pairs={{0,1},{1,0},{2,3},{3,2},{4,5},{5,4},{6,7},{7,6},{8,9},{9,8},{10,11... | collective-permute-start | bytes 73736 | tf_op jit(solution)/shard_map/ppermute | solution.py:90
  35.1 3.8 %collective-permute-start.7 = (f32[48,128]{1,0:T(8,128)S(1)}, f32[48,128]{1,0:T(8,128)S(1)}, u32[]{:S(2)}, u32[]{:S(2)}) collective-permute-start(f32[48,128]{1,0:T(8,128)S(1)} %add.122), channel_id=1, source_target_pairs={{0,2},{1,3},{2,0},{3,1},{4,6},{5,7},{6,4},{7,5},{8,10},{9,11},{10,... | collective-permute-start | bytes 73736 | tf_op jit(solution)/shard_map/ppermute | solution.py:90
  39.0 4.7 %collective-permute-start.8 = (f32[48,128]{1,0:T(8,128)S(1)}, f32[48,128]{1,0:T(8,128)S(1)}, u32[]{:S(2)}, u32[]{:S(2)}) collective-permute-start(f32[48,128]{1,0:T(8,128)S(1)} %add.123), channel_id=1, source_target_pairs={{0,4},{1,5},{2,6},{3,7},{4,0},{5,1},{6,2},{7,3},{8,12},{9,13},{10,... | collective-permute-start | bytes 73736 | tf_op jit(solution)/shard_map/ppermute | solution.py:90
  51.2 0.8 %copy-start.2 = (f32[2,36,36]{2,1,0:T(8,128)S(1)}, f32[2,36,36]{2,1,0:T(8,128)}, u32[]{:S(2)}) copy-start(f32[2,36,36]{2,1,0:T(8,128)} %get-tuple-element.17) | copy-start | bytes 31108

commit v7 on v5

--- a/solution.py
+++ b/solution.py
@@ -38,13 +38,14 @@
 
 
 def complex_gram(first_block, second_block):
-    highest = lax.Precision.HIGHEST
-    first_flat = first_block.reshape(first_block.shape[0], first_block.shape[1], -1)
-    second_flat = second_block.reshape(second_block.shape[0], second_block.shape[1], -1)
-    real_part = jnp.einsum("pjc,pkc->jk", first_flat, second_flat, precision=highest)
-    imag_part = jnp.einsum(
-        "jc,kc->jk", first_flat[0], second_flat[1], precision=highest
-    ) - jnp.einsum("jc,kc->jk", first_flat[1], second_flat[0], precision=highest)
+    count = first_block.shape[1]
+    first_flat = first_block.reshape((2 * count,) + first_block.shape[2:])
+    second_flat = second_block.reshape((2 * count,) + second_block.shape[2:])
+    products = jnp.einsum(
+        "jrc,krc->jk", first_flat, second_flat, precision=lax.Precision.HIGHEST
+    )
+    real_part = products[:count, :count] + products[count:, count:]
+    imag_part = products[:count, count:] - products[count:, :count]
     return (real_part, imag_part)
 
 
@@ -103,10 +104,13 @@
     return jnp.dot(mixing.T, jnp.dot(matrix, mixing, precision=highest), precision=highest)
 
 
-def exchange_rim(cells, axis, dim, width, low_angle, high_angle):
+def exchange_rim(cells, axis, dim, width, low_angle, high_angle, strips=None):
     count = lax.axis_size(axis)
-    head = lax.slice_in_dim(cells, 0, width, axis=dim)
-    tail = lax.slice_in_dim(cells, cells.shape[dim] - width, cells.shape[dim], axis=dim)
+    if strips is None:
+        head = lax.slice_in_dim(cells, 0, width, axis=dim)
+        tail = lax.slice_in_dim(cells, cells.shape[dim] - width, cells.shape[dim], axis=dim)
+    else:
+        head, tail = strips
     if count % 2:
         before = lax.ppermute(tail.reshape(-1), axis, [(i, (i + 1) % count) for i in range(count)])
         after = lax.ppermute(head.reshape(-1), axis, [((i + 1) % count, i) for i in range(count)])
@@ -248,12 +252,22 @@
     height = bands.shape[2]
     breadth = bands.shape[3]
     levels = jnp.arange(permittivity.shape[0], dtype=jnp.int32)
-    stiffness = jnp.sum(
-        jnp.where(
-            materials[None] == levels[:, None, None], (1.0 / permittivity)[:, None, None], 0.0
-        ),
-        axis=0,
-    )
+
+    def stiffness_of(cells):
+        return jnp.sum(
+            jnp.where(
+                cells[None] == levels[:, None, None], (1.0 / permittivity)[:, None, None], 0.0
+            ),
+            axis=0,
+        )
+
+    def strip_of(start, stop):
+        field_rows = jnp.concatenate(
+            [bands[:, :, start:stop], directions[:, :, start:stop]], axis=1
+        ).reshape(4 * band_count, stop - start, breadth)
+        return jnp.concatenate([field_rows, stiffness_of(materials[start:stop])[None]], axis=0)
+
+    stiffness = stiffness_of(materials)
     angle_row = 2.0 * math.pi * wavevector[0].astype(jnp.float32) / KDEN
     angle_col = 2.0 * math.pi * wavevector[1].astype(jnp.float32) / KDEN
     row_index = lax.axis_index("row")
@@ -269,6 +283,7 @@
         2,
         jnp.where(row_index == 0, -angle_row, 0.0),
         jnp.where(row_index == lax.axis_size("row") - 1, angle_row, 0.0),
+        (strip_of(0, 2), strip_of(height - 2, height)),
     )
     padded = exchange_rim(
         padded,

time: 51.1 us -> 51 us (level)
  matrix products: 2.71 us -> 1.37 us
  starting transfers between devices: 9.55 us -> 10.7 us
  other arithmetic: 3.14 us -> 3.79 us
  waiting for transfers between devices: 17.6 us -> 17 us
    slice x1 -> x3, local copies, waits for them, and re-layouts: 0.49 us -> 2.74 us  [the longest x1 0.99 us: strip_of(): directions[:, :, start:stop]]
    unnamed x17 -> x16, local copies, waits for them, and re-layouts: 3.67 us -> 1.46 us
    ppermute x2, waiting for transfers between devices: 1.73 us -> 0.01 us  [exchange_rim(): lax.ppermute(jnp.where(even, tail, head).reshape(-1), axis, [(i, i ^ 1) f...]
    ppermute x2, waiting for transfers between devices: 0.62 us -> 2.3 us  [exchange_rim(): lax.ppermute(jnp.where(even, head, tail).reshape(-1), axis, [(i, (i + 1)...]
    dot_general x6 -> x2, matrix products: 2.23 us -> 0.94 us  [complex_gram(): jnp.einsum('jrc,krc->jk', first_flat, second_flat, precision=lax.Precisio...]
    ppermute x2, starting transfers between devices: 0.59 us -> 1.83 us  [exchange_rim(): lax.ppermute(jnp.where(even, tail, head).reshape(-1), axis, [(i, i ^ 1) f...]
    concatenate x1, other arithmetic: 0.96 us -> 0.02 us  [body(): fields = jnp.concatenate([bands, directions], axis=1)]
    ppermute x2, starting transfers between devices: 7.04 us -> 6.27 us  [exchange_rim(): lax.ppermute(jnp.where(even, head, tail).reshape(-1), axis, [(i, (i + 1)...]
  transfers between devices with their start and end apart: 9 -> 9, of which waited for: 7 -> 7; matrix products, arithmetic and copies ran while one was open for 2% -> 1% of each run, Pallas kernels for 0% -> 0%
where the time goes in v7:
time: 51 us; the launch traced here: 50.6 us
  waiting for transfers between devices  17 us (33%)
  starting transfers between devices  10.7 us (21%)
  local copies, waits for them, and re-layouts  9.16 us (18%)
  Pallas kernels  5.63 us (11%)
  other arithmetic  3.79 us (7%)
  between operations  3.03 us (6%)
  matrix products  1.37 us (3%)
    ppermute x5, waiting for transfers between devices, tree_sum(): lax.ppermute(value, axis, [(i, i ^ step) for i in range(count)])  14.7 us
    ppermute x2, starting transfers between devices, exchange_rim(): lax.ppermute(jnp.where(even, head, tail).reshape(-1), axis, [(i, (i + 1)...  6.27 us
    pallas_call x1, Pallas kernels, matrix_stage(): pl.pallas_call(functools.partial(matrix_kernel, band_count=band_count, sc...  5.63 us
    ppermute x5, starting transfers between devices, tree_sum(): lax.ppermute(value, axis, [(i, i ^ step) for i in range(count)])  2.57 us
    ppermute x2, waiting for transfers between devices, exchange_rim(): lax.ppermute(jnp.where(even, head, tail).reshape(-1), axis, [(i, (i + 1)...  2.3 us
    ppermute x2, starting transfers between devices, exchange_rim(): lax.ppermute(jnp.where(even, tail, head).reshape(-1), axis, [(i, i ^ 1) f...  1.83 us
    unnamed x16, local copies, waits for them, and re-layouts  1.46 us
  transfers between devices with their start and end apart: 9, of which 7 were waited for; matrix products, arithmetic and copies ran while one was open for 1% of the time, Pallas kernels for 0%

profile of v7, /device:TPU:0, one launch (start us, length us, event | category | flops | bytes accessed | tf_op | source)
XLA Modules:
  0.0 50.6 jit_solution(10950252196946546750)
XLA Ops:
  0.7 0.7 %broadcast_divide_fusion.1 = f32[8]{0:T(128)S(1)} fusion(f32[8]{0:T(128)} %param.8), kind=kLoop, calls=%fused_computation.102 | loop fusion | flops 8 | bytes 64 | tf_op jit(solution)/shard_map/div | solution.py:259
  1.4 0.8 %fusion.37 = (s32[2,128]{1,0:T(2,128)S(1)}, s32[2,128]{1,0:T(2,128)S(1)}) fusion(s32[8,128]{1,0:T(8,128)} %param.7), kind=kLoop, calls=%fused_computation.105 | loop fusion | bytes 4096 | tf_op jit(solution)/shard_map/slice | solution.py:268
  2.2 1.0 %fusion.35 = (f32[2,12,2,128]{3,2,1,0:T(2,128)S(1)}, f32[2,12,2,128]{3,2,1,0:T(2,128)S(1)}) fusion(f32[2,12,8,128]{3,2,1,0:T(8,128)} %param.5), kind=kLoop, calls=%fused_computation.103 | loop fusion | bytes 98304 | tf_op jit(solution)/shard_map/slice | solution.py:266
  3.2 1.0 %fusion.36 = (f32[2,12,2,128]{3,2,1,0:T(2,128)S(1)}, f32[2,12,2,128]{3,2,1,0:T(2,128)S(1)}) fusion(f32[2,12,8,128]{3,2,1,0:T(8,128)} %param.6), kind=kLoop, calls=%fused_computation.104 | loop fusion | bytes 98304 | tf_op jit(solution)/shard_map/slice | solution.py:266
  4.5 0.5 %collective-permute-start.1 = (f32[12544]{0:T(1024)S(1)}, f32[12544]{0:T(1024)S(1)}, u32[]{:S(2)}, u32[]{:S(2)}) collective-permute-start(f32[12544]{0:T(1024)S(1)} %select_n.109), channel_id=1, source_target_pairs={{0,8},{8,0},{16,24},{24,16},{1,9},{9,1},{17,25},{25,17},{2,10},{10... | collective-permute-start | bytes 150536 | tf_op jit(solution)/shard_map/ppermute | solution.py:119
  5.1 2.7 %collective-permute-start = (f32[12544]{0:T(1024)S(1)}, f32[12544]{0:T(1024)S(1)}, u32[]{:S(2)}, u32[]{:S(2)}) collective-permute-start(f32[12544]{0:T(1024)S(1)} %select_n.107), channel_id=1, source_target_pairs={{0,24},{8,16},{16,8},{24,0},{1,25},{9,17},{17,9},{25,1},{2,26},{10... | collective-permute-start | bytes 150536 | tf_op jit(solution)/shard_map/ppermute | solution.py:122
  7.9 0.6 %fusion.38 = (s32[1]{0:T(128)}, s32[1]{0:T(128)}) fusion(s32[2]{0:T(128)S(1)} %copy-done.4), kind=kLoop, calls=%fused_computation.106 | loop fusion | bytes 16 | tf_op jit(solution)/shard_map/slice | solution.py:272
  10.7 1.3 %collective-permute-start.3 = (f32[1176]{0:T(1024)S(1)}, f32[1176]{0:T(1024)S(1)}, u32[]{:S(2)}, u32[]{:S(2)}) collective-permute-start(f32[1176]{0:T(1024)S(1)} %reshape.267), channel_id=1, source_target_pairs={{0,1},{1,0},{2,3},{3,2},{4,5},{5,4},{6,7},{7,6},{8,9},{9,8},{10,11... | collective-permute-start | bytes 14120 | tf_op jit(solution)/shard_map/ppermute | solution.py:119
  12.0 3.6 %collective-permute-start.2 = (f32[1176]{0:T(1024)S(1)}, f32[1176]{0:T(1024)S(1)}, u32[]{:S(2)}, u32[]{:S(2)}) collective-permute-start(f32[1176]{0:T(1024)S(1)} %reshape.266), channel_id=1, source_target_pairs={{0,7},{1,2},{2,1},{3,4},{4,3},{5,6},{6,5},{7,0},{8,15},{9,10},{10,... | collective-permute-start | bytes 14120 | tf_op jit(solution)/shard_map/ppermute | solution.py:122
  16.6 1.8 %collective-permute-done.2 = f32[1176]{0:T(1024)S(1)} collective-permute-done((f32[1176]{0:T(1024)S(1)}, f32[1176]{0:T(1024)S(1)}, u32[]{:S(2)}, u32[]{:S(2)}) %collective-permute-start.2) | collective-permute-done | bytes 4736 | tf_op jit(solution)/shard_map/ppermute | solution.py:122
  20.6 0.6 %pad_maximum_fusion.1 = f32[48,12,132]{2,1,0:T(8,128)S(1)} fusion(f32[49,12,2]{2,1,0:T(8,128)S(1)} %copy.93, f32[49,12,2]{2,1,0:T(8,128)S(1)} %copy.92, f32[1,2,128]{2,1,0:T(2,128)S(1)} %get-tuple-element.62, f32[48,2,128]{2,1,0:T(2,128)S(1)} %bitcast.69, f32[1,8,128]{2,1,0:T(8,128)S(1)} %bitcast.81, f32[48,8,128]{2,1,0:T(8,128)S(1)} %bitcast.63, ...), kind=kLoop, calls=%fused_computation.3 | loop fusion | flops 532224 | bytes 614592 | tf_op jit(solution)/shard_map/concatenate | solution.py:131
  21.4 0.6 %broadcast_divide_fusion = (f32[2,12,10,130]{3,2,1,0:T(8,128)S(1)}, f32[2,12,10,130]{3,2,1,0:T(8,128)S(1)}, f32[2,12,10,130]{3,2,1,0:T(8,128)S(1)}, f32[2,12,10,130]{3,2,1,0:T(8,128)S(1)}) fusion(f32[10,130]{1,0:T(8,128)S(1)} %get-tuple-element.27, f32[2,24,12,132]{3,2,1,0:T(8,128)S(1)} %bitcast.57, f32[10,130]{1,0:T(8,128)S(1)} %get-tuple-element.31, ...), kind=kLoop, calls=%fused_computation.36 | loop fusion | flops 343200 | bytes 1274000 | tf_op jit(solution)/shard_map/div | solution.py:303
  24.3 1.2 %collective-permute-done.4 = f32[4608]{0:T(1024)S(1)} collective-permute-done((f32[4608]{0:T(1024)S(1)}, f32[4608]{0:T(1024)S(1)}, u32[]{:S(2)}, u32[]{:S(2)}) %collective-permute-start.4) | collective-permute-done | bytes 18464 | tf_op jit(solution)/shard_map/ppermute | solution.py:148
  25.5 1.5 %collective-permute-start.5 = (f32[4608]{0:T(1024)S(1)}, f32[4608]{0:T(1024)S(1)}, u32[]{:S(2)}, u32[]{:S(2)}) collective-permute-start(f32[4608]{0:T(1024)S(1)} %add.132), channel_id=1, source_target_pairs={{0,16},{8,24},{16,0},{24,8},{1,17},{9,25},{17,1},{25,9},{2,18},{10... | collective-permute-start | bytes 55304 | tf_op jit(solution)/shard_map/ppermute | solution.py:148
  27.0 2.3 %collective-permute-done.5 = f32[4608]{0:T(1024)S(1)} collective-permute-done((f32[4608]{0:T(1024)S(1)}, f32[4608]{0:T(1024)S(1)}, u32[]{:S(2)}, u32[]{:S(2)}) %collective-permute-start.5) | collective-permute-done | bytes 18464 | tf_op jit(solution)/shard_map/ppermute | solution.py:148
  29.3 3.8 %collective-permute-done.6 = f32[4608]{0:T(1024)S(1)} collective-permute-done((f32[4608]{0:T(1024)S(1)}, f32[4608]{0:T(1024)S(1)}, u32[]{:S(2)}, u32[]{:S(2)}) %collective-permute-start.6) | collective-permute-done | bytes 18464 | tf_op jit(solution)/shard_map/ppermute | solution.py:148
  33.1 3.8 %collective-permute-done.7 = f32[4608]{0:T(1024)S(1)} collective-permute-done((f32[4608]{0:T(1024)S(1)}, f32[4608]{0:T(1024)S(1)}, u32[]{:S(2)}, u32[]{:S(2)}) %collective-permute-start.7) | collective-permute-done | bytes 18464 | tf_op jit(solution)/shard_map/ppermute | solution.py:148
  36.8 1.0 %collective-permute-start.8 = (f32[4608]{0:T(1024)S(1)}, f32[4608]{0:T(1024)S(1)}, u32[]{:S(2)}, u32[]{:S(2)}) collective-permute-start(f32[4608]{0:T(1024)S(1)} %add.135), channel_id=1, source_target_pairs={{0,4},{1,5},{2,6},{3,7},{4,0},{5,1},{6,2},{7,3},{8,12},{9,13},{10,... | collective-permute-start | bytes 55304 | tf_op jit(solution)/shard_map/ppermute | solution.py:148
  37.8 3.7 %collective-permute-done.8 = f32[4608]{0:T(1024)S(1)} collective-permute-done((f32[4608]{0:T(1024)S(1)}, f32[4608]{0:T(1024)S(1)}, u32[]{:S(2)}, u32[]{:S(2)}) %collective-permute-start.8) | collective-permute-done | bytes 18464 | tf_op jit(solution)/shard_map/ppermute | solution.py:148
  41.5 0.7 %reshape.274.packed_ref = f32[2,48,48]{2,1,0:T(8,128)} reshape(f32[4608]{0:T(1024)S(1)} %add.136) | data formatting | bytes 36864 | tf_op jit(solution)/shard_map/reshape | solution.py:318
  42.2 5.6 %shard_map.68 = (f32[128,128]{1,0:T(8,128)}, f32[128,128]{1,0:T(8,128)}) custom-call(f32[2,48,48]{2,1,0:T(8,128)} %reshape.274.packed_ref), custom_call_target="tpu_custom_call" | custom-call | tf_op jit(solution)/shard_map/pallas_call | solution.py:241
  47.9 0.8 %slice_bitcast_fusion = f32[72,96]{0,1:T(8,128)S(1)} fusion(f32[128,128]{1,0:T(8,128)} %get-tuple-element.4), kind=kLoop, calls=%fused_computation.46 | loop fusion | bytes 55296 | tf_op jit(solution)/shard_map/jrc,jk->krc/dot_general | solution.py:325
  49.2 0.8 %copy.97 = f32[2,36,8,128]{3,2,1,0:T(8,128)} copy(f32[2,36,8,128]{3,1,2,0:T(8,128)S(1)} %fusion.12) | data formatting | bytes 589824
  50.0 0.6 %copy.98 = f32[2,36,36]{2,0,1:T(2,128)} copy(f32[2,36,36]{2,1,0:T(8,128)S(1)} %pad_maximum_fusion.18) | data formatting | bytes 20736
  (88 shorter events, 6.7 us)
Async XLA Ops:
  0.6 7.1 %copy-start.3 = (s32[8,128]{1,0:T(8,128)S(1)}, s32[8,128]{1,0:T(8,128)}, u32[]{:S(2)}) copy-start(s32[8,128]{1,0:T(8,128)} %param.7) | copy-start | bytes 12292
  0.6 7.2 %copy-start.1 = (f32[2,12,8,128]{3,2,1,0:T(8,128)S(1)}, f32[2,12,8,128]{3,2,1,0:T(8,128)}, u32[]{:S(2)}) copy-start(f32[2,12,8,128]{3,2,1,0:T(8,128)} %param.5) | copy-start | bytes 294916
  0.7 7.2 %copy-start = (f32[2,12,8,128]{3,2,1,0:T(8,128)S(1)}, f32[2,12,8,128]{3,2,1,0:T(8,128)}, u32[]{:S(2)}) copy-start(f32[2,12,8,128]{3,2,1,0:T(8,128)} %param.6) | copy-start | bytes 294916
  0.7 7.2 %copy-start.4 = (s32[2]{0:T(128)S(1)}, s32[2]{0:T(128)}, u32[]{:S(2)}) copy-start(s32[2]{0:T(128)} %param.9) | copy-start | bytes 28
  4.5 5.0 %collective-permute-start.1 = (f32[12544]{0:T(1024)S(1)}, f32[12544]{0:T(1024)S(1)}, u32[]{:S(2)}, u32[]{:S(2)}) collective-permute-start(f32[12544]{0:T(1024)S(1)} %select_n.109), channel_id=1, source_target_pairs={{0,8},{8,0},{16,24},{24,16},{1,9},{9,1},{17,25},{25,17},{2,10},{10... | collective-permute-start | bytes 150536 | tf_op jit(solution)/shard_map/ppermute | solution.py:119
  5.1 4.9 %collective-permute-start = (f32[12544]{0:T(1024)S(1)}, f32[12544]{0:T(1024)S(1)}, u32[]{:S(2)}, u32[]{:S(2)}) collective-permute-start(f32[12544]{0:T(1024)S(1)} %select_n.107), channel_id=1, source_target_pairs={{0,24},{8,16},{16,8},{24,0},{1,25},{9,17},{17,9},{25,1},{2,26},{10... | collective-permute-start | bytes 150536 | tf_op jit(solution)/shard_map/ppermute | solution.py:122
  10.7 5.9 %collective-permute-start.3 = (f32[1176]{0:T(1024)S(1)}, f32[1176]{0:T(1024)S(1)}, u32[]{:S(2)}, u32[]{:S(2)}) collective-permute-start(f32[1176]{0:T(1024)S(1)} %reshape.267), channel_id=1, source_target_pairs={{0,1},{1,0},{2,3},{3,2},{4,5},{5,4},{6,7},{7,6},{8,9},{9,8},{10,11... | collective-permute-start | bytes 14120 | tf_op jit(solution)/shard_map/ppermute | solution.py:119
  12.0 6.3 %collective-permute-start.2 = (f32[1176]{0:T(1024)S(1)}, f32[1176]{0:T(1024)S(1)}, u32[]{:S(2)}, u32[]{:S(2)}) collective-permute-start(f32[1176]{0:T(1024)S(1)} %reshape.266), channel_id=1, source_target_pairs={{0,7},{1,2},{2,1},{3,4},{4,3},{5,6},{6,5},{7,0},{8,15},{9,10},{10,... | collective-permute-start | bytes 14120 | tf_op jit(solution)/shard_map/ppermute | solution.py:122
  24.2 1.3 %collective-permute-start.4 = (f32[4608]{0:T(1024)S(1)}, f32[4608]{0:T(1024)S(1)}, u32[]{:S(2)}, u32[]{:S(2)}) collective-permute-start(f32[4608]{0:T(1024)S(1)} %reshape.273), channel_id=1, source_target_pairs={{0,8},{8,0},{16,24},{24,16},{1,9},{9,1},{17,25},{25,17},{2,10},{10... | collective-permute-start | bytes 55304 | tf_op jit(solution)/shard_map/ppermute | solution.py:148
  25.5 3.8 %collective-permute-start.5 = (f32[4608]{0:T(1024)S(1)}, f32[4608]{0:T(1024)S(1)}, u32[]{:S(2)}, u32[]{:S(2)}) collective-permute-start(f32[4608]{0:T(1024)S(1)} %add.132), channel_id=1, source_target_pairs={{0,16},{8,24},{16,0},{24,8},{1,17},{9,25},{17,1},{25,9},{2,18},{10... | collective-permute-start | bytes 55304 | tf_op jit(solution)/shard_map/ppermute | solution.py:148
  29.3 3.8 %collective-permute-start.6 = (f32[4608]{0:T(1024)S(1)}, f32[4608]{0:T(1024)S(1)}, u32[]{:S(2)}, u32[]{:S(2)}) collective-permute-start(f32[4608]{0:T(1024)S(1)} %add.133), channel_id=1, source_target_pairs={{0,1},{1,0},{2,3},{3,2},{4,5},{5,4},{6,7},{7,6},{8,9},{9,8},{10,11... | collective-permute-start | bytes 55304 | tf_op jit(solution)/shard_map/ppermute | solution.py:148
  33.1 3.8 %collective-permute-start.7 = (f32[4608]{0:T(1024)S(1)}, f32[4608]{0:T(1024)S(1)}, u32[]{:S(2)}, u32[]{:S(2)}) collective-permute-start(f32[4608]{0:T(1024)S(1)} %add.134), channel_id=1, source_target_pairs={{0,2},{1,3},{2,0},{3,1},{4,6},{5,7},{6,4},{7,5},{8,10},{9,11},{10,... | collective-permute-start | bytes 55304 | tf_op jit(solution)/shard_map/ppermute | solution.py:148
  36.8 4.7 %collective-permute-start.8 = (f32[4608]{0:T(1024)S(1)}, f32[4608]{0:T(1024)S(1)}, u32[]{:S(2)}, u32[]{:S(2)}) collective-permute-start(f32[4608]{0:T(1024)S(1)} %add.135), channel_id=1, source_target_pairs={{0,4},{1,5},{2,6},{3,7},{4,0},{5,1},{6,2},{7,3},{8,12},{9,13},{10,... | collective-permute-start | bytes 55304 | tf_op jit(solution)/shard_map/ppermute | solution.py:148
  47.9 2.1 %copy-start.2 = (f32[128,128]{1,0:T(8,128)S(1)}, f32[128,128]{1,0:T(8,128)}, u32[]{:S(2)}) copy-start(f32[128,128]{1,0:T(8,128)} %get-tuple-element.5) | copy-start | bytes 196612

commit v8 on v7

--- a/solution.py
+++ b/solution.py
@@ -104,7 +104,7 @@
     return jnp.dot(mixing.T, jnp.dot(matrix, mixing, precision=highest), precision=highest)
 
 
-def exchange_rim(cells, axis, dim, width, low_angle, high_angle, strips=None):
+def exchange_rim(cells, axis, dim, width, strips=None):
     count = lax.axis_size(axis)
     if strips is None:
         head = lax.slice_in_dim(cells, 0, width, axis=dim)
@@ -128,15 +128,7 @@
         after = jnp.where(even, first, second)
     before = before.reshape(tail.shape)
     after = after.reshape(head.shape)
-    return jnp.concatenate(
-        [rotate_rim(before, low_angle), cells, rotate_rim(after, high_angle)], axis=dim
-    )
-
-
-def rotate_rim(rim, phase_angle):
-    field_part = rim[:-1].reshape((2, -1) + rim.shape[1:])
-    turned = rotate(field_part, phase_angle).reshape((-1,) + rim.shape[1:])
-    return jnp.concatenate([turned, rim[-1:]], axis=0)
+    return jnp.concatenate([before, cells, after], axis=dim)
 
 
 def tree_sum(value, axis):
@@ -276,25 +268,19 @@
     packed = jnp.concatenate(
         [fields.reshape(4 * band_count, height, breadth), stiffness[None]], axis=0
     )
-    padded = exchange_rim(
-        packed,
-        "row",
-        1,
-        2,
-        jnp.where(row_index == 0, -angle_row, 0.0),
-        jnp.where(row_index == lax.axis_size("row") - 1, angle_row, 0.0),
-        (strip_of(0, 2), strip_of(height - 2, height)),
-    )
-    padded = exchange_rim(
-        padded,
-        "col",
-        2,
-        2,
-        jnp.where(col_index == 0, -angle_col, 0.0),
-        jnp.where(col_index == lax.axis_size("col") - 1, angle_col, 0.0),
-    )
+    padded = exchange_rim(packed, "row", 1, 2, (strip_of(0, 2), strip_of(height - 2, height)))
+    padded = exchange_rim(padded, "col", 2, 2)
     stiff_wide = padded[-1]
     field_wide = padded[:-1].reshape(2, 2 * band_count, height + 4, breadth + 4)
+    row_place = jnp.arange(height + 4)
+    col_place = jnp.arange(breadth + 4)
+    row_phase = jnp.where(row_place < 2, jnp.where(row_index == 0, -angle_row, 0.0), 0.0) + jnp.where(
+        row_place >= height + 2, jnp.where(row_index == lax.axis_size("row") - 1, angle_row, 0.0), 0.0
+    )
+    col_phase = jnp.where(col_place < 2, jnp.where(col_index == 0, -angle_col, 0.0), 0.0) + jnp.where(
+        col_place >= breadth + 2, jnp.where(col_index == lax.axis_size("col") - 1, angle_col, 0.0), 0.0
+    )
+    field_wide = rotate(field_wide, row_phase[:, None] + col_phase[None, :])
     band_wide = field_wide[:, :band_count]
     applied_ring, diagonal_ring = stencil(band_wide, stiff_wide)
     stiff_ring = stiff_wide[1:-1, 1:-1]

time: 51 us -> 50 us (0.980)
  local copies, waits for them, and re-layouts: 9.16 us -> 7.91 us
  between operations: 3.03 us -> 2.41 us
  waiting for transfers between devices: 17 us -> 17.6 us
    another operation x4 -> x2, other arithmetic: 0.12 us -> 1.17 us  [rotate(): jnp.stack([values[0] * cosine - values[1] * sine_part, values[0] * sine_p...]
    concatenate x4 -> x1, other arithmetic: 0.82 us -> 0.08 us  [exchange_rim(): return jnp.concatenate([before, cells, after], axis=dim)]
    concatenate x2 -> x0, local copies, waits for them, and re-layouts: 0.58 us -> none  [rotate_rim(): return jnp.concatenate([turned, rim[-1:]], axis=0)]
    another operation x4 -> x0, local copies, waits for them, and re-layouts: 0.53 us -> none  [rotate(): jnp.stack([values[0] * cosine - values[1] * sine_part, values[0] * sine_p...]
  transfers between devices with their start and end apart: 9 -> 9, of which waited for: 7 -> 7; matrix products, arithmetic and copies ran while one was open for 1% -> 2% of each run, Pallas kernels for 0% -> 0%
where the time goes in v8:
time: 50 us; the launch traced here: 49.7 us
  waiting for transfers between devices  17.6 us (35%)
  starting transfers between devices  10.7 us (21%)
  local copies, waits for them, and re-layouts  7.91 us (16%)
  Pallas kernels  5.62 us (11%)
  other arithmetic  4.12 us (8%)
  between operations  2.41 us (5%)
  matrix products  1.36 us (3%)
    ppermute x5, waiting for transfers between devices, tree_sum(): lax.ppermute(value, axis, [(i, i ^ step) for i in range(count)])  14.9 us
    ppermute x2, starting transfers between devices, exchange_rim(): lax.ppermute(jnp.where(even, head, tail).reshape(-1), axis, [(i, (i + 1)...  6.27 us
    pallas_call x1, Pallas kernels, matrix_stage(): pl.pallas_call(functools.partial(matrix_kernel, band_count=band_count, sc...  5.62 us
    ppermute x2, waiting for transfers between devices, exchange_rim(): lax.ppermute(jnp.where(even, head, tail).reshape(-1), axis, [(i, (i + 1)...  2.71 us
    ppermute x5, starting transfers between devices, tree_sum(): lax.ppermute(value, axis, [(i, i ^ step) for i in range(count)])  2.39 us
    ppermute x2, starting transfers between devices, exchange_rim(): lax.ppermute(jnp.where(even, tail, head).reshape(-1), axis, [(i, i ^ 1) f...  2.01 us
    unnamed x16, local copies, waits for them, and re-layouts  1.46 us
    another operation x2, other arithmetic, rotate(): jnp.stack([values[0] * cosine - values[1] * sine_part, values[0] * sine_p...  1.17 us
  transfers between devices with their start and end apart: 9, of which 7 were waited for; matrix products, arithmetic and copies ran while one was open for 2% of the time, Pallas kernels for 0%

profile of v8, /device:TPU:0, one launch (start us, length us, event | category | flops | bytes accessed | tf_op | source)
XLA Modules:
  0.0 49.7 jit_solution(10717690616553306576)
XLA Ops:
  0.7 0.7 %broadcast_divide_fusion.2 = f32[8]{0:T(128)S(1)} fusion(f32[8]{0:T(128)} %param.8), kind=kLoop, calls=%fused_computation.112 | loop fusion | flops 8 | bytes 64 | tf_op jit(solution)/shard_map/div | solution.py:251
  1.4 0.8 %fusion.47 = (s32[2,128]{1,0:T(2,128)S(1)}, s32[2,128]{1,0:T(2,128)S(1)}) fusion(s32[8,128]{1,0:T(8,128)} %param.7), kind=kLoop, calls=%fused_computation.115 | loop fusion | bytes 4096 | tf_op jit(solution)/shard_map/slice | solution.py:260
  2.2 1.0 %fusion.45 = (f32[2,12,2,128]{3,2,1,0:T(2,128)S(1)}, f32[2,12,2,128]{3,2,1,0:T(2,128)S(1)}) fusion(f32[2,12,8,128]{3,2,1,0:T(8,128)} %param.5), kind=kLoop, calls=%fused_computation.113 | loop fusion | bytes 98304 | tf_op jit(solution)/shard_map/slice | solution.py:258
  3.2 1.0 %fusion.46 = (f32[2,12,2,128]{3,2,1,0:T(2,128)S(1)}, f32[2,12,2,128]{3,2,1,0:T(2,128)S(1)}) fusion(f32[2,12,8,128]{3,2,1,0:T(8,128)} %param.6), kind=kLoop, calls=%fused_computation.114 | loop fusion | bytes 98304 | tf_op jit(solution)/shard_map/slice | solution.py:258
  5.1 2.7 %collective-permute-start = (f32[12544]{0:T(1024)S(1)}, f32[12544]{0:T(1024)S(1)}, u32[]{:S(2)}, u32[]{:S(2)}) collective-permute-start(f32[12544]{0:T(1024)S(1)} %select_n.137), channel_id=1, source_target_pairs={{0,24},{8,16},{16,8},{24,0},{1,25},{9,17},{17,9},{25,1},{2,26},{10... | collective-permute-start | bytes 150536 | tf_op jit(solution)/shard_map/ppermute | solution.py:122
  7.9 0.6 %fusion.48 = (s32[1]{0:T(128)}, s32[1]{0:T(128)}) fusion(s32[2]{0:T(128)S(1)} %copy-done.4), kind=kLoop, calls=%fused_computation.116 | loop fusion | bytes 16 | tf_op jit(solution)/shard_map/slice | solution.py:263
  10.7 1.5 %collective-permute-start.3 = (f32[1176]{0:T(1024)S(1)}, f32[1176]{0:T(1024)S(1)}, u32[]{:S(2)}, u32[]{:S(2)}) collective-permute-start(f32[1176]{0:T(1024)S(1)} %reshape.162), channel_id=1, source_target_pairs={{0,1},{1,0},{2,3},{3,2},{4,5},{5,4},{6,7},{7,6},{8,9},{9,8},{10,11... | collective-permute-start | bytes 14120 | tf_op jit(solution)/shard_map/ppermute | solution.py:119
  12.2 3.6 %collective-permute-start.2 = (f32[1176]{0:T(1024)S(1)}, f32[1176]{0:T(1024)S(1)}, u32[]{:S(2)}, u32[]{:S(2)}) collective-permute-start(f32[1176]{0:T(1024)S(1)} %reshape.161), channel_id=1, source_target_pairs={{0,7},{1,2},{2,1},{3,4},{4,3},{5,6},{6,5},{7,0},{8,15},{9,10},{10,... | collective-permute-start | bytes 14120 | tf_op jit(solution)/shard_map/ppermute | solution.py:122
  15.9 2.6 %collective-permute-done.2 = f32[1176]{0:T(1024)S(1)} collective-permute-done((f32[1176]{0:T(1024)S(1)}, f32[1176]{0:T(1024)S(1)}, u32[]{:S(2)}, u32[]{:S(2)}) %collective-permute-start.2) | collective-permute-done | bytes 4736 | tf_op jit(solution)/shard_map/ppermute | solution.py:122
  19.2 0.6 %subtract_bitcast_fusion = f32[1,24,12,132]{3,2,1,0:T(8,128)S(1)} fusion(f32[12,132]{1,0:T(8,128)S(1)} %get-tuple-element.50, f32[12,132]{1,0:T(8,128)S(1)} %get-tuple-element.49, f32[49,12,2]{2,1,0:T(8,128)S(1)} %reshape.164, f32[49,2,128]{2,1,0:T(2,128)S(1)} %reshape.160, f32[1,8,128]{2,1,0:T(8,128)S(1)} %bitcast.60, f32[48,8,128]{2,1,0:T(8,128)S(1)} %bitcast.53, ...), kind=kLoop, calls=%fused_computation.38 | loop fusion | flops 494208 | bytes 475200 | tf_op jit(solution)/shard_map/stack | solution.py:18
  19.8 0.6 %add_bitcast_fusion = f32[1,24,12,132]{3,2,1,0:T(8,128)S(1)} fusion(f32[12,132]{1,0:T(8,128)S(1)} %get-tuple-element.50, f32[12,132]{1,0:T(8,128)S(1)} %get-tuple-element.49, f32[49,12,2]{2,1,0:T(8,128)S(1)} %reshape.164, f32[49,2,128]{2,1,0:T(2,128)S(1)} %reshape.160, f32[1,8,128]{2,1,0:T(8,128)S(1)} %bitcast.61, f32[48,8,128]{2,1,0:T(8,128)S(1)} %bitcast.54, ...), kind=kLoop, calls=%fused_computation.37 | loop fusion | flops 494208 | bytes 475200 | tf_op jit(solution)/shard_map/stack | solution.py:18
  20.4 0.6 %broadcast_divide_fusion.1 = (f32[2,12,10,130]{3,2,1,0:T(8,128)S(1)}, f32[2,12,10,130]{3,2,1,0:T(8,128)S(1)}, f32[2,12,10,130]{3,2,1,0:T(8,128)S(1)}) fusion(f32[10,130]{1,0:T(8,128)S(1)} %get-tuple-element.27, f32[10,130]{1,0:T(8,128)S(1)} %get-tuple-element.31, f32[10,130]{1,0:T(8,128)S(1)} %get-tuple-element.30, f32[10,130]{1,0:T(8,128)S(1)} %get-tuple-element.28, ...), kind=kLoop, calls=%fused_computation.52 | loop fusion | flops 530400 | bytes 704528 | tf_op jit(solution)/shard_map/div | solution.py:289
  23.3 1.2 %collective-permute-done.4 = f32[4608]{0:T(1024)S(1)} collective-permute-done((f32[4608]{0:T(1024)S(1)}, f32[4608]{0:T(1024)S(1)}, u32[]{:S(2)}, u32[]{:S(2)}) %collective-permute-start.4) | collective-permute-done | bytes 18464 | tf_op jit(solution)/shard_map/ppermute | solution.py:140
  24.5 1.3 %collective-permute-start.5 = (f32[4608]{0:T(1024)S(1)}, f32[4608]{0:T(1024)S(1)}, u32[]{:S(2)}, u32[]{:S(2)}) collective-permute-start(f32[4608]{0:T(1024)S(1)} %add.155), channel_id=1, source_target_pairs={{0,16},{8,24},{16,0},{24,8},{1,17},{9,25},{17,1},{25,9},{2,18},{10... | collective-permute-start | bytes 55304 | tf_op jit(solution)/shard_map/ppermute | solution.py:140
  25.9 2.4 %collective-permute-done.5 = f32[4608]{0:T(1024)S(1)} collective-permute-done((f32[4608]{0:T(1024)S(1)}, f32[4608]{0:T(1024)S(1)}, u32[]{:S(2)}, u32[]{:S(2)}) %collective-permute-start.5) | collective-permute-done | bytes 18464 | tf_op jit(solution)/shard_map/ppermute | solution.py:140
  28.3 3.8 %collective-permute-done.6 = f32[4608]{0:T(1024)S(1)} collective-permute-done((f32[4608]{0:T(1024)S(1)}, f32[4608]{0:T(1024)S(1)}, u32[]{:S(2)}, u32[]{:S(2)}) %collective-permute-start.6) | collective-permute-done | bytes 18464 | tf_op jit(solution)/shard_map/ppermute | solution.py:140
  32.1 3.8 %collective-permute-done.7 = f32[4608]{0:T(1024)S(1)} collective-permute-done((f32[4608]{0:T(1024)S(1)}, f32[4608]{0:T(1024)S(1)}, u32[]{:S(2)}, u32[]{:S(2)}) %collective-permute-start.7) | collective-permute-done | bytes 18464 | tf_op jit(solution)/shard_map/ppermute | solution.py:140
  35.9 1.0 %collective-permute-start.8 = (f32[4608]{0:T(1024)S(1)}, f32[4608]{0:T(1024)S(1)}, u32[]{:S(2)}, u32[]{:S(2)}) collective-permute-start(f32[4608]{0:T(1024)S(1)} %add.158), channel_id=1, source_target_pairs={{0,4},{1,5},{2,6},{3,7},{4,0},{5,1},{6,2},{7,3},{8,12},{9,13},{10,... | collective-permute-start | bytes 55304 | tf_op jit(solution)/shard_map/ppermute | solution.py:140
  36.9 3.7 %collective-permute-done.8 = f32[4608]{0:T(1024)S(1)} collective-permute-done((f32[4608]{0:T(1024)S(1)}, f32[4608]{0:T(1024)S(1)}, u32[]{:S(2)}, u32[]{:S(2)}) %collective-permute-start.8) | collective-permute-done | bytes 18464 | tf_op jit(solution)/shard_map/ppermute | solution.py:140
  40.6 0.7 %reshape.168.packed_ref = f32[2,48,48]{2,1,0:T(8,128)} reshape(f32[4608]{0:T(1024)S(1)} %add.159) | data formatting | bytes 36864 | tf_op jit(solution)/shard_map/reshape | solution.py:304
  41.3 5.6 %shard_map.68 = (f32[128,128]{1,0:T(8,128)}, f32[128,128]{1,0:T(8,128)}) custom-call(f32[2,48,48]{2,1,0:T(8,128)} %reshape.168.packed_ref), custom_call_target="tpu_custom_call" | custom-call | tf_op jit(solution)/shard_map/pallas_call | solution.py:233
  46.9 0.8 %slice_bitcast_fusion = f32[72,96]{0,1:T(8,128)S(1)} fusion(f32[128,128]{1,0:T(8,128)} %get-tuple-element.4), kind=kLoop, calls=%fused_computation.60 | loop fusion | bytes 55296 | tf_op jit(solution)/shard_map/jrc,jk->krc/dot_general | solution.py:311
  48.2 0.8 %copy.63 = f32[2,36,8,128]{3,2,1,0:T(8,128)} copy(f32[2,36,8,128]{3,1,2,0:T(8,128)S(1)} %fusion.20) | data formatting | bytes 589824
  49.0 0.6 %copy.64 = f32[2,36,36]{2,0,1:T(2,128)} copy(f32[2,36,36]{2,1,0:T(8,128)S(1)} %pad_maximum_fusion.15) | data formatting | bytes 20736
  (73 shorter events, 5.3 us)
Async XLA Ops:
  0.6 7.1 %copy-start.3 = (s32[8,128]{1,0:T(8,128)S(1)}, s32[8,128]{1,0:T(8,128)}, u32[]{:S(2)}) copy-start(s32[8,128]{1,0:T(8,128)} %param.7) | copy-start | bytes 12292
  0.6 7.2 %copy-start.1 = (f32[2,12,8,128]{3,2,1,0:T(8,128)S(1)}, f32[2,12,8,128]{3,2,1,0:T(8,128)}, u32[]{:S(2)}) copy-start(f32[2,12,8,128]{3,2,1,0:T(8,128)} %param.5) | copy-start | bytes 294916
  0.7 7.2 %copy-start = (f32[2,12,8,128]{3,2,1,0:T(8,128)S(1)}, f32[2,12,8,128]{3,2,1,0:T(8,128)}, u32[]{:S(2)}) copy-start(f32[2,12,8,128]{3,2,1,0:T(8,128)} %param.6) | copy-start | bytes 294916
  0.7 7.2 %copy-start.4 = (s32[2]{0:T(128)S(1)}, s32[2]{0:T(128)}, u32[]{:S(2)}) copy-start(s32[2]{0:T(128)} %param.9) | copy-start | bytes 28
  4.5 5.4 %collective-permute-start.1 = (f32[12544]{0:T(1024)S(1)}, f32[12544]{0:T(1024)S(1)}, u32[]{:S(2)}, u32[]{:S(2)}) collective-permute-start(f32[12544]{0:T(1024)S(1)} %select_n.139), channel_id=1, source_target_pairs={{0,8},{8,0},{16,24},{24,16},{1,9},{9,1},{17,25},{25,17},{2,10},{10... | collective-permute-start | bytes 150536 | tf_op jit(solution)/shard_map/ppermute | solution.py:119
  5.1 4.9 %collective-permute-start = (f32[12544]{0:T(1024)S(1)}, f32[12544]{0:T(1024)S(1)}, u32[]{:S(2)}, u32[]{:S(2)}) collective-permute-start(f32[12544]{0:T(1024)S(1)} %select_n.137), channel_id=1, source_target_pairs={{0,24},{8,16},{16,8},{24,0},{1,25},{9,17},{17,9},{25,1},{2,26},{10... | collective-permute-start | bytes 150536 | tf_op jit(solution)/shard_map/ppermute | solution.py:122
  10.7 5.2 %collective-permute-start.3 = (f32[1176]{0:T(1024)S(1)}, f32[1176]{0:T(1024)S(1)}, u32[]{:S(2)}, u32[]{:S(2)}) collective-permute-start(f32[1176]{0:T(1024)S(1)} %reshape.162), channel_id=1, source_target_pairs={{0,1},{1,0},{2,3},{3,2},{4,5},{5,4},{6,7},{7,6},{8,9},{9,8},{10,11... | collective-permute-start | bytes 14120 | tf_op jit(solution)/shard_map/ppermute | solution.py:119
  12.2 6.3 %collective-permute-start.2 = (f32[1176]{0:T(1024)S(1)}, f32[1176]{0:T(1024)S(1)}, u32[]{:S(2)}, u32[]{:S(2)}) collective-permute-start(f32[1176]{0:T(1024)S(1)} %reshape.161), channel_id=1, source_target_pairs={{0,7},{1,2},{2,1},{3,4},{4,3},{5,6},{6,5},{7,0},{8,15},{9,10},{10,... | collective-permute-start | bytes 14120 | tf_op jit(solution)/shard_map/ppermute | solution.py:122
  23.3 1.3 %collective-permute-start.4 = (f32[4608]{0:T(1024)S(1)}, f32[4608]{0:T(1024)S(1)}, u32[]{:S(2)}, u32[]{:S(2)}) collective-permute-start(f32[4608]{0:T(1024)S(1)} %reshape.167), channel_id=1, source_target_pairs={{0,8},{8,0},{16,24},{24,16},{1,9},{9,1},{17,25},{25,17},{2,10},{10... | collective-permute-start | bytes 55304 | tf_op jit(solution)/shard_map/ppermute | solution.py:140
  24.5 3.8 %collective-permute-start.5 = (f32[4608]{0:T(1024)S(1)}, f32[4608]{0:T(1024)S(1)}, u32[]{:S(2)}, u32[]{:S(2)}) collective-permute-start(f32[4608]{0:T(1024)S(1)} %add.155), channel_id=1, source_target_pairs={{0,16},{8,24},{16,0},{24,8},{1,17},{9,25},{17,1},{25,9},{2,18},{10... | collective-permute-start | bytes 55304 | tf_op jit(solution)/shard_map/ppermute | solution.py:140
  28.3 3.8 %collective-permute-start.6 = (f32[4608]{0:T(1024)S(1)}, f32[4608]{0:T(1024)S(1)}, u32[]{:S(2)}, u32[]{:S(2)}) collective-permute-start(f32[4608]{0:T(1024)S(1)} %add.156), channel_id=1, source_target_pairs={{0,1},{1,0},{2,3},{3,2},{4,5},{5,4},{6,7},{7,6},{8,9},{9,8},{10,11... | collective-permute-start | bytes 55304 | tf_op jit(solution)/shard_map/ppermute | solution.py:140
  32.1 3.8 %collective-permute-start.7 = (f32[4608]{0:T(1024)S(1)}, f32[4608]{0:T(1024)S(1)}, u32[]{:S(2)}, u32[]{:S(2)}) collective-permute-start(f32[4608]{0:T(1024)S(1)} %add.157), channel_id=1, source_target_pairs={{0,2},{1,3},{2,0},{3,1},{4,6},{5,7},{6,4},{7,5},{8,10},{9,11},{10,... | collective-permute-start | bytes 55304 | tf_op jit(solution)/shard_map/ppermute | solution.py:140
  35.9 4.7 %collective-permute-start.8 = (f32[4608]{0:T(1024)S(1)}, f32[4608]{0:T(1024)S(1)}, u32[]{:S(2)}, u32[]{:S(2)}) collective-permute-start(f32[4608]{0:T(1024)S(1)} %add.158), channel_id=1, source_target_pairs={{0,4},{1,5},{2,6},{3,7},{4,0},{5,1},{6,2},{7,3},{8,12},{9,13},{10,... | collective-permute-start | bytes 55304 | tf_op jit(solution)/shard_map/ppermute | solution.py:140
  46.9 2.1 %copy-start.2 = (f32[128,128]{1,0:T(8,128)S(1)}, f32[128,128]{1,0:T(8,128)}, u32[]{:S(2)}) copy-start(f32[128,128]{1,0:T(8,128)} %get-tuple-element.5) | copy-start | bytes 196612

commit v9 on v8

--- a/solution.py
+++ b/solution.py
@@ -248,7 +248,9 @@
     def stiffness_of(cells):
         return jnp.sum(
             jnp.where(
-                cells[None] == levels[:, None, None], (1.0 / permittivity)[:, None, None], 0.0
+                cells[None] == levels.astype(jnp.float32)[:, None, None],
+                (1.0 / permittivity)[:, None, None],
+                0.0,
             ),
             axis=0,
         )
@@ -257,20 +259,20 @@
         field_rows = jnp.concatenate(
             [bands[:, :, start:stop], directions[:, :, start:stop]], axis=1
         ).reshape(4 * band_count, stop - start, breadth)
-        return jnp.concatenate([field_rows, stiffness_of(materials[start:stop])[None]], axis=0)
-
-    stiffness = stiffness_of(materials)
+        return jnp.concatenate([field_rows, material_grid[None, start:stop]], axis=0)
+
+    material_grid = materials.astype(jnp.float32)
     angle_row = 2.0 * math.pi * wavevector[0].astype(jnp.float32) / KDEN
     angle_col = 2.0 * math.pi * wavevector[1].astype(jnp.float32) / KDEN
     row_index = lax.axis_index("row")
     col_index = lax.axis_index("col")
     fields = jnp.concatenate([bands, directions], axis=1)
     packed = jnp.concatenate(
-        [fields.reshape(4 * band_count, height, breadth), stiffness[None]], axis=0
+        [fields.reshape(4 * band_count, height, breadth), material_grid[None]], axis=0
     )
     padded = exchange_rim(packed, "row", 1, 2, (strip_of(0, 2), strip_of(height - 2, height)))
     padded = exchange_rim(padded, "col", 2, 2)
-    stiff_wide = padded[-1]
+    stiff_wide = stiffness_of(padded[-1])
     field_wide = padded[:-1].reshape(2, 2 * band_count, height + 4, breadth + 4)
     row_place = jnp.arange(height + 4)
     col_place = jnp.arange(breadth + 4)

time: 50 us -> 49.3 us (0.986)
  local copies, waits for them, and re-layouts: 7.91 us -> 7.14 us
    slice x1, local copies, waits for them, and re-layouts: 0.77 us -> 0.01 us  [strip_of(): material_grid[None, start:stop]]
    broadcast_in_dim x0 -> x1, other arithmetic: none -> 0.73 us  [body(): material_grid[None]]
    div x1, other arithmetic: 0.72 us -> 0.01 us  [stiffness_of(): 1.0 / permittivity]
  transfers between devices with their start and end apart: 9 -> 9, of which waited for: 7 -> 6; matrix products, arithmetic and copies ran while one was open for 2% -> 2% of each run, Pallas kernels for 0% -> 0%
where the time goes in v9:
time: 49.3 us; the launch traced here: 49 us
  waiting for transfers between devices  17.7 us (36%)
  starting transfers between devices  10.7 us (22%)
  local copies, waits for them, and re-layouts  7.14 us (14%)
  Pallas kernels  5.62 us (11%)
  other arithmetic  4.06 us (8%)
  between operations  2.4 us (5%)
  matrix products  1.37 us (3%)
    ppermute x5, waiting for transfers between devices, tree_sum(): lax.ppermute(value, axis, [(i, i ^ step) for i in range(count)])  14.9 us
    ppermute x2, starting transfers between devices, exchange_rim(): lax.ppermute(jnp.where(even, head, tail).reshape(-1), axis, [(i, (i + 1)...  6.27 us
    pallas_call x1, Pallas kernels, matrix_stage(): pl.pallas_call(functools.partial(matrix_kernel, band_count=band_count, sc...  5.62 us
    ppermute x2, waiting for transfers between devices, exchange_rim(): lax.ppermute(jnp.where(even, head, tail).reshape(-1), axis, [(i, (i + 1)...  2.79 us
    ppermute x5, starting transfers between devices, tree_sum(): lax.ppermute(value, axis, [(i, i ^ step) for i in range(count)])  2.33 us
    ppermute x2, starting transfers between devices, exchange_rim(): lax.ppermute(jnp.where(even, tail, head).reshape(-1), axis, [(i, i ^ 1) f...  2.06 us
    unnamed x16, local copies, waits for them, and re-layouts  1.45 us
    another operation x2, other arithmetic, rotate(): jnp.stack([values[0] * cosine - values[1] * sine_part, values[0] * sine_p...  1.17 us
  transfers between devices with their start and end apart: 9, of which 6 were waited for; matrix products, arithmetic and copies ran while one was open for 2% of the time, Pallas kernels for 0%

profile of v9, /device:TPU:0, one launch (start us, length us, event | category | flops | bytes accessed | tf_op | source)
XLA Modules:
  0.0 49.0 jit_solution(18391503293436776312)
XLA Ops:
  0.7 0.7 %convert_bitcast_fusion = (f32[1,8,128]{2,1,0:T(8,128)S(1)}, f32[8,128]{1,0:T(8,128)S(1)}) fusion(s32[8,128]{1,0:T(8,128)} %param.7), kind=kLoop, calls=%fused_computation.109 | loop fusion | flops 1024 | bytes 12288 | tf_op jit(solution)/shard_map/broadcast_in_dim | solution.py:271
  1.4 1.0 %fusion.45 = (f32[2,12,2,128]{3,2,1,0:T(2,128)S(1)}, f32[2,12,2,128]{3,2,1,0:T(2,128)S(1)}) fusion(f32[2,12,8,128]{3,2,1,0:T(8,128)} %param.5), kind=kLoop, calls=%fused_computation.110 | loop fusion | bytes 98304 | tf_op jit(solution)/shard_map/slice | solution.py:260
  2.4 1.0 %fusion.46 = (f32[2,12,2,128]{3,2,1,0:T(2,128)S(1)}, f32[2,12,2,128]{3,2,1,0:T(2,128)S(1)}) fusion(f32[2,12,8,128]{3,2,1,0:T(8,128)} %param.6), kind=kLoop, calls=%fused_computation.111 | loop fusion | bytes 98304 | tf_op jit(solution)/shard_map/slice | solution.py:260
  3.6 0.5 %collective-permute-start.1 = (f32[12544]{0:T(1024)S(1)}, f32[12544]{0:T(1024)S(1)}, u32[]{:S(2)}, u32[]{:S(2)}) collective-permute-start(f32[12544]{0:T(1024)S(1)} %select_n.130), channel_id=1, source_target_pairs={{0,8},{8,0},{16,24},{24,16},{1,9},{9,1},{17,25},{25,17},{2,10},{10... | collective-permute-start | bytes 150536 | tf_op jit(solution)/shard_map/ppermute | solution.py:119
  4.2 2.7 %collective-permute-start = (f32[12544]{0:T(1024)S(1)}, f32[12544]{0:T(1024)S(1)}, u32[]{:S(2)}, u32[]{:S(2)}) collective-permute-start(f32[12544]{0:T(1024)S(1)} %select_n.128), channel_id=1, source_target_pairs={{0,24},{8,16},{16,8},{24,0},{1,25},{9,17},{17,9},{25,1},{2,26},{10... | collective-permute-start | bytes 150536 | tf_op jit(solution)/shard_map/ppermute | solution.py:122
  6.9 0.6 %fusion.48 = (s32[1]{0:T(128)}, s32[1]{0:T(128)}) fusion(s32[2]{0:T(128)S(1)} %copy-done.3), kind=kLoop, calls=%fused_computation.113 | loop fusion | bytes 16 | tf_op jit(solution)/shard_map/slice | solution.py:265
  9.8 1.5 %collective-permute-start.3 = (f32[1176]{0:T(1024)S(1)}, f32[1176]{0:T(1024)S(1)}, u32[]{:S(2)}, u32[]{:S(2)}) collective-permute-start(f32[1176]{0:T(1024)S(1)} %reshape.163), channel_id=1, source_target_pairs={{0,1},{1,0},{2,3},{3,2},{4,5},{5,4},{6,7},{7,6},{8,9},{9,8},{10,11... | collective-permute-start | bytes 14120 | tf_op jit(solution)/shard_map/ppermute | solution.py:119
  11.4 3.6 %collective-permute-start.2 = (f32[1176]{0:T(1024)S(1)}, f32[1176]{0:T(1024)S(1)}, u32[]{:S(2)}, u32[]{:S(2)}) collective-permute-start(f32[1176]{0:T(1024)S(1)} %reshape.162), channel_id=1, source_target_pairs={{0,7},{1,2},{2,1},{3,4},{4,3},{5,6},{6,5},{7,0},{8,15},{9,10},{10,... | collective-permute-start | bytes 14120 | tf_op jit(solution)/shard_map/ppermute | solution.py:122
  15.0 2.8 %collective-permute-done.2 = f32[1176]{0:T(1024)S(1)} collective-permute-done((f32[1176]{0:T(1024)S(1)}, f32[1176]{0:T(1024)S(1)}, u32[]{:S(2)}, u32[]{:S(2)}) %collective-permute-start.2) | collective-permute-done | bytes 4736 | tf_op jit(solution)/shard_map/ppermute | solution.py:122
  18.5 0.6 %subtract_bitcast_fusion = f32[1,24,12,132]{3,2,1,0:T(8,128)S(1)} fusion(f32[12,132]{1,0:T(8,128)S(1)} %get-tuple-element.50, f32[12,132]{1,0:T(8,128)S(1)} %get-tuple-element.49, f32[49,12,2]{2,1,0:T(8,128)S(1)} %reshape.165, f32[49,2,128]{2,1,0:T(2,128)S(1)} %reshape.161, f32[1,8,128]{2,1,0:T(8,128)S(1)} %get-tuple-element.45, ...), kind=kLoop, calls=%fused_computation.38 | loop fusion | flops 494208 | bytes 475200 | tf_op jit(solution)/shard_map/stack | solution.py:18
  19.1 0.6 %add_bitcast_fusion = f32[1,24,12,132]{3,2,1,0:T(8,128)S(1)} fusion(f32[12,132]{1,0:T(8,128)S(1)} %get-tuple-element.50, f32[12,132]{1,0:T(8,128)S(1)} %get-tuple-element.49, f32[49,12,2]{2,1,0:T(8,128)S(1)} %reshape.165, f32[49,2,128]{2,1,0:T(2,128)S(1)} %reshape.161, f32[1,8,128]{2,1,0:T(8,128)S(1)} %get-tuple-element.45, f32[48,8,128]{2,1,0:T(8,128)S(1)} %bitcast.53, ...), kind=kLoop, calls=%fused_computation.37 | loop fusion | flops 494208 | bytes 475200 | tf_op jit(solution)/shard_map/stack | solution.py:18
  19.7 0.6 %broadcast_divide_fusion.1 = (f32[2,12,10,130]{3,2,1,0:T(8,128)S(1)}, f32[2,12,10,130]{3,2,1,0:T(8,128)S(1)}, f32[2,12,10,130]{3,2,1,0:T(8,128)S(1)}) fusion(f32[10,130]{1,0:T(8,128)S(1)} %get-tuple-element.25, f32[10,130]{1,0:T(8,128)S(1)} %get-tuple-element.29, f32[10,130]{1,0:T(8,128)S(1)} %get-tuple-element.28, f32[10,130]{1,0:T(8,128)S(1)} %get-tuple-element.26, ...), kind=kLoop, calls=%fused_computation.52 | loop fusion | flops 530400 | bytes 704528 | tf_op jit(solution)/shard_map/div | solution.py:291
  22.7 1.2 %collective-permute-done.4 = f32[4608]{0:T(1024)S(1)} collective-permute-done((f32[4608]{0:T(1024)S(1)}, f32[4608]{0:T(1024)S(1)}, u32[]{:S(2)}, u32[]{:S(2)}) %collective-permute-start.4) | collective-permute-done | bytes 18464 | tf_op jit(solution)/shard_map/ppermute | solution.py:140
  23.8 1.3 %collective-permute-start.5 = (f32[4608]{0:T(1024)S(1)}, f32[4608]{0:T(1024)S(1)}, u32[]{:S(2)}, u32[]{:S(2)}) collective-permute-start(f32[4608]{0:T(1024)S(1)} %add.155), channel_id=1, source_target_pairs={{0,16},{8,24},{16,0},{24,8},{1,17},{9,25},{17,1},{25,9},{2,18},{10... | collective-permute-start | bytes 55304 | tf_op jit(solution)/shard_map/ppermute | solution.py:140
  25.1 2.5 %collective-permute-done.5 = f32[4608]{0:T(1024)S(1)} collective-permute-done((f32[4608]{0:T(1024)S(1)}, f32[4608]{0:T(1024)S(1)}, u32[]{:S(2)}, u32[]{:S(2)}) %collective-permute-start.5) | collective-permute-done | bytes 18464 | tf_op jit(solution)/shard_map/ppermute | solution.py:140
  27.6 3.8 %collective-permute-done.6 = f32[4608]{0:T(1024)S(1)} collective-permute-done((f32[4608]{0:T(1024)S(1)}, f32[4608]{0:T(1024)S(1)}, u32[]{:S(2)}, u32[]{:S(2)}) %collective-permute-start.6) | collective-permute-done | bytes 18464 | tf_op jit(solution)/shard_map/ppermute | solution.py:140
  31.4 3.8 %collective-permute-done.7 = f32[4608]{0:T(1024)S(1)} collective-permute-done((f32[4608]{0:T(1024)S(1)}, f32[4608]{0:T(1024)S(1)}, u32[]{:S(2)}, u32[]{:S(2)}) %collective-permute-start.7) | collective-permute-done | bytes 18464 | tf_op jit(solution)/shard_map/ppermute | solution.py:140
  35.2 1.0 %collective-permute-start.8 = (f32[4608]{0:T(1024)S(1)}, f32[4608]{0:T(1024)S(1)}, u32[]{:S(2)}, u32[]{:S(2)}) collective-permute-start(f32[4608]{0:T(1024)S(1)} %add.158), channel_id=1, source_target_pairs={{0,4},{1,5},{2,6},{3,7},{4,0},{5,1},{6,2},{7,3},{8,12},{9,13},{10,... | collective-permute-start | bytes 55304 | tf_op jit(solution)/shard_map/ppermute | solution.py:140
  36.2 3.7 %collective-permute-done.8 = f32[4608]{0:T(1024)S(1)} collective-permute-done((f32[4608]{0:T(1024)S(1)}, f32[4608]{0:T(1024)S(1)}, u32[]{:S(2)}, u32[]{:S(2)}) %collective-permute-start.8) | collective-permute-done | bytes 18464 | tf_op jit(solution)/shard_map/ppermute | solution.py:140
  39.9 0.7 %reshape.169.packed_ref = f32[2,48,48]{2,1,0:T(8,128)} reshape(f32[4608]{0:T(1024)S(1)} %add.159) | data formatting | bytes 36864 | tf_op jit(solution)/shard_map/reshape | solution.py:306
  40.6 5.6 %shard_map.68 = (f32[128,128]{1,0:T(8,128)}, f32[128,128]{1,0:T(8,128)}) custom-call(f32[2,48,48]{2,1,0:T(8,128)} %reshape.169.packed_ref), custom_call_target="tpu_custom_call" | custom-call | tf_op jit(solution)/shard_map/pallas_call | solution.py:233
  46.2 0.8 %slice_bitcast_fusion = f32[72,96]{0,1:T(8,128)S(1)} fusion(f32[128,128]{1,0:T(8,128)} %get-tuple-element.4), kind=kLoop, calls=%fused_computation.61 | loop fusion | bytes 55296 | tf_op jit(solution)/shard_map/jrc,jk->krc/dot_general | solution.py:313
  47.6 0.8 %copy.64 = f32[2,36,8,128]{3,2,1,0:T(8,128)} copy(f32[2,36,8,128]{3,1,2,0:T(8,128)S(1)} %fusion.20) | data formatting | bytes 589824
  48.4 0.6 %copy.65 = f32[2,36,36]{2,0,1:T(2,128)} copy(f32[2,36,36]{2,1,0:T(8,128)S(1)} %pad_maximum_fusion.15) | data formatting | bytes 20736
  (74 shorter events, 4.7 us)
Async XLA Ops:
  0.6 8.4 %copy-start.1 = (f32[2,12,8,128]{3,2,1,0:T(8,128)S(1)}, f32[2,12,8,128]{3,2,1,0:T(8,128)}, u32[]{:S(2)}) copy-start(f32[2,12,8,128]{3,2,1,0:T(8,128)} %param.5) | copy-start | bytes 294916
  0.6 8.4 %copy-start = (f32[2,12,8,128]{3,2,1,0:T(8,128)S(1)}, f32[2,12,8,128]{3,2,1,0:T(8,128)}, u32[]{:S(2)}) copy-start(f32[2,12,8,128]{3,2,1,0:T(8,128)} %param.6) | copy-start | bytes 294916
  0.7 6.3 %copy-start.4 = (f32[8]{0:T(128)S(1)}, f32[8]{0:T(128)}, u32[]{:S(2)}) copy-start(f32[8]{0:T(128)} %param.8) | copy-start | bytes 100
  0.7 6.2 %copy-start.3 = (s32[2]{0:T(128)S(1)}, s32[2]{0:T(128)}, u32[]{:S(2)}) copy-start(s32[2]{0:T(128)} %param.9) | copy-start | bytes 28
  3.6 5.4 %collective-permute-start.1 = (f32[12544]{0:T(1024)S(1)}, f32[12544]{0:T(1024)S(1)}, u32[]{:S(2)}, u32[]{:S(2)}) collective-permute-start(f32[12544]{0:T(1024)S(1)} %select_n.130), channel_id=1, source_target_pairs={{0,8},{8,0},{16,24},{24,16},{1,9},{9,1},{17,25},{25,17},{2,10},{10... | collective-permute-start | bytes 150536 | tf_op jit(solution)/shard_map/ppermute | solution.py:119
  4.2 4.9 %collective-permute-start = (f32[12544]{0:T(1024)S(1)}, f32[12544]{0:T(1024)S(1)}, u32[]{:S(2)}, u32[]{:S(2)}) collective-permute-start(f32[12544]{0:T(1024)S(1)} %select_n.128), channel_id=1, source_target_pairs={{0,24},{8,16},{16,8},{24,0},{1,25},{9,17},{17,9},{25,1},{2,26},{10... | collective-permute-start | bytes 150536 | tf_op jit(solution)/shard_map/ppermute | solution.py:122
  9.8 5.1 %collective-permute-start.3 = (f32[1176]{0:T(1024)S(1)}, f32[1176]{0:T(1024)S(1)}, u32[]{:S(2)}, u32[]{:S(2)}) collective-permute-start(f32[1176]{0:T(1024)S(1)} %reshape.163), channel_id=1, source_target_pairs={{0,1},{1,0},{2,3},{3,2},{4,5},{5,4},{6,7},{7,6},{8,9},{9,8},{10,11... | collective-permute-start | bytes 14120 | tf_op jit(solution)/shard_map/ppermute | solution.py:119
  11.4 6.3 %collective-permute-start.2 = (f32[1176]{0:T(1024)S(1)}, f32[1176]{0:T(1024)S(1)}, u32[]{:S(2)}, u32[]{:S(2)}) collective-permute-start(f32[1176]{0:T(1024)S(1)} %reshape.162), channel_id=1, source_target_pairs={{0,7},{1,2},{2,1},{3,4},{4,3},{5,6},{6,5},{7,0},{8,15},{9,10},{10,... | collective-permute-start | bytes 14120 | tf_op jit(solution)/shard_map/ppermute | solution.py:122
  22.6 1.3 %collective-permute-start.4 = (f32[4608]{0:T(1024)S(1)}, f32[4608]{0:T(1024)S(1)}, u32[]{:S(2)}, u32[]{:S(2)}) collective-permute-start(f32[4608]{0:T(1024)S(1)} %reshape.168), channel_id=1, source_target_pairs={{0,8},{8,0},{16,24},{24,16},{1,9},{9,1},{17,25},{25,17},{2,10},{10... | collective-permute-start | bytes 55304 | tf_op jit(solution)/shard_map/ppermute | solution.py:140
  23.8 3.8 %collective-permute-start.5 = (f32[4608]{0:T(1024)S(1)}, f32[4608]{0:T(1024)S(1)}, u32[]{:S(2)}, u32[]{:S(2)}) collective-permute-start(f32[4608]{0:T(1024)S(1)} %add.155), channel_id=1, source_target_pairs={{0,16},{8,24},{16,0},{24,8},{1,17},{9,25},{17,1},{25,9},{2,18},{10... | collective-permute-start | bytes 55304 | tf_op jit(solution)/shard_map/ppermute | solution.py:140
  27.6 3.8 %collective-permute-start.6 = (f32[4608]{0:T(1024)S(1)}, f32[4608]{0:T(1024)S(1)}, u32[]{:S(2)}, u32[]{:S(2)}) collective-permute-start(f32[4608]{0:T(1024)S(1)} %add.156), channel_id=1, source_target_pairs={{0,1},{1,0},{2,3},{3,2},{4,5},{5,4},{6,7},{7,6},{8,9},{9,8},{10,11... | collective-permute-start | bytes 55304 | tf_op jit(solution)/shard_map/ppermute | solution.py:140
  31.4 3.8 %collective-permute-start.7 = (f32[4608]{0:T(1024)S(1)}, f32[4608]{0:T(1024)S(1)}, u32[]{:S(2)}, u32[]{:S(2)}) collective-permute-start(f32[4608]{0:T(1024)S(1)} %add.157), channel_id=1, source_target_pairs={{0,2},{1,3},{2,0},{3,1},{4,6},{5,7},{6,4},{7,5},{8,10},{9,11},{10,... | collective-permute-start | bytes 55304 | tf_op jit(solution)/shard_map/ppermute | solution.py:140
  35.2 4.7 %collective-permute-start.8 = (f32[4608]{0:T(1024)S(1)}, f32[4608]{0:T(1024)S(1)}, u32[]{:S(2)}, u32[]{:S(2)}) collective-permute-start(f32[4608]{0:T(1024)S(1)} %add.158), channel_id=1, source_target_pairs={{0,4},{1,5},{2,6},{3,7},{4,0},{5,1},{6,2},{7,3},{8,12},{9,13},{10,... | collective-permute-start | bytes 55304 | tf_op jit(solution)/shard_map/ppermute | solution.py:140
  46.2 2.1 %copy-start.2 = (f32[128,128]{1,0:T(8,128)S(1)}, f32[128,128]{1,0:T(8,128)}, u32[]{:S(2)}) copy-start(f32[128,128]{1,0:T(8,128)} %get-tuple-element.5) | copy-start | bytes 196612

commit v10 on v9

--- a/solution.py
+++ b/solution.py
@@ -158,7 +158,7 @@
     return (real_part, imag_lower - imag_lower.T)
 
 
-def matrix_kernel(packed_ref, basis_ref, red_ref, work_ref, *, band_count, scale):
+def matrix_kernel(packed_ref, field_ref, basis_ref, red_ref, work_ref, *, band_count, scale):
     highest = lax.Precision.HIGHEST
 
     def dot(first, second):
@@ -223,20 +223,26 @@
         (rows >= half) & (rows < half + raw) & (cols == rows - half + raw)
     )
     packed_rotation = dot(pick_rows.astype(jnp.float32), dot(rotation, pick_cols.astype(jnp.float32)))
-    basis_ref[...] = scale * packed_rotation
-
-
-def matrix_stage(packed, band_count, scale):
+    work_ref[0] = scale * packed_rotation.T
+    rotation_t = work_ref[0, : 2 * raw, : 2 * ext]
+    for row in range(field_ref.shape[1]):
+        basis_ref[:, row, :] = dot(rotation_t, field_ref[:, row, :])
+
+
+def matrix_stage(packed, fields, band_count, scale):
     size = 128
+    raw = 3 * band_count
     vmem = pl.BlockSpec(memory_space=pltpu.VMEM)
-    square = jax.ShapeDtypeStruct((size, size), jnp.float32)
     return pl.pallas_call(
         functools.partial(matrix_kernel, band_count=band_count, scale=scale),
-        out_shape=(square, square),
-        in_specs=[vmem],
+        out_shape=(
+            jax.ShapeDtypeStruct((2 * raw,) + fields.shape[1:], jnp.float32),
+            jax.ShapeDtypeStruct((size, size), jnp.float32),
+        ),
+        in_specs=[vmem, vmem],
         out_specs=(vmem, vmem),
         scratch_shapes=[pltpu.VMEM((2, size, size), jnp.float32)],
-    )(packed)
+    )(packed, fields)
 
 
 def body(bands, directions, materials, permittivity, wavevector):
@@ -307,15 +313,12 @@
     raw_count = 3 * band_count
     ext_count = 4 * band_count
     scale_factor = math.sqrt(height * breadth * lax.axis_size("row") * lax.axis_size("col"))
-    mix, red = matrix_stage(summed, band_count, scale_factor)
+    basis, red = matrix_stage(
+        summed, extended.reshape(2 * ext_count, height, breadth), band_count, scale_factor
+    )
     half = red.shape[0] // 2
     reduced = jnp.stack([red[:raw_count, :raw_count], red[half : half + raw_count, :raw_count]])
-    basis = jnp.einsum(
-        "jrc,jk->krc",
-        extended.reshape(2 * ext_count, height, breadth),
-        mix[: 2 * ext_count, : 2 * raw_count],
-        precision=lax.Precision.HIGHEST,
-    ).reshape(2, raw_count, height, breadth)
+    basis = basis.reshape(2, raw_count, height, breadth)
     return (basis, reduced)
 
 

time: 49.3 us -> 48.9 us (level)
  Pallas kernels: 5.62 us -> 6.7 us
  local copies, waits for them, and re-layouts: 7.14 us -> 6.13 us
    pallas_call x1, Pallas kernels: 5.62 us -> 6.7 us  [matrix_stage(): pl.pallas_call(functools.partial(matrix_kernel, band_count=band_count, sc...]
    dot_general x3 -> x0, local copies, waits for them, and re-layouts: 0.91 us -> none  [body(): jnp.einsum('jrc,jk->krc', extended.reshape(2 * ext_count, height, breadth...]
    unnamed x16 -> x15, local copies, waits for them, and re-layouts: 1.45 us -> 0.68 us
    another operation x1, local copies, waits for them, and re-layouts: 0.01 us -> 0.75 us  [body(): jnp.stack([red[:raw_count, :raw_count], red[half:half + raw_count, :raw_c...]
where the time goes in v10:
time: 48.9 us; the launch traced here: 48.6 us
  waiting for transfers between devices  17.7 us (36%)
  starting transfers between devices  10.7 us (22%)
  Pallas kernels  6.7 us (14%)
  local copies, waits for them, and re-layouts  6.13 us (13%)
  other arithmetic  4.06 us (8%)
  between operations  2.38 us (5%)
  matrix products  0.95 us (2%)
    ppermute x5, waiting for transfers between devices, tree_sum(): lax.ppermute(value, axis, [(i, i ^ step) for i in range(count)])  14.9 us
    pallas_call x1, Pallas kernels, matrix_stage(): pl.pallas_call(functools.partial(matrix_kernel, band_count=band_count, sc...  6.7 us
    ppermute x2, starting transfers between devices, exchange_rim(): lax.ppermute(jnp.where(even, head, tail).reshape(-1), axis, [(i, (i + 1)...  6.27 us
    ppermute x2, waiting for transfers between devices, exchange_rim(): lax.ppermute(jnp.where(even, head, tail).reshape(-1), axis, [(i, (i + 1)...  2.79 us
    ppermute x5, starting transfers between devices, tree_sum(): lax.ppermute(value, axis, [(i, i ^ step) for i in range(count)])  2.33 us
    ppermute x2, starting transfers between devices, exchange_rim(): lax.ppermute(jnp.where(even, tail, head).reshape(-1), axis, [(i, i ^ 1) f...  2.06 us
    another operation x2, other arithmetic, rotate(): jnp.stack([values[0] * cosine - values[1] * sine_part, values[0] * sine_p...  1.17 us
    slice x1, local copies, waits for them, and re-layouts, strip_of(): directions[:, :, start:stop]  0.99 us
  transfers between devices with their start and end apart: 9, of which 6 were waited for; matrix products, arithmetic and copies ran while one was open for 2% of the time, Pallas kernels for 0%

profile of v10, /device:TPU:0, one launch (start us, length us, event | category | flops | bytes accessed | tf_op | source)
XLA Modules:
  0.0 48.6 jit_solution(5973578273319812554)
XLA Ops:
  0.7 0.7 %convert_bitcast_fusion = (f32[1,8,128]{2,1,0:T(8,128)S(1)}, f32[8,128]{1,0:T(8,128)S(1)}) fusion(s32[8,128]{1,0:T(8,128)} %param.7), kind=kLoop, calls=%fused_computation.108 | loop fusion | flops 1024 | bytes 12288 | tf_op jit(solution)/shard_map/broadcast_in_dim | solution.py:277
  1.4 1.0 %fusion.45 = (f32[2,12,2,128]{3,2,1,0:T(2,128)S(1)}, f32[2,12,2,128]{3,2,1,0:T(2,128)S(1)}) fusion(f32[2,12,8,128]{3,2,1,0:T(8,128)} %param.5), kind=kLoop, calls=%fused_computation.109 | loop fusion | bytes 98304 | tf_op jit(solution)/shard_map/slice | solution.py:266
  2.4 1.0 %fusion.46 = (f32[2,12,2,128]{3,2,1,0:T(2,128)S(1)}, f32[2,12,2,128]{3,2,1,0:T(2,128)S(1)}) fusion(f32[2,12,8,128]{3,2,1,0:T(8,128)} %param.6), kind=kLoop, calls=%fused_computation.110 | loop fusion | bytes 98304 | tf_op jit(solution)/shard_map/slice | solution.py:266
  3.6 0.5 %collective-permute-start.1 = (f32[12544]{0:T(1024)S(1)}, f32[12544]{0:T(1024)S(1)}, u32[]{:S(2)}, u32[]{:S(2)}) collective-permute-start(f32[12544]{0:T(1024)S(1)} %select_n.130), channel_id=1, source_target_pairs={{0,8},{8,0},{16,24},{24,16},{1,9},{9,1},{17,25},{25,17},{2,10},{10... | collective-permute-start | bytes 150536 | tf_op jit(solution)/shard_map/ppermute | solution.py:119
  4.2 2.7 %collective-permute-start = (f32[12544]{0:T(1024)S(1)}, f32[12544]{0:T(1024)S(1)}, u32[]{:S(2)}, u32[]{:S(2)}) collective-permute-start(f32[12544]{0:T(1024)S(1)} %select_n.128), channel_id=1, source_target_pairs={{0,24},{8,16},{16,8},{24,0},{1,25},{9,17},{17,9},{25,1},{2,26},{10... | collective-permute-start | bytes 150536 | tf_op jit(solution)/shard_map/ppermute | solution.py:122
  6.9 0.6 %fusion.48 = (s32[1]{0:T(128)}, s32[1]{0:T(128)}) fusion(s32[2]{0:T(128)S(1)} %copy-done.3), kind=kLoop, calls=%fused_computation.112 | loop fusion | bytes 16 | tf_op jit(solution)/shard_map/slice | solution.py:271
  9.8 1.5 %collective-permute-start.3 = (f32[1176]{0:T(1024)S(1)}, f32[1176]{0:T(1024)S(1)}, u32[]{:S(2)}, u32[]{:S(2)}) collective-permute-start(f32[1176]{0:T(1024)S(1)} %reshape.164), channel_id=1, source_target_pairs={{0,1},{1,0},{2,3},{3,2},{4,5},{5,4},{6,7},{7,6},{8,9},{9,8},{10,11... | collective-permute-start | bytes 14120 | tf_op jit(solution)/shard_map/ppermute | solution.py:119
  11.4 3.6 %collective-permute-start.2 = (f32[1176]{0:T(1024)S(1)}, f32[1176]{0:T(1024)S(1)}, u32[]{:S(2)}, u32[]{:S(2)}) collective-permute-start(f32[1176]{0:T(1024)S(1)} %reshape.163), channel_id=1, source_target_pairs={{0,7},{1,2},{2,1},{3,4},{4,3},{5,6},{6,5},{7,0},{8,15},{9,10},{10,... | collective-permute-start | bytes 14120 | tf_op jit(solution)/shard_map/ppermute | solution.py:122
  15.0 2.8 %collective-permute-done.2 = f32[1176]{0:T(1024)S(1)} collective-permute-done((f32[1176]{0:T(1024)S(1)}, f32[1176]{0:T(1024)S(1)}, u32[]{:S(2)}, u32[]{:S(2)}) %collective-permute-start.2) | collective-permute-done | bytes 4736 | tf_op jit(solution)/shard_map/ppermute | solution.py:122
  18.5 0.6 %subtract_bitcast_fusion = f32[1,24,12,132]{3,2,1,0:T(8,128)S(1)} fusion(f32[12,132]{1,0:T(8,128)S(1)} %get-tuple-element.50, f32[12,132]{1,0:T(8,128)S(1)} %get-tuple-element.49, f32[49,12,2]{2,1,0:T(8,128)S(1)} %reshape.166, f32[49,2,128]{2,1,0:T(2,128)S(1)} %reshape.162, f32[1,8,128]{2,1,0:T(8,128)S(1)} %get-tuple-element.45, ...), kind=kLoop, calls=%fused_computation.38 | loop fusion | flops 494208 | bytes 475200 | tf_op jit(solution)/shard_map/stack | solution.py:18
  19.1 0.6 %add_bitcast_fusion = f32[1,24,12,132]{3,2,1,0:T(8,128)S(1)} fusion(f32[12,132]{1,0:T(8,128)S(1)} %get-tuple-element.50, f32[12,132]{1,0:T(8,128)S(1)} %get-tuple-element.49, f32[49,12,2]{2,1,0:T(8,128)S(1)} %reshape.166, f32[49,2,128]{2,1,0:T(2,128)S(1)} %reshape.162, f32[1,8,128]{2,1,0:T(8,128)S(1)} %get-tuple-element.45, f32[48,8,128]{2,1,0:T(8,128)S(1)} %bitcast.43, ...), kind=kLoop, calls=%fused_computation.37 | loop fusion | flops 494208 | bytes 475200 | tf_op jit(solution)/shard_map/stack | solution.py:18
  19.7 0.6 %broadcast_divide_fusion.1 = (f32[2,12,10,130]{3,2,1,0:T(8,128)S(1)}, f32[2,12,10,130]{3,2,1,0:T(8,128)S(1)}, f32[2,12,10,130]{3,2,1,0:T(8,128)S(1)}) fusion(f32[10,130]{1,0:T(8,128)S(1)} %get-tuple-element.25, f32[10,130]{1,0:T(8,128)S(1)} %get-tuple-element.29, f32[10,130]{1,0:T(8,128)S(1)} %get-tuple-element.28, f32[10,130]{1,0:T(8,128)S(1)} %get-tuple-element.26, ...), kind=kLoop, calls=%fused_computation.54 | loop fusion | flops 530400 | bytes 704528 | tf_op jit(solution)/shard_map/div | solution.py:297
  21.8 0.5 convolution_bitcast_fusion
  22.6 1.2 %collective-permute-done.4 = f32[4608]{0:T(1024)S(1)} collective-permute-done((f32[4608]{0:T(1024)S(1)}, f32[4608]{0:T(1024)S(1)}, u32[]{:S(2)}, u32[]{:S(2)}) %collective-permute-start.4) | collective-permute-done | bytes 18464 | tf_op jit(solution)/shard_map/ppermute | solution.py:140
  23.8 1.3 %collective-permute-start.5 = (f32[4608]{0:T(1024)S(1)}, f32[4608]{0:T(1024)S(1)}, u32[]{:S(2)}, u32[]{:S(2)}) collective-permute-start(f32[4608]{0:T(1024)S(1)} %add.155), channel_id=1, source_target_pairs={{0,16},{8,24},{16,0},{24,8},{1,17},{9,25},{17,1},{25,9},{2,18},{10... | collective-permute-start | bytes 55304 | tf_op jit(solution)/shard_map/ppermute | solution.py:140
  25.1 2.5 %collective-permute-done.5 = f32[4608]{0:T(1024)S(1)} collective-permute-done((f32[4608]{0:T(1024)S(1)}, f32[4608]{0:T(1024)S(1)}, u32[]{:S(2)}, u32[]{:S(2)}) %collective-permute-start.5) | collective-permute-done | bytes 18464 | tf_op jit(solution)/shard_map/ppermute | solution.py:140
  27.6 3.8 %collective-permute-done.6 = f32[4608]{0:T(1024)S(1)} collective-permute-done((f32[4608]{0:T(1024)S(1)}, f32[4608]{0:T(1024)S(1)}, u32[]{:S(2)}, u32[]{:S(2)}) %collective-permute-start.6) | collective-permute-done | bytes 18464 | tf_op jit(solution)/shard_map/ppermute | solution.py:140
  31.4 3.8 %collective-permute-done.7 = f32[4608]{0:T(1024)S(1)} collective-permute-done((f32[4608]{0:T(1024)S(1)}, f32[4608]{0:T(1024)S(1)}, u32[]{:S(2)}, u32[]{:S(2)}) %collective-permute-start.7) | collective-permute-done | bytes 18464 | tf_op jit(solution)/shard_map/ppermute | solution.py:140
  35.1 1.0 %collective-permute-start.8 = (f32[4608]{0:T(1024)S(1)}, f32[4608]{0:T(1024)S(1)}, u32[]{:S(2)}, u32[]{:S(2)}) collective-permute-start(f32[4608]{0:T(1024)S(1)} %add.158), channel_id=1, source_target_pairs={{0,4},{1,5},{2,6},{3,7},{4,0},{5,1},{6,2},{7,3},{8,12},{9,13},{10,... | collective-permute-start | bytes 55304 | tf_op jit(solution)/shard_map/ppermute | solution.py:140
  36.1 3.7 %collective-permute-done.8 = f32[4608]{0:T(1024)S(1)} collective-permute-done((f32[4608]{0:T(1024)S(1)}, f32[4608]{0:T(1024)S(1)}, u32[]{:S(2)}, u32[]{:S(2)}) %collective-permute-start.8) | collective-permute-done | bytes 18464 | tf_op jit(solution)/shard_map/ppermute | solution.py:140
  39.8 0.7 %reshape.170.packed_ref = f32[2,48,48]{2,1,0:T(8,128)} reshape(f32[4608]{0:T(1024)S(1)} %add.159) | data formatting | bytes 36864 | tf_op jit(solution)/shard_map/reshape | solution.py:312
  40.5 6.7 %shard_map.68 = (f32[72,8,128]{2,1,0:T(8,128)}, f32[128,128]{1,0:T(8,128)}) custom-call(f32[2,48,48]{2,1,0:T(8,128)} %reshape.170.packed_ref, f32[96,8,128]{2,1,0:T(8,128)} %bitcast.39), custom_call_target="tpu_custom_call" | custom-call | tf_op jit(solution)/shard_map/pallas_call | solution.py:236
  47.2 0.7 %slice_bitcast_fusion.1 = (f32[1,36,36]{2,1,0:T(8,128)S(1)}, f32[1,36,36]{2,1,0:T(8,128)S(1)}) fusion(f32[128,128]{1,0:T(8,128)} %get-tuple-element.5), kind=kLoop, calls=%fused_computation.78 | loop fusion | bytes 20736 | tf_op jit(solution)/shard_map/stack | solution.py:320
  48.0 0.6 %copy.65 = f32[2,36,36]{2,0,1:T(2,128)} copy(f32[2,36,36]{2,1,0:T(8,128)S(1)} %pad_maximum_fusion.15) | data formatting | bytes 20736
  (68 shorter events, 3.6 us)
Async XLA Ops:
  0.6 8.4 %copy-start.2 = (f32[2,12,8,128]{3,2,1,0:T(8,128)S(1)}, f32[2,12,8,128]{3,2,1,0:T(8,128)}, u32[]{:S(2)}) copy-start(f32[2,12,8,128]{3,2,1,0:T(8,128)} %param.5) | copy-start | bytes 294916
  0.6 8.4 %copy-start.1 = (f32[2,12,8,128]{3,2,1,0:T(8,128)S(1)}, f32[2,12,8,128]{3,2,1,0:T(8,128)}, u32[]{:S(2)}) copy-start(f32[2,12,8,128]{3,2,1,0:T(8,128)} %param.6) | copy-start | bytes 294916
  0.7 6.3 %copy-start.4 = (f32[8]{0:T(128)S(1)}, f32[8]{0:T(128)}, u32[]{:S(2)}) copy-start(f32[8]{0:T(128)} %param.8) | copy-start | bytes 100
  0.7 6.2 %copy-start.3 = (s32[2]{0:T(128)S(1)}, s32[2]{0:T(128)}, u32[]{:S(2)}) copy-start(s32[2]{0:T(128)} %param.9) | copy-start | bytes 28
  3.6 5.4 %collective-permute-start.1 = (f32[12544]{0:T(1024)S(1)}, f32[12544]{0:T(1024)S(1)}, u32[]{:S(2)}, u32[]{:S(2)}) collective-permute-start(f32[12544]{0:T(1024)S(1)} %select_n.130), channel_id=1, source_target_pairs={{0,8},{8,0},{16,24},{24,16},{1,9},{9,1},{17,25},{25,17},{2,10},{10... | collective-permute-start | bytes 150536 | tf_op jit(solution)/shard_map/ppermute | solution.py:119
  4.2 4.9 %collective-permute-start = (f32[12544]{0:T(1024)S(1)}, f32[12544]{0:T(1024)S(1)}, u32[]{:S(2)}, u32[]{:S(2)}) collective-permute-start(f32[12544]{0:T(1024)S(1)} %select_n.128), channel_id=1, source_target_pairs={{0,24},{8,16},{16,8},{24,0},{1,25},{9,17},{17,9},{25,1},{2,26},{10... | collective-permute-start | bytes 150536 | tf_op jit(solution)/shard_map/ppermute | solution.py:122
  9.8 5.1 %collective-permute-start.3 = (f32[1176]{0:T(1024)S(1)}, f32[1176]{0:T(1024)S(1)}, u32[]{:S(2)}, u32[]{:S(2)}) collective-permute-start(f32[1176]{0:T(1024)S(1)} %reshape.164), channel_id=1, source_target_pairs={{0,1},{1,0},{2,3},{3,2},{4,5},{5,4},{6,7},{7,6},{8,9},{9,8},{10,11... | collective-permute-start | bytes 14120 | tf_op jit(solution)/shard_map/ppermute | solution.py:119
  11.4 6.3 %collective-permute-start.2 = (f32[1176]{0:T(1024)S(1)}, f32[1176]{0:T(1024)S(1)}, u32[]{:S(2)}, u32[]{:S(2)}) collective-permute-start(f32[1176]{0:T(1024)S(1)} %reshape.163), channel_id=1, source_target_pairs={{0,7},{1,2},{2,1},{3,4},{4,3},{5,6},{6,5},{7,0},{8,15},{9,10},{10,... | collective-permute-start | bytes 14120 | tf_op jit(solution)/shard_map/ppermute | solution.py:122
  21.3 19.2 %copy-start = (f32[2,48,8,128]{3,2,1,0:T(8,128)}, f32[2,48,8,128]{3,2,1,0:T(8,128)S(1)}, u32[]{:S(2)}) copy-start(f32[2,48,8,128]{3,2,1,0:T(8,128)S(1)} %pad_maximum_fusion.7) | copy-start | bytes 1179652
  22.5 1.3 %collective-permute-start.4 = (f32[4608]{0:T(1024)S(1)}, f32[4608]{0:T(1024)S(1)}, u32[]{:S(2)}, u32[]{:S(2)}) collective-permute-start(f32[4608]{0:T(1024)S(1)} %reshape.169), channel_id=1, source_target_pairs={{0,8},{8,0},{16,24},{24,16},{1,9},{9,1},{17,25},{25,17},{2,10},{10... | collective-permute-start | bytes 55304 | tf_op jit(solution)/shard_map/ppermute | solution.py:140
  23.8 3.8 %collective-permute-start.5 = (f32[4608]{0:T(1024)S(1)}, f32[4608]{0:T(1024)S(1)}, u32[]{:S(2)}, u32[]{:S(2)}) collective-permute-start(f32[4608]{0:T(1024)S(1)} %add.155), channel_id=1, source_target_pairs={{0,16},{8,24},{16,0},{24,8},{1,17},{9,25},{17,1},{25,9},{2,18},{10... | collective-permute-start | bytes 55304 | tf_op jit(solution)/shard_map/ppermute | solution.py:140
  27.6 3.8 %collective-permute-start.6 = (f32[4608]{0:T(1024)S(1)}, f32[4608]{0:T(1024)S(1)}, u32[]{:S(2)}, u32[]{:S(2)}) collective-permute-start(f32[4608]{0:T(1024)S(1)} %add.156), channel_id=1, source_target_pairs={{0,1},{1,0},{2,3},{3,2},{4,5},{5,4},{6,7},{7,6},{8,9},{9,8},{10,11... | collective-permute-start | bytes 55304 | tf_op jit(solution)/shard_map/ppermute | solution.py:140
  31.3 3.8 %collective-permute-start.7 = (f32[4608]{0:T(1024)S(1)}, f32[4608]{0:T(1024)S(1)}, u32[]{:S(2)}, u32[]{:S(2)}) collective-permute-start(f32[4608]{0:T(1024)S(1)} %add.157), channel_id=1, source_target_pairs={{0,2},{1,3},{2,0},{3,1},{4,6},{5,7},{6,4},{7,5},{8,10},{9,11},{10,... | collective-permute-start | bytes 55304 | tf_op jit(solution)/shard_map/ppermute | solution.py:140
  35.1 4.7 %collective-permute-start.8 = (f32[4608]{0:T(1024)S(1)}, f32[4608]{0:T(1024)S(1)}, u32[]{:S(2)}, u32[]{:S(2)}) collective-permute-start(f32[4608]{0:T(1024)S(1)} %add.158), channel_id=1, source_target_pairs={{0,4},{1,5},{2,6},{3,7},{4,0},{5,1},{6,2},{7,3},{8,12},{9,13},{10,... | collective-permute-start | bytes 55304 | tf_op jit(solution)/shard_map/ppermute | solution.py:140

commit v11 on v10

--- a/solution.py
+++ b/solution.py
@@ -214,7 +214,9 @@
     root = inverse / jnp.sqrt(magnitude)
     root = embed(jnp.where(corner, root, 0.0), jnp.where(corner, spread(root, 0), 0.0))
     rotation = dot(mixing, root)
-    red_ref[...] = dot(rotation.T, dot(embed(ham_re, ham_im), rotation))
+    work_ref[1] = dot(rotation.T, dot(embed(ham_re, ham_im), rotation))
+    red_ref[:, 0, :] = work_ref[1, :raw, :raw]
+    red_ref[:, 1, :] = work_ref[1, half : half + raw, :raw]
     rotation = jnp.where(corner | ~((rows < half) | (cols < half)), rotation, -rotation)
     pick_rows = ((rows < ext) & (cols == rows)) | (
         (rows >= ext) & (rows < 2 * ext) & (cols == rows - ext + half)
@@ -237,7 +239,7 @@
         functools.partial(matrix_kernel, band_count=band_count, scale=scale),
         out_shape=(
             jax.ShapeDtypeStruct((2 * raw,) + fields.shape[1:], jnp.float32),
-            jax.ShapeDtypeStruct((size, size), jnp.float32),
+            jax.ShapeDtypeStruct((raw, 2, raw), jnp.float32),
         ),
         in_specs=[vmem, vmem],
         out_specs=(vmem, vmem),
@@ -316,8 +318,7 @@
     basis, red = matrix_stage(
         summed, extended.reshape(2 * ext_count, height, breadth), band_count, scale_factor
     )
-    half = red.shape[0] // 2
-    reduced = jnp.stack([red[:raw_count, :raw_count], red[half : half + raw_count, :raw_count]])
+    reduced = jnp.transpose(red, (1, 0, 2))
     basis = basis.reshape(2, raw_count, height, breadth)
     return (basis, reduced)
 

time: 48.9 us -> 47.5 us (0.971)
  local copies, waits for them, and re-layouts: 6.13 us -> 4.74 us
    another operation x1 -> x0, local copies, waits for them, and re-layouts: 0.75 us -> none  [body(): jnp.stack([red[:raw_count, :raw_count], red[half:half + raw_count, :raw_c...]
    unnamed x15 -> x14, local copies, waits for them, and re-layouts: 0.68 us -> 0.05 us
where the time goes in v11:
time: 47.5 us; the launch traced here: 47.2 us
  waiting for transfers between devices  17.7 us (37%)
  starting transfers between devices  10.7 us (23%)
  Pallas kernels  6.68 us (14%)
  local copies, waits for them, and re-layouts  4.74 us (10%)
  other arithmetic  4.05 us (9%)
  between operations  2.38 us (5%)
  matrix products  0.95 us (2%)
    ppermute x5, waiting for transfers between devices, tree_sum(): lax.ppermute(value, axis, [(i, i ^ step) for i in range(count)])  14.9 us
    pallas_call x1, Pallas kernels, matrix_stage(): pl.pallas_call(functools.partial(matrix_kernel, band_count=band_count, sc...  6.68 us
    ppermute x2, starting transfers between devices, exchange_rim(): lax.ppermute(jnp.where(even, head, tail).reshape(-1), axis, [(i, (i + 1)...  6.27 us
    ppermute x2, waiting for transfers between devices, exchange_rim(): lax.ppermute(jnp.where(even, head, tail).reshape(-1), axis, [(i, (i + 1)...  2.79 us
    ppermute x5, starting transfers between devices, tree_sum(): lax.ppermute(value, axis, [(i, i ^ step) for i in range(count)])  2.33 us
    ppermute x2, starting transfers between devices, exchange_rim(): lax.ppermute(jnp.where(even, tail, head).reshape(-1), axis, [(i, i ^ 1) f...  2.06 us
    another operation x2, other arithmetic, rotate(): jnp.stack([values[0] * cosine - values[1] * sine_part, values[0] * sine_p...  1.17 us
    slice x1, local copies, waits for them, and re-layouts, strip_of(): directions[:, :, start:stop]  0.99 us
  transfers between devices with their start and end apart: 9, of which 6 were waited for; matrix products, arithmetic and copies ran while one was open for 2% of the time, Pallas kernels for 0%

profile of v11, /device:TPU:0, one launch (start us, length us, event | category | flops | bytes accessed | tf_op | source)
XLA Modules:
  0.0 47.2 jit_solution(5062792303353320838)
XLA Ops:
  0.7 0.7 %convert_bitcast_fusion = (f32[1,8,128]{2,1,0:T(8,128)S(1)}, f32[8,128]{1,0:T(8,128)S(1)}) fusion(s32[8,128]{1,0:T(8,128)} %param.7), kind=kLoop, calls=%fused_computation.105 | loop fusion | flops 1024 | bytes 12288 | tf_op jit(solution)/shard_map/broadcast_in_dim | solution.py:279
  1.4 1.0 %fusion.45 = (f32[2,12,2,128]{3,2,1,0:T(2,128)S(1)}, f32[2,12,2,128]{3,2,1,0:T(2,128)S(1)}) fusion(f32[2,12,8,128]{3,2,1,0:T(8,128)} %param.5), kind=kLoop, calls=%fused_computation.106 | loop fusion | bytes 98304 | tf_op jit(solution)/shard_map/slice | solution.py:268
  2.4 1.0 %fusion.46 = (f32[2,12,2,128]{3,2,1,0:T(2,128)S(1)}, f32[2,12,2,128]{3,2,1,0:T(2,128)S(1)}) fusion(f32[2,12,8,128]{3,2,1,0:T(8,128)} %param.6), kind=kLoop, calls=%fused_computation.107 | loop fusion | bytes 98304 | tf_op jit(solution)/shard_map/slice | solution.py:268
  3.6 0.5 %collective-permute-start.1 = (f32[12544]{0:T(1024)S(1)}, f32[12544]{0:T(1024)S(1)}, u32[]{:S(2)}, u32[]{:S(2)}) collective-permute-start(f32[12544]{0:T(1024)S(1)} %select_n.130), channel_id=1, source_target_pairs={{0,8},{8,0},{16,24},{24,16},{1,9},{9,1},{17,25},{25,17},{2,10},{10... | collective-permute-start | bytes 150536 | tf_op jit(solution)/shard_map/ppermute | solution.py:119
  4.2 2.7 %collective-permute-start = (f32[12544]{0:T(1024)S(1)}, f32[12544]{0:T(1024)S(1)}, u32[]{:S(2)}, u32[]{:S(2)}) collective-permute-start(f32[12544]{0:T(1024)S(1)} %select_n.128), channel_id=1, source_target_pairs={{0,24},{8,16},{16,8},{24,0},{1,25},{9,17},{17,9},{25,1},{2,26},{10... | collective-permute-start | bytes 150536 | tf_op jit(solution)/shard_map/ppermute | solution.py:122
  6.9 0.6 %fusion.48 = (s32[1]{0:T(128)}, s32[1]{0:T(128)}) fusion(s32[2]{0:T(128)S(1)} %copy-done.3), kind=kLoop, calls=%fused_computation.109 | loop fusion | bytes 16 | tf_op jit(solution)/shard_map/slice | solution.py:273
  9.8 1.5 %collective-permute-start.3 = (f32[1176]{0:T(1024)S(1)}, f32[1176]{0:T(1024)S(1)}, u32[]{:S(2)}, u32[]{:S(2)}) collective-permute-start(f32[1176]{0:T(1024)S(1)} %reshape.164), channel_id=1, source_target_pairs={{0,1},{1,0},{2,3},{3,2},{4,5},{5,4},{6,7},{7,6},{8,9},{9,8},{10,11... | collective-permute-start | bytes 14120 | tf_op jit(solution)/shard_map/ppermute | solution.py:119
  11.4 3.6 %collective-permute-start.2 = (f32[1176]{0:T(1024)S(1)}, f32[1176]{0:T(1024)S(1)}, u32[]{:S(2)}, u32[]{:S(2)}) collective-permute-start(f32[1176]{0:T(1024)S(1)} %reshape.163), channel_id=1, source_target_pairs={{0,7},{1,2},{2,1},{3,4},{4,3},{5,6},{6,5},{7,0},{8,15},{9,10},{10,... | collective-permute-start | bytes 14120 | tf_op jit(solution)/shard_map/ppermute | solution.py:122
  15.0 2.8 %collective-permute-done.2 = f32[1176]{0:T(1024)S(1)} collective-permute-done((f32[1176]{0:T(1024)S(1)}, f32[1176]{0:T(1024)S(1)}, u32[]{:S(2)}, u32[]{:S(2)}) %collective-permute-start.2) | collective-permute-done | bytes 4736 | tf_op jit(solution)/shard_map/ppermute | solution.py:122
  18.5 0.6 %subtract_bitcast_fusion = f32[1,24,12,132]{3,2,1,0:T(8,128)S(1)} fusion(f32[12,132]{1,0:T(8,128)S(1)} %get-tuple-element.36, f32[12,132]{1,0:T(8,128)S(1)} %get-tuple-element.35, f32[49,12,2]{2,1,0:T(8,128)S(1)} %reshape.166, f32[49,2,128]{2,1,0:T(2,128)S(1)} %reshape.162, f32[1,8,128]{2,1,0:T(8,128)S(1)} %get-tuple-element.31, ...), kind=kLoop, calls=%fused_computation.38 | loop fusion | flops 494208 | bytes 475200 | tf_op jit(solution)/shard_map/stack | solution.py:18
  19.1 0.6 %add_bitcast_fusion = f32[1,24,12,132]{3,2,1,0:T(8,128)S(1)} fusion(f32[12,132]{1,0:T(8,128)S(1)} %get-tuple-element.36, f32[12,132]{1,0:T(8,128)S(1)} %get-tuple-element.35, f32[49,12,2]{2,1,0:T(8,128)S(1)} %reshape.166, f32[49,2,128]{2,1,0:T(2,128)S(1)} %reshape.162, f32[1,8,128]{2,1,0:T(8,128)S(1)} %get-tuple-element.31, f32[48,8,128]{2,1,0:T(8,128)S(1)} %bitcast.40, ...), kind=kLoop, calls=%fused_computation.37 | loop fusion | flops 494208 | bytes 475200 | tf_op jit(solution)/shard_map/stack | solution.py:18
  19.7 0.6 %broadcast_divide_fusion.1 = (f32[2,12,10,130]{3,2,1,0:T(8,128)S(1)}, f32[2,12,10,130]{3,2,1,0:T(8,128)S(1)}, f32[2,12,10,130]{3,2,1,0:T(8,128)S(1)}) fusion(f32[10,130]{1,0:T(8,128)S(1)} %get-tuple-element.13, f32[10,130]{1,0:T(8,128)S(1)} %get-tuple-element.17, f32[10,130]{1,0:T(8,128)S(1)} %get-tuple-element.16, f32[10,130]{1,0:T(8,128)S(1)} %get-tuple-element.14, ...), kind=kLoop, calls=%fused_computation.54 | loop fusion | flops 530400 | bytes 704528 | tf_op jit(solution)/shard_map/div | solution.py:299
  20.8 0.4 fusion.17
  21.3 0.5 convolution_bitcast_fusion.1
  21.8 0.5 %convolution_bitcast_fusion = f32[96,96]{1,0:T(8,128)S(1)} fusion(f32[96,8,128]{2,0,1:T(8,128)S(1)} %bitcast.41, f32[96,8,128]{2,1,0:T(8,128)S(1)} %bitcast.35), kind=kOutput, calls=%fused_computation.13 | convolution fusion | flops 113246208 | bytes 823296 | tf_op jit(solution)/shard_map/jrc,krc->jk/dot_general | solution.py:44
  22.6 1.2 %collective-permute-done.4 = f32[4608]{0:T(1024)S(1)} collective-permute-done((f32[4608]{0:T(1024)S(1)}, f32[4608]{0:T(1024)S(1)}, u32[]{:S(2)}, u32[]{:S(2)}) %collective-permute-start.4) | collective-permute-done | bytes 18464 | tf_op jit(solution)/shard_map/ppermute | solution.py:140
  23.8 1.3 %collective-permute-start.5 = (f32[4608]{0:T(1024)S(1)}, f32[4608]{0:T(1024)S(1)}, u32[]{:S(2)}, u32[]{:S(2)}) collective-permute-start(f32[4608]{0:T(1024)S(1)} %add.155), channel_id=1, source_target_pairs={{0,16},{8,24},{16,0},{24,8},{1,17},{9,25},{17,1},{25,9},{2,18},{10... | collective-permute-start | bytes 55304 | tf_op jit(solution)/shard_map/ppermute | solution.py:140
  25.1 2.5 %collective-permute-done.5 = f32[4608]{0:T(1024)S(1)} collective-permute-done((f32[4608]{0:T(1024)S(1)}, f32[4608]{0:T(1024)S(1)}, u32[]{:S(2)}, u32[]{:S(2)}) %collective-permute-start.5) | collective-permute-done | bytes 18464 | tf_op jit(solution)/shard_map/ppermute | solution.py:140
  27.6 3.8 %collective-permute-done.6 = f32[4608]{0:T(1024)S(1)} collective-permute-done((f32[4608]{0:T(1024)S(1)}, f32[4608]{0:T(1024)S(1)}, u32[]{:S(2)}, u32[]{:S(2)}) %collective-permute-start.6) | collective-permute-done | bytes 18464 | tf_op jit(solution)/shard_map/ppermute | solution.py:140
  31.4 3.8 %collective-permute-done.7 = f32[4608]{0:T(1024)S(1)} collective-permute-done((f32[4608]{0:T(1024)S(1)}, f32[4608]{0:T(1024)S(1)}, u32[]{:S(2)}, u32[]{:S(2)}) %collective-permute-start.7) | collective-permute-done | bytes 18464 | tf_op jit(solution)/shard_map/ppermute | solution.py:140
  35.1 1.0 %collective-permute-start.8 = (f32[4608]{0:T(1024)S(1)}, f32[4608]{0:T(1024)S(1)}, u32[]{:S(2)}, u32[]{:S(2)}) collective-permute-start(f32[4608]{0:T(1024)S(1)} %add.158), channel_id=1, source_target_pairs={{0,4},{1,5},{2,6},{3,7},{4,0},{5,1},{6,2},{7,3},{8,12},{9,13},{10,... | collective-permute-start | bytes 55304 | tf_op jit(solution)/shard_map/ppermute | solution.py:140
  36.1 3.7 %collective-permute-done.8 = f32[4608]{0:T(1024)S(1)} collective-permute-done((f32[4608]{0:T(1024)S(1)}, f32[4608]{0:T(1024)S(1)}, u32[]{:S(2)}, u32[]{:S(2)}) %collective-permute-start.8) | collective-permute-done | bytes 18464 | tf_op jit(solution)/shard_map/ppermute | solution.py:140
  39.8 0.7 %reshape.170.packed_ref = f32[2,48,48]{2,1,0:T(8,128)} reshape(f32[4608]{0:T(1024)S(1)} %add.159) | data formatting | bytes 36864 | tf_op jit(solution)/shard_map/reshape | solution.py:314
  40.5 6.7 %shard_map.68 = (f32[72,8,128]{2,1,0:T(8,128)}, f32[36,2,36]{2,1,0:T(2,128)}) custom-call(f32[2,48,48]{2,1,0:T(8,128)} %reshape.170.packed_ref, f32[96,8,128]{2,1,0:T(8,128)} %bitcast.36), custom_call_target="tpu_custom_call" | custom-call | tf_op jit(solution)/shard_map/pallas_call | solution.py:238
  (65 shorter events, 2.8 us)
Async XLA Ops:
  0.6 8.4 %copy-start.2 = (f32[2,12,8,128]{3,2,1,0:T(8,128)S(1)}, f32[2,12,8,128]{3,2,1,0:T(8,128)}, u32[]{:S(2)}) copy-start(f32[2,12,8,128]{3,2,1,0:T(8,128)} %param.5) | copy-start | bytes 294916
  0.6 8.4 %copy-start.1 = (f32[2,12,8,128]{3,2,1,0:T(8,128)S(1)}, f32[2,12,8,128]{3,2,1,0:T(8,128)}, u32[]{:S(2)}) copy-start(f32[2,12,8,128]{3,2,1,0:T(8,128)} %param.6) | copy-start | bytes 294916
  0.7 6.3 %copy-start.4 = (f32[8]{0:T(128)S(1)}, f32[8]{0:T(128)}, u32[]{:S(2)}) copy-start(f32[8]{0:T(128)} %param.8) | copy-start | bytes 100
  0.7 6.2 %copy-start.3 = (s32[2]{0:T(128)S(1)}, s32[2]{0:T(128)}, u32[]{:S(2)}) copy-start(s32[2]{0:T(128)} %param.9) | copy-start | bytes 28
  3.6 5.4 %collective-permute-start.1 = (f32[12544]{0:T(1024)S(1)}, f32[12544]{0:T(1024)S(1)}, u32[]{:S(2)}, u32[]{:S(2)}) collective-permute-start(f32[12544]{0:T(1024)S(1)} %select_n.130), channel_id=1, source_target_pairs={{0,8},{8,0},{16,24},{24,16},{1,9},{9,1},{17,25},{25,17},{2,10},{10... | collective-permute-start | bytes 150536 | tf_op jit(solution)/shard_map/ppermute | solution.py:119
  4.2 4.9 %collective-permute-start = (f32[12544]{0:T(1024)S(1)}, f32[12544]{0:T(1024)S(1)}, u32[]{:S(2)}, u32[]{:S(2)}) collective-permute-start(f32[12544]{0:T(1024)S(1)} %select_n.128), channel_id=1, source_target_pairs={{0,24},{8,16},{16,8},{24,0},{1,25},{9,17},{17,9},{25,1},{2,26},{10... | collective-permute-start | bytes 150536 | tf_op jit(solution)/shard_map/ppermute | solution.py:122
  9.8 5.1 %collective-permute-start.3 = (f32[1176]{0:T(1024)S(1)}, f32[1176]{0:T(1024)S(1)}, u32[]{:S(2)}, u32[]{:S(2)}) collective-permute-start(f32[1176]{0:T(1024)S(1)} %reshape.164), channel_id=1, source_target_pairs={{0,1},{1,0},{2,3},{3,2},{4,5},{5,4},{6,7},{7,6},{8,9},{9,8},{10,11... | collective-permute-start | bytes 14120 | tf_op jit(solution)/shard_map/ppermute | solution.py:119
  11.4 6.3 %collective-permute-start.2 = (f32[1176]{0:T(1024)S(1)}, f32[1176]{0:T(1024)S(1)}, u32[]{:S(2)}, u32[]{:S(2)}) collective-permute-start(f32[1176]{0:T(1024)S(1)} %reshape.163), channel_id=1, source_target_pairs={{0,7},{1,2},{2,1},{3,4},{4,3},{5,6},{6,5},{7,0},{8,15},{9,10},{10,... | collective-permute-start | bytes 14120 | tf_op jit(solution)/shard_map/ppermute | solution.py:122
  21.3 19.2 %copy-start = (f32[2,48,8,128]{3,2,1,0:T(8,128)}, f32[2,48,8,128]{3,2,1,0:T(8,128)S(1)}, u32[]{:S(2)}) copy-start(f32[2,48,8,128]{3,2,1,0:T(8,128)S(1)} %pad_maximum_fusion.7) | copy-start | bytes 1179652
  22.5 1.3 %collective-permute-start.4 = (f32[4608]{0:T(1024)S(1)}, f32[4608]{0:T(1024)S(1)}, u32[]{:S(2)}, u32[]{:S(2)}) collective-permute-start(f32[4608]{0:T(1024)S(1)} %reshape.169), channel_id=1, source_target_pairs={{0,8},{8,0},{16,24},{24,16},{1,9},{9,1},{17,25},{25,17},{2,10},{10... | collective-permute-start | bytes 55304 | tf_op jit(solution)/shard_map/ppermute | solution.py:140
  23.8 3.8 %collective-permute-start.5 = (f32[4608]{0:T(1024)S(1)}, f32[4608]{0:T(1024)S(1)}, u32[]{:S(2)}, u32[]{:S(2)}) collective-permute-start(f32[4608]{0:T(1024)S(1)} %add.155), channel_id=1, source_target_pairs={{0,16},{8,24},{16,0},{24,8},{1,17},{9,25},{17,1},{25,9},{2,18},{10... | collective-permute-start | bytes 55304 | tf_op jit(solution)/shard_map/ppermute | solution.py:140
  27.6 3.8 %collective-permute-start.6 = (f32[4608]{0:T(1024)S(1)}, f32[4608]{0:T(1024)S(1)}, u32[]{:S(2)}, u32[]{:S(2)}) collective-permute-start(f32[4608]{0:T(1024)S(1)} %add.156), channel_id=1, source_target_pairs={{0,1},{1,0},{2,3},{3,2},{4,5},{5,4},{6,7},{7,6},{8,9},{9,8},{10,11... | collective-permute-start | bytes 55304 | tf_op jit(solution)/shard_map/ppermute | solution.py:140
  31.3 3.8 %collective-permute-start.7 = (f32[4608]{0:T(1024)S(1)}, f32[4608]{0:T(1024)S(1)}, u32[]{:S(2)}, u32[]{:S(2)}) collective-permute-start(f32[4608]{0:T(1024)S(1)} %add.157), channel_id=1, source_target_pairs={{0,2},{1,3},{2,0},{3,1},{4,6},{5,7},{6,4},{7,5},{8,10},{9,11},{10,... | collective-permute-start | bytes 55304 | tf_op jit(solution)/shard_map/ppermute | solution.py:140
  35.1 4.7 %collective-permute-start.8 = (f32[4608]{0:T(1024)S(1)}, f32[4608]{0:T(1024)S(1)}, u32[]{:S(2)}, u32[]{:S(2)}) collective-permute-start(f32[4608]{0:T(1024)S(1)} %add.158), channel_id=1, source_target_pairs={{0,4},{1,5},{2,6},{3,7},{4,0},{5,1},{6,2},{7,3},{8,12},{9,13},{10,... | collective-permute-start | bytes 55304 | tf_op jit(solution)/shard_map/ppermute | solution.py:140

commit v12 on v11

--- a/solution.py
+++ b/solution.py
@@ -267,7 +267,8 @@
         field_rows = jnp.concatenate(
             [bands[:, :, start:stop], directions[:, :, start:stop]], axis=1
         ).reshape(4 * band_count, stop - start, breadth)
-        return jnp.concatenate([field_rows, material_grid[None, start:stop]], axis=0)
+        material_rows = materials[start:stop].astype(jnp.float32)
+        return jnp.concatenate([field_rows, material_rows[None]], axis=0)
 
     material_grid = materials.astype(jnp.float32)
     angle_row = 2.0 * math.pi * wavevector[0].astype(jnp.float32) / KDEN

time: 47.5 us -> 47.5 us (level)
    convert_element_type x0 -> x1, other arithmetic: none -> 0.77 us  [strip_of(): material_rows = materials[start:stop].astype(jnp.float32)]
    broadcast_in_dim x1, other arithmetic: 0.73 us -> 0.01 us  [body(): material_grid[None]]
where the time goes in v12:
time: 47.5 us; the launch traced here: 47.3 us
  waiting for transfers between devices  17.7 us (37%)
  starting transfers between devices  10.7 us (23%)
  Pallas kernels  6.68 us (14%)
  local copies, waits for them, and re-layouts  4.74 us (10%)
  other arithmetic  4.1 us (9%)
  between operations  2.4 us (5%)
  matrix products  0.95 us (2%)
    ppermute x5, waiting for transfers between devices, tree_sum(): lax.ppermute(value, axis, [(i, i ^ step) for i in range(count)])  15 us
    pallas_call x1, Pallas kernels, matrix_stage(): pl.pallas_call(functools.partial(matrix_kernel, band_count=band_count, sc...  6.68 us
    ppermute x2, starting transfers between devices, exchange_rim(): lax.ppermute(jnp.where(even, head, tail).reshape(-1), axis, [(i, (i + 1)...  6.27 us
    ppermute x2, waiting for transfers between devices, exchange_rim(): lax.ppermute(jnp.where(even, head, tail).reshape(-1), axis, [(i, (i + 1)...  2.78 us
    ppermute x5, starting transfers between devices, tree_sum(): lax.ppermute(value, axis, [(i, i ^ step) for i in range(count)])  2.32 us
    ppermute x2, starting transfers between devices, exchange_rim(): lax.ppermute(jnp.where(even, tail, head).reshape(-1), axis, [(i, i ^ 1) f...  2.07 us
    another operation x2, other arithmetic, rotate(): jnp.stack([values[0] * cosine - values[1] * sine_part, values[0] * sine_p...  1.17 us
    slice x1, local copies, waits for them, and re-layouts, strip_of(): directions[:, :, start:stop]  0.99 us
  transfers between devices with their start and end apart: 9, of which 6 were waited for; matrix products, arithmetic and copies ran while one was open for 2% of the time, Pallas kernels for 0%

profile of v12, /device:TPU:0, one launch (start us, length us, event | category | flops | bytes accessed | tf_op | source)
XLA Modules:
  0.0 47.3 jit_solution(9595766290962946378)
XLA Ops:
  0.7 0.8 %slice_convert_fusion.1 = (f32[2,128]{1,0:T(2,128)S(1)}, f32[2,128]{1,0:T(2,128)S(1)}) fusion(s32[8,128]{1,0:T(8,128)} %param.7), kind=kLoop, calls=%fused_computation.104 | loop fusion | flops 512 | bytes 4096 | tf_op jit(solution)/shard_map/convert_element_type | solution.py:270
  1.5 1.0 %fusion.45 = (f32[2,12,2,128]{3,2,1,0:T(2,128)S(1)}, f32[2,12,2,128]{3,2,1,0:T(2,128)S(1)}) fusion(f32[2,12,8,128]{3,2,1,0:T(8,128)} %param.5), kind=kLoop, calls=%fused_computation.108 | loop fusion | bytes 98304 | tf_op jit(solution)/shard_map/slice | solution.py:268
  2.5 1.0 %fusion.46 = (f32[2,12,2,128]{3,2,1,0:T(2,128)S(1)}, f32[2,12,2,128]{3,2,1,0:T(2,128)S(1)}) fusion(f32[2,12,8,128]{3,2,1,0:T(8,128)} %param.6), kind=kLoop, calls=%fused_computation.109 | loop fusion | bytes 98304 | tf_op jit(solution)/shard_map/slice | solution.py:268
  3.7 0.5 %collective-permute-start.1 = (f32[12544]{0:T(1024)S(1)}, f32[12544]{0:T(1024)S(1)}, u32[]{:S(2)}, u32[]{:S(2)}) collective-permute-start(f32[12544]{0:T(1024)S(1)} %select_n.130), channel_id=1, source_target_pairs={{0,8},{8,0},{16,24},{24,16},{1,9},{9,1},{17,25},{25,17},{2,10},{10... | collective-permute-start | bytes 150536 | tf_op jit(solution)/shard_map/ppermute | solution.py:119
  4.3 2.7 %collective-permute-start = (f32[12544]{0:T(1024)S(1)}, f32[12544]{0:T(1024)S(1)}, u32[]{:S(2)}, u32[]{:S(2)}) collective-permute-start(f32[12544]{0:T(1024)S(1)} %select_n.128), channel_id=1, source_target_pairs={{0,24},{8,16},{16,8},{24,0},{1,25},{9,17},{17,9},{25,1},{2,26},{10... | collective-permute-start | bytes 150536 | tf_op jit(solution)/shard_map/ppermute | solution.py:122
  7.0 0.6 %fusion.47 = (s32[1]{0:T(128)}, s32[1]{0:T(128)}) fusion(s32[2]{0:T(128)S(1)} %copy-done.4), kind=kLoop, calls=%fused_computation.110 | loop fusion | bytes 16 | tf_op jit(solution)/shard_map/slice | solution.py:274
  9.9 1.6 %collective-permute-start.3 = (f32[1176]{0:T(1024)S(1)}, f32[1176]{0:T(1024)S(1)}, u32[]{:S(2)}, u32[]{:S(2)}) collective-permute-start(f32[1176]{0:T(1024)S(1)} %reshape.164), channel_id=1, source_target_pairs={{0,1},{1,0},{2,3},{3,2},{4,5},{5,4},{6,7},{7,6},{8,9},{9,8},{10,11... | collective-permute-start | bytes 14120 | tf_op jit(solution)/shard_map/ppermute | solution.py:119
  11.4 3.6 %collective-permute-start.2 = (f32[1176]{0:T(1024)S(1)}, f32[1176]{0:T(1024)S(1)}, u32[]{:S(2)}, u32[]{:S(2)}) collective-permute-start(f32[1176]{0:T(1024)S(1)} %reshape.163), channel_id=1, source_target_pairs={{0,7},{1,2},{2,1},{3,4},{4,3},{5,6},{6,5},{7,0},{8,15},{9,10},{10,... | collective-permute-start | bytes 14120 | tf_op jit(solution)/shard_map/ppermute | solution.py:122
  15.0 2.8 %collective-permute-done.2 = f32[1176]{0:T(1024)S(1)} collective-permute-done((f32[1176]{0:T(1024)S(1)}, f32[1176]{0:T(1024)S(1)}, u32[]{:S(2)}, u32[]{:S(2)}) %collective-permute-start.2) | collective-permute-done | bytes 4736 | tf_op jit(solution)/shard_map/ppermute | solution.py:122
  18.6 0.6 %subtract_bitcast_fusion = f32[1,24,12,132]{3,2,1,0:T(8,128)S(1)} fusion(f32[12,132]{1,0:T(8,128)S(1)} %get-tuple-element.34, f32[12,132]{1,0:T(8,128)S(1)} %get-tuple-element.33, f32[49,12,2]{2,1,0:T(8,128)S(1)} %reshape.166, f32[49,2,128]{2,1,0:T(2,128)S(1)} %reshape.162, f32[1,8,128]{2,1,0:T(8,128)S(1)} %convert_bitcast_fusion, ...), kind=kLoop, calls=%fused_computation.38 | loop fusion | flops 494208 | bytes 475200 | tf_op jit(solution)/shard_map/stack | solution.py:18
  19.2 0.6 %add_bitcast_fusion = f32[1,24,12,132]{3,2,1,0:T(8,128)S(1)} fusion(f32[12,132]{1,0:T(8,128)S(1)} %get-tuple-element.34, f32[12,132]{1,0:T(8,128)S(1)} %get-tuple-element.33, f32[49,12,2]{2,1,0:T(8,128)S(1)} %reshape.166, f32[49,2,128]{2,1,0:T(2,128)S(1)} %reshape.162, f32[1,8,128]{2,1,0:T(8,128)S(1)} %convert_bitcast_fusion, f32[48,8,128]{2,1,0:T(8,128)S(1)} %bitcast.38, ...), kind=kLoop, calls=%fused_computation.37 | loop fusion | flops 494208 | bytes 475200 | tf_op jit(solution)/shard_map/stack | solution.py:18
  19.8 0.6 %broadcast_divide_fusion.1 = (f32[2,12,10,130]{3,2,1,0:T(8,128)S(1)}, f32[2,12,10,130]{3,2,1,0:T(8,128)S(1)}, f32[2,12,10,130]{3,2,1,0:T(8,128)S(1)}) fusion(f32[10,130]{1,0:T(8,128)S(1)} %get-tuple-element.13, f32[10,130]{1,0:T(8,128)S(1)} %get-tuple-element.17, f32[10,130]{1,0:T(8,128)S(1)} %get-tuple-element.16, f32[10,130]{1,0:T(8,128)S(1)} %get-tuple-element.14, ...), kind=kLoop, calls=%fused_computation.54 | loop fusion | flops 530400 | bytes 704528 | tf_op jit(solution)/shard_map/div | solution.py:300
  20.9 0.4 fusion.17
  21.4 0.5 convolution_bitcast_fusion.1
  21.9 0.5 %convolution_bitcast_fusion = f32[96,96]{1,0:T(8,128)S(1)} fusion(f32[96,8,128]{2,0,1:T(8,128)S(1)} %bitcast.39, f32[96,8,128]{2,1,0:T(8,128)S(1)} %bitcast.33), kind=kOutput, calls=%fused_computation.13 | convolution fusion | flops 113246208 | bytes 823296 | tf_op jit(solution)/shard_map/jrc,krc->jk/dot_general | solution.py:44
  22.6 1.2 %collective-permute-done.4 = f32[4608]{0:T(1024)S(1)} collective-permute-done((f32[4608]{0:T(1024)S(1)}, f32[4608]{0:T(1024)S(1)}, u32[]{:S(2)}, u32[]{:S(2)}) %collective-permute-start.4) | collective-permute-done | bytes 18464 | tf_op jit(solution)/shard_map/ppermute | solution.py:140
  23.8 1.3 %collective-permute-start.5 = (f32[4608]{0:T(1024)S(1)}, f32[4608]{0:T(1024)S(1)}, u32[]{:S(2)}, u32[]{:S(2)}) collective-permute-start(f32[4608]{0:T(1024)S(1)} %add.155), channel_id=1, source_target_pairs={{0,16},{8,24},{16,0},{24,8},{1,17},{9,25},{17,1},{25,9},{2,18},{10... | collective-permute-start | bytes 55304 | tf_op jit(solution)/shard_map/ppermute | solution.py:140
  25.1 2.5 %collective-permute-done.5 = f32[4608]{0:T(1024)S(1)} collective-permute-done((f32[4608]{0:T(1024)S(1)}, f32[4608]{0:T(1024)S(1)}, u32[]{:S(2)}, u32[]{:S(2)}) %collective-permute-start.5) | collective-permute-done | bytes 18464 | tf_op jit(solution)/shard_map/ppermute | solution.py:140
  27.6 3.8 %collective-permute-done.6 = f32[4608]{0:T(1024)S(1)} collective-permute-done((f32[4608]{0:T(1024)S(1)}, f32[4608]{0:T(1024)S(1)}, u32[]{:S(2)}, u32[]{:S(2)}) %collective-permute-start.6) | collective-permute-done | bytes 18464 | tf_op jit(solution)/shard_map/ppermute | solution.py:140
  31.4 3.8 %collective-permute-done.7 = f32[4608]{0:T(1024)S(1)} collective-permute-done((f32[4608]{0:T(1024)S(1)}, f32[4608]{0:T(1024)S(1)}, u32[]{:S(2)}, u32[]{:S(2)}) %collective-permute-start.7) | collective-permute-done | bytes 18464 | tf_op jit(solution)/shard_map/ppermute | solution.py:140
  35.2 1.0 %collective-permute-start.8 = (f32[4608]{0:T(1024)S(1)}, f32[4608]{0:T(1024)S(1)}, u32[]{:S(2)}, u32[]{:S(2)}) collective-permute-start(f32[4608]{0:T(1024)S(1)} %add.158), channel_id=1, source_target_pairs={{0,4},{1,5},{2,6},{3,7},{4,0},{5,1},{6,2},{7,3},{8,12},{9,13},{10,... | collective-permute-start | bytes 55304 | tf_op jit(solution)/shard_map/ppermute | solution.py:140
  36.2 3.7 %collective-permute-done.8 = f32[4608]{0:T(1024)S(1)} collective-permute-done((f32[4608]{0:T(1024)S(1)}, f32[4608]{0:T(1024)S(1)}, u32[]{:S(2)}, u32[]{:S(2)}) %collective-permute-start.8) | collective-permute-done | bytes 18464 | tf_op jit(solution)/shard_map/ppermute | solution.py:140
  39.9 0.7 %reshape.170.packed_ref = f32[2,48,48]{2,1,0:T(8,128)} reshape(f32[4608]{0:T(1024)S(1)} %add.159) | data formatting | bytes 36864 | tf_op jit(solution)/shard_map/reshape | solution.py:315
  40.6 6.7 %shard_map.68 = (f32[72,8,128]{2,1,0:T(8,128)}, f32[36,2,36]{2,1,0:T(2,128)}) custom-call(f32[2,48,48]{2,1,0:T(8,128)} %reshape.170.packed_ref, f32[96,8,128]{2,1,0:T(8,128)} %bitcast.34), custom_call_target="tpu_custom_call" | custom-call | tf_op jit(solution)/shard_map/pallas_call | solution.py:238
  (67 shorter events, 2.8 us)
Async XLA Ops:
  0.6 6.3 %copy-start.3 = (s32[8,128]{1,0:T(8,128)S(1)}, s32[8,128]{1,0:T(8,128)}, u32[]{:S(2)}) copy-start(s32[8,128]{1,0:T(8,128)} %param.7) | copy-start | bytes 12292
  0.6 8.4 %copy-start.2 = (f32[2,12,8,128]{3,2,1,0:T(8,128)S(1)}, f32[2,12,8,128]{3,2,1,0:T(8,128)}, u32[]{:S(2)}) copy-start(f32[2,12,8,128]{3,2,1,0:T(8,128)} %param.5) | copy-start | bytes 294916
  0.7 8.4 %copy-start.1 = (f32[2,12,8,128]{3,2,1,0:T(8,128)S(1)}, f32[2,12,8,128]{3,2,1,0:T(8,128)}, u32[]{:S(2)}) copy-start(f32[2,12,8,128]{3,2,1,0:T(8,128)} %param.6) | copy-start | bytes 294916
  0.7 6.3 %copy-start.5 = (f32[8]{0:T(128)S(1)}, f32[8]{0:T(128)}, u32[]{:S(2)}) copy-start(f32[8]{0:T(128)} %param.8) | copy-start | bytes 100
  0.7 6.3 %copy-start.4 = (s32[2]{0:T(128)S(1)}, s32[2]{0:T(128)}, u32[]{:S(2)}) copy-start(s32[2]{0:T(128)} %param.9) | copy-start | bytes 28
  3.7 5.5 %collective-permute-start.1 = (f32[12544]{0:T(1024)S(1)}, f32[12544]{0:T(1024)S(1)}, u32[]{:S(2)}, u32[]{:S(2)}) collective-permute-start(f32[12544]{0:T(1024)S(1)} %select_n.130), channel_id=1, source_target_pairs={{0,8},{8,0},{16,24},{24,16},{1,9},{9,1},{17,25},{25,17},{2,10},{10... | collective-permute-start | bytes 150536 | tf_op jit(solution)/shard_map/ppermute | solution.py:119
  4.3 4.9 %collective-permute-start = (f32[12544]{0:T(1024)S(1)}, f32[12544]{0:T(1024)S(1)}, u32[]{:S(2)}, u32[]{:S(2)}) collective-permute-start(f32[12544]{0:T(1024)S(1)} %select_n.128), channel_id=1, source_target_pairs={{0,24},{8,16},{16,8},{24,0},{1,25},{9,17},{17,9},{25,1},{2,26},{10... | collective-permute-start | bytes 150536 | tf_op jit(solution)/shard_map/ppermute | solution.py:122
  9.9 5.1 %collective-permute-start.3 = (f32[1176]{0:T(1024)S(1)}, f32[1176]{0:T(1024)S(1)}, u32[]{:S(2)}, u32[]{:S(2)}) collective-permute-start(f32[1176]{0:T(1024)S(1)} %reshape.164), channel_id=1, source_target_pairs={{0,1},{1,0},{2,3},{3,2},{4,5},{5,4},{6,7},{7,6},{8,9},{9,8},{10,11... | collective-permute-start | bytes 14120 | tf_op jit(solution)/shard_map/ppermute | solution.py:119
  11.4 6.3 %collective-permute-start.2 = (f32[1176]{0:T(1024)S(1)}, f32[1176]{0:T(1024)S(1)}, u32[]{:S(2)}, u32[]{:S(2)}) collective-permute-start(f32[1176]{0:T(1024)S(1)} %reshape.163), channel_id=1, source_target_pairs={{0,7},{1,2},{2,1},{3,4},{4,3},{5,6},{6,5},{7,0},{8,15},{9,10},{10,... | collective-permute-start | bytes 14120 | tf_op jit(solution)/shard_map/ppermute | solution.py:122
  21.4 19.2 %copy-start = (f32[2,48,8,128]{3,2,1,0:T(8,128)}, f32[2,48,8,128]{3,2,1,0:T(8,128)S(1)}, u32[]{:S(2)}) copy-start(f32[2,48,8,128]{3,2,1,0:T(8,128)S(1)} %pad_maximum_fusion.7) | copy-start | bytes 1179652
  22.6 1.3 %collective-permute-start.4 = (f32[4608]{0:T(1024)S(1)}, f32[4608]{0:T(1024)S(1)}, u32[]{:S(2)}, u32[]{:S(2)}) collective-permute-start(f32[4608]{0:T(1024)S(1)} %reshape.169), channel_id=1, source_target_pairs={{0,8},{8,0},{16,24},{24,16},{1,9},{9,1},{17,25},{25,17},{2,10},{10... | collective-permute-start | bytes 55304 | tf_op jit(solution)/shard_map/ppermute | solution.py:140
  23.8 3.8 %collective-permute-start.5 = (f32[4608]{0:T(1024)S(1)}, f32[4608]{0:T(1024)S(1)}, u32[]{:S(2)}, u32[]{:S(2)}) collective-permute-start(f32[4608]{0:T(1024)S(1)} %add.155), channel_id=1, source_target_pairs={{0,16},{8,24},{16,0},{24,8},{1,17},{9,25},{17,1},{25,9},{2,18},{10... | collective-permute-start | bytes 55304 | tf_op jit(solution)/shard_map/ppermute | solution.py:140
  27.6 3.8 %collective-permute-start.6 = (f32[4608]{0:T(1024)S(1)}, f32[4608]{0:T(1024)S(1)}, u32[]{:S(2)}, u32[]{:S(2)}) collective-permute-start(f32[4608]{0:T(1024)S(1)} %add.156), channel_id=1, source_target_pairs={{0,1},{1,0},{2,3},{3,2},{4,5},{5,4},{6,7},{7,6},{8,9},{9,8},{10,11... | collective-permute-start | bytes 55304 | tf_op jit(solution)/shard_map/ppermute | solution.py:140
  31.4 3.8 %collective-permute-start.7 = (f32[4608]{0:T(1024)S(1)}, f32[4608]{0:T(1024)S(1)}, u32[]{:S(2)}, u32[]{:S(2)}) collective-permute-start(f32[4608]{0:T(1024)S(1)} %add.157), channel_id=1, source_target_pairs={{0,2},{1,3},{2,0},{3,1},{4,6},{5,7},{6,4},{7,5},{8,10},{9,11},{10,... | collective-permute-start | bytes 55304 | tf_op jit(solution)/shard_map/ppermute | solution.py:140
  35.2 4.7 %collective-permute-start.8 = (f32[4608]{0:T(1024)S(1)}, f32[4608]{0:T(1024)S(1)}, u32[]{:S(2)}, u32[]{:S(2)}) collective-permute-start(f32[4608]{0:T(1024)S(1)} %add.158), channel_id=1, source_target_pairs={{0,4},{1,5},{2,6},{3,7},{4,0},{5,1},{6,2},{7,3},{8,12},{9,13},{10,... | collective-permute-start | bytes 55304 | tf_op jit(solution)/shard_map/ppermute | solution.py:140

commit v13 on v11

--- a/solution.py
+++ b/solution.py
@@ -116,16 +116,14 @@
         after = lax.ppermute(head.reshape(-1), axis, [((i + 1) % count, i) for i in range(count)])
     else:
         even = lax.axis_index(axis) % 2 == 0
-        first = lax.ppermute(
-            jnp.where(even, tail, head).reshape(-1), axis, [(i, i ^ 1) for i in range(count)]
+        both = jnp.concatenate([head.reshape(-1), tail.reshape(-1)])
+        first = lax.ppermute(both, axis, [(i, i ^ 1) for i in range(count)])
+        second = lax.ppermute(
+            both, axis, [(i, (i + 1) % count if i % 2 else (i - 1) % count) for i in range(count)]
         )
-        second = lax.ppermute(
-            jnp.where(even, head, tail).reshape(-1),
-            axis,
-            [(i, (i + 1) % count if i % 2 else (i - 1) % count) for i in range(count)],
-        )
-        before = jnp.where(even, second, first)
-        after = jnp.where(even, first, second)
+        split = head.size
+        before = jnp.where(even, second[split:], first[split:])
+        after = jnp.where(even, first[:split], second[:split])
     before = before.reshape(tail.shape)
     after = after.reshape(head.shape)
     return jnp.concatenate([before, cells, after], axis=dim)

time: 47.5 us -> 48.5 us (1.021)
  waiting for transfers between devices: 17.7 us -> 18.5 us
    ppermute x4, waiting for transfers between devices: 2.8 us -> 3.83 us  [the longest x2 3.83 us: exchange_rim(): lax.ppermute(both, axis, [(i, (i + 1) % count if i % 2 else (i - 1) % cou...]
  transfers between devices with their start and end apart: 9 -> 9, of which waited for: 6 -> 7; matrix products, arithmetic and copies ran while one was open for 2% -> 2% of each run, Pallas kernels for 0% -> 0%
where the time goes in v13:
time: 48.5 us; the launch traced here: 48.2 us
  waiting for transfers between devices  18.5 us (38%)
  starting transfers between devices  10.7 us (22%)
  Pallas kernels  6.68 us (14%)
  local copies, waits for them, and re-layouts  4.95 us (10%)
  other arithmetic  4.04 us (8%)
  between operations  2.38 us (5%)
  matrix products  0.95 us (2%)
    ppermute x5, waiting for transfers between devices, tree_sum(): lax.ppermute(value, axis, [(i, i ^ step) for i in range(count)])  14.7 us
    pallas_call x1, Pallas kernels, matrix_stage(): pl.pallas_call(functools.partial(matrix_kernel, band_count=band_count, sc...  6.68 us
    ppermute x2, starting transfers between devices, exchange_rim(): lax.ppermute(both, axis, [(i, (i + 1) % count if i % 2 else (i - 1) % cou...  6.22 us
    ppermute x2, waiting for transfers between devices, exchange_rim(): lax.ppermute(both, axis, [(i, (i + 1) % count if i % 2 else (i - 1) % cou...  3.83 us
    ppermute x5, starting transfers between devices, tree_sum(): lax.ppermute(value, axis, [(i, i ^ step) for i in range(count)])  2.57 us
    ppermute x2, starting transfers between devices, exchange_rim(): first = lax.ppermute(both, axis, [(i, i ^ 1) for i in range(count)])  1.92 us
    another operation x2, other arithmetic, rotate(): jnp.stack([values[0] * cosine - values[1] * sine_part, values[0] * sine_p...  1.17 us
    slice x1, local copies, waits for them, and re-layouts, strip_of(): directions[:, :, start:stop]  0.99 us
  transfers between devices with their start and end apart: 9, of which 7 were waited for; matrix products, arithmetic and copies ran while one was open for 2% of the time, Pallas kernels for 0%

profile of v13, /device:TPU:0, one launch (start us, length us, event | category | flops | bytes accessed | tf_op | source)
XLA Modules:
  0.0 48.2 jit_solution(12536335116755503117)
XLA Ops:
  0.7 0.7 %convert_bitcast_fusion = (f32[1,8,128]{2,1,0:T(8,128)S(1)}, f32[8,128]{1,0:T(8,128)S(1)}) fusion(s32[8,128]{1,0:T(8,128)} %param.7), kind=kLoop, calls=%fused_computation.104 | loop fusion | flops 1024 | bytes 12288 | tf_op jit(solution)/shard_map/broadcast_in_dim | solution.py:277
  1.4 1.0 %fusion.44 = (f32[2,12,2,128]{3,2,1,0:T(2,128)S(1)}, f32[2,12,2,128]{3,2,1,0:T(2,128)S(1)}) fusion(f32[2,12,8,128]{3,2,1,0:T(8,128)} %param.5), kind=kLoop, calls=%fused_computation.106 | loop fusion | bytes 98304 | tf_op jit(solution)/shard_map/slice | solution.py:266
  2.4 1.0 %fusion.45 = (f32[2,12,2,128]{3,2,1,0:T(2,128)S(1)}, f32[2,12,2,128]{3,2,1,0:T(2,128)S(1)}) fusion(f32[2,12,8,128]{3,2,1,0:T(8,128)} %param.6), kind=kLoop, calls=%fused_computation.107 | loop fusion | bytes 98304 | tf_op jit(solution)/shard_map/slice | solution.py:266
  3.7 0.5 %collective-permute-start.1 = (f32[25088]{0:T(1024)S(1)}, f32[25088]{0:T(1024)S(1)}, u32[]{:S(2)}, u32[]{:S(2)}) collective-permute-start(f32[25088]{0:T(1024)S(1)} %constant_dynamic-update-slice_fusion), channel_id=1, source_target_pairs={{0,8},{8,0},{16,24},{24,16},{1,9},{9,1},{17,25},{25,17},{2,10},{10... | collective-permute-start | bytes 301064 | tf_op jit(solution)/shard_map/ppermute | solution.py:120
  4.3 2.6 %collective-permute-start = (f32[25088]{0:T(1024)S(1)}, f32[25088]{0:T(1024)S(1)}, u32[]{:S(2)}, u32[]{:S(2)}) collective-permute-start(f32[25088]{0:T(1024)S(1)} %constant_dynamic-update-slice_fusion), channel_id=1, source_target_pairs={{0,24},{8,16},{16,8},{24,0},{1,25},{9,17},{17,9},{25,1},{2,26},{10... | collective-permute-start | bytes 301064 | tf_op jit(solution)/shard_map/ppermute | solution.py:121
  6.9 0.6 %fusion.47 = (s32[1]{0:T(128)}, s32[1]{0:T(128)}) fusion(s32[2]{0:T(128)S(1)} %copy-done.3), kind=kLoop, calls=%fused_computation.109 | loop fusion | bytes 16 | tf_op jit(solution)/shard_map/slice | solution.py:271
  9.1 1.0 %collective-permute-done = f32[25088]{0:T(1024)S(1)} collective-permute-done((f32[25088]{0:T(1024)S(1)}, f32[25088]{0:T(1024)S(1)}, u32[]{:S(2)}, u32[]{:S(2)}) %collective-permute-start) | collective-permute-done | bytes 100384 | tf_op jit(solution)/shard_map/ppermute | solution.py:121
  10.9 1.4 %collective-permute-start.3 = (f32[2352]{0:T(1024)S(1)}, f32[2352]{0:T(1024)S(1)}, u32[]{:S(2)}, u32[]{:S(2)}) collective-permute-start(f32[2352]{0:T(1024)S(1)} %pad_maximum_fusion.15), channel_id=1, source_target_pairs={{0,1},{1,0},{2,3},{3,2},{4,5},{5,4},{6,7},{7,6},{8,9},{9,8},{10,11... | collective-permute-start | bytes 28232 | tf_op jit(solution)/shard_map/ppermute | solution.py:120
  12.3 3.6 %collective-permute-start.2 = (f32[2352]{0:T(1024)S(1)}, f32[2352]{0:T(1024)S(1)}, u32[]{:S(2)}, u32[]{:S(2)}) collective-permute-start(f32[2352]{0:T(1024)S(1)} %pad_maximum_fusion.15), channel_id=1, source_target_pairs={{0,7},{1,2},{2,1},{3,4},{4,3},{5,6},{6,5},{7,0},{8,15},{9,10},{10,... | collective-permute-start | bytes 28232 | tf_op jit(solution)/shard_map/ppermute | solution.py:121
  15.9 2.8 %collective-permute-done.2 = f32[2352]{0:T(1024)S(1)} collective-permute-done((f32[2352]{0:T(1024)S(1)}, f32[2352]{0:T(1024)S(1)}, u32[]{:S(2)}, u32[]{:S(2)}) %collective-permute-start.2) | collective-permute-done | bytes 9440 | tf_op jit(solution)/shard_map/ppermute | solution.py:121
  19.6 0.6 %subtract_bitcast_fusion = f32[1,24,12,132]{3,2,1,0:T(8,128)S(1)} fusion(f32[12,132]{1,0:T(8,128)S(1)} %get-tuple-element.34, f32[12,132]{1,0:T(8,128)S(1)} %get-tuple-element.33, f32[49,12,2]{2,1,0:T(8,128)S(1)} %select_n.116, f32[49,2,128]{2,1,0:T(2,128)S(1)} %select_n.112, f32[1,8,128]{2,1,0:T(8,128)S(1)} %get-tuple-element.29, ...), kind=kLoop, calls=%fused_computation.38 | loop fusion | flops 494208 | bytes 475200 | tf_op jit(solution)/shard_map/stack | solution.py:18
  20.1 0.6 %add_bitcast_fusion = f32[1,24,12,132]{3,2,1,0:T(8,128)S(1)} fusion(f32[12,132]{1,0:T(8,128)S(1)} %get-tuple-element.34, f32[12,132]{1,0:T(8,128)S(1)} %get-tuple-element.33, f32[49,12,2]{2,1,0:T(8,128)S(1)} %select_n.116, f32[49,2,128]{2,1,0:T(2,128)S(1)} %select_n.112, f32[1,8,128]{2,1,0:T(8,128)S(1)} %get-tuple-element.29, f32[48,8,128]{2,1,0:T(8,128)S(1)} %bitcast.40, ...), kind=kLoop, calls=%fused_computation.37 | loop fusion | flops 494208 | bytes 475200 | tf_op jit(solution)/shard_map/stack | solution.py:18
  20.7 0.6 %broadcast_divide_fusion.1 = (f32[2,12,10,130]{3,2,1,0:T(8,128)S(1)}, f32[2,12,10,130]{3,2,1,0:T(8,128)S(1)}, f32[2,12,10,130]{3,2,1,0:T(8,128)S(1)}) fusion(f32[10,130]{1,0:T(8,128)S(1)} %get-tuple-element.13, f32[10,130]{1,0:T(8,128)S(1)} %get-tuple-element.17, f32[10,130]{1,0:T(8,128)S(1)} %get-tuple-element.16, f32[10,130]{1,0:T(8,128)S(1)} %get-tuple-element.14, ...), kind=kLoop, calls=%fused_computation.52 | loop fusion | flops 530400 | bytes 704528 | tf_op jit(solution)/shard_map/div | solution.py:297
  22.4 0.5 convolution_bitcast_fusion.1
  22.9 0.5 convolution_bitcast_fusion
  23.6 1.2 %collective-permute-done.4 = f32[4608]{0:T(1024)S(1)} collective-permute-done((f32[4608]{0:T(1024)S(1)}, f32[4608]{0:T(1024)S(1)}, u32[]{:S(2)}, u32[]{:S(2)}) %collective-permute-start.4) | collective-permute-done | bytes 18464 | tf_op jit(solution)/shard_map/ppermute | solution.py:138
  24.8 1.5 %collective-permute-start.5 = (f32[4608]{0:T(1024)S(1)}, f32[4608]{0:T(1024)S(1)}, u32[]{:S(2)}, u32[]{:S(2)}) collective-permute-start(f32[4608]{0:T(1024)S(1)} %add.155), channel_id=1, source_target_pairs={{0,16},{8,24},{16,0},{24,8},{1,17},{9,25},{17,1},{25,9},{2,18},{10... | collective-permute-start | bytes 55304 | tf_op jit(solution)/shard_map/ppermute | solution.py:138
  26.3 2.3 %collective-permute-done.5 = f32[4608]{0:T(1024)S(1)} collective-permute-done((f32[4608]{0:T(1024)S(1)}, f32[4608]{0:T(1024)S(1)}, u32[]{:S(2)}, u32[]{:S(2)}) %collective-permute-start.5) | collective-permute-done | bytes 18464 | tf_op jit(solution)/shard_map/ppermute | solution.py:138
  28.6 3.8 %collective-permute-done.6 = f32[4608]{0:T(1024)S(1)} collective-permute-done((f32[4608]{0:T(1024)S(1)}, f32[4608]{0:T(1024)S(1)}, u32[]{:S(2)}, u32[]{:S(2)}) %collective-permute-start.6) | collective-permute-done | bytes 18464 | tf_op jit(solution)/shard_map/ppermute | solution.py:138
  32.4 3.8 %collective-permute-done.7 = f32[4608]{0:T(1024)S(1)} collective-permute-done((f32[4608]{0:T(1024)S(1)}, f32[4608]{0:T(1024)S(1)}, u32[]{:S(2)}, u32[]{:S(2)}) %collective-permute-start.7) | collective-permute-done | bytes 18464 | tf_op jit(solution)/shard_map/ppermute | solution.py:138
  36.2 1.0 %collective-permute-start.8 = (f32[4608]{0:T(1024)S(1)}, f32[4608]{0:T(1024)S(1)}, u32[]{:S(2)}, u32[]{:S(2)}) collective-permute-start(f32[4608]{0:T(1024)S(1)} %add.158), channel_id=1, source_target_pairs={{0,4},{1,5},{2,6},{3,7},{4,0},{5,1},{6,2},{7,3},{8,12},{9,13},{10,... | collective-permute-start | bytes 55304 | tf_op jit(solution)/shard_map/ppermute | solution.py:138
  37.1 3.7 %collective-permute-done.8 = f32[4608]{0:T(1024)S(1)} collective-permute-done((f32[4608]{0:T(1024)S(1)}, f32[4608]{0:T(1024)S(1)}, u32[]{:S(2)}, u32[]{:S(2)}) %collective-permute-start.8) | collective-permute-done | bytes 18464 | tf_op jit(solution)/shard_map/ppermute | solution.py:138
  40.9 0.7 %reshape.228.packed_ref = f32[2,48,48]{2,1,0:T(8,128)} reshape(f32[4608]{0:T(1024)S(1)} %add.159) | data formatting | bytes 36864 | tf_op jit(solution)/shard_map/reshape | solution.py:312
  41.6 6.7 %shard_map.68 = (f32[72,8,128]{2,1,0:T(8,128)}, f32[36,2,36]{2,1,0:T(2,128)}) custom-call(f32[2,48,48]{2,1,0:T(8,128)} %reshape.228.packed_ref, f32[96,8,128]{2,1,0:T(8,128)} %bitcast.36), custom_call_target="tpu_custom_call" | custom-call | tf_op jit(solution)/shard_map/pallas_call | solution.py:236
  (70 shorter events, 3.3 us)
Async XLA Ops:
  0.6 8.4 %copy-start.2 = (f32[2,12,8,128]{3,2,1,0:T(8,128)S(1)}, f32[2,12,8,128]{3,2,1,0:T(8,128)}, u32[]{:S(2)}) copy-start(f32[2,12,8,128]{3,2,1,0:T(8,128)} %param.5) | copy-start | bytes 294916
  0.6 8.4 %copy-start.1 = (f32[2,12,8,128]{3,2,1,0:T(8,128)S(1)}, f32[2,12,8,128]{3,2,1,0:T(8,128)}, u32[]{:S(2)}) copy-start(f32[2,12,8,128]{3,2,1,0:T(8,128)} %param.6) | copy-start | bytes 294916
  0.7 6.3 %copy-start.4 = (f32[8]{0:T(128)S(1)}, f32[8]{0:T(128)}, u32[]{:S(2)}) copy-start(f32[8]{0:T(128)} %param.8) | copy-start | bytes 100
  0.7 6.2 %copy-start.3 = (s32[2]{0:T(128)S(1)}, s32[2]{0:T(128)}, u32[]{:S(2)}) copy-start(s32[2]{0:T(128)} %param.9) | copy-start | bytes 28
  3.7 5.3 %collective-permute-start.1 = (f32[25088]{0:T(1024)S(1)}, f32[25088]{0:T(1024)S(1)}, u32[]{:S(2)}, u32[]{:S(2)}) collective-permute-start(f32[25088]{0:T(1024)S(1)} %constant_dynamic-update-slice_fusion), channel_id=1, source_target_pairs={{0,8},{8,0},{16,24},{24,16},{1,9},{9,1},{17,25},{25,17},{2,10},{10... | collective-permute-start | bytes 301064 | tf_op jit(solution)/shard_map/ppermute | solution.py:120
  4.3 5.8 %collective-permute-start = (f32[25088]{0:T(1024)S(1)}, f32[25088]{0:T(1024)S(1)}, u32[]{:S(2)}, u32[]{:S(2)}) collective-permute-start(f32[25088]{0:T(1024)S(1)} %constant_dynamic-update-slice_fusion), channel_id=1, source_target_pairs={{0,24},{8,16},{16,8},{24,0},{1,25},{9,17},{17,9},{25,1},{2,26},{10... | collective-permute-start | bytes 301064 | tf_op jit(solution)/shard_map/ppermute | solution.py:121
  10.9 5.0 %collective-permute-start.3 = (f32[2352]{0:T(1024)S(1)}, f32[2352]{0:T(1024)S(1)}, u32[]{:S(2)}, u32[]{:S(2)}) collective-permute-start(f32[2352]{0:T(1024)S(1)} %pad_maximum_fusion.15), channel_id=1, source_target_pairs={{0,1},{1,0},{2,3},{3,2},{4,5},{5,4},{6,7},{7,6},{8,9},{9,8},{10,11... | collective-permute-start | bytes 28232 | tf_op jit(solution)/shard_map/ppermute | solution.py:120
  12.3 6.4 %collective-permute-start.2 = (f32[2352]{0:T(1024)S(1)}, f32[2352]{0:T(1024)S(1)}, u32[]{:S(2)}, u32[]{:S(2)}) collective-permute-start(f32[2352]{0:T(1024)S(1)} %pad_maximum_fusion.15), channel_id=1, source_target_pairs={{0,7},{1,2},{2,1},{3,4},{4,3},{5,6},{6,5},{7,0},{8,15},{9,10},{10,... | collective-permute-start | bytes 28232 | tf_op jit(solution)/shard_map/ppermute | solution.py:121
  22.4 19.2 %copy-start = (f32[2,48,8,128]{3,2,1,0:T(8,128)}, f32[2,48,8,128]{3,2,1,0:T(8,128)S(1)}, u32[]{:S(2)}) copy-start(f32[2,48,8,128]{3,2,1,0:T(8,128)S(1)} %pad_maximum_fusion.7) | copy-start | bytes 1179652
  23.5 1.3 %collective-permute-start.4 = (f32[4608]{0:T(1024)S(1)}, f32[4608]{0:T(1024)S(1)}, u32[]{:S(2)}, u32[]{:S(2)}) collective-permute-start(f32[4608]{0:T(1024)S(1)} %reshape.227), channel_id=1, source_target_pairs={{0,8},{8,0},{16,24},{24,16},{1,9},{9,1},{17,25},{25,17},{2,10},{10... | collective-permute-start | bytes 55304 | tf_op jit(solution)/shard_map/ppermute | solution.py:138
  24.8 3.8 %collective-permute-start.5 = (f32[4608]{0:T(1024)S(1)}, f32[4608]{0:T(1024)S(1)}, u32[]{:S(2)}, u32[]{:S(2)}) collective-permute-start(f32[4608]{0:T(1024)S(1)} %add.155), channel_id=1, source_target_pairs={{0,16},{8,24},{16,0},{24,8},{1,17},{9,25},{17,1},{25,9},{2,18},{10... | collective-permute-start | bytes 55304 | tf_op jit(solution)/shard_map/ppermute | solution.py:138
  28.6 3.8 %collective-permute-start.6 = (f32[4608]{0:T(1024)S(1)}, f32[4608]{0:T(1024)S(1)}, u32[]{:S(2)}, u32[]{:S(2)}) collective-permute-start(f32[4608]{0:T(1024)S(1)} %add.156), channel_id=1, source_target_pairs={{0,1},{1,0},{2,3},{3,2},{4,5},{5,4},{6,7},{7,6},{8,9},{9,8},{10,11... | collective-permute-start | bytes 55304 | tf_op jit(solution)/shard_map/ppermute | solution.py:138
  32.4 3.8 %collective-permute-start.7 = (f32[4608]{0:T(1024)S(1)}, f32[4608]{0:T(1024)S(1)}, u32[]{:S(2)}, u32[]{:S(2)}) collective-permute-start(f32[4608]{0:T(1024)S(1)} %add.157), channel_id=1, source_target_pairs={{0,2},{1,3},{2,0},{3,1},{4,6},{5,7},{6,4},{7,5},{8,10},{9,11},{10,... | collective-permute-start | bytes 55304 | tf_op jit(solution)/shard_map/ppermute | solution.py:138
  36.2 4.7 %collective-permute-start.8 = (f32[4608]{0:T(1024)S(1)}, f32[4608]{0:T(1024)S(1)}, u32[]{:S(2)}, u32[]{:S(2)}) collective-permute-start(f32[4608]{0:T(1024)S(1)} %add.158), channel_id=1, source_target_pairs={{0,4},{1,5},{2,6},{3,7},{4,0},{5,1},{6,2},{7,3},{8,12},{9,13},{10,... | collective-permute-start | bytes 55304 | tf_op jit(solution)/shard_map/ppermute | solution.py:138

commit v14 on v11

--- a/solution.py
+++ b/solution.py
@@ -210,7 +210,8 @@
     inverse = identity
     for _ in range(NS_STEPS):
         factor = 1.5 * identity - 0.5 * dot(inverse, current)
-        current, inverse = dot(current, factor), dot(factor, inverse)
+        both = dot(factor, jnp.concatenate([current, inverse], axis=1))
+        current, inverse = both[:, :size], both[:, size:]
     root = inverse / jnp.sqrt(magnitude)
     root = embed(jnp.where(corner, root, 0.0), jnp.where(corner, spread(root, 0), 0.0))
     rotation = dot(mixing, root)
@@ -227,8 +228,13 @@
     packed_rotation = dot(pick_rows.astype(jnp.float32), dot(rotation, pick_cols.astype(jnp.float32)))
     work_ref[0] = scale * packed_rotation.T
     rotation_t = work_ref[0, : 2 * raw, : 2 * ext]
-    for row in range(field_ref.shape[1]):
-        basis_ref[:, row, :] = dot(rotation_t, field_ref[:, row, :])
+    lanes = field_ref.shape[2]
+    row_count = field_ref.shape[1]
+    rotated = dot(
+        rotation_t, jnp.concatenate([field_ref[:, row, :] for row in range(row_count)], axis=1)
+    )
+    for row in range(row_count):
+        basis_ref[:, row, :] = rotated[:, row * lanes : (row + 1) * lanes]
 
 
 def matrix_stage(packed, fields, band_count, scale):

time: 47.5 us -> 47.7 us (level)
  no operation moved by 1% of the time
where the time goes in v14:
time: 47.7 us; the launch traced here: 47.5 us
  waiting for transfers between devices  17.7 us (37%)
  starting transfers between devices  10.7 us (22%)
  Pallas kernels  6.93 us (15%)
  local copies, waits for them, and re-layouts  4.74 us (10%)
  other arithmetic  4.05 us (8%)
  between operations  2.38 us (5%)
  matrix products  0.95 us (2%)
    ppermute x5, waiting for transfers between devices, tree_sum(): lax.ppermute(value, axis, [(i, i ^ step) for i in range(count)])  14.9 us
    pallas_call x1, Pallas kernels, matrix_stage(): pl.pallas_call(functools.partial(matrix_kernel, band_count=band_count, sc...  6.93 us
    ppermute x2, starting transfers between devices, exchange_rim(): lax.ppermute(jnp.where(even, head, tail).reshape(-1), axis, [(i, (i + 1)...  6.27 us
    ppermute x2, waiting for transfers between devices, exchange_rim(): lax.ppermute(jnp.where(even, head, tail).reshape(-1), axis, [(i, (i + 1)...  2.79 us
    ppermute x5, starting transfers between devices, tree_sum(): lax.ppermute(value, axis, [(i, i ^ step) for i in range(count)])  2.33 us
    ppermute x2, starting transfers between devices, exchange_rim(): lax.ppermute(jnp.where(even, tail, head).reshape(-1), axis, [(i, i ^ 1) f...  2.06 us
    another operation x2, other arithmetic, rotate(): jnp.stack([values[0] * cosine - values[1] * sine_part, values[0] * sine_p...  1.17 us
    slice x1, local copies, waits for them, and re-layouts, strip_of(): directions[:, :, start:stop]  0.99 us
  transfers between devices with their start and end apart: 9, of which 6 were waited for; matrix products, arithmetic and copies ran while one was open for 2% of the time, Pallas kernels for 0%

profile of v14, /device:TPU:0, one launch (start us, length us, event | category | flops | bytes accessed | tf_op | source)
XLA Modules:
  0.0 47.5 jit_solution(9056091684841115427)
XLA Ops:
  0.7 0.7 %convert_bitcast_fusion = (f32[1,8,128]{2,1,0:T(8,128)S(1)}, f32[8,128]{1,0:T(8,128)S(1)}) fusion(s32[8,128]{1,0:T(8,128)} %param.7), kind=kLoop, calls=%fused_computation.105 | loop fusion | flops 1024 | bytes 12288 | tf_op jit(solution)/shard_map/broadcast_in_dim | solution.py:285
  1.4 1.0 %fusion.45 = (f32[2,12,2,128]{3,2,1,0:T(2,128)S(1)}, f32[2,12,2,128]{3,2,1,0:T(2,128)S(1)}) fusion(f32[2,12,8,128]{3,2,1,0:T(8,128)} %param.5), kind=kLoop, calls=%fused_computation.106 | loop fusion | bytes 98304 | tf_op jit(solution)/shard_map/slice | solution.py:274
  2.4 1.0 %fusion.46 = (f32[2,12,2,128]{3,2,1,0:T(2,128)S(1)}, f32[2,12,2,128]{3,2,1,0:T(2,128)S(1)}) fusion(f32[2,12,8,128]{3,2,1,0:T(8,128)} %param.6), kind=kLoop, calls=%fused_computation.107 | loop fusion | bytes 98304 | tf_op jit(solution)/shard_map/slice | solution.py:274
  3.6 0.5 %collective-permute-start.1 = (f32[12544]{0:T(1024)S(1)}, f32[12544]{0:T(1024)S(1)}, u32[]{:S(2)}, u32[]{:S(2)}) collective-permute-start(f32[12544]{0:T(1024)S(1)} %select_n.130), channel_id=1, source_target_pairs={{0,8},{8,0},{16,24},{24,16},{1,9},{9,1},{17,25},{25,17},{2,10},{10... | collective-permute-start | bytes 150536 | tf_op jit(solution)/shard_map/ppermute | solution.py:119
  4.2 2.7 %collective-permute-start = (f32[12544]{0:T(1024)S(1)}, f32[12544]{0:T(1024)S(1)}, u32[]{:S(2)}, u32[]{:S(2)}) collective-permute-start(f32[12544]{0:T(1024)S(1)} %select_n.128), channel_id=1, source_target_pairs={{0,24},{8,16},{16,8},{24,0},{1,25},{9,17},{17,9},{25,1},{2,26},{10... | collective-permute-start | bytes 150536 | tf_op jit(solution)/shard_map/ppermute | solution.py:122
  6.9 0.6 %fusion.48 = (s32[1]{0:T(128)}, s32[1]{0:T(128)}) fusion(s32[2]{0:T(128)S(1)} %copy-done.3), kind=kLoop, calls=%fused_computation.109 | loop fusion | bytes 16 | tf_op jit(solution)/shard_map/slice | solution.py:279
  9.8 1.5 %collective-permute-start.3 = (f32[1176]{0:T(1024)S(1)}, f32[1176]{0:T(1024)S(1)}, u32[]{:S(2)}, u32[]{:S(2)}) collective-permute-start(f32[1176]{0:T(1024)S(1)} %reshape.164), channel_id=1, source_target_pairs={{0,1},{1,0},{2,3},{3,2},{4,5},{5,4},{6,7},{7,6},{8,9},{9,8},{10,11... | collective-permute-start | bytes 14120 | tf_op jit(solution)/shard_map/ppermute | solution.py:119
  11.4 3.6 %collective-permute-start.2 = (f32[1176]{0:T(1024)S(1)}, f32[1176]{0:T(1024)S(1)}, u32[]{:S(2)}, u32[]{:S(2)}) collective-permute-start(f32[1176]{0:T(1024)S(1)} %reshape.163), channel_id=1, source_target_pairs={{0,7},{1,2},{2,1},{3,4},{4,3},{5,6},{6,5},{7,0},{8,15},{9,10},{10,... | collective-permute-start | bytes 14120 | tf_op jit(solution)/shard_map/ppermute | solution.py:122
  15.0 2.8 %collective-permute-done.2 = f32[1176]{0:T(1024)S(1)} collective-permute-done((f32[1176]{0:T(1024)S(1)}, f32[1176]{0:T(1024)S(1)}, u32[]{:S(2)}, u32[]{:S(2)}) %collective-permute-start.2) | collective-permute-done | bytes 4736 | tf_op jit(solution)/shard_map/ppermute | solution.py:122
  18.5 0.6 %subtract_bitcast_fusion = f32[1,24,12,132]{3,2,1,0:T(8,128)S(1)} fusion(f32[12,132]{1,0:T(8,128)S(1)} %get-tuple-element.36, f32[12,132]{1,0:T(8,128)S(1)} %get-tuple-element.35, f32[49,12,2]{2,1,0:T(8,128)S(1)} %reshape.166, f32[49,2,128]{2,1,0:T(2,128)S(1)} %reshape.162, f32[1,8,128]{2,1,0:T(8,128)S(1)} %get-tuple-element.31, ...), kind=kLoop, calls=%fused_computation.38 | loop fusion | flops 494208 | bytes 475200 | tf_op jit(solution)/shard_map/stack | solution.py:18
  19.1 0.6 %add_bitcast_fusion = f32[1,24,12,132]{3,2,1,0:T(8,128)S(1)} fusion(f32[12,132]{1,0:T(8,128)S(1)} %get-tuple-element.36, f32[12,132]{1,0:T(8,128)S(1)} %get-tuple-element.35, f32[49,12,2]{2,1,0:T(8,128)S(1)} %reshape.166, f32[49,2,128]{2,1,0:T(2,128)S(1)} %reshape.162, f32[1,8,128]{2,1,0:T(8,128)S(1)} %get-tuple-element.31, f32[48,8,128]{2,1,0:T(8,128)S(1)} %bitcast.40, ...), kind=kLoop, calls=%fused_computation.37 | loop fusion | flops 494208 | bytes 475200 | tf_op jit(solution)/shard_map/stack | solution.py:18
  19.7 0.6 %broadcast_divide_fusion.1 = (f32[2,12,10,130]{3,2,1,0:T(8,128)S(1)}, f32[2,12,10,130]{3,2,1,0:T(8,128)S(1)}, f32[2,12,10,130]{3,2,1,0:T(8,128)S(1)}) fusion(f32[10,130]{1,0:T(8,128)S(1)} %get-tuple-element.13, f32[10,130]{1,0:T(8,128)S(1)} %get-tuple-element.17, f32[10,130]{1,0:T(8,128)S(1)} %get-tuple-element.16, f32[10,130]{1,0:T(8,128)S(1)} %get-tuple-element.14, ...), kind=kLoop, calls=%fused_computation.54 | loop fusion | flops 530400 | bytes 704528 | tf_op jit(solution)/shard_map/div | solution.py:305
  20.8 0.4 fusion.17
  21.3 0.5 convolution_bitcast_fusion.1
  21.8 0.5 %convolution_bitcast_fusion = f32[96,96]{1,0:T(8,128)S(1)} fusion(f32[96,8,128]{2,0,1:T(8,128)S(1)} %bitcast.41, f32[96,8,128]{2,1,0:T(8,128)S(1)} %bitcast.35), kind=kOutput, calls=%fused_computation.13 | convolution fusion | flops 113246208 | bytes 823296 | tf_op jit(solution)/shard_map/jrc,krc->jk/dot_general | solution.py:44
  22.6 1.2 %collective-permute-done.4 = f32[4608]{0:T(1024)S(1)} collective-permute-done((f32[4608]{0:T(1024)S(1)}, f32[4608]{0:T(1024)S(1)}, u32[]{:S(2)}, u32[]{:S(2)}) %collective-permute-start.4) | collective-permute-done | bytes 18464 | tf_op jit(solution)/shard_map/ppermute | solution.py:140
  23.8 1.3 %collective-permute-start.5 = (f32[4608]{0:T(1024)S(1)}, f32[4608]{0:T(1024)S(1)}, u32[]{:S(2)}, u32[]{:S(2)}) collective-permute-start(f32[4608]{0:T(1024)S(1)} %add.155), channel_id=1, source_target_pairs={{0,16},{8,24},{16,0},{24,8},{1,17},{9,25},{17,1},{25,9},{2,18},{10... | collective-permute-start | bytes 55304 | tf_op jit(solution)/shard_map/ppermute | solution.py:140
  25.1 2.5 %collective-permute-done.5 = f32[4608]{0:T(1024)S(1)} collective-permute-done((f32[4608]{0:T(1024)S(1)}, f32[4608]{0:T(1024)S(1)}, u32[]{:S(2)}, u32[]{:S(2)}) %collective-permute-start.5) | collective-permute-done | bytes 18464 | tf_op jit(solution)/shard_map/ppermute | solution.py:140
  27.6 3.8 %collective-permute-done.6 = f32[4608]{0:T(1024)S(1)} collective-permute-done((f32[4608]{0:T(1024)S(1)}, f32[4608]{0:T(1024)S(1)}, u32[]{:S(2)}, u32[]{:S(2)}) %collective-permute-start.6) | collective-permute-done | bytes 18464 | tf_op jit(solution)/shard_map/ppermute | solution.py:140
  31.4 3.8 %collective-permute-done.7 = f32[4608]{0:T(1024)S(1)} collective-permute-done((f32[4608]{0:T(1024)S(1)}, f32[4608]{0:T(1024)S(1)}, u32[]{:S(2)}, u32[]{:S(2)}) %collective-permute-start.7) | collective-permute-done | bytes 18464 | tf_op jit(solution)/shard_map/ppermute | solution.py:140
  35.1 1.0 %collective-permute-start.8 = (f32[4608]{0:T(1024)S(1)}, f32[4608]{0:T(1024)S(1)}, u32[]{:S(2)}, u32[]{:S(2)}) collective-permute-start(f32[4608]{0:T(1024)S(1)} %add.158), channel_id=1, source_target_pairs={{0,4},{1,5},{2,6},{3,7},{4,0},{5,1},{6,2},{7,3},{8,12},{9,13},{10,... | collective-permute-start | bytes 55304 | tf_op jit(solution)/shard_map/ppermute | solution.py:140
  36.1 3.7 %collective-permute-done.8 = f32[4608]{0:T(1024)S(1)} collective-permute-done((f32[4608]{0:T(1024)S(1)}, f32[4608]{0:T(1024)S(1)}, u32[]{:S(2)}, u32[]{:S(2)}) %collective-permute-start.8) | collective-permute-done | bytes 18464 | tf_op jit(solution)/shard_map/ppermute | solution.py:140
  39.8 0.7 %reshape.170.packed_ref = f32[2,48,48]{2,1,0:T(8,128)} reshape(f32[4608]{0:T(1024)S(1)} %add.159) | data formatting | bytes 36864 | tf_op jit(solution)/shard_map/reshape | solution.py:320
  40.5 6.9 %shard_map.68 = (f32[72,8,128]{2,1,0:T(8,128)}, f32[36,2,36]{2,1,0:T(2,128)}) custom-call(f32[2,48,48]{2,1,0:T(8,128)} %reshape.170.packed_ref, f32[96,8,128]{2,1,0:T(8,128)} %bitcast.36), custom_call_target="tpu_custom_call" | custom-call | tf_op jit(solution)/shard_map/pallas_call | solution.py:244
  (65 shorter events, 2.8 us)
Async XLA Ops:
  0.6 8.4 %copy-start.2 = (f32[2,12,8,128]{3,2,1,0:T(8,128)S(1)}, f32[2,12,8,128]{3,2,1,0:T(8,128)}, u32[]{:S(2)}) copy-start(f32[2,12,8,128]{3,2,1,0:T(8,128)} %param.5) | copy-start | bytes 294916
  0.6 8.4 %copy-start.1 = (f32[2,12,8,128]{3,2,1,0:T(8,128)S(1)}, f32[2,12,8,128]{3,2,1,0:T(8,128)}, u32[]{:S(2)}) copy-start(f32[2,12,8,128]{3,2,1,0:T(8,128)} %param.6) | copy-start | bytes 294916
  0.7 6.3 %copy-start.4 = (f32[8]{0:T(128)S(1)}, f32[8]{0:T(128)}, u32[]{:S(2)}) copy-start(f32[8]{0:T(128)} %param.8) | copy-start | bytes 100
  0.7 6.2 %copy-start.3 = (s32[2]{0:T(128)S(1)}, s32[2]{0:T(128)}, u32[]{:S(2)}) copy-start(s32[2]{0:T(128)} %param.9) | copy-start | bytes 28
  3.6 5.4 %collective-permute-start.1 = (f32[12544]{0:T(1024)S(1)}, f32[12544]{0:T(1024)S(1)}, u32[]{:S(2)}, u32[]{:S(2)}) collective-permute-start(f32[12544]{0:T(1024)S(1)} %select_n.130), channel_id=1, source_target_pairs={{0,8},{8,0},{16,24},{24,16},{1,9},{9,1},{17,25},{25,17},{2,10},{10... | collective-permute-start | bytes 150536 | tf_op jit(solution)/shard_map/ppermute | solution.py:119
  4.2 4.9 %collective-permute-start = (f32[12544]{0:T(1024)S(1)}, f32[12544]{0:T(1024)S(1)}, u32[]{:S(2)}, u32[]{:S(2)}) collective-permute-start(f32[12544]{0:T(1024)S(1)} %select_n.128), channel_id=1, source_target_pairs={{0,24},{8,16},{16,8},{24,0},{1,25},{9,17},{17,9},{25,1},{2,26},{10... | collective-permute-start | bytes 150536 | tf_op jit(solution)/shard_map/ppermute | solution.py:122
  9.8 5.1 %collective-permute-start.3 = (f32[1176]{0:T(1024)S(1)}, f32[1176]{0:T(1024)S(1)}, u32[]{:S(2)}, u32[]{:S(2)}) collective-permute-start(f32[1176]{0:T(1024)S(1)} %reshape.164), channel_id=1, source_target_pairs={{0,1},{1,0},{2,3},{3,2},{4,5},{5,4},{6,7},{7,6},{8,9},{9,8},{10,11... | collective-permute-start | bytes 14120 | tf_op jit(solution)/shard_map/ppermute | solution.py:119
  11.4 6.3 %collective-permute-start.2 = (f32[1176]{0:T(1024)S(1)}, f32[1176]{0:T(1024)S(1)}, u32[]{:S(2)}, u32[]{:S(2)}) collective-permute-start(f32[1176]{0:T(1024)S(1)} %reshape.163), channel_id=1, source_target_pairs={{0,7},{1,2},{2,1},{3,4},{4,3},{5,6},{6,5},{7,0},{8,15},{9,10},{10,... | collective-permute-start | bytes 14120 | tf_op jit(solution)/shard_map/ppermute | solution.py:122
  21.3 19.2 %copy-start = (f32[2,48,8,128]{3,2,1,0:T(8,128)}, f32[2,48,8,128]{3,2,1,0:T(8,128)S(1)}, u32[]{:S(2)}) copy-start(f32[2,48,8,128]{3,2,1,0:T(8,128)S(1)} %pad_maximum_fusion.7) | copy-start | bytes 1179652
  22.5 1.3 %collective-permute-start.4 = (f32[4608]{0:T(1024)S(1)}, f32[4608]{0:T(1024)S(1)}, u32[]{:S(2)}, u32[]{:S(2)}) collective-permute-start(f32[4608]{0:T(1024)S(1)} %reshape.169), channel_id=1, source_target_pairs={{0,8},{8,0},{16,24},{24,16},{1,9},{9,1},{17,25},{25,17},{2,10},{10... | collective-permute-start | bytes 55304 | tf_op jit(solution)/shard_map/ppermute | solution.py:140
  23.8 3.8 %collective-permute-start.5 = (f32[4608]{0:T(1024)S(1)}, f32[4608]{0:T(1024)S(1)}, u32[]{:S(2)}, u32[]{:S(2)}) collective-permute-start(f32[4608]{0:T(1024)S(1)} %add.155), channel_id=1, source_target_pairs={{0,16},{8,24},{16,0},{24,8},{1,17},{9,25},{17,1},{25,9},{2,18},{10... | collective-permute-start | bytes 55304 | tf_op jit(solution)/shard_map/ppermute | solution.py:140
  27.6 3.8 %collective-permute-start.6 = (f32[4608]{0:T(1024)S(1)}, f32[4608]{0:T(1024)S(1)}, u32[]{:S(2)}, u32[]{:S(2)}) collective-permute-start(f32[4608]{0:T(1024)S(1)} %add.156), channel_id=1, source_target_pairs={{0,1},{1,0},{2,3},{3,2},{4,5},{5,4},{6,7},{7,6},{8,9},{9,8},{10,11... | collective-permute-start | bytes 55304 | tf_op jit(solution)/shard_map/ppermute | solution.py:140
  31.3 3.8 %collective-permute-start.7 = (f32[4608]{0:T(1024)S(1)}, f32[4608]{0:T(1024)S(1)}, u32[]{:S(2)}, u32[]{:S(2)}) collective-permute-start(f32[4608]{0:T(1024)S(1)} %add.157), channel_id=1, source_target_pairs={{0,2},{1,3},{2,0},{3,1},{4,6},{5,7},{6,4},{7,5},{8,10},{9,11},{10,... | collective-permute-start | bytes 55304 | tf_op jit(solution)/shard_map/ppermute | solution.py:140
  35.1 4.7 %collective-permute-start.8 = (f32[4608]{0:T(1024)S(1)}, f32[4608]{0:T(1024)S(1)}, u32[]{:S(2)}, u32[]{:S(2)}) collective-permute-start(f32[4608]{0:T(1024)S(1)} %add.158), channel_id=1, source_target_pairs={{0,4},{1,5},{2,6},{3,7},{4,0},{5,1},{6,2},{7,3},{8,12},{9,13},{10,... | collective-permute-start | bytes 55304 | tf_op jit(solution)/shard_map/ppermute | solution.py:140

commit v15 on v11

--- a/solution.py
+++ b/solution.py
@@ -104,7 +104,7 @@
     return jnp.dot(mixing.T, jnp.dot(matrix, mixing, precision=highest), precision=highest)
 
 
-def exchange_rim(cells, axis, dim, width, strips=None):
+def exchange_rim(cells, axis, dim, width, strips=None, angle=None):
     count = lax.axis_size(axis)
     if strips is None:
         head = lax.slice_in_dim(cells, 0, width, axis=dim)
@@ -126,9 +126,20 @@
         )
         before = jnp.where(even, second, first)
         after = jnp.where(even, first, second)
+    if angle is not None:
+        index = lax.axis_index(axis)
+        before = turn_flat(before, jnp.where(index == 0, -angle, 0.0), cells.shape[0])
+        after = turn_flat(after, jnp.where(index == count - 1, angle, 0.0), cells.shape[0])
     before = before.reshape(tail.shape)
     after = after.reshape(head.shape)
     return jnp.concatenate([before, cells, after], axis=dim)
+
+
+def turn_flat(flat, phase_angle, channels):
+    share = flat.shape[0] // channels
+    half = (channels - 1) // 2 * share
+    turned = rotate(jnp.stack([flat[:half], flat[half : 2 * half]]), phase_angle)
+    return jnp.concatenate([turned[0], turned[1], flat[2 * half :]])
 
 
 def tree_sum(value, axis):
@@ -272,25 +283,16 @@
     material_grid = materials.astype(jnp.float32)
     angle_row = 2.0 * math.pi * wavevector[0].astype(jnp.float32) / KDEN
     angle_col = 2.0 * math.pi * wavevector[1].astype(jnp.float32) / KDEN
-    row_index = lax.axis_index("row")
-    col_index = lax.axis_index("col")
     fields = jnp.concatenate([bands, directions], axis=1)
     packed = jnp.concatenate(
         [fields.reshape(4 * band_count, height, breadth), material_grid[None]], axis=0
     )
-    padded = exchange_rim(packed, "row", 1, 2, (strip_of(0, 2), strip_of(height - 2, height)))
-    padded = exchange_rim(padded, "col", 2, 2)
+    padded = exchange_rim(
+        packed, "row", 1, 2, (strip_of(0, 2), strip_of(height - 2, height)), angle_row
+    )
+    padded = exchange_rim(padded, "col", 2, 2, angle=angle_col)
     stiff_wide = stiffness_of(padded[-1])
     field_wide = padded[:-1].reshape(2, 2 * band_count, height + 4, breadth + 4)
-    row_place = jnp.arange(height + 4)
-    col_place = jnp.arange(breadth + 4)
-    row_phase = jnp.where(row_place < 2, jnp.where(row_index == 0, -angle_row, 0.0), 0.0) + jnp.where(
-        row_place >= height + 2, jnp.where(row_index == lax.axis_size("row") - 1, angle_row, 0.0), 0.0
-    )
-    col_phase = jnp.where(col_place < 2, jnp.where(col_index == 0, -angle_col, 0.0), 0.0) + jnp.where(
-        col_place >= breadth + 2, jnp.where(col_index == lax.axis_size("col") - 1, angle_col, 0.0), 0.0
-    )
-    field_wide = rotate(field_wide, row_phase[:, None] + col_phase[None, :])
     band_wide = field_wide[:, :band_count]
     applied_ring, diagonal_ring = stencil(band_wide, stiff_wide)
     stiff_ring = stiff_wide[1:-1, 1:-1]

time: 47.5 us -> 47 us (0.989)
  between operations: 2.38 us -> 2.99 us
  waiting for transfers between devices: 17.7 us -> 17.1 us
  other arithmetic: 4.05 us -> 3.5 us
    another operation x2 -> x0, other arithmetic: 1.17 us -> none  [rotate(): jnp.stack([values[0] * cosine - values[1] * sine_part, values[0] * sine_p...]
    concatenate x1 -> x2, other arithmetic: 0.08 us -> 0.67 us  [exchange_rim(): return jnp.concatenate([before, cells, after], axis=dim)]
  transfers between devices with their start and end apart: 9 -> 9, of which waited for: 6 -> 7; matrix products, arithmetic and copies ran while one was open for 2% -> 1% of each run, Pallas kernels for 0% -> 0%
where the time goes in v15:
time: 47 us; the launch traced here: 46.8 us
  waiting for transfers between devices  17.1 us (36%)
  starting transfers between devices  10.7 us (23%)
  Pallas kernels  6.68 us (14%)
  local copies, waits for them, and re-layouts  4.92 us (10%)
  other arithmetic  3.5 us (7%)
  between operations  2.99 us (6%)
  matrix products  0.95 us (2%)
    ppermute x5, waiting for transfers between devices, tree_sum(): lax.ppermute(value, axis, [(i, i ^ step) for i in range(count)])  14.7 us
    pallas_call x1, Pallas kernels, matrix_stage(): pl.pallas_call(functools.partial(matrix_kernel, band_count=band_count, sc...  6.68 us
    ppermute x2, starting transfers between devices, exchange_rim(): lax.ppermute(jnp.where(even, head, tail).reshape(-1), axis, [(i, (i + 1)...  6.27 us
    ppermute x5, starting transfers between devices, tree_sum(): lax.ppermute(value, axis, [(i, i ^ step) for i in range(count)])  2.56 us
    ppermute x2, waiting for transfers between devices, exchange_rim(): lax.ppermute(jnp.where(even, head, tail).reshape(-1), axis, [(i, (i + 1)...  2.36 us
    ppermute x2, starting transfers between devices, exchange_rim(): lax.ppermute(jnp.where(even, tail, head).reshape(-1), axis, [(i, i ^ 1) f...  1.83 us
    slice x1, local copies, waits for them, and re-layouts, strip_of(): directions[:, :, start:stop]  0.99 us
    slice x1, local copies, waits for them, and re-layouts, strip_of(): bands[:, :, start:stop]  0.99 us
  transfers between devices with their start and end apart: 9, of which 7 were waited for; matrix products, arithmetic and copies ran while one was open for 1% of the time, Pallas kernels for 0%

profile of v15, /device:TPU:0, one launch (start us, length us, event | category | flops | bytes accessed | tf_op | source)
XLA Modules:
  0.0 46.8 jit_solution(15734318727054697405)
XLA Ops:
  0.7 0.8 %convert_bitcast_fusion = (f32[1,8,128]{2,1,0:T(8,128)S(1)}, f32[8,128]{1,0:T(8,128)S(1)}) fusion(s32[8,128]{1,0:T(8,128)} %param.7), kind=kLoop, calls=%fused_computation.87 | loop fusion | flops 1024 | bytes 12288 | tf_op jit(solution)/shard_map/broadcast_in_dim | solution.py:288
  1.5 1.0 %fusion.33 = (f32[2,12,2,128]{3,2,1,0:T(2,128)S(1)}, f32[2,12,2,128]{3,2,1,0:T(2,128)S(1)}) fusion(f32[2,12,8,128]{3,2,1,0:T(8,128)} %param.5), kind=kLoop, calls=%fused_computation.88 | loop fusion | bytes 98304 | tf_op jit(solution)/shard_map/slice | solution.py:279
  2.5 1.0 %fusion.34 = (f32[2,12,2,128]{3,2,1,0:T(2,128)S(1)}, f32[2,12,2,128]{3,2,1,0:T(2,128)S(1)}) fusion(f32[2,12,8,128]{3,2,1,0:T(8,128)} %param.6), kind=kLoop, calls=%fused_computation.89 | loop fusion | bytes 98304 | tf_op jit(solution)/shard_map/slice | solution.py:279
  3.7 0.5 %collective-permute-start.1 = (f32[12544]{0:T(1024)S(1)}, f32[12544]{0:T(1024)S(1)}, u32[]{:S(2)}, u32[]{:S(2)}) collective-permute-start(f32[12544]{0:T(1024)S(1)} %select_n.100), channel_id=1, source_target_pairs={{0,8},{8,0},{16,24},{24,16},{1,9},{9,1},{17,25},{25,17},{2,10},{10... | collective-permute-start | bytes 150536 | tf_op jit(solution)/shard_map/ppermute | solution.py:119
  4.2 2.7 %collective-permute-start = (f32[12544]{0:T(1024)S(1)}, f32[12544]{0:T(1024)S(1)}, u32[]{:S(2)}, u32[]{:S(2)}) collective-permute-start(f32[12544]{0:T(1024)S(1)} %select_n.98), channel_id=1, source_target_pairs={{0,24},{8,16},{16,8},{24,0},{1,25},{9,17},{17,9},{25,1},{2,26},{10... | collective-permute-start | bytes 150536 | tf_op jit(solution)/shard_map/ppermute | solution.py:122
  7.0 0.6 %fusion.36 = (s32[1]{0:T(128)}, s32[1]{0:T(128)}) fusion(s32[2]{0:T(128)S(1)} %copy-done.3), kind=kLoop, calls=%fused_computation.91 | loop fusion | bytes 16 | tf_op jit(solution)/shard_map/slice | solution.py:285
  8.6 0.6 %collective-permute-done = f32[12544]{0:T(1024)S(1)} collective-permute-done((f32[12544]{0:T(1024)S(1)}, f32[12544]{0:T(1024)S(1)}, u32[]{:S(2)}, u32[]{:S(2)}) %collective-permute-start) | collective-permute-done | bytes 50208 | tf_op jit(solution)/shard_map/ppermute | solution.py:122
  9.9 1.3 %collective-permute-start.3 = (f32[1176]{0:T(1024)S(1)}, f32[1176]{0:T(1024)S(1)}, u32[]{:S(2)}, u32[]{:S(2)}) collective-permute-start(f32[1176]{0:T(1024)S(1)} %reshape.89), channel_id=1, source_target_pairs={{0,1},{1,0},{2,3},{3,2},{4,5},{5,4},{6,7},{7,6},{8,9},{9,8},{10,11... | collective-permute-start | bytes 14120 | tf_op jit(solution)/shard_map/ppermute | solution.py:119
  11.3 3.6 %collective-permute-start.2 = (f32[1176]{0:T(1024)S(1)}, f32[1176]{0:T(1024)S(1)}, u32[]{:S(2)}, u32[]{:S(2)}) collective-permute-start(f32[1176]{0:T(1024)S(1)} %reshape.88), channel_id=1, source_target_pairs={{0,7},{1,2},{2,1},{3,4},{4,3},{5,6},{6,5},{7,0},{8,15},{9,10},{10,... | collective-permute-start | bytes 14120 | tf_op jit(solution)/shard_map/ppermute | solution.py:122
  15.8 1.8 %collective-permute-done.2 = f32[1176]{0:T(1024)S(1)} collective-permute-done((f32[1176]{0:T(1024)S(1)}, f32[1176]{0:T(1024)S(1)}, u32[]{:S(2)}, u32[]{:S(2)}) %collective-permute-start.2) | collective-permute-done | bytes 4736 | tf_op jit(solution)/shard_map/ppermute | solution.py:122
  18.4 0.6 %pad_maximum_fusion.1 = f32[48,12,132]{2,1,0:T(8,128)S(1)} fusion(f32[49,12,2]{2,1,0:T(8,128)S(1)} %reshape.91, f32[49,12,2]{2,1,0:T(8,128)S(1)} %reshape.90, f32[49,2,128]{2,1,0:T(2,128)S(1)} %reshape.87, f32[49,2,128]{2,1,0:T(2,128)S(1)} %reshape.85, f32[1,8,128]{2,1,0:T(8,128)S(1)} %get-tuple-element.40, f32[48,8,128]{2,1,0:T(8,128)S(1)} %bitcast.37), kind=kLoop, calls=%fused_computation.3 | loop fusion | flops 380160 | bytes 614592 | tf_op jit(solution)/shard_map/concatenate | solution.py:135
  19.3 0.6 %broadcast_divide_fusion = (f32[2,12,10,130]{3,2,1,0:T(8,128)S(1)}, f32[2,12,10,130]{3,2,1,0:T(8,128)S(1)}, f32[2,12,10,130]{3,2,1,0:T(8,128)S(1)}, f32[2,12,10,130]{3,2,1,0:T(8,128)S(1)}) fusion(f32[10,130]{1,0:T(8,128)S(1)} %get-tuple-element.13, f32[2,24,12,132]{3,2,1,0:T(8,128)S(1)} %bitcast.31, f32[10,130]{1,0:T(8,128)S(1)} %get-tuple-element.17, ...), kind=kLoop, calls=%fused_computation.34 | loop fusion | flops 343200 | bytes 1274000 | tf_op jit(solution)/shard_map/div | solution.py:301
  20.3 0.4 fusion.7
  20.9 0.5 %convolution_bitcast_fusion.1 = f32[96,96]{1,0:T(8,128)S(1)} fusion(f32[96,8,128]{2,1,0:T(8,128)S(1)} %bitcast.32), kind=kOutput, calls=%fused_computation.2 | convolution fusion | flops 113246208 | bytes 430080 | tf_op jit(solution)/shard_map/jrc,krc->jk/dot_general | solution.py:44
  21.3 0.5 %convolution_bitcast_fusion = f32[96,96]{1,0:T(8,128)S(1)} fusion(f32[96,8,128]{2,0,1:T(8,128)S(1)} %bitcast.38, f32[96,8,128]{2,1,0:T(8,128)S(1)} %bitcast.33), kind=kOutput, calls=%fused_computation.1 | convolution fusion | flops 113246208 | bytes 823296 | tf_op jit(solution)/shard_map/jrc,krc->jk/dot_general | solution.py:44
  22.2 1.2 %collective-permute-done.4 = f32[4608]{0:T(1024)S(1)} collective-permute-done((f32[4608]{0:T(1024)S(1)}, f32[4608]{0:T(1024)S(1)}, u32[]{:S(2)}, u32[]{:S(2)}) %collective-permute-start.4) | collective-permute-done | bytes 18464 | tf_op jit(solution)/shard_map/ppermute | solution.py:151
  23.3 1.5 %collective-permute-start.5 = (f32[4608]{0:T(1024)S(1)}, f32[4608]{0:T(1024)S(1)}, u32[]{:S(2)}, u32[]{:S(2)}) collective-permute-start(f32[4608]{0:T(1024)S(1)} %add.128), channel_id=1, source_target_pairs={{0,16},{8,24},{16,0},{24,8},{1,17},{9,25},{17,1},{25,9},{2,18},{10... | collective-permute-start | bytes 55304 | tf_op jit(solution)/shard_map/ppermute | solution.py:151
  24.9 2.3 %collective-permute-done.5 = f32[4608]{0:T(1024)S(1)} collective-permute-done((f32[4608]{0:T(1024)S(1)}, f32[4608]{0:T(1024)S(1)}, u32[]{:S(2)}, u32[]{:S(2)}) %collective-permute-start.5) | collective-permute-done | bytes 18464 | tf_op jit(solution)/shard_map/ppermute | solution.py:151
  27.1 3.8 %collective-permute-done.6 = f32[4608]{0:T(1024)S(1)} collective-permute-done((f32[4608]{0:T(1024)S(1)}, f32[4608]{0:T(1024)S(1)}, u32[]{:S(2)}, u32[]{:S(2)}) %collective-permute-start.6) | collective-permute-done | bytes 18464 | tf_op jit(solution)/shard_map/ppermute | solution.py:151
  30.9 3.8 %collective-permute-done.7 = f32[4608]{0:T(1024)S(1)} collective-permute-done((f32[4608]{0:T(1024)S(1)}, f32[4608]{0:T(1024)S(1)}, u32[]{:S(2)}, u32[]{:S(2)}) %collective-permute-start.7) | collective-permute-done | bytes 18464 | tf_op jit(solution)/shard_map/ppermute | solution.py:151
  34.7 1.0 %collective-permute-start.8 = (f32[4608]{0:T(1024)S(1)}, f32[4608]{0:T(1024)S(1)}, u32[]{:S(2)}, u32[]{:S(2)}) collective-permute-start(f32[4608]{0:T(1024)S(1)} %add.131), channel_id=1, source_target_pairs={{0,4},{1,5},{2,6},{3,7},{4,0},{5,1},{6,2},{7,3},{8,12},{9,13},{10,... | collective-permute-start | bytes 55304 | tf_op jit(solution)/shard_map/ppermute | solution.py:151
  35.7 3.7 %collective-permute-done.8 = f32[4608]{0:T(1024)S(1)} collective-permute-done((f32[4608]{0:T(1024)S(1)}, f32[4608]{0:T(1024)S(1)}, u32[]{:S(2)}, u32[]{:S(2)}) %collective-permute-start.8) | collective-permute-done | bytes 18464 | tf_op jit(solution)/shard_map/ppermute | solution.py:151
  39.4 0.7 %reshape.96.packed_ref = f32[2,48,48]{2,1,0:T(8,128)} reshape(f32[4608]{0:T(1024)S(1)} %add.132) | data formatting | bytes 36864 | tf_op jit(solution)/shard_map/reshape | solution.py:316
  40.1 6.7 %shard_map.68 = (f32[72,8,128]{2,1,0:T(8,128)}, f32[36,2,36]{2,1,0:T(2,128)}) custom-call(f32[2,48,48]{2,1,0:T(8,128)} %reshape.96.packed_ref, f32[96,8,128]{2,1,0:T(8,128)} %bitcast.34), custom_call_target="tpu_custom_call" | custom-call | tf_op jit(solution)/shard_map/pallas_call | solution.py:249
  (73 shorter events, 2.9 us)
Async XLA Ops:
  0.6 6.3 %copy-start.2 = (f32[2,12,8,128]{3,2,1,0:T(8,128)S(1)}, f32[2,12,8,128]{3,2,1,0:T(8,128)}, u32[]{:S(2)}) copy-start(f32[2,12,8,128]{3,2,1,0:T(8,128)} %param.5) | copy-start | bytes 294916
  0.6 6.3 %copy-start.1 = (f32[2,12,8,128]{3,2,1,0:T(8,128)S(1)}, f32[2,12,8,128]{3,2,1,0:T(8,128)}, u32[]{:S(2)}) copy-start(f32[2,12,8,128]{3,2,1,0:T(8,128)} %param.6) | copy-start | bytes 294916
  0.7 6.3 %copy-start.4 = (f32[8]{0:T(128)S(1)}, f32[8]{0:T(128)}, u32[]{:S(2)}) copy-start(f32[8]{0:T(128)} %param.8) | copy-start | bytes 100
  0.7 6.3 %copy-start.3 = (s32[2]{0:T(128)S(1)}, s32[2]{0:T(128)}, u32[]{:S(2)}) copy-start(s32[2]{0:T(128)} %param.9) | copy-start | bytes 28
  3.7 4.9 %collective-permute-start.1 = (f32[12544]{0:T(1024)S(1)}, f32[12544]{0:T(1024)S(1)}, u32[]{:S(2)}, u32[]{:S(2)}) collective-permute-start(f32[12544]{0:T(1024)S(1)} %select_n.100), channel_id=1, source_target_pairs={{0,8},{8,0},{16,24},{24,16},{1,9},{9,1},{17,25},{25,17},{2,10},{10... | collective-permute-start | bytes 150536 | tf_op jit(solution)/shard_map/ppermute | solution.py:119
  4.2 4.9 %collective-permute-start = (f32[12544]{0:T(1024)S(1)}, f32[12544]{0:T(1024)S(1)}, u32[]{:S(2)}, u32[]{:S(2)}) collective-permute-start(f32[12544]{0:T(1024)S(1)} %select_n.98), channel_id=1, source_target_pairs={{0,24},{8,16},{16,8},{24,0},{1,25},{9,17},{17,9},{25,1},{2,26},{10... | collective-permute-start | bytes 150536 | tf_op jit(solution)/shard_map/ppermute | solution.py:122
  9.9 5.9 %collective-permute-start.3 = (f32[1176]{0:T(1024)S(1)}, f32[1176]{0:T(1024)S(1)}, u32[]{:S(2)}, u32[]{:S(2)}) collective-permute-start(f32[1176]{0:T(1024)S(1)} %reshape.89), channel_id=1, source_target_pairs={{0,1},{1,0},{2,3},{3,2},{4,5},{5,4},{6,7},{7,6},{8,9},{9,8},{10,11... | collective-permute-start | bytes 14120 | tf_op jit(solution)/shard_map/ppermute | solution.py:119
  11.3 6.3 %collective-permute-start.2 = (f32[1176]{0:T(1024)S(1)}, f32[1176]{0:T(1024)S(1)}, u32[]{:S(2)}, u32[]{:S(2)}) collective-permute-start(f32[1176]{0:T(1024)S(1)} %reshape.88), channel_id=1, source_target_pairs={{0,7},{1,2},{2,1},{3,4},{4,3},{5,6},{6,5},{7,0},{8,15},{9,10},{10,... | collective-permute-start | bytes 14120 | tf_op jit(solution)/shard_map/ppermute | solution.py:122
  20.8 19.3 %copy-start = (f32[2,48,8,128]{3,2,1,0:T(8,128)}, f32[2,48,8,128]{3,2,1,0:T(8,128)S(1)}, u32[]{:S(2)}) copy-start(f32[2,48,8,128]{3,2,1,0:T(8,128)S(1)} %pad_maximum_fusion.7) | copy-start | bytes 1179652
  22.1 1.3 %collective-permute-start.4 = (f32[4608]{0:T(1024)S(1)}, f32[4608]{0:T(1024)S(1)}, u32[]{:S(2)}, u32[]{:S(2)}) collective-permute-start(f32[4608]{0:T(1024)S(1)} %reshape.95), channel_id=1, source_target_pairs={{0,8},{8,0},{16,24},{24,16},{1,9},{9,1},{17,25},{25,17},{2,10},{10... | collective-permute-start | bytes 55304 | tf_op jit(solution)/shard_map/ppermute | solution.py:151
  23.3 3.8 %collective-permute-start.5 = (f32[4608]{0:T(1024)S(1)}, f32[4608]{0:T(1024)S(1)}, u32[]{:S(2)}, u32[]{:S(2)}) collective-permute-start(f32[4608]{0:T(1024)S(1)} %add.128), channel_id=1, source_target_pairs={{0,16},{8,24},{16,0},{24,8},{1,17},{9,25},{17,1},{25,9},{2,18},{10... | collective-permute-start | bytes 55304 | tf_op jit(solution)/shard_map/ppermute | solution.py:151
  27.1 3.8 %collective-permute-start.6 = (f32[4608]{0:T(1024)S(1)}, f32[4608]{0:T(1024)S(1)}, u32[]{:S(2)}, u32[]{:S(2)}) collective-permute-start(f32[4608]{0:T(1024)S(1)} %add.129), channel_id=1, source_target_pairs={{0,1},{1,0},{2,3},{3,2},{4,5},{5,4},{6,7},{7,6},{8,9},{9,8},{10,11... | collective-permute-start | bytes 55304 | tf_op jit(solution)/shard_map/ppermute | solution.py:151
  30.9 3.8 %collective-permute-start.7 = (f32[4608]{0:T(1024)S(1)}, f32[4608]{0:T(1024)S(1)}, u32[]{:S(2)}, u32[]{:S(2)}) collective-permute-start(f32[4608]{0:T(1024)S(1)} %add.130), channel_id=1, source_target_pairs={{0,2},{1,3},{2,0},{3,1},{4,6},{5,7},{6,4},{7,5},{8,10},{9,11},{10,... | collective-permute-start | bytes 55304 | tf_op jit(solution)/shard_map/ppermute | solution.py:151
  34.7 4.7 %collective-permute-start.8 = (f32[4608]{0:T(1024)S(1)}, f32[4608]{0:T(1024)S(1)}, u32[]{:S(2)}, u32[]{:S(2)}) collective-permute-start(f32[4608]{0:T(1024)S(1)} %add.131), channel_id=1, source_target_pairs={{0,4},{1,5},{2,6},{3,7},{4,0},{5,1},{6,2},{7,3},{8,12},{9,13},{10,... | collective-permute-start | bytes 55304 | tf_op jit(solution)/shard_map/ppermute | solution.py:151

commit v16 on v15

--- a/solution.py
+++ b/solution.py
@@ -37,71 +37,10 @@
     return (diagonal * inner_cells - neighbours, diagonal)
 
 
-def complex_gram(first_block, second_block):
-    count = first_block.shape[1]
-    first_flat = first_block.reshape((2 * count,) + first_block.shape[2:])
-    second_flat = second_block.reshape((2 * count,) + second_block.shape[2:])
-    products = jnp.einsum(
-        "jrc,krc->jk", first_flat, second_flat, precision=lax.Precision.HIGHEST
-    )
+def combine_parts(products, count):
     real_part = products[:count, :count] + products[count:, count:]
     imag_part = products[:count, count:] - products[count:, :count]
     return (real_part, imag_part)
-
-
-def inverse_root(gram_real, gram_imag):
-    highest = lax.Precision.HIGHEST
-    order_size = gram_real.shape[0]
-    upper_half = jnp.concatenate([gram_real, -gram_imag], axis=1)
-    lower_half = jnp.concatenate([gram_imag, gram_real], axis=1)
-    embedded = jnp.concatenate([upper_half, lower_half], axis=0)
-    magnitude = jnp.sqrt(jnp.sum(embedded * embedded))
-    identity = jnp.eye(2 * order_size, dtype=embedded.dtype)
-
-    def newton(turn_index, carried):
-        current, inverse = carried
-        factor = 1.5 * identity - 0.5 * jnp.dot(inverse, current, precision=highest)
-        return (
-            jnp.dot(current, factor, precision=highest),
-            jnp.dot(factor, inverse, precision=highest),
-        )
-
-    current, inverse = lax.fori_loop(0, NS_STEPS, newton, (embedded / magnitude, identity))
-    root_full = inverse / jnp.sqrt(magnitude)
-    return (root_full[:order_size, :order_size], root_full[order_size:, :order_size])
-
-
-def reduce_matrix(root_real, root_imag, ham_real, ham_imag):
-    highest = lax.Precision.HIGHEST
-    prod_real = jnp.dot(ham_real, root_real, precision=highest) - jnp.dot(
-        ham_imag, root_imag, precision=highest
-    )
-    prod_imag = jnp.dot(ham_real, root_imag, precision=highest) + jnp.dot(
-        ham_imag, root_real, precision=highest
-    )
-    red_real = jnp.dot(root_real.T, prod_real, precision=highest) + jnp.dot(
-        root_imag.T, prod_imag, precision=highest
-    )
-    red_imag = jnp.dot(root_real.T, prod_imag, precision=highest) - jnp.dot(
-        root_imag.T, prod_real, precision=highest
-    )
-    return jnp.stack([red_real, red_imag])
-
-
-def rotate_basis(raw_basis, root_real, root_imag, scale_factor):
-    highest = lax.Precision.HIGHEST
-    basis_real = jnp.einsum("jrc,jk->krc", raw_basis[0], root_real, precision=highest) - jnp.einsum(
-        "jrc,jk->krc", raw_basis[1], root_imag, precision=highest
-    )
-    basis_imag = jnp.einsum("jrc,jk->krc", raw_basis[0], root_imag, precision=highest) + jnp.einsum(
-        "jrc,jk->krc", raw_basis[1], root_real, precision=highest
-    )
-    return scale_factor * jnp.stack([basis_real, basis_imag])
-
-
-def project_mixing(mixing, matrix):
-    highest = lax.Precision.HIGHEST
-    return jnp.dot(mixing.T, jnp.dot(matrix, mixing, precision=highest), precision=highest)
 
 
 def exchange_rim(cells, axis, dim, width, strips=None, angle=None):
@@ -310,8 +249,17 @@
     scaled_bands = scaled_ring[:, band_count : 2 * band_count, 1:-1, 1:-1]
     extended = jnp.concatenate([bands, scaled_image, scaled_bands, directions], axis=1)
     extended_applied = jnp.concatenate([applied_cycle, extra_applied], axis=1)
-    local_gram = complex_gram(extended, extended)
-    local_ham = complex_gram(extended, extended_applied)
+    count = extended.shape[1]
+    products = jnp.einsum(
+        "jrc,krc->jk",
+        extended.reshape((2 * count,) + extended.shape[2:]),
+        jnp.concatenate([extended, extended_applied], axis=0).reshape(
+            (4 * count,) + extended.shape[2:]
+        ),
+        precision=lax.Precision.HIGHEST,
+    )
+    local_gram = combine_parts(products[:, : 2 * count], count)
+    local_ham = combine_parts(products[:, 2 * count :], count)
     summed = jnp.stack([pack_hermitian(*local_gram), pack_hermitian(*local_ham)])
     summed = tree_sum(tree_sum(summed.reshape(-1), "row"), "col").reshape(summed.shape)
     raw_count = 3 * band_count

time: 47 us -> 47.2 us (level)
    dot_general x2 -> x1, matrix products: 0.95 us -> 0.89 us  [body(): jnp.einsum('jrc,krc->jk', extended.reshape((2 * count,) + extended.shape[...]
where the time goes in v16:
time: 47.2 us; the launch traced here: 46.9 us
  waiting for transfers between devices  17.1 us (36%)
  starting transfers between devices  10.7 us (23%)
  Pallas kernels  6.7 us (14%)
  local copies, waits for them, and re-layouts  5.14 us (11%)
  other arithmetic  3.47 us (7%)
  between operations  2.99 us (6%)
  matrix products  0.89 us (2%)
    ppermute x5, waiting for transfers between devices, tree_sum(): lax.ppermute(value, axis, [(i, i ^ step) for i in range(count)])  14.7 us
    pallas_call x1, Pallas kernels, matrix_stage(): pl.pallas_call(functools.partial(matrix_kernel, band_count=band_count, sc...  6.7 us
    ppermute x2, starting transfers between devices, exchange_rim(): lax.ppermute(jnp.where(even, head, tail).reshape(-1), axis, [(i, (i + 1)...  6.27 us
    ppermute x5, starting transfers between devices, tree_sum(): lax.ppermute(value, axis, [(i, i ^ step) for i in range(count)])  2.56 us
    ppermute x2, waiting for transfers between devices, exchange_rim(): lax.ppermute(jnp.where(even, head, tail).reshape(-1), axis, [(i, (i + 1)...  2.36 us
    ppermute x2, starting transfers between devices, exchange_rim(): lax.ppermute(jnp.where(even, tail, head).reshape(-1), axis, [(i, i ^ 1) f...  1.83 us
    slice x1, local copies, waits for them, and re-layouts, strip_of(): directions[:, :, start:stop]  0.99 us
    slice x1, local copies, waits for them, and re-layouts, strip_of(): bands[:, :, start:stop]  0.99 us
  transfers between devices with their start and end apart: 9, of which 7 were waited for; matrix products, arithmetic and copies ran while one was open for 1% of the time, Pallas kernels for 0%

profile of v16, /device:TPU:0, one launch (start us, length us, event | category | flops | bytes accessed | tf_op | source)
XLA Modules:
  0.0 46.9 jit_solution(538165135228034292)
XLA Ops:
  0.7 0.8 %convert_bitcast_fusion = (f32[1,8,128]{2,1,0:T(8,128)S(1)}, f32[8,128]{1,0:T(8,128)S(1)}) fusion(s32[8,128]{1,0:T(8,128)} %param.7), kind=kLoop, calls=%fused_computation.85 | loop fusion | flops 1024 | bytes 12288 | tf_op jit(solution)/shard_map/broadcast_in_dim | solution.py:227
  1.5 1.0 %fusion.32 = (f32[2,12,2,128]{3,2,1,0:T(2,128)S(1)}, f32[2,12,2,128]{3,2,1,0:T(2,128)S(1)}) fusion(f32[2,12,8,128]{3,2,1,0:T(8,128)} %param.5), kind=kLoop, calls=%fused_computation.86 | loop fusion | bytes 98304 | tf_op jit(solution)/shard_map/slice | solution.py:218
  2.5 1.0 %fusion.33 = (f32[2,12,2,128]{3,2,1,0:T(2,128)S(1)}, f32[2,12,2,128]{3,2,1,0:T(2,128)S(1)}) fusion(f32[2,12,8,128]{3,2,1,0:T(8,128)} %param.6), kind=kLoop, calls=%fused_computation.87 | loop fusion | bytes 98304 | tf_op jit(solution)/shard_map/slice | solution.py:218
  3.7 0.5 %collective-permute-start.1 = (f32[12544]{0:T(1024)S(1)}, f32[12544]{0:T(1024)S(1)}, u32[]{:S(2)}, u32[]{:S(2)}) collective-permute-start(f32[12544]{0:T(1024)S(1)} %select_n.100), channel_id=1, source_target_pairs={{0,8},{8,0},{16,24},{24,16},{1,9},{9,1},{17,25},{25,17},{2,10},{10... | collective-permute-start | bytes 150536 | tf_op jit(solution)/shard_map/ppermute | solution.py:58
  4.2 2.7 %collective-permute-start = (f32[12544]{0:T(1024)S(1)}, f32[12544]{0:T(1024)S(1)}, u32[]{:S(2)}, u32[]{:S(2)}) collective-permute-start(f32[12544]{0:T(1024)S(1)} %select_n.98), channel_id=1, source_target_pairs={{0,24},{8,16},{16,8},{24,0},{1,25},{9,17},{17,9},{25,1},{2,26},{10... | collective-permute-start | bytes 150536 | tf_op jit(solution)/shard_map/ppermute | solution.py:61
  7.0 0.6 %fusion.35 = (s32[1]{0:T(128)}, s32[1]{0:T(128)}) fusion(s32[2]{0:T(128)S(1)} %copy-done.3), kind=kLoop, calls=%fused_computation.89 | loop fusion | bytes 16 | tf_op jit(solution)/shard_map/slice | solution.py:224
  8.6 0.6 %collective-permute-done = f32[12544]{0:T(1024)S(1)} collective-permute-done((f32[12544]{0:T(1024)S(1)}, f32[12544]{0:T(1024)S(1)}, u32[]{:S(2)}, u32[]{:S(2)}) %collective-permute-start) | collective-permute-done | bytes 50208 | tf_op jit(solution)/shard_map/ppermute | solution.py:61
  9.7 0.2 reshape.87
  9.9 1.3 %collective-permute-start.3 = (f32[1176]{0:T(1024)S(1)}, f32[1176]{0:T(1024)S(1)}, u32[]{:S(2)}, u32[]{:S(2)}) collective-permute-start(f32[1176]{0:T(1024)S(1)} %reshape.87), channel_id=1, source_target_pairs={{0,1},{1,0},{2,3},{3,2},{4,5},{5,4},{6,7},{7,6},{8,9},{9,8},{10,11... | collective-permute-start | bytes 14120 | tf_op jit(solution)/shard_map/ppermute | solution.py:58
  11.3 3.6 %collective-permute-start.2 = (f32[1176]{0:T(1024)S(1)}, f32[1176]{0:T(1024)S(1)}, u32[]{:S(2)}, u32[]{:S(2)}) collective-permute-start(f32[1176]{0:T(1024)S(1)} %reshape.86), channel_id=1, source_target_pairs={{0,7},{1,2},{2,1},{3,4},{4,3},{5,6},{6,5},{7,0},{8,15},{9,10},{10,... | collective-permute-start | bytes 14120 | tf_op jit(solution)/shard_map/ppermute | solution.py:61
  15.8 1.8 %collective-permute-done.2 = f32[1176]{0:T(1024)S(1)} collective-permute-done((f32[1176]{0:T(1024)S(1)}, f32[1176]{0:T(1024)S(1)}, u32[]{:S(2)}, u32[]{:S(2)}) %collective-permute-start.2) | collective-permute-done | bytes 4736 | tf_op jit(solution)/shard_map/ppermute | solution.py:61
  18.4 0.6 %pad_maximum_fusion.1 = f32[48,12,132]{2,1,0:T(8,128)S(1)} fusion(f32[49,12,2]{2,1,0:T(8,128)S(1)} %reshape.89, f32[49,12,2]{2,1,0:T(8,128)S(1)} %reshape.88, f32[49,2,128]{2,1,0:T(2,128)S(1)} %reshape.85, f32[49,2,128]{2,1,0:T(2,128)S(1)} %reshape.83, f32[1,8,128]{2,1,0:T(8,128)S(1)} %get-tuple-element.42, f32[48,8,128]{2,1,0:T(8,128)S(1)} %bitcast.35), kind=kLoop, calls=%fused_computation.2 | loop fusion | flops 380160 | bytes 614592 | tf_op jit(solution)/shard_map/concatenate | solution.py:74
  19.3 0.6 %broadcast_divide_fusion = (f32[2,12,10,130]{3,2,1,0:T(8,128)S(1)}, f32[2,12,10,130]{3,2,1,0:T(8,128)S(1)}, f32[2,12,10,130]{3,2,1,0:T(8,128)S(1)}, f32[2,12,10,130]{3,2,1,0:T(8,128)S(1)}) fusion(f32[10,130]{1,0:T(8,128)S(1)} %get-tuple-element.13, f32[2,24,12,132]{3,2,1,0:T(8,128)S(1)} %bitcast.29, f32[10,130]{1,0:T(8,128)S(1)} %get-tuple-element.17, ...), kind=kLoop, calls=%fused_computation.32 | loop fusion | flops 343200 | bytes 1274000 | tf_op jit(solution)/shard_map/div | solution.py:240
  20.4 0.4 fusion.6
  21.1 0.9 %convolution_bitcast_fusion = f32[96,192]{1,0:T(8,128)S(1)} fusion(f32[192,8,128]{2,0,1:T(8,128)S(1)} %bitcast.32, f32[96,8,128]{2,1,0:T(8,128)S(1)} %bitcast.30), kind=kOutput, calls=%fused_computation.1 | convolution fusion | flops 226492416 | bytes 1253376 | tf_op jit(solution)/shard_map/jrc,krc->jk/dot_general | solution.py:253
  22.3 1.2 %collective-permute-done.4 = f32[4608]{0:T(1024)S(1)} collective-permute-done((f32[4608]{0:T(1024)S(1)}, f32[4608]{0:T(1024)S(1)}, u32[]{:S(2)}, u32[]{:S(2)}) %collective-permute-start.4) | collective-permute-done | bytes 18464 | tf_op jit(solution)/shard_map/ppermute | solution.py:90
  23.5 1.5 %collective-permute-start.5 = (f32[4608]{0:T(1024)S(1)}, f32[4608]{0:T(1024)S(1)}, u32[]{:S(2)}, u32[]{:S(2)}) collective-permute-start(f32[4608]{0:T(1024)S(1)} %add.128), channel_id=1, source_target_pairs={{0,16},{8,24},{16,0},{24,8},{1,17},{9,25},{17,1},{25,9},{2,18},{10... | collective-permute-start | bytes 55304 | tf_op jit(solution)/shard_map/ppermute | solution.py:90
  25.0 2.3 %collective-permute-done.5 = f32[4608]{0:T(1024)S(1)} collective-permute-done((f32[4608]{0:T(1024)S(1)}, f32[4608]{0:T(1024)S(1)}, u32[]{:S(2)}, u32[]{:S(2)}) %collective-permute-start.5) | collective-permute-done | bytes 18464 | tf_op jit(solution)/shard_map/ppermute | solution.py:90
  27.3 3.8 %collective-permute-done.6 = f32[4608]{0:T(1024)S(1)} collective-permute-done((f32[4608]{0:T(1024)S(1)}, f32[4608]{0:T(1024)S(1)}, u32[]{:S(2)}, u32[]{:S(2)}) %collective-permute-start.6) | collective-permute-done | bytes 18464 | tf_op jit(solution)/shard_map/ppermute | solution.py:90
  31.1 3.8 %collective-permute-done.7 = f32[4608]{0:T(1024)S(1)} collective-permute-done((f32[4608]{0:T(1024)S(1)}, f32[4608]{0:T(1024)S(1)}, u32[]{:S(2)}, u32[]{:S(2)}) %collective-permute-start.7) | collective-permute-done | bytes 18464 | tf_op jit(solution)/shard_map/ppermute | solution.py:90
  34.8 1.0 %collective-permute-start.8 = (f32[4608]{0:T(1024)S(1)}, f32[4608]{0:T(1024)S(1)}, u32[]{:S(2)}, u32[]{:S(2)}) collective-permute-start(f32[4608]{0:T(1024)S(1)} %add.131), channel_id=1, source_target_pairs={{0,4},{1,5},{2,6},{3,7},{4,0},{5,1},{6,2},{7,3},{8,12},{9,13},{10,... | collective-permute-start | bytes 55304 | tf_op jit(solution)/shard_map/ppermute | solution.py:90
  35.8 3.7 %collective-permute-done.8 = f32[4608]{0:T(1024)S(1)} collective-permute-done((f32[4608]{0:T(1024)S(1)}, f32[4608]{0:T(1024)S(1)}, u32[]{:S(2)}, u32[]{:S(2)}) %collective-permute-start.8) | collective-permute-done | bytes 18464 | tf_op jit(solution)/shard_map/ppermute | solution.py:90
  39.5 0.7 %reshape.94.packed_ref = f32[2,48,48]{2,1,0:T(8,128)} reshape(f32[4608]{0:T(1024)S(1)} %add.132) | data formatting | bytes 36864 | tf_op jit(solution)/shard_map/reshape | solution.py:264
  40.2 6.7 %shard_map.68 = (f32[72,8,128]{2,1,0:T(8,128)}, f32[36,2,36]{2,1,0:T(2,128)}) custom-call(f32[2,48,48]{2,1,0:T(8,128)} %reshape.94.packed_ref, f32[96,8,128]{2,1,0:T(8,128)} %bitcast.31), custom_call_target="tpu_custom_call" | custom-call | tf_op jit(solution)/shard_map/pallas_call | solution.py:188
  (71 shorter events, 2.9 us)
Async XLA Ops:
  0.6 6.3 %copy-start.2 = (f32[2,12,8,128]{3,2,1,0:T(8,128)S(1)}, f32[2,12,8,128]{3,2,1,0:T(8,128)}, u32[]{:S(2)}) copy-start(f32[2,12,8,128]{3,2,1,0:T(8,128)} %param.5) | copy-start | bytes 294916
  0.6 6.3 %copy-start.1 = (f32[2,12,8,128]{3,2,1,0:T(8,128)S(1)}, f32[2,12,8,128]{3,2,1,0:T(8,128)}, u32[]{:S(2)}) copy-start(f32[2,12,8,128]{3,2,1,0:T(8,128)} %param.6) | copy-start | bytes 294916
  0.7 6.3 %copy-start.4 = (f32[8]{0:T(128)S(1)}, f32[8]{0:T(128)}, u32[]{:S(2)}) copy-start(f32[8]{0:T(128)} %param.8) | copy-start | bytes 100
  0.7 6.3 %copy-start.3 = (s32[2]{0:T(128)S(1)}, s32[2]{0:T(128)}, u32[]{:S(2)}) copy-start(s32[2]{0:T(128)} %param.9) | copy-start | bytes 28
  3.7 4.9 %collective-permute-start.1 = (f32[12544]{0:T(1024)S(1)}, f32[12544]{0:T(1024)S(1)}, u32[]{:S(2)}, u32[]{:S(2)}) collective-permute-start(f32[12544]{0:T(1024)S(1)} %select_n.100), channel_id=1, source_target_pairs={{0,8},{8,0},{16,24},{24,16},{1,9},{9,1},{17,25},{25,17},{2,10},{10... | collective-permute-start | bytes 150536 | tf_op jit(solution)/shard_map/ppermute | solution.py:58
  4.2 4.9 %collective-permute-start = (f32[12544]{0:T(1024)S(1)}, f32[12544]{0:T(1024)S(1)}, u32[]{:S(2)}, u32[]{:S(2)}) collective-permute-start(f32[12544]{0:T(1024)S(1)} %select_n.98), channel_id=1, source_target_pairs={{0,24},{8,16},{16,8},{24,0},{1,25},{9,17},{17,9},{25,1},{2,26},{10... | collective-permute-start | bytes 150536 | tf_op jit(solution)/shard_map/ppermute | solution.py:61
  9.9 5.9 %collective-permute-start.3 = (f32[1176]{0:T(1024)S(1)}, f32[1176]{0:T(1024)S(1)}, u32[]{:S(2)}, u32[]{:S(2)}) collective-permute-start(f32[1176]{0:T(1024)S(1)} %reshape.87), channel_id=1, source_target_pairs={{0,1},{1,0},{2,3},{3,2},{4,5},{5,4},{6,7},{7,6},{8,9},{9,8},{10,11... | collective-permute-start | bytes 14120 | tf_op jit(solution)/shard_map/ppermute | solution.py:58
  11.3 6.3 %collective-permute-start.2 = (f32[1176]{0:T(1024)S(1)}, f32[1176]{0:T(1024)S(1)}, u32[]{:S(2)}, u32[]{:S(2)}) collective-permute-start(f32[1176]{0:T(1024)S(1)} %reshape.86), channel_id=1, source_target_pairs={{0,7},{1,2},{2,1},{3,4},{4,3},{5,6},{6,5},{7,0},{8,15},{9,10},{10,... | collective-permute-start | bytes 14120 | tf_op jit(solution)/shard_map/ppermute | solution.py:61
  20.3 0.8 %copy-start = (f32[2,48,8,128]{3,2,1,0:T(8,128)}, f32[2,48,8,128]{3,2,1,0:T(8,128)S(1)}, u32[]{:S(2)}) copy-start(f32[2,48,8,128]{3,2,1,0:T(8,128)S(1)} %pad_maximum_fusion.7) | copy-start | bytes 1179652
  22.2 1.3 %collective-permute-start.4 = (f32[4608]{0:T(1024)S(1)}, f32[4608]{0:T(1024)S(1)}, u32[]{:S(2)}, u32[]{:S(2)}) collective-permute-start(f32[4608]{0:T(1024)S(1)} %reshape.93), channel_id=1, source_target_pairs={{0,8},{8,0},{16,24},{24,16},{1,9},{9,1},{17,25},{25,17},{2,10},{10... | collective-permute-start | bytes 55304 | tf_op jit(solution)/shard_map/ppermute | solution.py:90
  23.5 3.8 %collective-permute-start.5 = (f32[4608]{0:T(1024)S(1)}, f32[4608]{0:T(1024)S(1)}, u32[]{:S(2)}, u32[]{:S(2)}) collective-permute-start(f32[4608]{0:T(1024)S(1)} %add.128), channel_id=1, source_target_pairs={{0,16},{8,24},{16,0},{24,8},{1,17},{9,25},{17,1},{25,9},{2,18},{10... | collective-permute-start | bytes 55304 | tf_op jit(solution)/shard_map/ppermute | solution.py:90
  27.3 3.8 %collective-permute-start.6 = (f32[4608]{0:T(1024)S(1)}, f32[4608]{0:T(1024)S(1)}, u32[]{:S(2)}, u32[]{:S(2)}) collective-permute-start(f32[4608]{0:T(1024)S(1)} %add.129), channel_id=1, source_target_pairs={{0,1},{1,0},{2,3},{3,2},{4,5},{5,4},{6,7},{7,6},{8,9},{9,8},{10,11... | collective-permute-start | bytes 55304 | tf_op jit(solution)/shard_map/ppermute | solution.py:90
  31.1 3.8 %collective-permute-start.7 = (f32[4608]{0:T(1024)S(1)}, f32[4608]{0:T(1024)S(1)}, u32[]{:S(2)}, u32[]{:S(2)}) collective-permute-start(f32[4608]{0:T(1024)S(1)} %add.130), channel_id=1, source_target_pairs={{0,2},{1,3},{2,0},{3,1},{4,6},{5,7},{6,4},{7,5},{8,10},{9,11},{10,... | collective-permute-start | bytes 55304 | tf_op jit(solution)/shard_map/ppermute | solution.py:90
  34.8 4.7 %collective-permute-start.8 = (f32[4608]{0:T(1024)S(1)}, f32[4608]{0:T(1024)S(1)}, u32[]{:S(2)}, u32[]{:S(2)}) collective-permute-start(f32[4608]{0:T(1024)S(1)} %add.131), channel_id=1, source_target_pairs={{0,4},{1,5},{2,6},{3,7},{4,0},{5,1},{6,2},{7,3},{8,12},{9,13},{10,... | collective-permute-start | bytes 55304 | tf_op jit(solution)/shard_map/ppermute | solution.py:90

commit v17 on v15

--- a/solution.py
+++ b/solution.py
@@ -313,7 +313,7 @@
     local_gram = complex_gram(extended, extended)
     local_ham = complex_gram(extended, extended_applied)
     summed = jnp.stack([pack_hermitian(*local_gram), pack_hermitian(*local_ham)])
-    summed = tree_sum(tree_sum(summed.reshape(-1), "row"), "col").reshape(summed.shape)
+    summed = tree_sum(tree_sum(summed.reshape(-1), "col"), "row").reshape(summed.shape)
     raw_count = 3 * band_count
     ext_count = 4 * band_count
     scale_factor = math.sqrt(height * breadth * lax.axis_size("row") * lax.axis_size("col"))

time: 47 us -> 47 us (level)
  no operation moved by 1% of the time
where the time goes in v17:
time: 47 us; the launch traced here: 46.8 us
  waiting for transfers between devices  17 us (36%)
  starting transfers between devices  10.7 us (23%)
  Pallas kernels  6.68 us (14%)
  local copies, waits for them, and re-layouts  4.92 us (10%)
  other arithmetic  3.5 us (7%)
  between operations  2.99 us (6%)
  matrix products  0.95 us (2%)
    ppermute x5, waiting for transfers between devices, tree_sum(): lax.ppermute(value, axis, [(i, i ^ step) for i in range(count)])  14.7 us
    pallas_call x1, Pallas kernels, matrix_stage(): pl.pallas_call(functools.partial(matrix_kernel, band_count=band_count, sc...  6.68 us
    ppermute x2, starting transfers between devices, exchange_rim(): lax.ppermute(jnp.where(even, head, tail).reshape(-1), axis, [(i, (i + 1)...  6.27 us
    ppermute x5, starting transfers between devices, tree_sum(): lax.ppermute(value, axis, [(i, i ^ step) for i in range(count)])  2.59 us
    ppermute x2, waiting for transfers between devices, exchange_rim(): lax.ppermute(jnp.where(even, head, tail).reshape(-1), axis, [(i, (i + 1)...  2.36 us
    ppermute x2, starting transfers between devices, exchange_rim(): lax.ppermute(jnp.where(even, tail, head).reshape(-1), axis, [(i, i ^ 1) f...  1.83 us
    slice x1, local copies, waits for them, and re-layouts, strip_of(): directions[:, :, start:stop]  0.99 us
    slice x1, local copies, waits for them, and re-layouts, strip_of(): bands[:, :, start:stop]  0.99 us
  transfers between devices with their start and end apart: 9, of which 7 were waited for; matrix products, arithmetic and copies ran while one was open for 1% of the time, Pallas kernels for 0%

profile of v17, /device:TPU:0, one launch (start us, length us, event | category | flops | bytes accessed | tf_op | source)
XLA Modules:
  0.0 46.8 jit_solution(12053817942502961066)
XLA Ops:
  0.7 0.8 %convert_bitcast_fusion = (f32[1,8,128]{2,1,0:T(8,128)S(1)}, f32[8,128]{1,0:T(8,128)S(1)}) fusion(s32[8,128]{1,0:T(8,128)} %param.7), kind=kLoop, calls=%fused_computation.87 | loop fusion | flops 1024 | bytes 12288 | tf_op jit(solution)/shard_map/broadcast_in_dim | solution.py:288
  1.5 1.0 %fusion.33 = (f32[2,12,2,128]{3,2,1,0:T(2,128)S(1)}, f32[2,12,2,128]{3,2,1,0:T(2,128)S(1)}) fusion(f32[2,12,8,128]{3,2,1,0:T(8,128)} %param.5), kind=kLoop, calls=%fused_computation.88 | loop fusion | bytes 98304 | tf_op jit(solution)/shard_map/slice | solution.py:279
  2.5 1.0 %fusion.34 = (f32[2,12,2,128]{3,2,1,0:T(2,128)S(1)}, f32[2,12,2,128]{3,2,1,0:T(2,128)S(1)}) fusion(f32[2,12,8,128]{3,2,1,0:T(8,128)} %param.6), kind=kLoop, calls=%fused_computation.89 | loop fusion | bytes 98304 | tf_op jit(solution)/shard_map/slice | solution.py:279
  3.7 0.5 %collective-permute-start.1 = (f32[12544]{0:T(1024)S(1)}, f32[12544]{0:T(1024)S(1)}, u32[]{:S(2)}, u32[]{:S(2)}) collective-permute-start(f32[12544]{0:T(1024)S(1)} %select_n.100), channel_id=1, source_target_pairs={{0,8},{8,0},{16,24},{24,16},{1,9},{9,1},{17,25},{25,17},{2,10},{10... | collective-permute-start | bytes 150536 | tf_op jit(solution)/shard_map/ppermute | solution.py:119
  4.2 2.7 %collective-permute-start = (f32[12544]{0:T(1024)S(1)}, f32[12544]{0:T(1024)S(1)}, u32[]{:S(2)}, u32[]{:S(2)}) collective-permute-start(f32[12544]{0:T(1024)S(1)} %select_n.98), channel_id=1, source_target_pairs={{0,24},{8,16},{16,8},{24,0},{1,25},{9,17},{17,9},{25,1},{2,26},{10... | collective-permute-start | bytes 150536 | tf_op jit(solution)/shard_map/ppermute | solution.py:122
  7.0 0.6 %fusion.36 = (s32[1]{0:T(128)}, s32[1]{0:T(128)}) fusion(s32[2]{0:T(128)S(1)} %copy-done.3), kind=kLoop, calls=%fused_computation.91 | loop fusion | bytes 16 | tf_op jit(solution)/shard_map/slice | solution.py:285
  8.6 0.6 %collective-permute-done = f32[12544]{0:T(1024)S(1)} collective-permute-done((f32[12544]{0:T(1024)S(1)}, f32[12544]{0:T(1024)S(1)}, u32[]{:S(2)}, u32[]{:S(2)}) %collective-permute-start) | collective-permute-done | bytes 50208 | tf_op jit(solution)/shard_map/ppermute | solution.py:122
  9.9 1.3 %collective-permute-start.3 = (f32[1176]{0:T(1024)S(1)}, f32[1176]{0:T(1024)S(1)}, u32[]{:S(2)}, u32[]{:S(2)}) collective-permute-start(f32[1176]{0:T(1024)S(1)} %reshape.89), channel_id=1, source_target_pairs={{0,1},{1,0},{2,3},{3,2},{4,5},{5,4},{6,7},{7,6},{8,9},{9,8},{10,11... | collective-permute-start | bytes 14120 | tf_op jit(solution)/shard_map/ppermute | solution.py:119
  11.3 3.6 %collective-permute-start.2 = (f32[1176]{0:T(1024)S(1)}, f32[1176]{0:T(1024)S(1)}, u32[]{:S(2)}, u32[]{:S(2)}) collective-permute-start(f32[1176]{0:T(1024)S(1)} %reshape.88), channel_id=1, source_target_pairs={{0,7},{1,2},{2,1},{3,4},{4,3},{5,6},{6,5},{7,0},{8,15},{9,10},{10,... | collective-permute-start | bytes 14120 | tf_op jit(solution)/shard_map/ppermute | solution.py:122
  15.8 1.8 %collective-permute-done.2 = f32[1176]{0:T(1024)S(1)} collective-permute-done((f32[1176]{0:T(1024)S(1)}, f32[1176]{0:T(1024)S(1)}, u32[]{:S(2)}, u32[]{:S(2)}) %collective-permute-start.2) | collective-permute-done | bytes 4736 | tf_op jit(solution)/shard_map/ppermute | solution.py:122
  18.4 0.6 %pad_maximum_fusion.1 = f32[48,12,132]{2,1,0:T(8,128)S(1)} fusion(f32[49,12,2]{2,1,0:T(8,128)S(1)} %reshape.91, f32[49,12,2]{2,1,0:T(8,128)S(1)} %reshape.90, f32[49,2,128]{2,1,0:T(2,128)S(1)} %reshape.87, f32[49,2,128]{2,1,0:T(2,128)S(1)} %reshape.85, f32[1,8,128]{2,1,0:T(8,128)S(1)} %get-tuple-element.40, f32[48,8,128]{2,1,0:T(8,128)S(1)} %bitcast.37), kind=kLoop, calls=%fused_computation.3 | loop fusion | flops 380160 | bytes 614592 | tf_op jit(solution)/shard_map/concatenate | solution.py:135
  19.3 0.6 %broadcast_divide_fusion = (f32[2,12,10,130]{3,2,1,0:T(8,128)S(1)}, f32[2,12,10,130]{3,2,1,0:T(8,128)S(1)}, f32[2,12,10,130]{3,2,1,0:T(8,128)S(1)}, f32[2,12,10,130]{3,2,1,0:T(8,128)S(1)}) fusion(f32[10,130]{1,0:T(8,128)S(1)} %get-tuple-element.13, f32[2,24,12,132]{3,2,1,0:T(8,128)S(1)} %bitcast.31, f32[10,130]{1,0:T(8,128)S(1)} %get-tuple-element.17, ...), kind=kLoop, calls=%fused_computation.34 | loop fusion | flops 343200 | bytes 1274000 | tf_op jit(solution)/shard_map/div | solution.py:301
  20.3 0.4 fusion.7
  20.9 0.5 %convolution_bitcast_fusion.1 = f32[96,96]{1,0:T(8,128)S(1)} fusion(f32[96,8,128]{2,1,0:T(8,128)S(1)} %bitcast.32), kind=kOutput, calls=%fused_computation.2 | convolution fusion | flops 113246208 | bytes 430080 | tf_op jit(solution)/shard_map/jrc,krc->jk/dot_general | solution.py:44
  21.3 0.5 %convolution_bitcast_fusion = f32[96,96]{1,0:T(8,128)S(1)} fusion(f32[96,8,128]{2,0,1:T(8,128)S(1)} %bitcast.38, f32[96,8,128]{2,1,0:T(8,128)S(1)} %bitcast.33), kind=kOutput, calls=%fused_computation.1 | convolution fusion | flops 113246208 | bytes 823296 | tf_op jit(solution)/shard_map/jrc,krc->jk/dot_general | solution.py:44
  22.2 3.8 %collective-permute-done.4 = f32[4608]{0:T(1024)S(1)} collective-permute-done((f32[4608]{0:T(1024)S(1)}, f32[4608]{0:T(1024)S(1)}, u32[]{:S(2)}, u32[]{:S(2)}) %collective-permute-start.4) | collective-permute-done | bytes 18464 | tf_op jit(solution)/shard_map/ppermute | solution.py:151
  25.9 3.8 %collective-permute-done.5 = f32[4608]{0:T(1024)S(1)} collective-permute-done((f32[4608]{0:T(1024)S(1)}, f32[4608]{0:T(1024)S(1)}, u32[]{:S(2)}, u32[]{:S(2)}) %collective-permute-start.5) | collective-permute-done | bytes 18464 | tf_op jit(solution)/shard_map/ppermute | solution.py:151
  29.7 1.0 %collective-permute-start.6 = (f32[4608]{0:T(1024)S(1)}, f32[4608]{0:T(1024)S(1)}, u32[]{:S(2)}, u32[]{:S(2)}) collective-permute-start(f32[4608]{0:T(1024)S(1)} %add.129), channel_id=1, source_target_pairs={{0,4},{1,5},{2,6},{3,7},{4,0},{5,1},{6,2},{7,3},{8,12},{9,13},{10,... | collective-permute-start | bytes 55304 | tf_op jit(solution)/shard_map/ppermute | solution.py:151
  30.7 3.7 %collective-permute-done.6 = f32[4608]{0:T(1024)S(1)} collective-permute-done((f32[4608]{0:T(1024)S(1)}, f32[4608]{0:T(1024)S(1)}, u32[]{:S(2)}, u32[]{:S(2)}) %collective-permute-start.6) | collective-permute-done | bytes 18464 | tf_op jit(solution)/shard_map/ppermute | solution.py:151
  34.4 1.2 %collective-permute-done.7 = f32[4608]{0:T(1024)S(1)} collective-permute-done((f32[4608]{0:T(1024)S(1)}, f32[4608]{0:T(1024)S(1)}, u32[]{:S(2)}, u32[]{:S(2)}) %collective-permute-start.7) | collective-permute-done | bytes 18464 | tf_op jit(solution)/shard_map/ppermute | solution.py:151
  35.6 1.5 %collective-permute-start.8 = (f32[4608]{0:T(1024)S(1)}, f32[4608]{0:T(1024)S(1)}, u32[]{:S(2)}, u32[]{:S(2)}) collective-permute-start(f32[4608]{0:T(1024)S(1)} %add.131), channel_id=1, source_target_pairs={{0,16},{8,24},{16,0},{24,8},{1,17},{9,25},{17,1},{25,9},{2,18},{10... | collective-permute-start | bytes 55304 | tf_op jit(solution)/shard_map/ppermute | solution.py:151
  37.1 2.3 %collective-permute-done.8 = f32[4608]{0:T(1024)S(1)} collective-permute-done((f32[4608]{0:T(1024)S(1)}, f32[4608]{0:T(1024)S(1)}, u32[]{:S(2)}, u32[]{:S(2)}) %collective-permute-start.8) | collective-permute-done | bytes 18464 | tf_op jit(solution)/shard_map/ppermute | solution.py:151
  39.4 0.7 %reshape.96.packed_ref = f32[2,48,48]{2,1,0:T(8,128)} reshape(f32[4608]{0:T(1024)S(1)} %add.132) | data formatting | bytes 36864 | tf_op jit(solution)/shard_map/reshape | solution.py:316
  40.1 6.7 %shard_map.68 = (f32[72,8,128]{2,1,0:T(8,128)}, f32[36,2,36]{2,1,0:T(2,128)}) custom-call(f32[2,48,48]{2,1,0:T(8,128)} %reshape.96.packed_ref, f32[96,8,128]{2,1,0:T(8,128)} %bitcast.34), custom_call_target="tpu_custom_call" | custom-call | tf_op jit(solution)/shard_map/pallas_call | solution.py:249
  (73 shorter events, 2.9 us)
Async XLA Ops:
  0.6 6.3 %copy-start.2 = (f32[2,12,8,128]{3,2,1,0:T(8,128)S(1)}, f32[2,12,8,128]{3,2,1,0:T(8,128)}, u32[]{:S(2)}) copy-start(f32[2,12,8,128]{3,2,1,0:T(8,128)} %param.5) | copy-start | bytes 294916
  0.6 6.3 %copy-start.1 = (f32[2,12,8,128]{3,2,1,0:T(8,128)S(1)}, f32[2,12,8,128]{3,2,1,0:T(8,128)}, u32[]{:S(2)}) copy-start(f32[2,12,8,128]{3,2,1,0:T(8,128)} %param.6) | copy-start | bytes 294916
  0.7 6.3 %copy-start.4 = (f32[8]{0:T(128)S(1)}, f32[8]{0:T(128)}, u32[]{:S(2)}) copy-start(f32[8]{0:T(128)} %param.8) | copy-start | bytes 100
  0.7 6.3 %copy-start.3 = (s32[2]{0:T(128)S(1)}, s32[2]{0:T(128)}, u32[]{:S(2)}) copy-start(s32[2]{0:T(128)} %param.9) | copy-start | bytes 28
  3.7 4.9 %collective-permute-start.1 = (f32[12544]{0:T(1024)S(1)}, f32[12544]{0:T(1024)S(1)}, u32[]{:S(2)}, u32[]{:S(2)}) collective-permute-start(f32[12544]{0:T(1024)S(1)} %select_n.100), channel_id=1, source_target_pairs={{0,8},{8,0},{16,24},{24,16},{1,9},{9,1},{17,25},{25,17},{2,10},{10... | collective-permute-start | bytes 150536 | tf_op jit(solution)/shard_map/ppermute | solution.py:119
  4.2 4.9 %collective-permute-start = (f32[12544]{0:T(1024)S(1)}, f32[12544]{0:T(1024)S(1)}, u32[]{:S(2)}, u32[]{:S(2)}) collective-permute-start(f32[12544]{0:T(1024)S(1)} %select_n.98), channel_id=1, source_target_pairs={{0,24},{8,16},{16,8},{24,0},{1,25},{9,17},{17,9},{25,1},{2,26},{10... | collective-permute-start | bytes 150536 | tf_op jit(solution)/shard_map/ppermute | solution.py:122
  9.9 5.9 %collective-permute-start.3 = (f32[1176]{0:T(1024)S(1)}, f32[1176]{0:T(1024)S(1)}, u32[]{:S(2)}, u32[]{:S(2)}) collective-permute-start(f32[1176]{0:T(1024)S(1)} %reshape.89), channel_id=1, source_target_pairs={{0,1},{1,0},{2,3},{3,2},{4,5},{5,4},{6,7},{7,6},{8,9},{9,8},{10,11... | collective-permute-start | bytes 14120 | tf_op jit(solution)/shard_map/ppermute | solution.py:119
  11.3 6.3 %collective-permute-start.2 = (f32[1176]{0:T(1024)S(1)}, f32[1176]{0:T(1024)S(1)}, u32[]{:S(2)}, u32[]{:S(2)}) collective-permute-start(f32[1176]{0:T(1024)S(1)} %reshape.88), channel_id=1, source_target_pairs={{0,7},{1,2},{2,1},{3,4},{4,3},{5,6},{6,5},{7,0},{8,15},{9,10},{10,... | collective-permute-start | bytes 14120 | tf_op jit(solution)/shard_map/ppermute | solution.py:122
  20.8 19.3 %copy-start = (f32[2,48,8,128]{3,2,1,0:T(8,128)}, f32[2,48,8,128]{3,2,1,0:T(8,128)S(1)}, u32[]{:S(2)}) copy-start(f32[2,48,8,128]{3,2,1,0:T(8,128)S(1)} %pad_maximum_fusion.7) | copy-start | bytes 1179652
  22.1 3.8 %collective-permute-start.4 = (f32[4608]{0:T(1024)S(1)}, f32[4608]{0:T(1024)S(1)}, u32[]{:S(2)}, u32[]{:S(2)}) collective-permute-start(f32[4608]{0:T(1024)S(1)} %reshape.95), channel_id=1, source_target_pairs={{0,1},{1,0},{2,3},{3,2},{4,5},{5,4},{6,7},{7,6},{8,9},{9,8},{10,11... | collective-permute-start | bytes 55304 | tf_op jit(solution)/shard_map/ppermute | solution.py:151
  25.9 3.8 %collective-permute-start.5 = (f32[4608]{0:T(1024)S(1)}, f32[4608]{0:T(1024)S(1)}, u32[]{:S(2)}, u32[]{:S(2)}) collective-permute-start(f32[4608]{0:T(1024)S(1)} %add.128), channel_id=1, source_target_pairs={{0,2},{1,3},{2,0},{3,1},{4,6},{5,7},{6,4},{7,5},{8,10},{9,11},{10,... | collective-permute-start | bytes 55304 | tf_op jit(solution)/shard_map/ppermute | solution.py:151
  29.7 4.7 %collective-permute-start.6 = (f32[4608]{0:T(1024)S(1)}, f32[4608]{0:T(1024)S(1)}, u32[]{:S(2)}, u32[]{:S(2)}) collective-permute-start(f32[4608]{0:T(1024)S(1)} %add.129), channel_id=1, source_target_pairs={{0,4},{1,5},{2,6},{3,7},{4,0},{5,1},{6,2},{7,3},{8,12},{9,13},{10,... | collective-permute-start | bytes 55304 | tf_op jit(solution)/shard_map/ppermute | solution.py:151
  34.4 1.2 %collective-permute-start.7 = (f32[4608]{0:T(1024)S(1)}, f32[4608]{0:T(1024)S(1)}, u32[]{:S(2)}, u32[]{:S(2)}) collective-permute-start(f32[4608]{0:T(1024)S(1)} %add.130), channel_id=1, source_target_pairs={{0,8},{8,0},{16,24},{24,16},{1,9},{9,1},{17,25},{25,17},{2,10},{10... | collective-permute-start | bytes 55304 | tf_op jit(solution)/shard_map/ppermute | solution.py:151
  35.6 3.8 %collective-permute-start.8 = (f32[4608]{0:T(1024)S(1)}, f32[4608]{0:T(1024)S(1)}, u32[]{:S(2)}, u32[]{:S(2)}) collective-permute-start(f32[4608]{0:T(1024)S(1)} %add.131), channel_id=1, source_target_pairs={{0,16},{8,24},{16,0},{24,8},{1,17},{9,25},{17,1},{25,9},{2,18},{10... | collective-permute-start | bytes 55304 | tf_op jit(solution)/shard_map/ppermute | solution.py:151

commit v18 on v15

--- a/solution.py
+++ b/solution.py
@@ -204,9 +204,7 @@
     ham_re, ham_im = unpack(work_ref[1])
     band_diag = eye & (rows < band_count)
     quotient = jnp.where(band_diag, ham_re, 0.0) / jnp.where(band_diag, gram_re, 1.0)
-    to_row = ((rows == cols + 2 * band_count) & (cols < band_count)).astype(jnp.float32)
-    to_col = ((cols == rows + band_count) & (rows < band_count)).astype(jnp.float32)
-    shifted = dot(dot(to_row, quotient), to_col)
+    shifted = pltpu.roll(pltpu.roll(quotient, 2 * band_count, 0), band_count, 1)
     kept = (eye & (cols < 2 * band_count)) | (
         (rows == cols + band_count) & (cols >= 2 * band_count) & (cols < raw)
     )
@@ -229,13 +227,16 @@
     red_ref[:, 0, :] = work_ref[1, :raw, :raw]
     red_ref[:, 1, :] = work_ref[1, half : half + raw, :raw]
     rotation = jnp.where(corner | ~((rows < half) | (cols < half)), rotation, -rotation)
-    pick_rows = ((rows < ext) & (cols == rows)) | (
-        (rows >= ext) & (rows < 2 * ext) & (cols == rows - ext + half)
-    )
-    pick_cols = ((rows < raw) & (cols == rows)) | (
-        (rows >= half) & (rows < half + raw) & (cols == rows - half + raw)
-    )
-    packed_rotation = dot(pick_rows.astype(jnp.float32), dot(rotation, pick_cols.astype(jnp.float32)))
+    packed_rotation = jnp.where(
+        cols < raw,
+        rotation,
+        jnp.where(cols < 2 * raw, pltpu.roll(rotation, size - half + raw, 1), 0.0),
+    )
+    packed_rotation = jnp.where(
+        rows < ext,
+        packed_rotation,
+        jnp.where(rows < 2 * ext, pltpu.roll(packed_rotation, size - half + ext, 0), 0.0),
+    )
     work_ref[0] = scale * packed_rotation.T
     rotation_t = work_ref[0, : 2 * raw, : 2 * ext]
     for row in range(field_ref.shape[1]):

time: 47 us -> 46.4 us (0.987)
  Pallas kernels: 6.68 us -> 6.05 us
    pallas_call x1, Pallas kernels: 6.68 us -> 6.05 us  [matrix_stage(): pl.pallas_call(functools.partial(matrix_kernel, band_count=band_count, sc...]
where the time goes in v18:
time: 46.4 us; the launch traced here: 46.2 us
  waiting for transfers between devices  17.1 us (37%)
  starting transfers between devices  10.7 us (23%)
  Pallas kernels  6.05 us (13%)
  local copies, waits for them, and re-layouts  4.92 us (11%)
  other arithmetic  3.5 us (8%)
  between operations  2.99 us (6%)
  matrix products  0.95 us (2%)
    ppermute x5, waiting for transfers between devices, tree_sum(): lax.ppermute(value, axis, [(i, i ^ step) for i in range(count)])  14.7 us
    ppermute x2, starting transfers between devices, exchange_rim(): lax.ppermute(jnp.where(even, head, tail).reshape(-1), axis, [(i, (i + 1)...  6.27 us
    pallas_call x1, Pallas kernels, matrix_stage(): pl.pallas_call(functools.partial(matrix_kernel, band_count=band_count, sc...  6.05 us
    ppermute x5, starting transfers between devices, tree_sum(): lax.ppermute(value, axis, [(i, i ^ step) for i in range(count)])  2.56 us
    ppermute x2, waiting for transfers between devices, exchange_rim(): lax.ppermute(jnp.where(even, head, tail).reshape(-1), axis, [(i, (i + 1)...  2.36 us
    ppermute x2, starting transfers between devices, exchange_rim(): lax.ppermute(jnp.where(even, tail, head).reshape(-1), axis, [(i, i ^ 1) f...  1.83 us
    slice x1, local copies, waits for them, and re-layouts, strip_of(): directions[:, :, start:stop]  0.99 us
    slice x1, local copies, waits for them, and re-layouts, strip_of(): bands[:, :, start:stop]  0.99 us
  transfers between devices with their start and end apart: 9, of which 7 were waited for; matrix products, arithmetic and copies ran while one was open for 1% of the time, Pallas kernels for 0%

profile of v18, /device:TPU:0, one launch (start us, length us, event | category | flops | bytes accessed | tf_op | source)
XLA Modules:
  0.0 46.2 jit_solution(3518775915059453189)
XLA Ops:
  0.7 0.8 %convert_bitcast_fusion = (f32[1,8,128]{2,1,0:T(8,128)S(1)}, f32[8,128]{1,0:T(8,128)S(1)}) fusion(s32[8,128]{1,0:T(8,128)} %param.7), kind=kLoop, calls=%fused_computation.87 | loop fusion | flops 1024 | bytes 12288 | tf_op jit(solution)/shard_map/broadcast_in_dim | solution.py:289
  1.5 1.0 %fusion.33 = (f32[2,12,2,128]{3,2,1,0:T(2,128)S(1)}, f32[2,12,2,128]{3,2,1,0:T(2,128)S(1)}) fusion(f32[2,12,8,128]{3,2,1,0:T(8,128)} %param.5), kind=kLoop, calls=%fused_computation.88 | loop fusion | bytes 98304 | tf_op jit(solution)/shard_map/slice | solution.py:280
  2.5 1.0 %fusion.34 = (f32[2,12,2,128]{3,2,1,0:T(2,128)S(1)}, f32[2,12,2,128]{3,2,1,0:T(2,128)S(1)}) fusion(f32[2,12,8,128]{3,2,1,0:T(8,128)} %param.6), kind=kLoop, calls=%fused_computation.89 | loop fusion | bytes 98304 | tf_op jit(solution)/shard_map/slice | solution.py:280
  3.7 0.5 %collective-permute-start.1 = (f32[12544]{0:T(1024)S(1)}, f32[12544]{0:T(1024)S(1)}, u32[]{:S(2)}, u32[]{:S(2)}) collective-permute-start(f32[12544]{0:T(1024)S(1)} %select_n.100), channel_id=1, source_target_pairs={{0,8},{8,0},{16,24},{24,16},{1,9},{9,1},{17,25},{25,17},{2,10},{10... | collective-permute-start | bytes 150536 | tf_op jit(solution)/shard_map/ppermute | solution.py:119
  4.2 2.7 %collective-permute-start = (f32[12544]{0:T(1024)S(1)}, f32[12544]{0:T(1024)S(1)}, u32[]{:S(2)}, u32[]{:S(2)}) collective-permute-start(f32[12544]{0:T(1024)S(1)} %select_n.98), channel_id=1, source_target_pairs={{0,24},{8,16},{16,8},{24,0},{1,25},{9,17},{17,9},{25,1},{2,26},{10... | collective-permute-start | bytes 150536 | tf_op jit(solution)/shard_map/ppermute | solution.py:122
  7.0 0.6 %fusion.36 = (s32[1]{0:T(128)}, s32[1]{0:T(128)}) fusion(s32[2]{0:T(128)S(1)} %copy-done.3), kind=kLoop, calls=%fused_computation.91 | loop fusion | bytes 16 | tf_op jit(solution)/shard_map/slice | solution.py:286
  8.6 0.6 %collective-permute-done = f32[12544]{0:T(1024)S(1)} collective-permute-done((f32[12544]{0:T(1024)S(1)}, f32[12544]{0:T(1024)S(1)}, u32[]{:S(2)}, u32[]{:S(2)}) %collective-permute-start) | collective-permute-done | bytes 50208 | tf_op jit(solution)/shard_map/ppermute | solution.py:122
  9.9 1.3 %collective-permute-start.3 = (f32[1176]{0:T(1024)S(1)}, f32[1176]{0:T(1024)S(1)}, u32[]{:S(2)}, u32[]{:S(2)}) collective-permute-start(f32[1176]{0:T(1024)S(1)} %reshape.89), channel_id=1, source_target_pairs={{0,1},{1,0},{2,3},{3,2},{4,5},{5,4},{6,7},{7,6},{8,9},{9,8},{10,11... | collective-permute-start | bytes 14120 | tf_op jit(solution)/shard_map/ppermute | solution.py:119
  11.3 3.6 %collective-permute-start.2 = (f32[1176]{0:T(1024)S(1)}, f32[1176]{0:T(1024)S(1)}, u32[]{:S(2)}, u32[]{:S(2)}) collective-permute-start(f32[1176]{0:T(1024)S(1)} %reshape.88), channel_id=1, source_target_pairs={{0,7},{1,2},{2,1},{3,4},{4,3},{5,6},{6,5},{7,0},{8,15},{9,10},{10,... | collective-permute-start | bytes 14120 | tf_op jit(solution)/shard_map/ppermute | solution.py:122
  15.8 1.8 %collective-permute-done.2 = f32[1176]{0:T(1024)S(1)} collective-permute-done((f32[1176]{0:T(1024)S(1)}, f32[1176]{0:T(1024)S(1)}, u32[]{:S(2)}, u32[]{:S(2)}) %collective-permute-start.2) | collective-permute-done | bytes 4736 | tf_op jit(solution)/shard_map/ppermute | solution.py:122
  18.4 0.6 %pad_maximum_fusion.1 = f32[48,12,132]{2,1,0:T(8,128)S(1)} fusion(f32[49,12,2]{2,1,0:T(8,128)S(1)} %reshape.91, f32[49,12,2]{2,1,0:T(8,128)S(1)} %reshape.90, f32[49,2,128]{2,1,0:T(2,128)S(1)} %reshape.87, f32[49,2,128]{2,1,0:T(2,128)S(1)} %reshape.85, f32[1,8,128]{2,1,0:T(8,128)S(1)} %get-tuple-element.40, f32[48,8,128]{2,1,0:T(8,128)S(1)} %bitcast.37), kind=kLoop, calls=%fused_computation.3 | loop fusion | flops 380160 | bytes 614592 | tf_op jit(solution)/shard_map/concatenate | solution.py:135
  19.3 0.6 %broadcast_divide_fusion = (f32[2,12,10,130]{3,2,1,0:T(8,128)S(1)}, f32[2,12,10,130]{3,2,1,0:T(8,128)S(1)}, f32[2,12,10,130]{3,2,1,0:T(8,128)S(1)}, f32[2,12,10,130]{3,2,1,0:T(8,128)S(1)}) fusion(f32[10,130]{1,0:T(8,128)S(1)} %get-tuple-element.13, f32[2,24,12,132]{3,2,1,0:T(8,128)S(1)} %bitcast.31, f32[10,130]{1,0:T(8,128)S(1)} %get-tuple-element.17, ...), kind=kLoop, calls=%fused_computation.34 | loop fusion | flops 343200 | bytes 1274000 | tf_op jit(solution)/shard_map/div | solution.py:302
  20.3 0.4 fusion.7
  20.9 0.5 %convolution_bitcast_fusion.1 = f32[96,96]{1,0:T(8,128)S(1)} fusion(f32[96,8,128]{2,1,0:T(8,128)S(1)} %bitcast.32), kind=kOutput, calls=%fused_computation.2 | convolution fusion | flops 113246208 | bytes 430080 | tf_op jit(solution)/shard_map/jrc,krc->jk/dot_general | solution.py:44
  21.3 0.5 %convolution_bitcast_fusion = f32[96,96]{1,0:T(8,128)S(1)} fusion(f32[96,8,128]{2,0,1:T(8,128)S(1)} %bitcast.38, f32[96,8,128]{2,1,0:T(8,128)S(1)} %bitcast.33), kind=kOutput, calls=%fused_computation.1 | convolution fusion | flops 113246208 | bytes 823296 | tf_op jit(solution)/shard_map/jrc,krc->jk/dot_general | solution.py:44
  22.2 1.2 %collective-permute-done.4 = f32[4608]{0:T(1024)S(1)} collective-permute-done((f32[4608]{0:T(1024)S(1)}, f32[4608]{0:T(1024)S(1)}, u32[]{:S(2)}, u32[]{:S(2)}) %collective-permute-start.4) | collective-permute-done | bytes 18464 | tf_op jit(solution)/shard_map/ppermute | solution.py:151
  23.3 1.5 %collective-permute-start.5 = (f32[4608]{0:T(1024)S(1)}, f32[4608]{0:T(1024)S(1)}, u32[]{:S(2)}, u32[]{:S(2)}) collective-permute-start(f32[4608]{0:T(1024)S(1)} %add.128), channel_id=1, source_target_pairs={{0,16},{8,24},{16,0},{24,8},{1,17},{9,25},{17,1},{25,9},{2,18},{10... | collective-permute-start | bytes 55304 | tf_op jit(solution)/shard_map/ppermute | solution.py:151
  24.9 2.3 %collective-permute-done.5 = f32[4608]{0:T(1024)S(1)} collective-permute-done((f32[4608]{0:T(1024)S(1)}, f32[4608]{0:T(1024)S(1)}, u32[]{:S(2)}, u32[]{:S(2)}) %collective-permute-start.5) | collective-permute-done | bytes 18464 | tf_op jit(solution)/shard_map/ppermute | solution.py:151
  27.1 3.8 %collective-permute-done.6 = f32[4608]{0:T(1024)S(1)} collective-permute-done((f32[4608]{0:T(1024)S(1)}, f32[4608]{0:T(1024)S(1)}, u32[]{:S(2)}, u32[]{:S(2)}) %collective-permute-start.6) | collective-permute-done | bytes 18464 | tf_op jit(solution)/shard_map/ppermute | solution.py:151
  30.9 3.8 %collective-permute-done.7 = f32[4608]{0:T(1024)S(1)} collective-permute-done((f32[4608]{0:T(1024)S(1)}, f32[4608]{0:T(1024)S(1)}, u32[]{:S(2)}, u32[]{:S(2)}) %collective-permute-start.7) | collective-permute-done | bytes 18464 | tf_op jit(solution)/shard_map/ppermute | solution.py:151
  34.7 1.0 %collective-permute-start.8 = (f32[4608]{0:T(1024)S(1)}, f32[4608]{0:T(1024)S(1)}, u32[]{:S(2)}, u32[]{:S(2)}) collective-permute-start(f32[4608]{0:T(1024)S(1)} %add.131), channel_id=1, source_target_pairs={{0,4},{1,5},{2,6},{3,7},{4,0},{5,1},{6,2},{7,3},{8,12},{9,13},{10,... | collective-permute-start | bytes 55304 | tf_op jit(solution)/shard_map/ppermute | solution.py:151
  35.7 3.7 %collective-permute-done.8 = f32[4608]{0:T(1024)S(1)} collective-permute-done((f32[4608]{0:T(1024)S(1)}, f32[4608]{0:T(1024)S(1)}, u32[]{:S(2)}, u32[]{:S(2)}) %collective-permute-start.8) | collective-permute-done | bytes 18464 | tf_op jit(solution)/shard_map/ppermute | solution.py:151
  39.4 0.7 %reshape.96.packed_ref = f32[2,48,48]{2,1,0:T(8,128)} reshape(f32[4608]{0:T(1024)S(1)} %add.132) | data formatting | bytes 36864 | tf_op jit(solution)/shard_map/reshape | solution.py:317
  40.1 6.0 %shard_map.68 = (f32[72,8,128]{2,1,0:T(8,128)}, f32[36,2,36]{2,1,0:T(2,128)}) custom-call(f32[2,48,48]{2,1,0:T(8,128)} %reshape.96.packed_ref, f32[96,8,128]{2,1,0:T(8,128)} %bitcast.34), custom_call_target="tpu_custom_call" | custom-call | tf_op jit(solution)/shard_map/pallas_call | solution.py:250
  (73 shorter events, 2.9 us)
Async XLA Ops:
  0.6 6.3 %copy-start.2 = (f32[2,12,8,128]{3,2,1,0:T(8,128)S(1)}, f32[2,12,8,128]{3,2,1,0:T(8,128)}, u32[]{:S(2)}) copy-start(f32[2,12,8,128]{3,2,1,0:T(8,128)} %param.5) | copy-start | bytes 294916
  0.6 6.3 %copy-start.1 = (f32[2,12,8,128]{3,2,1,0:T(8,128)S(1)}, f32[2,12,8,128]{3,2,1,0:T(8,128)}, u32[]{:S(2)}) copy-start(f32[2,12,8,128]{3,2,1,0:T(8,128)} %param.6) | copy-start | bytes 294916
  0.7 6.3 %copy-start.4 = (f32[8]{0:T(128)S(1)}, f32[8]{0:T(128)}, u32[]{:S(2)}) copy-start(f32[8]{0:T(128)} %param.8) | copy-start | bytes 100
  0.7 6.3 %copy-start.3 = (s32[2]{0:T(128)S(1)}, s32[2]{0:T(128)}, u32[]{:S(2)}) copy-start(s32[2]{0:T(128)} %param.9) | copy-start | bytes 28
  3.7 4.9 %collective-permute-start.1 = (f32[12544]{0:T(1024)S(1)}, f32[12544]{0:T(1024)S(1)}, u32[]{:S(2)}, u32[]{:S(2)}) collective-permute-start(f32[12544]{0:T(1024)S(1)} %select_n.100), channel_id=1, source_target_pairs={{0,8},{8,0},{16,24},{24,16},{1,9},{9,1},{17,25},{25,17},{2,10},{10... | collective-permute-start | bytes 150536 | tf_op jit(solution)/shard_map/ppermute | solution.py:119
  4.2 4.9 %collective-permute-start = (f32[12544]{0:T(1024)S(1)}, f32[12544]{0:T(1024)S(1)}, u32[]{:S(2)}, u32[]{:S(2)}) collective-permute-start(f32[12544]{0:T(1024)S(1)} %select_n.98), channel_id=1, source_target_pairs={{0,24},{8,16},{16,8},{24,0},{1,25},{9,17},{17,9},{25,1},{2,26},{10... | collective-permute-start | bytes 150536 | tf_op jit(solution)/shard_map/ppermute | solution.py:122
  9.9 5.9 %collective-permute-start.3 = (f32[1176]{0:T(1024)S(1)}, f32[1176]{0:T(1024)S(1)}, u32[]{:S(2)}, u32[]{:S(2)}) collective-permute-start(f32[1176]{0:T(1024)S(1)} %reshape.89), channel_id=1, source_target_pairs={{0,1},{1,0},{2,3},{3,2},{4,5},{5,4},{6,7},{7,6},{8,9},{9,8},{10,11... | collective-permute-start | bytes 14120 | tf_op jit(solution)/shard_map/ppermute | solution.py:119
  11.3 6.3 %collective-permute-start.2 = (f32[1176]{0:T(1024)S(1)}, f32[1176]{0:T(1024)S(1)}, u32[]{:S(2)}, u32[]{:S(2)}) collective-permute-start(f32[1176]{0:T(1024)S(1)} %reshape.88), channel_id=1, source_target_pairs={{0,7},{1,2},{2,1},{3,4},{4,3},{5,6},{6,5},{7,0},{8,15},{9,10},{10,... | collective-permute-start | bytes 14120 | tf_op jit(solution)/shard_map/ppermute | solution.py:122
  20.8 19.3 %copy-start = (f32[2,48,8,128]{3,2,1,0:T(8,128)}, f32[2,48,8,128]{3,2,1,0:T(8,128)S(1)}, u32[]{:S(2)}) copy-start(f32[2,48,8,128]{3,2,1,0:T(8,128)S(1)} %pad_maximum_fusion.7) | copy-start | bytes 1179652
  22.1 1.3 %collective-permute-start.4 = (f32[4608]{0:T(1024)S(1)}, f32[4608]{0:T(1024)S(1)}, u32[]{:S(2)}, u32[]{:S(2)}) collective-permute-start(f32[4608]{0:T(1024)S(1)} %reshape.95), channel_id=1, source_target_pairs={{0,8},{8,0},{16,24},{24,16},{1,9},{9,1},{17,25},{25,17},{2,10},{10... | collective-permute-start | bytes 55304 | tf_op jit(solution)/shard_map/ppermute | solution.py:151
  23.3 3.8 %collective-permute-start.5 = (f32[4608]{0:T(1024)S(1)}, f32[4608]{0:T(1024)S(1)}, u32[]{:S(2)}, u32[]{:S(2)}) collective-permute-start(f32[4608]{0:T(1024)S(1)} %add.128), channel_id=1, source_target_pairs={{0,16},{8,24},{16,0},{24,8},{1,17},{9,25},{17,1},{25,9},{2,18},{10... | collective-permute-start | bytes 55304 | tf_op jit(solution)/shard_map/ppermute | solution.py:151
  27.1 3.8 %collective-permute-start.6 = (f32[4608]{0:T(1024)S(1)}, f32[4608]{0:T(1024)S(1)}, u32[]{:S(2)}, u32[]{:S(2)}) collective-permute-start(f32[4608]{0:T(1024)S(1)} %add.129), channel_id=1, source_target_pairs={{0,1},{1,0},{2,3},{3,2},{4,5},{5,4},{6,7},{7,6},{8,9},{9,8},{10,11... | collective-permute-start | bytes 55304 | tf_op jit(solution)/shard_map/ppermute | solution.py:151
  30.9 3.8 %collective-permute-start.7 = (f32[4608]{0:T(1024)S(1)}, f32[4608]{0:T(1024)S(1)}, u32[]{:S(2)}, u32[]{:S(2)}) collective-permute-start(f32[4608]{0:T(1024)S(1)} %add.130), channel_id=1, source_target_pairs={{0,2},{1,3},{2,0},{3,1},{4,6},{5,7},{6,4},{7,5},{8,10},{9,11},{10,... | collective-permute-start | bytes 55304 | tf_op jit(solution)/shard_map/ppermute | solution.py:151
  34.7 4.7 %collective-permute-start.8 = (f32[4608]{0:T(1024)S(1)}, f32[4608]{0:T(1024)S(1)}, u32[]{:S(2)}, u32[]{:S(2)}) collective-permute-start(f32[4608]{0:T(1024)S(1)} %add.131), channel_id=1, source_target_pairs={{0,4},{1,5},{2,6},{3,7},{4,0},{5,1},{6,2},{7,3},{8,12},{9,13},{10,... | collective-permute-start | bytes 55304 | tf_op jit(solution)/shard_map/ppermute | solution.py:151

commit v19 on v18

--- a/solution.py
+++ b/solution.py
@@ -217,9 +217,13 @@
     magnitude = jnp.sqrt(total)
     current = embedded / magnitude
     inverse = identity
-    for _ in range(NS_STEPS):
-        factor = 1.5 * identity - 0.5 * dot(inverse, current)
-        current, inverse = dot(current, factor), dot(factor, inverse)
+    for step in range(NS_STEPS):
+        if step == 0:
+            factor = 1.5 * identity - 0.5 * current
+            current, inverse = dot(current, factor), factor
+        else:
+            factor = 1.5 * identity - 0.5 * dot(inverse, current)
+            current, inverse = dot(current, factor), dot(factor, inverse)
     root = inverse / jnp.sqrt(magnitude)
     root = embed(jnp.where(corner, root, 0.0), jnp.where(corner, spread(root, 0), 0.0))
     rotation = dot(mixing, root)

time: 46.4 us -> 46.2 us (level)
  no operation moved by 1% of the time
where the time goes in v19:
time: 46.2 us; the launch traced here: 45.9 us
  waiting for transfers between devices  17.1 us (37%)
  starting transfers between devices  10.7 us (23%)
  Pallas kernels  5.82 us (13%)
  local copies, waits for them, and re-layouts  4.92 us (11%)
  other arithmetic  3.5 us (8%)
  between operations  2.99 us (6%)
  matrix products  0.95 us (2%)
    ppermute x5, waiting for transfers between devices, tree_sum(): lax.ppermute(value, axis, [(i, i ^ step) for i in range(count)])  14.7 us
    ppermute x2, starting transfers between devices, exchange_rim(): lax.ppermute(jnp.where(even, head, tail).reshape(-1), axis, [(i, (i + 1)...  6.27 us
    pallas_call x1, Pallas kernels, matrix_stage(): pl.pallas_call(functools.partial(matrix_kernel, band_count=band_count, sc...  5.82 us
    ppermute x5, starting transfers between devices, tree_sum(): lax.ppermute(value, axis, [(i, i ^ step) for i in range(count)])  2.56 us
    ppermute x2, waiting for transfers between devices, exchange_rim(): lax.ppermute(jnp.where(even, head, tail).reshape(-1), axis, [(i, (i + 1)...  2.36 us
    ppermute x2, starting transfers between devices, exchange_rim(): lax.ppermute(jnp.where(even, tail, head).reshape(-1), axis, [(i, i ^ 1) f...  1.83 us
    slice x1, local copies, waits for them, and re-layouts, strip_of(): directions[:, :, start:stop]  0.99 us
    slice x1, local copies, waits for them, and re-layouts, strip_of(): bands[:, :, start:stop]  0.99 us
  transfers between devices with their start and end apart: 9, of which 7 were waited for; matrix products, arithmetic and copies ran while one was open for 1% of the time, Pallas kernels for 0%

profile of v19, /device:TPU:0, one launch (start us, length us, event | category | flops | bytes accessed | tf_op | source)
XLA Modules:
  0.0 45.9 jit_solution(16202878820532365839)
XLA Ops:
  0.7 0.8 %convert_bitcast_fusion = (f32[1,8,128]{2,1,0:T(8,128)S(1)}, f32[8,128]{1,0:T(8,128)S(1)}) fusion(s32[8,128]{1,0:T(8,128)} %param.7), kind=kLoop, calls=%fused_computation.87 | loop fusion | flops 1024 | bytes 12288 | tf_op jit(solution)/shard_map/broadcast_in_dim | solution.py:293
  1.5 1.0 %fusion.33 = (f32[2,12,2,128]{3,2,1,0:T(2,128)S(1)}, f32[2,12,2,128]{3,2,1,0:T(2,128)S(1)}) fusion(f32[2,12,8,128]{3,2,1,0:T(8,128)} %param.5), kind=kLoop, calls=%fused_computation.88 | loop fusion | bytes 98304 | tf_op jit(solution)/shard_map/slice | solution.py:284
  2.5 1.0 %fusion.34 = (f32[2,12,2,128]{3,2,1,0:T(2,128)S(1)}, f32[2,12,2,128]{3,2,1,0:T(2,128)S(1)}) fusion(f32[2,12,8,128]{3,2,1,0:T(8,128)} %param.6), kind=kLoop, calls=%fused_computation.89 | loop fusion | bytes 98304 | tf_op jit(solution)/shard_map/slice | solution.py:284
  3.7 0.5 %collective-permute-start.1 = (f32[12544]{0:T(1024)S(1)}, f32[12544]{0:T(1024)S(1)}, u32[]{:S(2)}, u32[]{:S(2)}) collective-permute-start(f32[12544]{0:T(1024)S(1)} %select_n.100), channel_id=1, source_target_pairs={{0,8},{8,0},{16,24},{24,16},{1,9},{9,1},{17,25},{25,17},{2,10},{10... | collective-permute-start | bytes 150536 | tf_op jit(solution)/shard_map/ppermute | solution.py:119
  4.2 2.7 %collective-permute-start = (f32[12544]{0:T(1024)S(1)}, f32[12544]{0:T(1024)S(1)}, u32[]{:S(2)}, u32[]{:S(2)}) collective-permute-start(f32[12544]{0:T(1024)S(1)} %select_n.98), channel_id=1, source_target_pairs={{0,24},{8,16},{16,8},{24,0},{1,25},{9,17},{17,9},{25,1},{2,26},{10... | collective-permute-start | bytes 150536 | tf_op jit(solution)/shard_map/ppermute | solution.py:122
  7.0 0.6 %fusion.36 = (s32[1]{0:T(128)}, s32[1]{0:T(128)}) fusion(s32[2]{0:T(128)S(1)} %copy-done.3), kind=kLoop, calls=%fused_computation.91 | loop fusion | bytes 16 | tf_op jit(solution)/shard_map/slice | solution.py:290
  8.6 0.6 %collective-permute-done = f32[12544]{0:T(1024)S(1)} collective-permute-done((f32[12544]{0:T(1024)S(1)}, f32[12544]{0:T(1024)S(1)}, u32[]{:S(2)}, u32[]{:S(2)}) %collective-permute-start) | collective-permute-done | bytes 50208 | tf_op jit(solution)/shard_map/ppermute | solution.py:122
  9.9 1.3 %collective-permute-start.3 = (f32[1176]{0:T(1024)S(1)}, f32[1176]{0:T(1024)S(1)}, u32[]{:S(2)}, u32[]{:S(2)}) collective-permute-start(f32[1176]{0:T(1024)S(1)} %reshape.89), channel_id=1, source_target_pairs={{0,1},{1,0},{2,3},{3,2},{4,5},{5,4},{6,7},{7,6},{8,9},{9,8},{10,11... | collective-permute-start | bytes 14120 | tf_op jit(solution)/shard_map/ppermute | solution.py:119
  11.3 3.6 %collective-permute-start.2 = (f32[1176]{0:T(1024)S(1)}, f32[1176]{0:T(1024)S(1)}, u32[]{:S(2)}, u32[]{:S(2)}) collective-permute-start(f32[1176]{0:T(1024)S(1)} %reshape.88), channel_id=1, source_target_pairs={{0,7},{1,2},{2,1},{3,4},{4,3},{5,6},{6,5},{7,0},{8,15},{9,10},{10,... | collective-permute-start | bytes 14120 | tf_op jit(solution)/shard_map/ppermute | solution.py:122
  15.8 1.8 %collective-permute-done.2 = f32[1176]{0:T(1024)S(1)} collective-permute-done((f32[1176]{0:T(1024)S(1)}, f32[1176]{0:T(1024)S(1)}, u32[]{:S(2)}, u32[]{:S(2)}) %collective-permute-start.2) | collective-permute-done | bytes 4736 | tf_op jit(solution)/shard_map/ppermute | solution.py:122
  18.4 0.6 %pad_maximum_fusion.1 = f32[48,12,132]{2,1,0:T(8,128)S(1)} fusion(f32[49,12,2]{2,1,0:T(8,128)S(1)} %reshape.91, f32[49,12,2]{2,1,0:T(8,128)S(1)} %reshape.90, f32[49,2,128]{2,1,0:T(2,128)S(1)} %reshape.87, f32[49,2,128]{2,1,0:T(2,128)S(1)} %reshape.85, f32[1,8,128]{2,1,0:T(8,128)S(1)} %get-tuple-element.40, f32[48,8,128]{2,1,0:T(8,128)S(1)} %bitcast.37), kind=kLoop, calls=%fused_computation.3 | loop fusion | flops 380160 | bytes 614592 | tf_op jit(solution)/shard_map/concatenate | solution.py:135
  19.3 0.6 %broadcast_divide_fusion = (f32[2,12,10,130]{3,2,1,0:T(8,128)S(1)}, f32[2,12,10,130]{3,2,1,0:T(8,128)S(1)}, f32[2,12,10,130]{3,2,1,0:T(8,128)S(1)}, f32[2,12,10,130]{3,2,1,0:T(8,128)S(1)}) fusion(f32[10,130]{1,0:T(8,128)S(1)} %get-tuple-element.13, f32[2,24,12,132]{3,2,1,0:T(8,128)S(1)} %bitcast.31, f32[10,130]{1,0:T(8,128)S(1)} %get-tuple-element.17, ...), kind=kLoop, calls=%fused_computation.34 | loop fusion | flops 343200 | bytes 1274000 | tf_op jit(solution)/shard_map/div | solution.py:306
  20.3 0.4 fusion.7
  20.9 0.5 %convolution_bitcast_fusion.1 = f32[96,96]{1,0:T(8,128)S(1)} fusion(f32[96,8,128]{2,1,0:T(8,128)S(1)} %bitcast.32), kind=kOutput, calls=%fused_computation.2 | convolution fusion | flops 113246208 | bytes 430080 | tf_op jit(solution)/shard_map/jrc,krc->jk/dot_general | solution.py:44
  21.3 0.5 %convolution_bitcast_fusion = f32[96,96]{1,0:T(8,128)S(1)} fusion(f32[96,8,128]{2,0,1:T(8,128)S(1)} %bitcast.38, f32[96,8,128]{2,1,0:T(8,128)S(1)} %bitcast.33), kind=kOutput, calls=%fused_computation.1 | convolution fusion | flops 113246208 | bytes 823296 | tf_op jit(solution)/shard_map/jrc,krc->jk/dot_general | solution.py:44
  22.2 1.2 %collective-permute-done.4 = f32[4608]{0:T(1024)S(1)} collective-permute-done((f32[4608]{0:T(1024)S(1)}, f32[4608]{0:T(1024)S(1)}, u32[]{:S(2)}, u32[]{:S(2)}) %collective-permute-start.4) | collective-permute-done | bytes 18464 | tf_op jit(solution)/shard_map/ppermute | solution.py:151
  23.3 1.5 %collective-permute-start.5 = (f32[4608]{0:T(1024)S(1)}, f32[4608]{0:T(1024)S(1)}, u32[]{:S(2)}, u32[]{:S(2)}) collective-permute-start(f32[4608]{0:T(1024)S(1)} %add.128), channel_id=1, source_target_pairs={{0,16},{8,24},{16,0},{24,8},{1,17},{9,25},{17,1},{25,9},{2,18},{10... | collective-permute-start | bytes 55304 | tf_op jit(solution)/shard_map/ppermute | solution.py:151
  24.9 2.3 %collective-permute-done.5 = f32[4608]{0:T(1024)S(1)} collective-permute-done((f32[4608]{0:T(1024)S(1)}, f32[4608]{0:T(1024)S(1)}, u32[]{:S(2)}, u32[]{:S(2)}) %collective-permute-start.5) | collective-permute-done | bytes 18464 | tf_op jit(solution)/shard_map/ppermute | solution.py:151
  27.1 3.8 %collective-permute-done.6 = f32[4608]{0:T(1024)S(1)} collective-permute-done((f32[4608]{0:T(1024)S(1)}, f32[4608]{0:T(1024)S(1)}, u32[]{:S(2)}, u32[]{:S(2)}) %collective-permute-start.6) | collective-permute-done | bytes 18464 | tf_op jit(solution)/shard_map/ppermute | solution.py:151
  30.9 3.8 %collective-permute-done.7 = f32[4608]{0:T(1024)S(1)} collective-permute-done((f32[4608]{0:T(1024)S(1)}, f32[4608]{0:T(1024)S(1)}, u32[]{:S(2)}, u32[]{:S(2)}) %collective-permute-start.7) | collective-permute-done | bytes 18464 | tf_op jit(solution)/shard_map/ppermute | solution.py:151
  34.7 1.0 %collective-permute-start.8 = (f32[4608]{0:T(1024)S(1)}, f32[4608]{0:T(1024)S(1)}, u32[]{:S(2)}, u32[]{:S(2)}) collective-permute-start(f32[4608]{0:T(1024)S(1)} %add.131), channel_id=1, source_target_pairs={{0,4},{1,5},{2,6},{3,7},{4,0},{5,1},{6,2},{7,3},{8,12},{9,13},{10,... | collective-permute-start | bytes 55304 | tf_op jit(solution)/shard_map/ppermute | solution.py:151
  35.7 3.7 %collective-permute-done.8 = f32[4608]{0:T(1024)S(1)} collective-permute-done((f32[4608]{0:T(1024)S(1)}, f32[4608]{0:T(1024)S(1)}, u32[]{:S(2)}, u32[]{:S(2)}) %collective-permute-start.8) | collective-permute-done | bytes 18464 | tf_op jit(solution)/shard_map/ppermute | solution.py:151
  39.4 0.7 %reshape.96.packed_ref = f32[2,48,48]{2,1,0:T(8,128)} reshape(f32[4608]{0:T(1024)S(1)} %add.132) | data formatting | bytes 36864 | tf_op jit(solution)/shard_map/reshape | solution.py:321
  40.1 5.8 %shard_map.68 = (f32[72,8,128]{2,1,0:T(8,128)}, f32[36,2,36]{2,1,0:T(2,128)}) custom-call(f32[2,48,48]{2,1,0:T(8,128)} %reshape.96.packed_ref, f32[96,8,128]{2,1,0:T(8,128)} %bitcast.34), custom_call_target="tpu_custom_call" | custom-call | tf_op jit(solution)/shard_map/pallas_call | solution.py:254
  (73 shorter events, 2.9 us)
Async XLA Ops:
  0.6 6.3 %copy-start.2 = (f32[2,12,8,128]{3,2,1,0:T(8,128)S(1)}, f32[2,12,8,128]{3,2,1,0:T(8,128)}, u32[]{:S(2)}) copy-start(f32[2,12,8,128]{3,2,1,0:T(8,128)} %param.5) | copy-start | bytes 294916
  0.6 6.3 %copy-start.1 = (f32[2,12,8,128]{3,2,1,0:T(8,128)S(1)}, f32[2,12,8,128]{3,2,1,0:T(8,128)}, u32[]{:S(2)}) copy-start(f32[2,12,8,128]{3,2,1,0:T(8,128)} %param.6) | copy-start | bytes 294916
  0.7 6.3 %copy-start.4 = (f32[8]{0:T(128)S(1)}, f32[8]{0:T(128)}, u32[]{:S(2)}) copy-start(f32[8]{0:T(128)} %param.8) | copy-start | bytes 100
  0.7 6.3 %copy-start.3 = (s32[2]{0:T(128)S(1)}, s32[2]{0:T(128)}, u32[]{:S(2)}) copy-start(s32[2]{0:T(128)} %param.9) | copy-start | bytes 28
  3.7 4.9 %collective-permute-start.1 = (f32[12544]{0:T(1024)S(1)}, f32[12544]{0:T(1024)S(1)}, u32[]{:S(2)}, u32[]{:S(2)}) collective-permute-start(f32[12544]{0:T(1024)S(1)} %select_n.100), channel_id=1, source_target_pairs={{0,8},{8,0},{16,24},{24,16},{1,9},{9,1},{17,25},{25,17},{2,10},{10... | collective-permute-start | bytes 150536 | tf_op jit(solution)/shard_map/ppermute | solution.py:119
  4.2 4.9 %collective-permute-start = (f32[12544]{0:T(1024)S(1)}, f32[12544]{0:T(1024)S(1)}, u32[]{:S(2)}, u32[]{:S(2)}) collective-permute-start(f32[12544]{0:T(1024)S(1)} %select_n.98), channel_id=1, source_target_pairs={{0,24},{8,16},{16,8},{24,0},{1,25},{9,17},{17,9},{25,1},{2,26},{10... | collective-permute-start | bytes 150536 | tf_op jit(solution)/shard_map/ppermute | solution.py:122
  9.9 5.9 %collective-permute-start.3 = (f32[1176]{0:T(1024)S(1)}, f32[1176]{0:T(1024)S(1)}, u32[]{:S(2)}, u32[]{:S(2)}) collective-permute-start(f32[1176]{0:T(1024)S(1)} %reshape.89), channel_id=1, source_target_pairs={{0,1},{1,0},{2,3},{3,2},{4,5},{5,4},{6,7},{7,6},{8,9},{9,8},{10,11... | collective-permute-start | bytes 14120 | tf_op jit(solution)/shard_map/ppermute | solution.py:119
  11.3 6.3 %collective-permute-start.2 = (f32[1176]{0:T(1024)S(1)}, f32[1176]{0:T(1024)S(1)}, u32[]{:S(2)}, u32[]{:S(2)}) collective-permute-start(f32[1176]{0:T(1024)S(1)} %reshape.88), channel_id=1, source_target_pairs={{0,7},{1,2},{2,1},{3,4},{4,3},{5,6},{6,5},{7,0},{8,15},{9,10},{10,... | collective-permute-start | bytes 14120 | tf_op jit(solution)/shard_map/ppermute | solution.py:122
  20.8 19.3 %copy-start = (f32[2,48,8,128]{3,2,1,0:T(8,128)}, f32[2,48,8,128]{3,2,1,0:T(8,128)S(1)}, u32[]{:S(2)}) copy-start(f32[2,48,8,128]{3,2,1,0:T(8,128)S(1)} %pad_maximum_fusion.7) | copy-start | bytes 1179652
  22.1 1.3 %collective-permute-start.4 = (f32[4608]{0:T(1024)S(1)}, f32[4608]{0:T(1024)S(1)}, u32[]{:S(2)}, u32[]{:S(2)}) collective-permute-start(f32[4608]{0:T(1024)S(1)} %reshape.95), channel_id=1, source_target_pairs={{0,8},{8,0},{16,24},{24,16},{1,9},{9,1},{17,25},{25,17},{2,10},{10... | collective-permute-start | bytes 55304 | tf_op jit(solution)/shard_map/ppermute | solution.py:151
  23.3 3.8 %collective-permute-start.5 = (f32[4608]{0:T(1024)S(1)}, f32[4608]{0:T(1024)S(1)}, u32[]{:S(2)}, u32[]{:S(2)}) collective-permute-start(f32[4608]{0:T(1024)S(1)} %add.128), channel_id=1, source_target_pairs={{0,16},{8,24},{16,0},{24,8},{1,17},{9,25},{17,1},{25,9},{2,18},{10... | collective-permute-start | bytes 55304 | tf_op jit(solution)/shard_map/ppermute | solution.py:151
  27.1 3.8 %collective-permute-start.6 = (f32[4608]{0:T(1024)S(1)}, f32[4608]{0:T(1024)S(1)}, u32[]{:S(2)}, u32[]{:S(2)}) collective-permute-start(f32[4608]{0:T(1024)S(1)} %add.129), channel_id=1, source_target_pairs={{0,1},{1,0},{2,3},{3,2},{4,5},{5,4},{6,7},{7,6},{8,9},{9,8},{10,11... | collective-permute-start | bytes 55304 | tf_op jit(solution)/shard_map/ppermute | solution.py:151
  30.9 3.8 %collective-permute-start.7 = (f32[4608]{0:T(1024)S(1)}, f32[4608]{0:T(1024)S(1)}, u32[]{:S(2)}, u32[]{:S(2)}) collective-permute-start(f32[4608]{0:T(1024)S(1)} %add.130), channel_id=1, source_target_pairs={{0,2},{1,3},{2,0},{3,1},{4,6},{5,7},{6,4},{7,5},{8,10},{9,11},{10,... | collective-permute-start | bytes 55304 | tf_op jit(solution)/shard_map/ppermute | solution.py:151
  34.7 4.7 %collective-permute-start.8 = (f32[4608]{0:T(1024)S(1)}, f32[4608]{0:T(1024)S(1)}, u32[]{:S(2)}, u32[]{:S(2)}) collective-permute-start(f32[4608]{0:T(1024)S(1)} %add.131), channel_id=1, source_target_pairs={{0,4},{1,5},{2,6},{3,7},{4,0},{5,1},{6,2},{7,3},{8,12},{9,13},{10,... | collective-permute-start | bytes 55304 | tf_op jit(solution)/shard_map/ppermute | solution.py:151

commit v20 on v19

--- a/solution.py
+++ b/solution.py
@@ -196,9 +196,10 @@
         return real_part + spread(spread(real_part, 0), 1) - spread(imag_part, 1) + spread(imag_part, 0)
 
     def unpack(packed):
-        real_part = jnp.where(upper, packed, 0.0) + jnp.where(strict, packed, 0.0).T
-        lower = jnp.where(upper, 0.0, packed)
-        return real_part, lower - lower.T
+        mirrored = packed.T
+        real_part = jnp.where(upper, packed, mirrored)
+        imag_part = jnp.where(upper, jnp.where(strict, -mirrored, 0.0), packed)
+        return real_part, imag_part
 
     gram_re, gram_im = unpack(work_ref[0])
     ham_re, ham_im = unpack(work_ref[1])

time: 46.2 us -> 46.1 us (level)
  no operation moved by 1% of the time
where the time goes in v20:
time: 46.1 us; the launch traced here: 45.9 us
  waiting for transfers between devices  17.1 us (37%)
  starting transfers between devices  10.7 us (23%)
  Pallas kernels  5.78 us (13%)
  local copies, waits for them, and re-layouts  4.92 us (11%)
  other arithmetic  3.5 us (8%)
  between operations  2.99 us (6%)
  matrix products  0.95 us (2%)
    ppermute x5, waiting for transfers between devices, tree_sum(): lax.ppermute(value, axis, [(i, i ^ step) for i in range(count)])  14.7 us
    ppermute x2, starting transfers between devices, exchange_rim(): lax.ppermute(jnp.where(even, head, tail).reshape(-1), axis, [(i, (i + 1)...  6.27 us
    pallas_call x1, Pallas kernels, matrix_stage(): pl.pallas_call(functools.partial(matrix_kernel, band_count=band_count, sc...  5.78 us
    ppermute x5, starting transfers between devices, tree_sum(): lax.ppermute(value, axis, [(i, i ^ step) for i in range(count)])  2.56 us
    ppermute x2, waiting for transfers between devices, exchange_rim(): lax.ppermute(jnp.where(even, head, tail).reshape(-1), axis, [(i, (i + 1)...  2.36 us
    ppermute x2, starting transfers between devices, exchange_rim(): lax.ppermute(jnp.where(even, tail, head).reshape(-1), axis, [(i, i ^ 1) f...  1.83 us
    slice x1, local copies, waits for them, and re-layouts, strip_of(): directions[:, :, start:stop]  0.99 us
    slice x1, local copies, waits for them, and re-layouts, strip_of(): bands[:, :, start:stop]  0.99 us
  transfers between devices with their start and end apart: 9, of which 7 were waited for; matrix products, arithmetic and copies ran while one was open for 1% of the time, Pallas kernels for 0%

profile of v20, /device:TPU:0, one launch (start us, length us, event | category | flops | bytes accessed | tf_op | source)
XLA Modules:
  0.0 45.9 jit_solution(4942745030915784260)
XLA Ops:
  0.7 0.8 %convert_bitcast_fusion = (f32[1,8,128]{2,1,0:T(8,128)S(1)}, f32[8,128]{1,0:T(8,128)S(1)}) fusion(s32[8,128]{1,0:T(8,128)} %param.7), kind=kLoop, calls=%fused_computation.87 | loop fusion | flops 1024 | bytes 12288 | tf_op jit(solution)/shard_map/broadcast_in_dim | solution.py:294
  1.5 1.0 %fusion.33 = (f32[2,12,2,128]{3,2,1,0:T(2,128)S(1)}, f32[2,12,2,128]{3,2,1,0:T(2,128)S(1)}) fusion(f32[2,12,8,128]{3,2,1,0:T(8,128)} %param.5), kind=kLoop, calls=%fused_computation.88 | loop fusion | bytes 98304 | tf_op jit(solution)/shard_map/slice | solution.py:285
  2.5 1.0 %fusion.34 = (f32[2,12,2,128]{3,2,1,0:T(2,128)S(1)}, f32[2,12,2,128]{3,2,1,0:T(2,128)S(1)}) fusion(f32[2,12,8,128]{3,2,1,0:T(8,128)} %param.6), kind=kLoop, calls=%fused_computation.89 | loop fusion | bytes 98304 | tf_op jit(solution)/shard_map/slice | solution.py:285
  3.7 0.5 %collective-permute-start.1 = (f32[12544]{0:T(1024)S(1)}, f32[12544]{0:T(1024)S(1)}, u32[]{:S(2)}, u32[]{:S(2)}) collective-permute-start(f32[12544]{0:T(1024)S(1)} %select_n.100), channel_id=1, source_target_pairs={{0,8},{8,0},{16,24},{24,16},{1,9},{9,1},{17,25},{25,17},{2,10},{10... | collective-permute-start | bytes 150536 | tf_op jit(solution)/shard_map/ppermute | solution.py:119
  4.2 2.7 %collective-permute-start = (f32[12544]{0:T(1024)S(1)}, f32[12544]{0:T(1024)S(1)}, u32[]{:S(2)}, u32[]{:S(2)}) collective-permute-start(f32[12544]{0:T(1024)S(1)} %select_n.98), channel_id=1, source_target_pairs={{0,24},{8,16},{16,8},{24,0},{1,25},{9,17},{17,9},{25,1},{2,26},{10... | collective-permute-start | bytes 150536 | tf_op jit(solution)/shard_map/ppermute | solution.py:122
  7.0 0.6 %fusion.36 = (s32[1]{0:T(128)}, s32[1]{0:T(128)}) fusion(s32[2]{0:T(128)S(1)} %copy-done.3), kind=kLoop, calls=%fused_computation.91 | loop fusion | bytes 16 | tf_op jit(solution)/shard_map/slice | solution.py:291
  8.6 0.6 %collective-permute-done = f32[12544]{0:T(1024)S(1)} collective-permute-done((f32[12544]{0:T(1024)S(1)}, f32[12544]{0:T(1024)S(1)}, u32[]{:S(2)}, u32[]{:S(2)}) %collective-permute-start) | collective-permute-done | bytes 50208 | tf_op jit(solution)/shard_map/ppermute | solution.py:122
  9.9 1.3 %collective-permute-start.3 = (f32[1176]{0:T(1024)S(1)}, f32[1176]{0:T(1024)S(1)}, u32[]{:S(2)}, u32[]{:S(2)}) collective-permute-start(f32[1176]{0:T(1024)S(1)} %reshape.89), channel_id=1, source_target_pairs={{0,1},{1,0},{2,3},{3,2},{4,5},{5,4},{6,7},{7,6},{8,9},{9,8},{10,11... | collective-permute-start | bytes 14120 | tf_op jit(solution)/shard_map/ppermute | solution.py:119
  11.3 3.6 %collective-permute-start.2 = (f32[1176]{0:T(1024)S(1)}, f32[1176]{0:T(1024)S(1)}, u32[]{:S(2)}, u32[]{:S(2)}) collective-permute-start(f32[1176]{0:T(1024)S(1)} %reshape.88), channel_id=1, source_target_pairs={{0,7},{1,2},{2,1},{3,4},{4,3},{5,6},{6,5},{7,0},{8,15},{9,10},{10,... | collective-permute-start | bytes 14120 | tf_op jit(solution)/shard_map/ppermute | solution.py:122
  15.8 1.8 %collective-permute-done.2 = f32[1176]{0:T(1024)S(1)} collective-permute-done((f32[1176]{0:T(1024)S(1)}, f32[1176]{0:T(1024)S(1)}, u32[]{:S(2)}, u32[]{:S(2)}) %collective-permute-start.2) | collective-permute-done | bytes 4736 | tf_op jit(solution)/shard_map/ppermute | solution.py:122
  18.4 0.6 %pad_maximum_fusion.1 = f32[48,12,132]{2,1,0:T(8,128)S(1)} fusion(f32[49,12,2]{2,1,0:T(8,128)S(1)} %reshape.91, f32[49,12,2]{2,1,0:T(8,128)S(1)} %reshape.90, f32[49,2,128]{2,1,0:T(2,128)S(1)} %reshape.87, f32[49,2,128]{2,1,0:T(2,128)S(1)} %reshape.85, f32[1,8,128]{2,1,0:T(8,128)S(1)} %get-tuple-element.40, f32[48,8,128]{2,1,0:T(8,128)S(1)} %bitcast.37), kind=kLoop, calls=%fused_computation.3 | loop fusion | flops 380160 | bytes 614592 | tf_op jit(solution)/shard_map/concatenate | solution.py:135
  19.3 0.6 %broadcast_divide_fusion = (f32[2,12,10,130]{3,2,1,0:T(8,128)S(1)}, f32[2,12,10,130]{3,2,1,0:T(8,128)S(1)}, f32[2,12,10,130]{3,2,1,0:T(8,128)S(1)}, f32[2,12,10,130]{3,2,1,0:T(8,128)S(1)}) fusion(f32[10,130]{1,0:T(8,128)S(1)} %get-tuple-element.13, f32[2,24,12,132]{3,2,1,0:T(8,128)S(1)} %bitcast.31, f32[10,130]{1,0:T(8,128)S(1)} %get-tuple-element.17, ...), kind=kLoop, calls=%fused_computation.34 | loop fusion | flops 343200 | bytes 1274000 | tf_op jit(solution)/shard_map/div | solution.py:307
  20.3 0.4 fusion.7
  20.9 0.5 %convolution_bitcast_fusion.1 = f32[96,96]{1,0:T(8,128)S(1)} fusion(f32[96,8,128]{2,1,0:T(8,128)S(1)} %bitcast.32), kind=kOutput, calls=%fused_computation.2 | convolution fusion | flops 113246208 | bytes 430080 | tf_op jit(solution)/shard_map/jrc,krc->jk/dot_general | solution.py:44
  21.3 0.5 %convolution_bitcast_fusion = f32[96,96]{1,0:T(8,128)S(1)} fusion(f32[96,8,128]{2,0,1:T(8,128)S(1)} %bitcast.38, f32[96,8,128]{2,1,0:T(8,128)S(1)} %bitcast.33), kind=kOutput, calls=%fused_computation.1 | convolution fusion | flops 113246208 | bytes 823296 | tf_op jit(solution)/shard_map/jrc,krc->jk/dot_general | solution.py:44
  22.2 1.2 %collective-permute-done.4 = f32[4608]{0:T(1024)S(1)} collective-permute-done((f32[4608]{0:T(1024)S(1)}, f32[4608]{0:T(1024)S(1)}, u32[]{:S(2)}, u32[]{:S(2)}) %collective-permute-start.4) | collective-permute-done | bytes 18464 | tf_op jit(solution)/shard_map/ppermute | solution.py:151
  23.3 1.5 %collective-permute-start.5 = (f32[4608]{0:T(1024)S(1)}, f32[4608]{0:T(1024)S(1)}, u32[]{:S(2)}, u32[]{:S(2)}) collective-permute-start(f32[4608]{0:T(1024)S(1)} %add.128), channel_id=1, source_target_pairs={{0,16},{8,24},{16,0},{24,8},{1,17},{9,25},{17,1},{25,9},{2,18},{10... | collective-permute-start | bytes 55304 | tf_op jit(solution)/shard_map/ppermute | solution.py:151
  24.9 2.3 %collective-permute-done.5 = f32[4608]{0:T(1024)S(1)} collective-permute-done((f32[4608]{0:T(1024)S(1)}, f32[4608]{0:T(1024)S(1)}, u32[]{:S(2)}, u32[]{:S(2)}) %collective-permute-start.5) | collective-permute-done | bytes 18464 | tf_op jit(solution)/shard_map/ppermute | solution.py:151
  27.1 3.8 %collective-permute-done.6 = f32[4608]{0:T(1024)S(1)} collective-permute-done((f32[4608]{0:T(1024)S(1)}, f32[4608]{0:T(1024)S(1)}, u32[]{:S(2)}, u32[]{:S(2)}) %collective-permute-start.6) | collective-permute-done | bytes 18464 | tf_op jit(solution)/shard_map/ppermute | solution.py:151
  30.9 3.8 %collective-permute-done.7 = f32[4608]{0:T(1024)S(1)} collective-permute-done((f32[4608]{0:T(1024)S(1)}, f32[4608]{0:T(1024)S(1)}, u32[]{:S(2)}, u32[]{:S(2)}) %collective-permute-start.7) | collective-permute-done | bytes 18464 | tf_op jit(solution)/shard_map/ppermute | solution.py:151
  34.7 1.0 %collective-permute-start.8 = (f32[4608]{0:T(1024)S(1)}, f32[4608]{0:T(1024)S(1)}, u32[]{:S(2)}, u32[]{:S(2)}) collective-permute-start(f32[4608]{0:T(1024)S(1)} %add.131), channel_id=1, source_target_pairs={{0,4},{1,5},{2,6},{3,7},{4,0},{5,1},{6,2},{7,3},{8,12},{9,13},{10,... | collective-permute-start | bytes 55304 | tf_op jit(solution)/shard_map/ppermute | solution.py:151
  35.7 3.7 %collective-permute-done.8 = f32[4608]{0:T(1024)S(1)} collective-permute-done((f32[4608]{0:T(1024)S(1)}, f32[4608]{0:T(1024)S(1)}, u32[]{:S(2)}, u32[]{:S(2)}) %collective-permute-start.8) | collective-permute-done | bytes 18464 | tf_op jit(solution)/shard_map/ppermute | solution.py:151
  39.4 0.7 %reshape.96.packed_ref = f32[2,48,48]{2,1,0:T(8,128)} reshape(f32[4608]{0:T(1024)S(1)} %add.132) | data formatting | bytes 36864 | tf_op jit(solution)/shard_map/reshape | solution.py:322
  40.1 5.8 %shard_map.68 = (f32[72,8,128]{2,1,0:T(8,128)}, f32[36,2,36]{2,1,0:T(2,128)}) custom-call(f32[2,48,48]{2,1,0:T(8,128)} %reshape.96.packed_ref, f32[96,8,128]{2,1,0:T(8,128)} %bitcast.34), custom_call_target="tpu_custom_call" | custom-call | tf_op jit(solution)/shard_map/pallas_call | solution.py:255
  (73 shorter events, 2.9 us)
Async XLA Ops:
  0.6 6.3 %copy-start.2 = (f32[2,12,8,128]{3,2,1,0:T(8,128)S(1)}, f32[2,12,8,128]{3,2,1,0:T(8,128)}, u32[]{:S(2)}) copy-start(f32[2,12,8,128]{3,2,1,0:T(8,128)} %param.5) | copy-start | bytes 294916
  0.6 6.3 %copy-start.1 = (f32[2,12,8,128]{3,2,1,0:T(8,128)S(1)}, f32[2,12,8,128]{3,2,1,0:T(8,128)}, u32[]{:S(2)}) copy-start(f32[2,12,8,128]{3,2,1,0:T(8,128)} %param.6) | copy-start | bytes 294916
  0.7 6.3 %copy-start.4 = (f32[8]{0:T(128)S(1)}, f32[8]{0:T(128)}, u32[]{:S(2)}) copy-start(f32[8]{0:T(128)} %param.8) | copy-start | bytes 100
  0.7 6.3 %copy-start.3 = (s32[2]{0:T(128)S(1)}, s32[2]{0:T(128)}, u32[]{:S(2)}) copy-start(s32[2]{0:T(128)} %param.9) | copy-start | bytes 28
  3.7 4.9 %collective-permute-start.1 = (f32[12544]{0:T(1024)S(1)}, f32[12544]{0:T(1024)S(1)}, u32[]{:S(2)}, u32[]{:S(2)}) collective-permute-start(f32[12544]{0:T(1024)S(1)} %select_n.100), channel_id=1, source_target_pairs={{0,8},{8,0},{16,24},{24,16},{1,9},{9,1},{17,25},{25,17},{2,10},{10... | collective-permute-start | bytes 150536 | tf_op jit(solution)/shard_map/ppermute | solution.py:119
  4.2 4.9 %collective-permute-start = (f32[12544]{0:T(1024)S(1)}, f32[12544]{0:T(1024)S(1)}, u32[]{:S(2)}, u32[]{:S(2)}) collective-permute-start(f32[12544]{0:T(1024)S(1)} %select_n.98), channel_id=1, source_target_pairs={{0,24},{8,16},{16,8},{24,0},{1,25},{9,17},{17,9},{25,1},{2,26},{10... | collective-permute-start | bytes 150536 | tf_op jit(solution)/shard_map/ppermute | solution.py:122
  9.9 5.9 %collective-permute-start.3 = (f32[1176]{0:T(1024)S(1)}, f32[1176]{0:T(1024)S(1)}, u32[]{:S(2)}, u32[]{:S(2)}) collective-permute-start(f32[1176]{0:T(1024)S(1)} %reshape.89), channel_id=1, source_target_pairs={{0,1},{1,0},{2,3},{3,2},{4,5},{5,4},{6,7},{7,6},{8,9},{9,8},{10,11... | collective-permute-start | bytes 14120 | tf_op jit(solution)/shard_map/ppermute | solution.py:119
  11.3 6.3 %collective-permute-start.2 = (f32[1176]{0:T(1024)S(1)}, f32[1176]{0:T(1024)S(1)}, u32[]{:S(2)}, u32[]{:S(2)}) collective-permute-start(f32[1176]{0:T(1024)S(1)} %reshape.88), channel_id=1, source_target_pairs={{0,7},{1,2},{2,1},{3,4},{4,3},{5,6},{6,5},{7,0},{8,15},{9,10},{10,... | collective-permute-start | bytes 14120 | tf_op jit(solution)/shard_map/ppermute | solution.py:122
  20.8 19.3 %copy-start = (f32[2,48,8,128]{3,2,1,0:T(8,128)}, f32[2,48,8,128]{3,2,1,0:T(8,128)S(1)}, u32[]{:S(2)}) copy-start(f32[2,48,8,128]{3,2,1,0:T(8,128)S(1)} %pad_maximum_fusion.7) | copy-start | bytes 1179652
  22.1 1.3 %collective-permute-start.4 = (f32[4608]{0:T(1024)S(1)}, f32[4608]{0:T(1024)S(1)}, u32[]{:S(2)}, u32[]{:S(2)}) collective-permute-start(f32[4608]{0:T(1024)S(1)} %reshape.95), channel_id=1, source_target_pairs={{0,8},{8,0},{16,24},{24,16},{1,9},{9,1},{17,25},{25,17},{2,10},{10... | collective-permute-start | bytes 55304 | tf_op jit(solution)/shard_map/ppermute | solution.py:151
  23.3 3.8 %collective-permute-start.5 = (f32[4608]{0:T(1024)S(1)}, f32[4608]{0:T(1024)S(1)}, u32[]{:S(2)}, u32[]{:S(2)}) collective-permute-start(f32[4608]{0:T(1024)S(1)} %add.128), channel_id=1, source_target_pairs={{0,16},{8,24},{16,0},{24,8},{1,17},{9,25},{17,1},{25,9},{2,18},{10... | collective-permute-start | bytes 55304 | tf_op jit(solution)/shard_map/ppermute | solution.py:151
  27.1 3.8 %collective-permute-start.6 = (f32[4608]{0:T(1024)S(1)}, f32[4608]{0:T(1024)S(1)}, u32[]{:S(2)}, u32[]{:S(2)}) collective-permute-start(f32[4608]{0:T(1024)S(1)} %add.129), channel_id=1, source_target_pairs={{0,1},{1,0},{2,3},{3,2},{4,5},{5,4},{6,7},{7,6},{8,9},{9,8},{10,11... | collective-permute-start | bytes 55304 | tf_op jit(solution)/shard_map/ppermute | solution.py:151
  30.9 3.8 %collective-permute-start.7 = (f32[4608]{0:T(1024)S(1)}, f32[4608]{0:T(1024)S(1)}, u32[]{:S(2)}, u32[]{:S(2)}) collective-permute-start(f32[4608]{0:T(1024)S(1)} %add.130), channel_id=1, source_target_pairs={{0,2},{1,3},{2,0},{3,1},{4,6},{5,7},{6,4},{7,5},{8,10},{9,11},{10,... | collective-permute-start | bytes 55304 | tf_op jit(solution)/shard_map/ppermute | solution.py:151
  34.7 4.7 %collective-permute-start.8 = (f32[4608]{0:T(1024)S(1)}, f32[4608]{0:T(1024)S(1)}, u32[]{:S(2)}, u32[]{:S(2)}) collective-permute-start(f32[4608]{0:T(1024)S(1)} %add.131), channel_id=1, source_target_pairs={{0,4},{1,5},{2,6},{3,7},{4,0},{5,1},{6,2},{7,3},{8,12},{9,13},{10,... | collective-permute-start | bytes 55304 | tf_op jit(solution)/shard_map/ppermute | solution.py:151

commit v21 on v19

--- a/solution.py
+++ b/solution.py
@@ -210,7 +210,13 @@
     )
     mixing = kept.astype(jnp.float32) - shifted
     mixing = mixing + spread(spread(mixing, 0), 1)
-    embedded = dot(mixing.T, dot(embed(gram_re, gram_im), mixing))
+    kept_t = (eye & (rows < 2 * band_count)) | (
+        (cols == rows + band_count) & (rows >= 2 * band_count) & (rows < raw)
+    )
+    shifted_t = pltpu.roll(pltpu.roll(quotient, band_count, 0), 2 * band_count, 1)
+    mixing_t = kept_t.astype(jnp.float32) - shifted_t
+    mixing_t = mixing_t + spread(spread(mixing_t, 0), 1)
+    embedded = dot(mixing_t, dot(embed(gram_re, gram_im), mixing))
     active = (rows < raw) | ((rows >= half) & (rows < half + raw))
     identity = (eye & active).astype(jnp.float32)
     total = jnp.sum(jnp.sum(embedded * embedded, axis=0, keepdims=True), axis=1, keepdims=True)

time: 46.2 us -> 46.1 us (level)
  no operation moved by 1% of the time
where the time goes in v21:
time: 46.1 us; the launch traced here: 45.9 us
  waiting for transfers between devices  17.1 us (37%)
  starting transfers between devices  10.7 us (23%)
  Pallas kernels  5.8 us (13%)
  local copies, waits for them, and re-layouts  4.92 us (11%)
  other arithmetic  3.5 us (8%)
  between operations  2.99 us (6%)
  matrix products  0.95 us (2%)
    ppermute x5, waiting for transfers between devices, tree_sum(): lax.ppermute(value, axis, [(i, i ^ step) for i in range(count)])  14.7 us
    ppermute x2, starting transfers between devices, exchange_rim(): lax.ppermute(jnp.where(even, head, tail).reshape(-1), axis, [(i, (i + 1)...  6.27 us
    pallas_call x1, Pallas kernels, matrix_stage(): pl.pallas_call(functools.partial(matrix_kernel, band_count=band_count, sc...  5.8 us
    ppermute x5, starting transfers between devices, tree_sum(): lax.ppermute(value, axis, [(i, i ^ step) for i in range(count)])  2.56 us
    ppermute x2, waiting for transfers between devices, exchange_rim(): lax.ppermute(jnp.where(even, head, tail).reshape(-1), axis, [(i, (i + 1)...  2.36 us
    ppermute x2, starting transfers between devices, exchange_rim(): lax.ppermute(jnp.where(even, tail, head).reshape(-1), axis, [(i, i ^ 1) f...  1.83 us
    slice x1, local copies, waits for them, and re-layouts, strip_of(): directions[:, :, start:stop]  0.99 us
    slice x1, local copies, waits for them, and re-layouts, strip_of(): bands[:, :, start:stop]  0.99 us
  transfers between devices with their start and end apart: 9, of which 7 were waited for; matrix products, arithmetic and copies ran while one was open for 1% of the time, Pallas kernels for 0%

profile of v21, /device:TPU:0, one launch (start us, length us, event | category | flops | bytes accessed | tf_op | source)
XLA Modules:
  0.0 45.9 jit_solution(6692970474075563318)
XLA Ops:
  0.7 0.8 %convert_bitcast_fusion = (f32[1,8,128]{2,1,0:T(8,128)S(1)}, f32[8,128]{1,0:T(8,128)S(1)}) fusion(s32[8,128]{1,0:T(8,128)} %param.7), kind=kLoop, calls=%fused_computation.87 | loop fusion | flops 1024 | bytes 12288 | tf_op jit(solution)/shard_map/broadcast_in_dim | solution.py:299
  1.5 1.0 %fusion.33 = (f32[2,12,2,128]{3,2,1,0:T(2,128)S(1)}, f32[2,12,2,128]{3,2,1,0:T(2,128)S(1)}) fusion(f32[2,12,8,128]{3,2,1,0:T(8,128)} %param.5), kind=kLoop, calls=%fused_computation.88 | loop fusion | bytes 98304 | tf_op jit(solution)/shard_map/slice | solution.py:290
  2.5 1.0 %fusion.34 = (f32[2,12,2,128]{3,2,1,0:T(2,128)S(1)}, f32[2,12,2,128]{3,2,1,0:T(2,128)S(1)}) fusion(f32[2,12,8,128]{3,2,1,0:T(8,128)} %param.6), kind=kLoop, calls=%fused_computation.89 | loop fusion | bytes 98304 | tf_op jit(solution)/shard_map/slice | solution.py:290
  3.7 0.5 %collective-permute-start.1 = (f32[12544]{0:T(1024)S(1)}, f32[12544]{0:T(1024)S(1)}, u32[]{:S(2)}, u32[]{:S(2)}) collective-permute-start(f32[12544]{0:T(1024)S(1)} %select_n.100), channel_id=1, source_target_pairs={{0,8},{8,0},{16,24},{24,16},{1,9},{9,1},{17,25},{25,17},{2,10},{10... | collective-permute-start | bytes 150536 | tf_op jit(solution)/shard_map/ppermute | solution.py:119
  4.2 2.7 %collective-permute-start = (f32[12544]{0:T(1024)S(1)}, f32[12544]{0:T(1024)S(1)}, u32[]{:S(2)}, u32[]{:S(2)}) collective-permute-start(f32[12544]{0:T(1024)S(1)} %select_n.98), channel_id=1, source_target_pairs={{0,24},{8,16},{16,8},{24,0},{1,25},{9,17},{17,9},{25,1},{2,26},{10... | collective-permute-start | bytes 150536 | tf_op jit(solution)/shard_map/ppermute | solution.py:122
  7.0 0.6 %fusion.36 = (s32[1]{0:T(128)}, s32[1]{0:T(128)}) fusion(s32[2]{0:T(128)S(1)} %copy-done.3), kind=kLoop, calls=%fused_computation.91 | loop fusion | bytes 16 | tf_op jit(solution)/shard_map/slice | solution.py:296
  8.6 0.6 %collective-permute-done = f32[12544]{0:T(1024)S(1)} collective-permute-done((f32[12544]{0:T(1024)S(1)}, f32[12544]{0:T(1024)S(1)}, u32[]{:S(2)}, u32[]{:S(2)}) %collective-permute-start) | collective-permute-done | bytes 50208 | tf_op jit(solution)/shard_map/ppermute | solution.py:122
  9.9 1.3 %collective-permute-start.3 = (f32[1176]{0:T(1024)S(1)}, f32[1176]{0:T(1024)S(1)}, u32[]{:S(2)}, u32[]{:S(2)}) collective-permute-start(f32[1176]{0:T(1024)S(1)} %reshape.89), channel_id=1, source_target_pairs={{0,1},{1,0},{2,3},{3,2},{4,5},{5,4},{6,7},{7,6},{8,9},{9,8},{10,11... | collective-permute-start | bytes 14120 | tf_op jit(solution)/shard_map/ppermute | solution.py:119
  11.3 3.6 %collective-permute-start.2 = (f32[1176]{0:T(1024)S(1)}, f32[1176]{0:T(1024)S(1)}, u32[]{:S(2)}, u32[]{:S(2)}) collective-permute-start(f32[1176]{0:T(1024)S(1)} %reshape.88), channel_id=1, source_target_pairs={{0,7},{1,2},{2,1},{3,4},{4,3},{5,6},{6,5},{7,0},{8,15},{9,10},{10,... | collective-permute-start | bytes 14120 | tf_op jit(solution)/shard_map/ppermute | solution.py:122
  15.8 1.8 %collective-permute-done.2 = f32[1176]{0:T(1024)S(1)} collective-permute-done((f32[1176]{0:T(1024)S(1)}, f32[1176]{0:T(1024)S(1)}, u32[]{:S(2)}, u32[]{:S(2)}) %collective-permute-start.2) | collective-permute-done | bytes 4736 | tf_op jit(solution)/shard_map/ppermute | solution.py:122
  18.4 0.6 %pad_maximum_fusion.1 = f32[48,12,132]{2,1,0:T(8,128)S(1)} fusion(f32[49,12,2]{2,1,0:T(8,128)S(1)} %reshape.91, f32[49,12,2]{2,1,0:T(8,128)S(1)} %reshape.90, f32[49,2,128]{2,1,0:T(2,128)S(1)} %reshape.87, f32[49,2,128]{2,1,0:T(2,128)S(1)} %reshape.85, f32[1,8,128]{2,1,0:T(8,128)S(1)} %get-tuple-element.40, f32[48,8,128]{2,1,0:T(8,128)S(1)} %bitcast.37), kind=kLoop, calls=%fused_computation.3 | loop fusion | flops 380160 | bytes 614592 | tf_op jit(solution)/shard_map/concatenate | solution.py:135
  19.3 0.6 %broadcast_divide_fusion = (f32[2,12,10,130]{3,2,1,0:T(8,128)S(1)}, f32[2,12,10,130]{3,2,1,0:T(8,128)S(1)}, f32[2,12,10,130]{3,2,1,0:T(8,128)S(1)}, f32[2,12,10,130]{3,2,1,0:T(8,128)S(1)}) fusion(f32[10,130]{1,0:T(8,128)S(1)} %get-tuple-element.13, f32[2,24,12,132]{3,2,1,0:T(8,128)S(1)} %bitcast.31, f32[10,130]{1,0:T(8,128)S(1)} %get-tuple-element.17, ...), kind=kLoop, calls=%fused_computation.34 | loop fusion | flops 343200 | bytes 1274000 | tf_op jit(solution)/shard_map/div | solution.py:312
  20.3 0.4 fusion.7
  20.9 0.5 %convolution_bitcast_fusion.1 = f32[96,96]{1,0:T(8,128)S(1)} fusion(f32[96,8,128]{2,1,0:T(8,128)S(1)} %bitcast.32), kind=kOutput, calls=%fused_computation.2 | convolution fusion | flops 113246208 | bytes 430080 | tf_op jit(solution)/shard_map/jrc,krc->jk/dot_general | solution.py:44
  21.3 0.5 %convolution_bitcast_fusion = f32[96,96]{1,0:T(8,128)S(1)} fusion(f32[96,8,128]{2,0,1:T(8,128)S(1)} %bitcast.38, f32[96,8,128]{2,1,0:T(8,128)S(1)} %bitcast.33), kind=kOutput, calls=%fused_computation.1 | convolution fusion | flops 113246208 | bytes 823296 | tf_op jit(solution)/shard_map/jrc,krc->jk/dot_general | solution.py:44
  22.2 1.2 %collective-permute-done.4 = f32[4608]{0:T(1024)S(1)} collective-permute-done((f32[4608]{0:T(1024)S(1)}, f32[4608]{0:T(1024)S(1)}, u32[]{:S(2)}, u32[]{:S(2)}) %collective-permute-start.4) | collective-permute-done | bytes 18464 | tf_op jit(solution)/shard_map/ppermute | solution.py:151
  23.3 1.5 %collective-permute-start.5 = (f32[4608]{0:T(1024)S(1)}, f32[4608]{0:T(1024)S(1)}, u32[]{:S(2)}, u32[]{:S(2)}) collective-permute-start(f32[4608]{0:T(1024)S(1)} %add.128), channel_id=1, source_target_pairs={{0,16},{8,24},{16,0},{24,8},{1,17},{9,25},{17,1},{25,9},{2,18},{10... | collective-permute-start | bytes 55304 | tf_op jit(solution)/shard_map/ppermute | solution.py:151
  24.9 2.3 %collective-permute-done.5 = f32[4608]{0:T(1024)S(1)} collective-permute-done((f32[4608]{0:T(1024)S(1)}, f32[4608]{0:T(1024)S(1)}, u32[]{:S(2)}, u32[]{:S(2)}) %collective-permute-start.5) | collective-permute-done | bytes 18464 | tf_op jit(solution)/shard_map/ppermute | solution.py:151
  27.1 3.8 %collective-permute-done.6 = f32[4608]{0:T(1024)S(1)} collective-permute-done((f32[4608]{0:T(1024)S(1)}, f32[4608]{0:T(1024)S(1)}, u32[]{:S(2)}, u32[]{:S(2)}) %collective-permute-start.6) | collective-permute-done | bytes 18464 | tf_op jit(solution)/shard_map/ppermute | solution.py:151
  30.9 3.8 %collective-permute-done.7 = f32[4608]{0:T(1024)S(1)} collective-permute-done((f32[4608]{0:T(1024)S(1)}, f32[4608]{0:T(1024)S(1)}, u32[]{:S(2)}, u32[]{:S(2)}) %collective-permute-start.7) | collective-permute-done | bytes 18464 | tf_op jit(solution)/shard_map/ppermute | solution.py:151
  34.7 1.0 %collective-permute-start.8 = (f32[4608]{0:T(1024)S(1)}, f32[4608]{0:T(1024)S(1)}, u32[]{:S(2)}, u32[]{:S(2)}) collective-permute-start(f32[4608]{0:T(1024)S(1)} %add.131), channel_id=1, source_target_pairs={{0,4},{1,5},{2,6},{3,7},{4,0},{5,1},{6,2},{7,3},{8,12},{9,13},{10,... | collective-permute-start | bytes 55304 | tf_op jit(solution)/shard_map/ppermute | solution.py:151
  35.7 3.7 %collective-permute-done.8 = f32[4608]{0:T(1024)S(1)} collective-permute-done((f32[4608]{0:T(1024)S(1)}, f32[4608]{0:T(1024)S(1)}, u32[]{:S(2)}, u32[]{:S(2)}) %collective-permute-start.8) | collective-permute-done | bytes 18464 | tf_op jit(solution)/shard_map/ppermute | solution.py:151
  39.4 0.7 %reshape.96.packed_ref = f32[2,48,48]{2,1,0:T(8,128)} reshape(f32[4608]{0:T(1024)S(1)} %add.132) | data formatting | bytes 36864 | tf_op jit(solution)/shard_map/reshape | solution.py:327
  40.1 5.8 %shard_map.68 = (f32[72,8,128]{2,1,0:T(8,128)}, f32[36,2,36]{2,1,0:T(2,128)}) custom-call(f32[2,48,48]{2,1,0:T(8,128)} %reshape.96.packed_ref, f32[96,8,128]{2,1,0:T(8,128)} %bitcast.34), custom_call_target="tpu_custom_call" | custom-call | tf_op jit(solution)/shard_map/pallas_call | solution.py:260
  (73 shorter events, 2.9 us)
Async XLA Ops:
  0.6 6.3 %copy-start.2 = (f32[2,12,8,128]{3,2,1,0:T(8,128)S(1)}, f32[2,12,8,128]{3,2,1,0:T(8,128)}, u32[]{:S(2)}) copy-start(f32[2,12,8,128]{3,2,1,0:T(8,128)} %param.5) | copy-start | bytes 294916
  0.6 6.3 %copy-start.1 = (f32[2,12,8,128]{3,2,1,0:T(8,128)S(1)}, f32[2,12,8,128]{3,2,1,0:T(8,128)}, u32[]{:S(2)}) copy-start(f32[2,12,8,128]{3,2,1,0:T(8,128)} %param.6) | copy-start | bytes 294916
  0.7 6.3 %copy-start.4 = (f32[8]{0:T(128)S(1)}, f32[8]{0:T(128)}, u32[]{:S(2)}) copy-start(f32[8]{0:T(128)} %param.8) | copy-start | bytes 100
  0.7 6.3 %copy-start.3 = (s32[2]{0:T(128)S(1)}, s32[2]{0:T(128)}, u32[]{:S(2)}) copy-start(s32[2]{0:T(128)} %param.9) | copy-start | bytes 28
  3.7 4.9 %collective-permute-start.1 = (f32[12544]{0:T(1024)S(1)}, f32[12544]{0:T(1024)S(1)}, u32[]{:S(2)}, u32[]{:S(2)}) collective-permute-start(f32[12544]{0:T(1024)S(1)} %select_n.100), channel_id=1, source_target_pairs={{0,8},{8,0},{16,24},{24,16},{1,9},{9,1},{17,25},{25,17},{2,10},{10... | collective-permute-start | bytes 150536 | tf_op jit(solution)/shard_map/ppermute | solution.py:119
  4.2 4.9 %collective-permute-start = (f32[12544]{0:T(1024)S(1)}, f32[12544]{0:T(1024)S(1)}, u32[]{:S(2)}, u32[]{:S(2)}) collective-permute-start(f32[12544]{0:T(1024)S(1)} %select_n.98), channel_id=1, source_target_pairs={{0,24},{8,16},{16,8},{24,0},{1,25},{9,17},{17,9},{25,1},{2,26},{10... | collective-permute-start | bytes 150536 | tf_op jit(solution)/shard_map/ppermute | solution.py:122
  9.9 5.9 %collective-permute-start.3 = (f32[1176]{0:T(1024)S(1)}, f32[1176]{0:T(1024)S(1)}, u32[]{:S(2)}, u32[]{:S(2)}) collective-permute-start(f32[1176]{0:T(1024)S(1)} %reshape.89), channel_id=1, source_target_pairs={{0,1},{1,0},{2,3},{3,2},{4,5},{5,4},{6,7},{7,6},{8,9},{9,8},{10,11... | collective-permute-start | bytes 14120 | tf_op jit(solution)/shard_map/ppermute | solution.py:119
  11.3 6.3 %collective-permute-start.2 = (f32[1176]{0:T(1024)S(1)}, f32[1176]{0:T(1024)S(1)}, u32[]{:S(2)}, u32[]{:S(2)}) collective-permute-start(f32[1176]{0:T(1024)S(1)} %reshape.88), channel_id=1, source_target_pairs={{0,7},{1,2},{2,1},{3,4},{4,3},{5,6},{6,5},{7,0},{8,15},{9,10},{10,... | collective-permute-start | bytes 14120 | tf_op jit(solution)/shard_map/ppermute | solution.py:122
  20.8 19.3 %copy-start = (f32[2,48,8,128]{3,2,1,0:T(8,128)}, f32[2,48,8,128]{3,2,1,0:T(8,128)S(1)}, u32[]{:S(2)}) copy-start(f32[2,48,8,128]{3,2,1,0:T(8,128)S(1)} %pad_maximum_fusion.7) | copy-start | bytes 1179652
  22.1 1.3 %collective-permute-start.4 = (f32[4608]{0:T(1024)S(1)}, f32[4608]{0:T(1024)S(1)}, u32[]{:S(2)}, u32[]{:S(2)}) collective-permute-start(f32[4608]{0:T(1024)S(1)} %reshape.95), channel_id=1, source_target_pairs={{0,8},{8,0},{16,24},{24,16},{1,9},{9,1},{17,25},{25,17},{2,10},{10... | collective-permute-start | bytes 55304 | tf_op jit(solution)/shard_map/ppermute | solution.py:151
  23.3 3.8 %collective-permute-start.5 = (f32[4608]{0:T(1024)S(1)}, f32[4608]{0:T(1024)S(1)}, u32[]{:S(2)}, u32[]{:S(2)}) collective-permute-start(f32[4608]{0:T(1024)S(1)} %add.128), channel_id=1, source_target_pairs={{0,16},{8,24},{16,0},{24,8},{1,17},{9,25},{17,1},{25,9},{2,18},{10... | collective-permute-start | bytes 55304 | tf_op jit(solution)/shard_map/ppermute | solution.py:151
  27.1 3.8 %collective-permute-start.6 = (f32[4608]{0:T(1024)S(1)}, f32[4608]{0:T(1024)S(1)}, u32[]{:S(2)}, u32[]{:S(2)}) collective-permute-start(f32[4608]{0:T(1024)S(1)} %add.129), channel_id=1, source_target_pairs={{0,1},{1,0},{2,3},{3,2},{4,5},{5,4},{6,7},{7,6},{8,9},{9,8},{10,11... | collective-permute-start | bytes 55304 | tf_op jit(solution)/shard_map/ppermute | solution.py:151
  30.9 3.8 %collective-permute-start.7 = (f32[4608]{0:T(1024)S(1)}, f32[4608]{0:T(1024)S(1)}, u32[]{:S(2)}, u32[]{:S(2)}) collective-permute-start(f32[4608]{0:T(1024)S(1)} %add.130), channel_id=1, source_target_pairs={{0,2},{1,3},{2,0},{3,1},{4,6},{5,7},{6,4},{7,5},{8,10},{9,11},{10,... | collective-permute-start | bytes 55304 | tf_op jit(solution)/shard_map/ppermute | solution.py:151
  34.7 4.7 %collective-permute-start.8 = (f32[4608]{0:T(1024)S(1)}, f32[4608]{0:T(1024)S(1)}, u32[]{:S(2)}, u32[]{:S(2)}) collective-permute-start(f32[4608]{0:T(1024)S(1)} %add.131), channel_id=1, source_target_pairs={{0,4},{1,5},{2,6},{3,7},{4,0},{5,1},{6,2},{7,3},{8,12},{9,13},{10,... | collective-permute-start | bytes 55304 | tf_op jit(solution)/shard_map/ppermute | solution.py:151

commit v22 on v19

--- a/solution.py
+++ b/solution.py
@@ -142,14 +142,22 @@
     return jnp.concatenate([turned[0], turned[1], flat[2 * half :]])
 
 
-def tree_sum(value, axis):
+def tree_sum(value, axis, radix=2):
     count = lax.axis_size(axis)
     if count & (count - 1):
         return lax.psum(value, axis)
+
+    def swap(part, step):
+        return lax.ppermute(part, axis, [(i, i ^ step) for i in range(count)])
+
     step = 1
     while step < count:
-        value = value + lax.ppermute(value, axis, [(i, i ^ step) for i in range(count)])
-        step *= 2
+        if radix == 4 and 4 * step <= count:
+            value = (value + swap(value, step)) + (swap(value, 2 * step) + swap(value, 3 * step))
+            step *= 4
+        else:
+            value = value + swap(value, step)
+            step *= 2
     return value
 
 
@@ -318,7 +326,7 @@
     local_gram = complex_gram(extended, extended)
     local_ham = complex_gram(extended, extended_applied)
     summed = jnp.stack([pack_hermitian(*local_gram), pack_hermitian(*local_ham)])
-    summed = tree_sum(tree_sum(summed.reshape(-1), "row"), "col").reshape(summed.shape)
+    summed = tree_sum(tree_sum(summed.reshape(-1), "row", radix=4), "col").reshape(summed.shape)
     raw_count = 3 * band_count
     ext_count = 4 * band_count
     scale_factor = math.sqrt(height * breadth * lax.axis_size("row") * lax.axis_size("col"))

time: 46.2 us -> 45.2 us (0.978)
  waiting for transfers between devices: 17.1 us -> 15.9 us
    ppermute x5 -> x6, waiting for transfers between devices: 14.7 us -> 13.5 us  [swap(): return lax.ppermute(part, axis, [(i, i ^ step) for i in range(count)])]
    ppermute x5 -> x6, starting transfers between devices: 2.56 us -> 2.79 us  [swap(): return lax.ppermute(part, axis, [(i, i ^ step) for i in range(count)])]
  transfers between devices with their start and end apart: 9 -> 10, of which waited for: 7 -> 7; matrix products, arithmetic and copies ran while one was open for 1% -> 1% of each run, Pallas kernels for 0% -> 0%
where the time goes in v22:
time: 45.2 us; the launch traced here: 45 us
  waiting for transfers between devices  15.9 us (35%)
  starting transfers between devices  10.9 us (24%)
  Pallas kernels  5.82 us (13%)
  local copies, waits for them, and re-layouts  4.92 us (11%)
  other arithmetic  3.5 us (8%)
  between operations  2.99 us (7%)
  matrix products  0.95 us (2%)
    ppermute x6, waiting for transfers between devices, swap(): return lax.ppermute(part, axis, [(i, i ^ step) for i in range(count)])  13.5 us
    ppermute x2, starting transfers between devices, exchange_rim(): lax.ppermute(jnp.where(even, head, tail).reshape(-1), axis, [(i, (i + 1)...  6.27 us
    pallas_call x1, Pallas kernels, matrix_stage(): pl.pallas_call(functools.partial(matrix_kernel, band_count=band_count, sc...  5.82 us
    ppermute x6, starting transfers between devices, swap(): return lax.ppermute(part, axis, [(i, i ^ step) for i in range(count)])  2.79 us
    ppermute x2, waiting for transfers between devices, exchange_rim(): lax.ppermute(jnp.where(even, head, tail).reshape(-1), axis, [(i, (i + 1)...  2.36 us
    ppermute x2, starting transfers between devices, exchange_rim(): lax.ppermute(jnp.where(even, tail, head).reshape(-1), axis, [(i, i ^ 1) f...  1.83 us
    slice x1, local copies, waits for them, and re-layouts, strip_of(): directions[:, :, start:stop]  0.99 us
    slice x1, local copies, waits for them, and re-layouts, strip_of(): bands[:, :, start:stop]  0.99 us
  transfers between devices with their start and end apart: 10, of which 7 were waited for; matrix products, arithmetic and copies ran while one was open for 1% of the time, Pallas kernels for 0%

profile of v22, /device:TPU:0, one launch (start us, length us, event | category | flops | bytes accessed | tf_op | source)
XLA Modules:
  0.0 45.0 jit_solution(17024822269920138344)
XLA Ops:
  0.7 0.8 %convert_bitcast_fusion = (f32[1,8,128]{2,1,0:T(8,128)S(1)}, f32[8,128]{1,0:T(8,128)S(1)}) fusion(s32[8,128]{1,0:T(8,128)} %param.7), kind=kLoop, calls=%fused_computation.88 | loop fusion | flops 1024 | bytes 12288 | tf_op jit(solution)/shard_map/broadcast_in_dim | solution.py:301
  1.5 1.0 %fusion.33 = (f32[2,12,2,128]{3,2,1,0:T(2,128)S(1)}, f32[2,12,2,128]{3,2,1,0:T(2,128)S(1)}) fusion(f32[2,12,8,128]{3,2,1,0:T(8,128)} %param.5), kind=kLoop, calls=%fused_computation.89 | loop fusion | bytes 98304 | tf_op jit(solution)/shard_map/slice | solution.py:292
  2.5 1.0 %fusion.34 = (f32[2,12,2,128]{3,2,1,0:T(2,128)S(1)}, f32[2,12,2,128]{3,2,1,0:T(2,128)S(1)}) fusion(f32[2,12,8,128]{3,2,1,0:T(8,128)} %param.6), kind=kLoop, calls=%fused_computation.90 | loop fusion | bytes 98304 | tf_op jit(solution)/shard_map/slice | solution.py:292
  3.7 0.5 %collective-permute-start.1 = (f32[12544]{0:T(1024)S(1)}, f32[12544]{0:T(1024)S(1)}, u32[]{:S(2)}, u32[]{:S(2)}) collective-permute-start(f32[12544]{0:T(1024)S(1)} %select_n.100), channel_id=1, source_target_pairs={{0,8},{8,0},{16,24},{24,16},{1,9},{9,1},{17,25},{25,17},{2,10},{10... | collective-permute-start | bytes 150536 | tf_op jit(solution)/shard_map/ppermute | solution.py:119
  4.2 2.7 %collective-permute-start = (f32[12544]{0:T(1024)S(1)}, f32[12544]{0:T(1024)S(1)}, u32[]{:S(2)}, u32[]{:S(2)}) collective-permute-start(f32[12544]{0:T(1024)S(1)} %select_n.98), channel_id=1, source_target_pairs={{0,24},{8,16},{16,8},{24,0},{1,25},{9,17},{17,9},{25,1},{2,26},{10... | collective-permute-start | bytes 150536 | tf_op jit(solution)/shard_map/ppermute | solution.py:122
  7.0 0.6 %fusion.36 = (s32[1]{0:T(128)}, s32[1]{0:T(128)}) fusion(s32[2]{0:T(128)S(1)} %copy-done.3), kind=kLoop, calls=%fused_computation.92 | loop fusion | bytes 16 | tf_op jit(solution)/shard_map/slice | solution.py:298
  8.6 0.6 %collective-permute-done = f32[12544]{0:T(1024)S(1)} collective-permute-done((f32[12544]{0:T(1024)S(1)}, f32[12544]{0:T(1024)S(1)}, u32[]{:S(2)}, u32[]{:S(2)}) %collective-permute-start) | collective-permute-done | bytes 50208 | tf_op jit(solution)/shard_map/ppermute | solution.py:122
  9.9 1.3 %collective-permute-start.3 = (f32[1176]{0:T(1024)S(1)}, f32[1176]{0:T(1024)S(1)}, u32[]{:S(2)}, u32[]{:S(2)}) collective-permute-start(f32[1176]{0:T(1024)S(1)} %reshape.89), channel_id=1, source_target_pairs={{0,1},{1,0},{2,3},{3,2},{4,5},{5,4},{6,7},{7,6},{8,9},{9,8},{10,11... | collective-permute-start | bytes 14120 | tf_op jit(solution)/shard_map/ppermute | solution.py:119
  11.3 3.6 %collective-permute-start.2 = (f32[1176]{0:T(1024)S(1)}, f32[1176]{0:T(1024)S(1)}, u32[]{:S(2)}, u32[]{:S(2)}) collective-permute-start(f32[1176]{0:T(1024)S(1)} %reshape.88), channel_id=1, source_target_pairs={{0,7},{1,2},{2,1},{3,4},{4,3},{5,6},{6,5},{7,0},{8,15},{9,10},{10,... | collective-permute-start | bytes 14120 | tf_op jit(solution)/shard_map/ppermute | solution.py:122
  15.8 1.8 %collective-permute-done.2 = f32[1176]{0:T(1024)S(1)} collective-permute-done((f32[1176]{0:T(1024)S(1)}, f32[1176]{0:T(1024)S(1)}, u32[]{:S(2)}, u32[]{:S(2)}) %collective-permute-start.2) | collective-permute-done | bytes 4736 | tf_op jit(solution)/shard_map/ppermute | solution.py:122
  18.4 0.6 %pad_maximum_fusion.1 = f32[48,12,132]{2,1,0:T(8,128)S(1)} fusion(f32[49,12,2]{2,1,0:T(8,128)S(1)} %reshape.91, f32[49,12,2]{2,1,0:T(8,128)S(1)} %reshape.90, f32[49,2,128]{2,1,0:T(2,128)S(1)} %reshape.87, f32[49,2,128]{2,1,0:T(2,128)S(1)} %reshape.85, f32[1,8,128]{2,1,0:T(8,128)S(1)} %get-tuple-element.40, f32[48,8,128]{2,1,0:T(8,128)S(1)} %bitcast.37), kind=kLoop, calls=%fused_computation.3 | loop fusion | flops 380160 | bytes 614592 | tf_op jit(solution)/shard_map/concatenate | solution.py:135
  19.3 0.6 %broadcast_divide_fusion = (f32[2,12,10,130]{3,2,1,0:T(8,128)S(1)}, f32[2,12,10,130]{3,2,1,0:T(8,128)S(1)}, f32[2,12,10,130]{3,2,1,0:T(8,128)S(1)}, f32[2,12,10,130]{3,2,1,0:T(8,128)S(1)}) fusion(f32[10,130]{1,0:T(8,128)S(1)} %get-tuple-element.13, f32[2,24,12,132]{3,2,1,0:T(8,128)S(1)} %bitcast.31, f32[10,130]{1,0:T(8,128)S(1)} %get-tuple-element.17, ...), kind=kLoop, calls=%fused_computation.34 | loop fusion | flops 343200 | bytes 1274000 | tf_op jit(solution)/shard_map/div | solution.py:314
  20.3 0.4 fusion.7
  20.9 0.5 %convolution_bitcast_fusion.1 = f32[96,96]{1,0:T(8,128)S(1)} fusion(f32[96,8,128]{2,1,0:T(8,128)S(1)} %bitcast.32), kind=kOutput, calls=%fused_computation.2 | convolution fusion | flops 113246208 | bytes 430080 | tf_op jit(solution)/shard_map/jrc,krc->jk/dot_general | solution.py:44
  21.3 0.5 %convolution_bitcast_fusion = f32[96,96]{1,0:T(8,128)S(1)} fusion(f32[96,8,128]{2,0,1:T(8,128)S(1)} %bitcast.38, f32[96,8,128]{2,1,0:T(8,128)S(1)} %bitcast.33), kind=kOutput, calls=%fused_computation.1 | convolution fusion | flops 113246208 | bytes 823296 | tf_op jit(solution)/shard_map/jrc,krc->jk/dot_general | solution.py:44
  22.3 1.4 %collective-permute-start.5 = (f32[4608]{0:T(1024)S(1)}, f32[4608]{0:T(1024)S(1)}, u32[]{:S(2)}, u32[]{:S(2)}) collective-permute-start(f32[4608]{0:T(1024)S(1)} %reshape.95), channel_id=1, source_target_pairs={{0,16},{8,24},{16,0},{24,8},{1,17},{9,25},{17,1},{25,9},{2,18},{10... | collective-permute-start | bytes 55304 | tf_op jit(solution)/shard_map/ppermute | solution.py:151
  24.0 1.5 %collective-permute-done.6 = f32[4608]{0:T(1024)S(1)} collective-permute-done((f32[4608]{0:T(1024)S(1)}, f32[4608]{0:T(1024)S(1)}, u32[]{:S(2)}, u32[]{:S(2)}) %collective-permute-start.6) | collective-permute-done | bytes 18464 | tf_op jit(solution)/shard_map/ppermute | solution.py:151
  25.5 0.6 %collective-permute-done.5 = f32[4608]{0:T(1024)S(1)} collective-permute-done((f32[4608]{0:T(1024)S(1)}, f32[4608]{0:T(1024)S(1)}, u32[]{:S(2)}, u32[]{:S(2)}) %collective-permute-start.5) | collective-permute-done | bytes 18464 | tf_op jit(solution)/shard_map/ppermute | solution.py:151
  26.2 3.8 %collective-permute-done.7 = f32[4608]{0:T(1024)S(1)} collective-permute-done((f32[4608]{0:T(1024)S(1)}, f32[4608]{0:T(1024)S(1)}, u32[]{:S(2)}, u32[]{:S(2)}) %collective-permute-start.7) | collective-permute-done | bytes 18464 | tf_op jit(solution)/shard_map/ppermute | solution.py:151
  30.0 3.8 %collective-permute-done.8 = f32[4608]{0:T(1024)S(1)} collective-permute-done((f32[4608]{0:T(1024)S(1)}, f32[4608]{0:T(1024)S(1)}, u32[]{:S(2)}, u32[]{:S(2)}) %collective-permute-start.8) | collective-permute-done | bytes 18464 | tf_op jit(solution)/shard_map/ppermute | solution.py:151
  33.8 0.8 %collective-permute-start.9 = (f32[4608]{0:T(1024)S(1)}, f32[4608]{0:T(1024)S(1)}, u32[]{:S(2)}, u32[]{:S(2)}) collective-permute-start(f32[4608]{0:T(1024)S(1)} %add.135), channel_id=1, source_target_pairs={{0,4},{1,5},{2,6},{3,7},{4,0},{5,1},{6,2},{7,3},{8,12},{9,13},{10,... | collective-permute-start | bytes 55304 | tf_op jit(solution)/shard_map/ppermute | solution.py:151
  34.6 3.9 %collective-permute-done.9 = f32[4608]{0:T(1024)S(1)} collective-permute-done((f32[4608]{0:T(1024)S(1)}, f32[4608]{0:T(1024)S(1)}, u32[]{:S(2)}, u32[]{:S(2)}) %collective-permute-start.9) | collective-permute-done | bytes 18464 | tf_op jit(solution)/shard_map/ppermute | solution.py:151
  38.5 0.7 %reshape.96.packed_ref = f32[2,48,48]{2,1,0:T(8,128)} reshape(f32[4608]{0:T(1024)S(1)} %add.136) | data formatting | bytes 36864 | tf_op jit(solution)/shard_map/reshape | solution.py:329
  39.2 5.8 %shard_map.68 = (f32[72,8,128]{2,1,0:T(8,128)}, f32[36,2,36]{2,1,0:T(2,128)}) custom-call(f32[2,48,48]{2,1,0:T(8,128)} %reshape.96.packed_ref, f32[96,8,128]{2,1,0:T(8,128)} %bitcast.34), custom_call_target="tpu_custom_call" | custom-call | tf_op jit(solution)/shard_map/pallas_call | solution.py:262
  (74 shorter events, 3.5 us)
Async XLA Ops:
  0.6 6.3 %copy-start.2 = (f32[2,12,8,128]{3,2,1,0:T(8,128)S(1)}, f32[2,12,8,128]{3,2,1,0:T(8,128)}, u32[]{:S(2)}) copy-start(f32[2,12,8,128]{3,2,1,0:T(8,128)} %param.5) | copy-start | bytes 294916
  0.6 6.3 %copy-start.1 = (f32[2,12,8,128]{3,2,1,0:T(8,128)S(1)}, f32[2,12,8,128]{3,2,1,0:T(8,128)}, u32[]{:S(2)}) copy-start(f32[2,12,8,128]{3,2,1,0:T(8,128)} %param.6) | copy-start | bytes 294916
  0.7 6.3 %copy-start.4 = (f32[8]{0:T(128)S(1)}, f32[8]{0:T(128)}, u32[]{:S(2)}) copy-start(f32[8]{0:T(128)} %param.8) | copy-start | bytes 100
  0.7 6.3 %copy-start.3 = (s32[2]{0:T(128)S(1)}, s32[2]{0:T(128)}, u32[]{:S(2)}) copy-start(s32[2]{0:T(128)} %param.9) | copy-start | bytes 28
  3.7 4.9 %collective-permute-start.1 = (f32[12544]{0:T(1024)S(1)}, f32[12544]{0:T(1024)S(1)}, u32[]{:S(2)}, u32[]{:S(2)}) collective-permute-start(f32[12544]{0:T(1024)S(1)} %select_n.100), channel_id=1, source_target_pairs={{0,8},{8,0},{16,24},{24,16},{1,9},{9,1},{17,25},{25,17},{2,10},{10... | collective-permute-start | bytes 150536 | tf_op jit(solution)/shard_map/ppermute | solution.py:119
  4.2 4.9 %collective-permute-start = (f32[12544]{0:T(1024)S(1)}, f32[12544]{0:T(1024)S(1)}, u32[]{:S(2)}, u32[]{:S(2)}) collective-permute-start(f32[12544]{0:T(1024)S(1)} %select_n.98), channel_id=1, source_target_pairs={{0,24},{8,16},{16,8},{24,0},{1,25},{9,17},{17,9},{25,1},{2,26},{10... | collective-permute-start | bytes 150536 | tf_op jit(solution)/shard_map/ppermute | solution.py:122
  9.9 5.9 %collective-permute-start.3 = (f32[1176]{0:T(1024)S(1)}, f32[1176]{0:T(1024)S(1)}, u32[]{:S(2)}, u32[]{:S(2)}) collective-permute-start(f32[1176]{0:T(1024)S(1)} %reshape.89), channel_id=1, source_target_pairs={{0,1},{1,0},{2,3},{3,2},{4,5},{5,4},{6,7},{7,6},{8,9},{9,8},{10,11... | collective-permute-start | bytes 14120 | tf_op jit(solution)/shard_map/ppermute | solution.py:119
  11.3 6.3 %collective-permute-start.2 = (f32[1176]{0:T(1024)S(1)}, f32[1176]{0:T(1024)S(1)}, u32[]{:S(2)}, u32[]{:S(2)}) collective-permute-start(f32[1176]{0:T(1024)S(1)} %reshape.88), channel_id=1, source_target_pairs={{0,7},{1,2},{2,1},{3,4},{4,3},{5,6},{6,5},{7,0},{8,15},{9,10},{10,... | collective-permute-start | bytes 14120 | tf_op jit(solution)/shard_map/ppermute | solution.py:122
  20.8 18.3 %copy-start = (f32[2,48,8,128]{3,2,1,0:T(8,128)}, f32[2,48,8,128]{3,2,1,0:T(8,128)S(1)}, u32[]{:S(2)}) copy-start(f32[2,48,8,128]{3,2,1,0:T(8,128)S(1)} %pad_maximum_fusion.7) | copy-start | bytes 1179652
  22.1 3.4 %collective-permute-start.6 = (f32[4608]{0:T(1024)S(1)}, f32[4608]{0:T(1024)S(1)}, u32[]{:S(2)}, u32[]{:S(2)}) collective-permute-start(f32[4608]{0:T(1024)S(1)} %reshape.95), channel_id=1, source_target_pairs={{0,24},{8,16},{16,8},{24,0},{1,25},{9,17},{17,9},{25,1},{2,26},{10... | collective-permute-start | bytes 55304 | tf_op jit(solution)/shard_map/ppermute | solution.py:151
  22.3 3.8 %collective-permute-start.5 = (f32[4608]{0:T(1024)S(1)}, f32[4608]{0:T(1024)S(1)}, u32[]{:S(2)}, u32[]{:S(2)}) collective-permute-start(f32[4608]{0:T(1024)S(1)} %reshape.95), channel_id=1, source_target_pairs={{0,16},{8,24},{16,0},{24,8},{1,17},{9,25},{17,1},{25,9},{2,18},{10... | collective-permute-start | bytes 55304 | tf_op jit(solution)/shard_map/ppermute | solution.py:151
  23.8 2.4 %collective-permute-start.4 = (f32[4608]{0:T(1024)S(1)}, f32[4608]{0:T(1024)S(1)}, u32[]{:S(2)}, u32[]{:S(2)}) collective-permute-start(f32[4608]{0:T(1024)S(1)} %reshape.95), channel_id=1, source_target_pairs={{0,8},{8,0},{16,24},{24,16},{1,9},{9,1},{17,25},{25,17},{2,10},{10... | collective-permute-start | bytes 55304 | tf_op jit(solution)/shard_map/ppermute | solution.py:151
  26.1 3.8 %collective-permute-start.7 = (f32[4608]{0:T(1024)S(1)}, f32[4608]{0:T(1024)S(1)}, u32[]{:S(2)}, u32[]{:S(2)}) collective-permute-start(f32[4608]{0:T(1024)S(1)} %add_add_fusion), channel_id=1, source_target_pairs={{0,1},{1,0},{2,3},{3,2},{4,5},{5,4},{6,7},{7,6},{8,9},{9,8},{10,11... | collective-permute-start | bytes 55304 | tf_op jit(solution)/shard_map/ppermute | solution.py:151
  30.0 3.8 %collective-permute-start.8 = (f32[4608]{0:T(1024)S(1)}, f32[4608]{0:T(1024)S(1)}, u32[]{:S(2)}, u32[]{:S(2)}) collective-permute-start(f32[4608]{0:T(1024)S(1)} %add.134), channel_id=1, source_target_pairs={{0,2},{1,3},{2,0},{3,1},{4,6},{5,7},{6,4},{7,5},{8,10},{9,11},{10,... | collective-permute-start | bytes 55304 | tf_op jit(solution)/shard_map/ppermute | solution.py:151
  33.8 4.7 %collective-permute-start.9 = (f32[4608]{0:T(1024)S(1)}, f32[4608]{0:T(1024)S(1)}, u32[]{:S(2)}, u32[]{:S(2)}) collective-permute-start(f32[4608]{0:T(1024)S(1)} %add.135), channel_id=1, source_target_pairs={{0,4},{1,5},{2,6},{3,7},{4,0},{5,1},{6,2},{7,3},{8,12},{9,13},{10,... | collective-permute-start | bytes 55304 | tf_op jit(solution)/shard_map/ppermute | solution.py:151

commit v23 on v22

--- a/solution.py
+++ b/solution.py
@@ -326,7 +326,7 @@
     local_gram = complex_gram(extended, extended)
     local_ham = complex_gram(extended, extended_applied)
     summed = jnp.stack([pack_hermitian(*local_gram), pack_hermitian(*local_ham)])
-    summed = tree_sum(tree_sum(summed.reshape(-1), "row", radix=4), "col").reshape(summed.shape)
+    summed = tree_sum(tree_sum(summed.reshape(-1), "row", radix=4), "col", radix=4).reshape(summed.shape)
     raw_count = 3 * band_count
     ext_count = 4 * band_count
     scale_factor = math.sqrt(height * breadth * lax.axis_size("row") * lax.axis_size("col"))

time: 45.2 us -> 43 us (0.951)
  waiting for transfers between devices: 15.9 us -> 8.24 us
  starting transfers between devices: 10.9 us -> 16.3 us
    ppermute x6 -> x7, waiting for transfers between devices: 13.5 us -> 5.87 us  [swap(): return lax.ppermute(part, axis, [(i, i ^ step) for i in range(count)])]
    ppermute x6 -> x7, starting transfers between devices: 2.79 us -> 8.21 us  [swap(): return lax.ppermute(part, axis, [(i, i ^ step) for i in range(count)])]
  transfers between devices with their start and end apart: 10 -> 11, of which waited for: 7 -> 7; matrix products, arithmetic and copies ran while one was open for 1% -> 2% of each run, Pallas kernels for 0% -> 0%
where the time goes in v23:
time: 43 us; the launch traced here: 42.7 us
  starting transfers between devices  16.3 us (38%)
  waiting for transfers between devices  8.24 us (19%)
  Pallas kernels  5.82 us (14%)
  local copies, waits for them, and re-layouts  4.93 us (11%)
  other arithmetic  3.5 us (8%)
  between operations  2.99 us (7%)
  matrix products  0.95 us (2%)
    ppermute x7, starting transfers between devices, swap(): return lax.ppermute(part, axis, [(i, i ^ step) for i in range(count)])  8.21 us
    ppermute x2, starting transfers between devices, exchange_rim(): lax.ppermute(jnp.where(even, head, tail).reshape(-1), axis, [(i, (i + 1)...  6.27 us
    ppermute x7, waiting for transfers between devices, swap(): return lax.ppermute(part, axis, [(i, i ^ step) for i in range(count)])  5.87 us
    pallas_call x1, Pallas kernels, matrix_stage(): pl.pallas_call(functools.partial(matrix_kernel, band_count=band_count, sc...  5.82 us
    ppermute x2, waiting for transfers between devices, exchange_rim(): lax.ppermute(jnp.where(even, head, tail).reshape(-1), axis, [(i, (i + 1)...  2.36 us
    ppermute x2, starting transfers between devices, exchange_rim(): lax.ppermute(jnp.where(even, tail, head).reshape(-1), axis, [(i, i ^ 1) f...  1.83 us
    slice x1, local copies, waits for them, and re-layouts, strip_of(): directions[:, :, start:stop]  0.99 us
    slice x1, local copies, waits for them, and re-layouts, strip_of(): bands[:, :, start:stop]  0.99 us
  transfers between devices with their start and end apart: 11, of which 7 were waited for; matrix products, arithmetic and copies ran while one was open for 2% of the time, Pallas kernels for 0%

profile of v23, /device:TPU:0, one launch (start us, length us, event | category | flops | bytes accessed | tf_op | source)
XLA Modules:
  0.0 42.7 jit_solution(7770127816066426687)
XLA Ops:
  0.7 0.8 %convert_bitcast_fusion = (f32[1,8,128]{2,1,0:T(8,128)S(1)}, f32[8,128]{1,0:T(8,128)S(1)}) fusion(s32[8,128]{1,0:T(8,128)} %param.7), kind=kLoop, calls=%fused_computation.89 | loop fusion | flops 1024 | bytes 12288 | tf_op jit(solution)/shard_map/broadcast_in_dim | solution.py:301
  1.5 1.0 %fusion.33 = (f32[2,12,2,128]{3,2,1,0:T(2,128)S(1)}, f32[2,12,2,128]{3,2,1,0:T(2,128)S(1)}) fusion(f32[2,12,8,128]{3,2,1,0:T(8,128)} %param.5), kind=kLoop, calls=%fused_computation.90 | loop fusion | bytes 98304 | tf_op jit(solution)/shard_map/slice | solution.py:292
  2.5 1.0 %fusion.34 = (f32[2,12,2,128]{3,2,1,0:T(2,128)S(1)}, f32[2,12,2,128]{3,2,1,0:T(2,128)S(1)}) fusion(f32[2,12,8,128]{3,2,1,0:T(8,128)} %param.6), kind=kLoop, calls=%fused_computation.91 | loop fusion | bytes 98304 | tf_op jit(solution)/shard_map/slice | solution.py:292
  3.7 0.5 %collective-permute-start.1 = (f32[12544]{0:T(1024)S(1)}, f32[12544]{0:T(1024)S(1)}, u32[]{:S(2)}, u32[]{:S(2)}) collective-permute-start(f32[12544]{0:T(1024)S(1)} %select_n.100), channel_id=1, source_target_pairs={{0,8},{8,0},{16,24},{24,16},{1,9},{9,1},{17,25},{25,17},{2,10},{10... | collective-permute-start | bytes 150536 | tf_op jit(solution)/shard_map/ppermute | solution.py:119
  4.2 2.7 %collective-permute-start = (f32[12544]{0:T(1024)S(1)}, f32[12544]{0:T(1024)S(1)}, u32[]{:S(2)}, u32[]{:S(2)}) collective-permute-start(f32[12544]{0:T(1024)S(1)} %select_n.98), channel_id=1, source_target_pairs={{0,24},{8,16},{16,8},{24,0},{1,25},{9,17},{17,9},{25,1},{2,26},{10... | collective-permute-start | bytes 150536 | tf_op jit(solution)/shard_map/ppermute | solution.py:122
  7.0 0.6 %fusion.36 = (s32[1]{0:T(128)}, s32[1]{0:T(128)}) fusion(s32[2]{0:T(128)S(1)} %copy-done.3), kind=kLoop, calls=%fused_computation.93 | loop fusion | bytes 16 | tf_op jit(solution)/shard_map/slice | solution.py:298
  8.6 0.6 %collective-permute-done = f32[12544]{0:T(1024)S(1)} collective-permute-done((f32[12544]{0:T(1024)S(1)}, f32[12544]{0:T(1024)S(1)}, u32[]{:S(2)}, u32[]{:S(2)}) %collective-permute-start) | collective-permute-done | bytes 50208 | tf_op jit(solution)/shard_map/ppermute | solution.py:122
  9.9 1.3 %collective-permute-start.3 = (f32[1176]{0:T(1024)S(1)}, f32[1176]{0:T(1024)S(1)}, u32[]{:S(2)}, u32[]{:S(2)}) collective-permute-start(f32[1176]{0:T(1024)S(1)} %reshape.89), channel_id=1, source_target_pairs={{0,1},{1,0},{2,3},{3,2},{4,5},{5,4},{6,7},{7,6},{8,9},{9,8},{10,11... | collective-permute-start | bytes 14120 | tf_op jit(solution)/shard_map/ppermute | solution.py:119
  11.3 3.6 %collective-permute-start.2 = (f32[1176]{0:T(1024)S(1)}, f32[1176]{0:T(1024)S(1)}, u32[]{:S(2)}, u32[]{:S(2)}) collective-permute-start(f32[1176]{0:T(1024)S(1)} %reshape.88), channel_id=1, source_target_pairs={{0,7},{1,2},{2,1},{3,4},{4,3},{5,6},{6,5},{7,0},{8,15},{9,10},{10,... | collective-permute-start | bytes 14120 | tf_op jit(solution)/shard_map/ppermute | solution.py:122
  15.8 1.8 %collective-permute-done.2 = f32[1176]{0:T(1024)S(1)} collective-permute-done((f32[1176]{0:T(1024)S(1)}, f32[1176]{0:T(1024)S(1)}, u32[]{:S(2)}, u32[]{:S(2)}) %collective-permute-start.2) | collective-permute-done | bytes 4736 | tf_op jit(solution)/shard_map/ppermute | solution.py:122
  18.4 0.6 %pad_maximum_fusion.1 = f32[48,12,132]{2,1,0:T(8,128)S(1)} fusion(f32[49,12,2]{2,1,0:T(8,128)S(1)} %reshape.91, f32[49,12,2]{2,1,0:T(8,128)S(1)} %reshape.90, f32[49,2,128]{2,1,0:T(2,128)S(1)} %reshape.87, f32[49,2,128]{2,1,0:T(2,128)S(1)} %reshape.85, f32[1,8,128]{2,1,0:T(8,128)S(1)} %get-tuple-element.40, f32[48,8,128]{2,1,0:T(8,128)S(1)} %bitcast.37), kind=kLoop, calls=%fused_computation.3 | loop fusion | flops 380160 | bytes 614592 | tf_op jit(solution)/shard_map/concatenate | solution.py:135
  19.3 0.6 %broadcast_divide_fusion = (f32[2,12,10,130]{3,2,1,0:T(8,128)S(1)}, f32[2,12,10,130]{3,2,1,0:T(8,128)S(1)}, f32[2,12,10,130]{3,2,1,0:T(8,128)S(1)}, f32[2,12,10,130]{3,2,1,0:T(8,128)S(1)}) fusion(f32[10,130]{1,0:T(8,128)S(1)} %get-tuple-element.13, f32[2,24,12,132]{3,2,1,0:T(8,128)S(1)} %bitcast.31, f32[10,130]{1,0:T(8,128)S(1)} %get-tuple-element.17, ...), kind=kLoop, calls=%fused_computation.34 | loop fusion | flops 343200 | bytes 1274000 | tf_op jit(solution)/shard_map/div | solution.py:314
  20.9 0.5 %convolution_bitcast_fusion.1 = f32[96,96]{1,0:T(8,128)S(1)} fusion(f32[96,8,128]{2,1,0:T(8,128)S(1)} %bitcast.32), kind=kOutput, calls=%fused_computation.2 | convolution fusion | flops 113246208 | bytes 430080 | tf_op jit(solution)/shard_map/jrc,krc->jk/dot_general | solution.py:44
  21.3 0.5 %convolution_bitcast_fusion = f32[96,96]{1,0:T(8,128)S(1)} fusion(f32[96,8,128]{2,0,1:T(8,128)S(1)} %bitcast.38, f32[96,8,128]{2,1,0:T(8,128)S(1)} %bitcast.33), kind=kOutput, calls=%fused_computation.1 | convolution fusion | flops 113246208 | bytes 823296 | tf_op jit(solution)/shard_map/jrc,krc->jk/dot_general | solution.py:44
  22.3 1.4 %collective-permute-start.5 = (f32[4608]{0:T(1024)S(1)}, f32[4608]{0:T(1024)S(1)}, u32[]{:S(2)}, u32[]{:S(2)}) collective-permute-start(f32[4608]{0:T(1024)S(1)} %reshape.95), channel_id=1, source_target_pairs={{0,16},{8,24},{16,0},{24,8},{1,17},{9,25},{17,1},{25,9},{2,18},{10... | collective-permute-start | bytes 55304 | tf_op jit(solution)/shard_map/ppermute | solution.py:151
  24.0 1.5 %collective-permute-done.6 = f32[4608]{0:T(1024)S(1)} collective-permute-done((f32[4608]{0:T(1024)S(1)}, f32[4608]{0:T(1024)S(1)}, u32[]{:S(2)}, u32[]{:S(2)}) %collective-permute-start.6) | collective-permute-done | bytes 18464 | tf_op jit(solution)/shard_map/ppermute | solution.py:151
  25.5 0.6 %collective-permute-done.5 = f32[4608]{0:T(1024)S(1)} collective-permute-done((f32[4608]{0:T(1024)S(1)}, f32[4608]{0:T(1024)S(1)}, u32[]{:S(2)}, u32[]{:S(2)}) %collective-permute-start.5) | collective-permute-done | bytes 18464 | tf_op jit(solution)/shard_map/ppermute | solution.py:151
  26.5 3.2 %collective-permute-start.7 = (f32[4608]{0:T(1024)S(1)}, f32[4608]{0:T(1024)S(1)}, u32[]{:S(2)}, u32[]{:S(2)}) collective-permute-start(f32[4608]{0:T(1024)S(1)} %add_add_fusion.1), channel_id=1, source_target_pairs={{0,1},{1,0},{2,3},{3,2},{4,5},{5,4},{6,7},{7,6},{8,9},{9,8},{10,11... | collective-permute-start | bytes 55304 | tf_op jit(solution)/shard_map/ppermute | solution.py:151
  29.7 1.2 %collective-permute-done.9 = f32[4608]{0:T(1024)S(1)} collective-permute-done((f32[4608]{0:T(1024)S(1)}, f32[4608]{0:T(1024)S(1)}, u32[]{:S(2)}, u32[]{:S(2)}) %collective-permute-start.9) | collective-permute-done | bytes 18464 | tf_op jit(solution)/shard_map/ppermute | solution.py:151
  30.9 0.6 %collective-permute-done.7 = f32[4608]{0:T(1024)S(1)} collective-permute-done((f32[4608]{0:T(1024)S(1)}, f32[4608]{0:T(1024)S(1)}, u32[]{:S(2)}, u32[]{:S(2)}) %collective-permute-start.7) | collective-permute-done | bytes 18464 | tf_op jit(solution)/shard_map/ppermute | solution.py:151
  31.5 2.7 %collective-permute-start.10 = (f32[4608]{0:T(1024)S(1)}, f32[4608]{0:T(1024)S(1)}, u32[]{:S(2)}, u32[]{:S(2)}) collective-permute-start(f32[4608]{0:T(1024)S(1)} %add_add_fusion), channel_id=1, source_target_pairs={{0,4},{1,5},{2,6},{3,7},{4,0},{5,1},{6,2},{7,3},{8,12},{9,13},{10,... | collective-permute-start | bytes 55304 | tf_op jit(solution)/shard_map/ppermute | solution.py:151
  34.2 2.0 %collective-permute-done.10 = f32[4608]{0:T(1024)S(1)} collective-permute-done((f32[4608]{0:T(1024)S(1)}, f32[4608]{0:T(1024)S(1)}, u32[]{:S(2)}, u32[]{:S(2)}) %collective-permute-start.10) | collective-permute-done | bytes 18464 | tf_op jit(solution)/shard_map/ppermute | solution.py:151
  36.2 0.7 %reshape.96.packed_ref = f32[2,48,48]{2,1,0:T(8,128)} reshape(f32[4608]{0:T(1024)S(1)} %add.140) | data formatting | bytes 36864 | tf_op jit(solution)/shard_map/reshape | solution.py:329
  36.9 5.8 %shard_map.68 = (f32[72,8,128]{2,1,0:T(8,128)}, f32[36,2,36]{2,1,0:T(2,128)}) custom-call(f32[2,48,48]{2,1,0:T(8,128)} %reshape.96.packed_ref, f32[96,8,128]{2,1,0:T(8,128)} %bitcast.34), custom_call_target="tpu_custom_call" | custom-call | tf_op jit(solution)/shard_map/pallas_call | solution.py:262
  (75 shorter events, 4.2 us)
Async XLA Ops:
  0.6 6.3 %copy-start.2 = (f32[2,12,8,128]{3,2,1,0:T(8,128)S(1)}, f32[2,12,8,128]{3,2,1,0:T(8,128)}, u32[]{:S(2)}) copy-start(f32[2,12,8,128]{3,2,1,0:T(8,128)} %param.5) | copy-start | bytes 294916
  0.6 6.3 %copy-start.1 = (f32[2,12,8,128]{3,2,1,0:T(8,128)S(1)}, f32[2,12,8,128]{3,2,1,0:T(8,128)}, u32[]{:S(2)}) copy-start(f32[2,12,8,128]{3,2,1,0:T(8,128)} %param.6) | copy-start | bytes 294916
  0.7 6.3 %copy-start.4 = (f32[8]{0:T(128)S(1)}, f32[8]{0:T(128)}, u32[]{:S(2)}) copy-start(f32[8]{0:T(128)} %param.8) | copy-start | bytes 100
  0.7 6.3 %copy-start.3 = (s32[2]{0:T(128)S(1)}, s32[2]{0:T(128)}, u32[]{:S(2)}) copy-start(s32[2]{0:T(128)} %param.9) | copy-start | bytes 28
  3.7 4.9 %collective-permute-start.1 = (f32[12544]{0:T(1024)S(1)}, f32[12544]{0:T(1024)S(1)}, u32[]{:S(2)}, u32[]{:S(2)}) collective-permute-start(f32[12544]{0:T(1024)S(1)} %select_n.100), channel_id=1, source_target_pairs={{0,8},{8,0},{16,24},{24,16},{1,9},{9,1},{17,25},{25,17},{2,10},{10... | collective-permute-start | bytes 150536 | tf_op jit(solution)/shard_map/ppermute | solution.py:119
  4.2 4.9 %collective-permute-start = (f32[12544]{0:T(1024)S(1)}, f32[12544]{0:T(1024)S(1)}, u32[]{:S(2)}, u32[]{:S(2)}) collective-permute-start(f32[12544]{0:T(1024)S(1)} %select_n.98), channel_id=1, source_target_pairs={{0,24},{8,16},{16,8},{24,0},{1,25},{9,17},{17,9},{25,1},{2,26},{10... | collective-permute-start | bytes 150536 | tf_op jit(solution)/shard_map/ppermute | solution.py:122
  9.9 5.9 %collective-permute-start.3 = (f32[1176]{0:T(1024)S(1)}, f32[1176]{0:T(1024)S(1)}, u32[]{:S(2)}, u32[]{:S(2)}) collective-permute-start(f32[1176]{0:T(1024)S(1)} %reshape.89), channel_id=1, source_target_pairs={{0,1},{1,0},{2,3},{3,2},{4,5},{5,4},{6,7},{7,6},{8,9},{9,8},{10,11... | collective-permute-start | bytes 14120 | tf_op jit(solution)/shard_map/ppermute | solution.py:119
  11.3 6.3 %collective-permute-start.2 = (f32[1176]{0:T(1024)S(1)}, f32[1176]{0:T(1024)S(1)}, u32[]{:S(2)}, u32[]{:S(2)}) collective-permute-start(f32[1176]{0:T(1024)S(1)} %reshape.88), channel_id=1, source_target_pairs={{0,7},{1,2},{2,1},{3,4},{4,3},{5,6},{6,5},{7,0},{8,15},{9,10},{10,... | collective-permute-start | bytes 14120 | tf_op jit(solution)/shard_map/ppermute | solution.py:122
  20.8 16.1 %copy-start = (f32[2,48,8,128]{3,2,1,0:T(8,128)}, f32[2,48,8,128]{3,2,1,0:T(8,128)S(1)}, u32[]{:S(2)}) copy-start(f32[2,48,8,128]{3,2,1,0:T(8,128)S(1)} %pad_maximum_fusion.7) | copy-start | bytes 1179652
  22.1 3.4 %collective-permute-start.6 = (f32[4608]{0:T(1024)S(1)}, f32[4608]{0:T(1024)S(1)}, u32[]{:S(2)}, u32[]{:S(2)}) collective-permute-start(f32[4608]{0:T(1024)S(1)} %reshape.95), channel_id=1, source_target_pairs={{0,24},{8,16},{16,8},{24,0},{1,25},{9,17},{17,9},{25,1},{2,26},{10... | collective-permute-start | bytes 55304 | tf_op jit(solution)/shard_map/ppermute | solution.py:151
  22.3 3.8 %collective-permute-start.5 = (f32[4608]{0:T(1024)S(1)}, f32[4608]{0:T(1024)S(1)}, u32[]{:S(2)}, u32[]{:S(2)}) collective-permute-start(f32[4608]{0:T(1024)S(1)} %reshape.95), channel_id=1, source_target_pairs={{0,16},{8,24},{16,0},{24,8},{1,17},{9,25},{17,1},{25,9},{2,18},{10... | collective-permute-start | bytes 55304 | tf_op jit(solution)/shard_map/ppermute | solution.py:151
  23.8 2.4 %collective-permute-start.4 = (f32[4608]{0:T(1024)S(1)}, f32[4608]{0:T(1024)S(1)}, u32[]{:S(2)}, u32[]{:S(2)}) collective-permute-start(f32[4608]{0:T(1024)S(1)} %reshape.95), channel_id=1, source_target_pairs={{0,8},{8,0},{16,24},{24,16},{1,9},{9,1},{17,25},{25,17},{2,10},{10... | collective-permute-start | bytes 55304 | tf_op jit(solution)/shard_map/ppermute | solution.py:151
  26.1 4.7 %collective-permute-start.9 = (f32[4608]{0:T(1024)S(1)}, f32[4608]{0:T(1024)S(1)}, u32[]{:S(2)}, u32[]{:S(2)}) collective-permute-start(f32[4608]{0:T(1024)S(1)} %add_add_fusion.1), channel_id=1, source_target_pairs={{0,3},{1,2},{2,1},{3,0},{4,7},{5,6},{6,5},{7,4},{8,11},{9,10},{10,... | collective-permute-start | bytes 55304 | tf_op jit(solution)/shard_map/ppermute | solution.py:151
  26.2 4.7 %collective-permute-start.8 = (f32[4608]{0:T(1024)S(1)}, f32[4608]{0:T(1024)S(1)}, u32[]{:S(2)}, u32[]{:S(2)}) collective-permute-start(f32[4608]{0:T(1024)S(1)} %add_add_fusion.1), channel_id=1, source_target_pairs={{0,2},{1,3},{2,0},{3,1},{4,6},{5,7},{6,4},{7,5},{8,10},{9,11},{10,... | collective-permute-start | bytes 55304 | tf_op jit(solution)/shard_map/ppermute | solution.py:151
  26.5 4.9 %collective-permute-start.7 = (f32[4608]{0:T(1024)S(1)}, f32[4608]{0:T(1024)S(1)}, u32[]{:S(2)}, u32[]{:S(2)}) collective-permute-start(f32[4608]{0:T(1024)S(1)} %add_add_fusion.1), channel_id=1, source_target_pairs={{0,1},{1,0},{2,3},{3,2},{4,5},{5,4},{6,7},{7,6},{8,9},{9,8},{10,11... | collective-permute-start | bytes 55304 | tf_op jit(solution)/shard_map/ppermute | solution.py:151
  31.5 4.7 %collective-permute-start.10 = (f32[4608]{0:T(1024)S(1)}, f32[4608]{0:T(1024)S(1)}, u32[]{:S(2)}, u32[]{:S(2)}) collective-permute-start(f32[4608]{0:T(1024)S(1)} %add_add_fusion), channel_id=1, source_target_pairs={{0,4},{1,5},{2,6},{3,7},{4,0},{5,1},{6,2},{7,3},{8,12},{9,13},{10,... | collective-permute-start | bytes 55304 | tf_op jit(solution)/shard_map/ppermute | solution.py:151

commit v24 on v23

--- a/solution.py
+++ b/solution.py
@@ -142,7 +142,7 @@
     return jnp.concatenate([turned[0], turned[1], flat[2 * half :]])
 
 
-def tree_sum(value, axis, radix=2):
+def tree_sum(value, axis, radix=2, late=False):
     count = lax.axis_size(axis)
     if count & (count - 1):
         return lax.psum(value, axis)
@@ -152,7 +152,7 @@
 
     step = 1
     while step < count:
-        if radix == 4 and 4 * step <= count:
+        if radix == 4 and 4 * step <= count and not (late and step == 1):
             value = (value + swap(value, step)) + (swap(value, 2 * step) + swap(value, 3 * step))
             step *= 4
         else:
@@ -326,7 +326,7 @@
     local_gram = complex_gram(extended, extended)
     local_ham = complex_gram(extended, extended_applied)
     summed = jnp.stack([pack_hermitian(*local_gram), pack_hermitian(*local_ham)])
-    summed = tree_sum(tree_sum(summed.reshape(-1), "row", radix=4), "col", radix=4).reshape(summed.shape)
+    summed = tree_sum(tree_sum(summed.reshape(-1), "row", radix=4), "col", radix=4, late=True).reshape(summed.shape)
     raw_count = 3 * band_count
     ext_count = 4 * band_count
     scale_factor = math.sqrt(height * breadth * lax.axis_size("row") * lax.axis_size("col"))

time: 43 us -> 43.6 us (1.014)
  waiting for transfers between devices: 8.24 us -> 10.7 us
  starting transfers between devices: 16.3 us -> 14.5 us
    ppermute x7, waiting for transfers between devices: 5.87 us -> 8.29 us  [swap(): return lax.ppermute(part, axis, [(i, i ^ step) for i in range(count)])]
    ppermute x7, starting transfers between devices: 8.21 us -> 6.38 us  [swap(): return lax.ppermute(part, axis, [(i, i ^ step) for i in range(count)])]
where the time goes in v24:
time: 43.6 us; the launch traced here: 43.3 us
  starting transfers between devices  14.5 us (33%)
  waiting for transfers between devices  10.7 us (25%)
  Pallas kernels  5.83 us (13%)
  local copies, waits for them, and re-layouts  4.92 us (11%)
  other arithmetic  3.5 us (8%)
  between operations  2.99 us (7%)
  matrix products  0.95 us (2%)
    ppermute x7, waiting for transfers between devices, swap(): return lax.ppermute(part, axis, [(i, i ^ step) for i in range(count)])  8.29 us
    ppermute x7, starting transfers between devices, swap(): return lax.ppermute(part, axis, [(i, i ^ step) for i in range(count)])  6.38 us
    ppermute x2, starting transfers between devices, exchange_rim(): lax.ppermute(jnp.where(even, head, tail).reshape(-1), axis, [(i, (i + 1)...  6.27 us
    pallas_call x1, Pallas kernels, matrix_stage(): pl.pallas_call(functools.partial(matrix_kernel, band_count=band_count, sc...  5.83 us
    ppermute x2, waiting for transfers between devices, exchange_rim(): lax.ppermute(jnp.where(even, head, tail).reshape(-1), axis, [(i, (i + 1)...  2.36 us
    ppermute x2, starting transfers between devices, exchange_rim(): lax.ppermute(jnp.where(even, tail, head).reshape(-1), axis, [(i, i ^ 1) f...  1.83 us
    slice x1, local copies, waits for them, and re-layouts, strip_of(): directions[:, :, start:stop]  0.99 us
    slice x1, local copies, waits for them, and re-layouts, strip_of(): bands[:, :, start:stop]  0.99 us
  transfers between devices with their start and end apart: 11, of which 7 were waited for; matrix products, arithmetic and copies ran while one was open for 2% of the time, Pallas kernels for 0%

profile of v24, /device:TPU:0, one launch (start us, length us, event | category | flops | bytes accessed | tf_op | source)
XLA Modules:
  0.0 43.3 jit_solution(1513378898020624528)
XLA Ops:
  0.7 0.8 %convert_bitcast_fusion = (f32[1,8,128]{2,1,0:T(8,128)S(1)}, f32[8,128]{1,0:T(8,128)S(1)}) fusion(s32[8,128]{1,0:T(8,128)} %param.7), kind=kLoop, calls=%fused_computation.89 | loop fusion | flops 1024 | bytes 12288 | tf_op jit(solution)/shard_map/broadcast_in_dim | solution.py:301
  1.5 1.0 %fusion.33 = (f32[2,12,2,128]{3,2,1,0:T(2,128)S(1)}, f32[2,12,2,128]{3,2,1,0:T(2,128)S(1)}) fusion(f32[2,12,8,128]{3,2,1,0:T(8,128)} %param.5), kind=kLoop, calls=%fused_computation.90 | loop fusion | bytes 98304 | tf_op jit(solution)/shard_map/slice | solution.py:292
  2.5 1.0 %fusion.34 = (f32[2,12,2,128]{3,2,1,0:T(2,128)S(1)}, f32[2,12,2,128]{3,2,1,0:T(2,128)S(1)}) fusion(f32[2,12,8,128]{3,2,1,0:T(8,128)} %param.6), kind=kLoop, calls=%fused_computation.91 | loop fusion | bytes 98304 | tf_op jit(solution)/shard_map/slice | solution.py:292
  3.7 0.5 %collective-permute-start.1 = (f32[12544]{0:T(1024)S(1)}, f32[12544]{0:T(1024)S(1)}, u32[]{:S(2)}, u32[]{:S(2)}) collective-permute-start(f32[12544]{0:T(1024)S(1)} %select_n.100), channel_id=1, source_target_pairs={{0,8},{8,0},{16,24},{24,16},{1,9},{9,1},{17,25},{25,17},{2,10},{10... | collective-permute-start | bytes 150536 | tf_op jit(solution)/shard_map/ppermute | solution.py:119
  4.2 2.7 %collective-permute-start = (f32[12544]{0:T(1024)S(1)}, f32[12544]{0:T(1024)S(1)}, u32[]{:S(2)}, u32[]{:S(2)}) collective-permute-start(f32[12544]{0:T(1024)S(1)} %select_n.98), channel_id=1, source_target_pairs={{0,24},{8,16},{16,8},{24,0},{1,25},{9,17},{17,9},{25,1},{2,26},{10... | collective-permute-start | bytes 150536 | tf_op jit(solution)/shard_map/ppermute | solution.py:122
  7.0 0.6 %fusion.36 = (s32[1]{0:T(128)}, s32[1]{0:T(128)}) fusion(s32[2]{0:T(128)S(1)} %copy-done.3), kind=kLoop, calls=%fused_computation.93 | loop fusion | bytes 16 | tf_op jit(solution)/shard_map/slice | solution.py:298
  8.6 0.6 %collective-permute-done = f32[12544]{0:T(1024)S(1)} collective-permute-done((f32[12544]{0:T(1024)S(1)}, f32[12544]{0:T(1024)S(1)}, u32[]{:S(2)}, u32[]{:S(2)}) %collective-permute-start) | collective-permute-done | bytes 50208 | tf_op jit(solution)/shard_map/ppermute | solution.py:122
  9.9 1.3 %collective-permute-start.3 = (f32[1176]{0:T(1024)S(1)}, f32[1176]{0:T(1024)S(1)}, u32[]{:S(2)}, u32[]{:S(2)}) collective-permute-start(f32[1176]{0:T(1024)S(1)} %reshape.89), channel_id=1, source_target_pairs={{0,1},{1,0},{2,3},{3,2},{4,5},{5,4},{6,7},{7,6},{8,9},{9,8},{10,11... | collective-permute-start | bytes 14120 | tf_op jit(solution)/shard_map/ppermute | solution.py:119
  11.3 3.6 %collective-permute-start.2 = (f32[1176]{0:T(1024)S(1)}, f32[1176]{0:T(1024)S(1)}, u32[]{:S(2)}, u32[]{:S(2)}) collective-permute-start(f32[1176]{0:T(1024)S(1)} %reshape.88), channel_id=1, source_target_pairs={{0,7},{1,2},{2,1},{3,4},{4,3},{5,6},{6,5},{7,0},{8,15},{9,10},{10,... | collective-permute-start | bytes 14120 | tf_op jit(solution)/shard_map/ppermute | solution.py:122
  15.8 1.8 %collective-permute-done.2 = f32[1176]{0:T(1024)S(1)} collective-permute-done((f32[1176]{0:T(1024)S(1)}, f32[1176]{0:T(1024)S(1)}, u32[]{:S(2)}, u32[]{:S(2)}) %collective-permute-start.2) | collective-permute-done | bytes 4736 | tf_op jit(solution)/shard_map/ppermute | solution.py:122
  18.4 0.6 %pad_maximum_fusion.1 = f32[48,12,132]{2,1,0:T(8,128)S(1)} fusion(f32[49,12,2]{2,1,0:T(8,128)S(1)} %reshape.91, f32[49,12,2]{2,1,0:T(8,128)S(1)} %reshape.90, f32[49,2,128]{2,1,0:T(2,128)S(1)} %reshape.87, f32[49,2,128]{2,1,0:T(2,128)S(1)} %reshape.85, f32[1,8,128]{2,1,0:T(8,128)S(1)} %get-tuple-element.40, f32[48,8,128]{2,1,0:T(8,128)S(1)} %bitcast.37), kind=kLoop, calls=%fused_computation.3 | loop fusion | flops 380160 | bytes 614592 | tf_op jit(solution)/shard_map/concatenate | solution.py:135
  19.3 0.6 %broadcast_divide_fusion = (f32[2,12,10,130]{3,2,1,0:T(8,128)S(1)}, f32[2,12,10,130]{3,2,1,0:T(8,128)S(1)}, f32[2,12,10,130]{3,2,1,0:T(8,128)S(1)}, f32[2,12,10,130]{3,2,1,0:T(8,128)S(1)}) fusion(f32[10,130]{1,0:T(8,128)S(1)} %get-tuple-element.13, f32[2,24,12,132]{3,2,1,0:T(8,128)S(1)} %bitcast.31, f32[10,130]{1,0:T(8,128)S(1)} %get-tuple-element.17, ...), kind=kLoop, calls=%fused_computation.34 | loop fusion | flops 343200 | bytes 1274000 | tf_op jit(solution)/shard_map/div | solution.py:314
  20.9 0.5 %convolution_bitcast_fusion.1 = f32[96,96]{1,0:T(8,128)S(1)} fusion(f32[96,8,128]{2,1,0:T(8,128)S(1)} %bitcast.32), kind=kOutput, calls=%fused_computation.2 | convolution fusion | flops 113246208 | bytes 430080 | tf_op jit(solution)/shard_map/jrc,krc->jk/dot_general | solution.py:44
  21.3 0.5 %convolution_bitcast_fusion = f32[96,96]{1,0:T(8,128)S(1)} fusion(f32[96,8,128]{2,0,1:T(8,128)S(1)} %bitcast.38, f32[96,8,128]{2,1,0:T(8,128)S(1)} %bitcast.33), kind=kOutput, calls=%fused_computation.1 | convolution fusion | flops 113246208 | bytes 823296 | tf_op jit(solution)/shard_map/jrc,krc->jk/dot_general | solution.py:44
  22.3 1.4 %collective-permute-start.5 = (f32[4608]{0:T(1024)S(1)}, f32[4608]{0:T(1024)S(1)}, u32[]{:S(2)}, u32[]{:S(2)}) collective-permute-start(f32[4608]{0:T(1024)S(1)} %reshape.95), channel_id=1, source_target_pairs={{0,16},{8,24},{16,0},{24,8},{1,17},{9,25},{17,1},{25,9},{2,18},{10... | collective-permute-start | bytes 55304 | tf_op jit(solution)/shard_map/ppermute | solution.py:151
  24.0 1.5 %collective-permute-done.6 = f32[4608]{0:T(1024)S(1)} collective-permute-done((f32[4608]{0:T(1024)S(1)}, f32[4608]{0:T(1024)S(1)}, u32[]{:S(2)}, u32[]{:S(2)}) %collective-permute-start.6) | collective-permute-done | bytes 18464 | tf_op jit(solution)/shard_map/ppermute | solution.py:151
  25.5 0.6 %collective-permute-done.5 = f32[4608]{0:T(1024)S(1)} collective-permute-done((f32[4608]{0:T(1024)S(1)}, f32[4608]{0:T(1024)S(1)}, u32[]{:S(2)}, u32[]{:S(2)}) %collective-permute-start.5) | collective-permute-done | bytes 18464 | tf_op jit(solution)/shard_map/ppermute | solution.py:151
  26.2 3.8 %collective-permute-done.7 = f32[4608]{0:T(1024)S(1)} collective-permute-done((f32[4608]{0:T(1024)S(1)}, f32[4608]{0:T(1024)S(1)}, u32[]{:S(2)}, u32[]{:S(2)}) %collective-permute-start.7) | collective-permute-done | bytes 18464 | tf_op jit(solution)/shard_map/ppermute | solution.py:151
  30.0 2.1 %collective-permute-start.10 = (f32[4608]{0:T(1024)S(1)}, f32[4608]{0:T(1024)S(1)}, u32[]{:S(2)}, u32[]{:S(2)}) collective-permute-start(f32[4608]{0:T(1024)S(1)} %add.137), channel_id=1, source_target_pairs={{0,6},{1,7},{2,4},{3,5},{4,2},{5,3},{6,0},{7,1},{8,14},{9,15},{10,... | collective-permute-start | bytes 55304 | tf_op jit(solution)/shard_map/ppermute | solution.py:151
  32.1 2.3 %collective-permute-start.8 = (f32[4608]{0:T(1024)S(1)}, f32[4608]{0:T(1024)S(1)}, u32[]{:S(2)}, u32[]{:S(2)}) collective-permute-start(f32[4608]{0:T(1024)S(1)} %add.137), channel_id=1, source_target_pairs={{0,2},{1,3},{2,0},{3,1},{4,6},{5,7},{6,4},{7,5},{8,10},{9,11},{10,... | collective-permute-start | bytes 55304 | tf_op jit(solution)/shard_map/ppermute | solution.py:151
  34.4 1.2 %collective-permute-done.10 = f32[4608]{0:T(1024)S(1)} collective-permute-done((f32[4608]{0:T(1024)S(1)}, f32[4608]{0:T(1024)S(1)}, u32[]{:S(2)}, u32[]{:S(2)}) %collective-permute-start.10) | collective-permute-done | bytes 18464 | tf_op jit(solution)/shard_map/ppermute | solution.py:151
  35.6 1.2 %collective-permute-done.9 = f32[4608]{0:T(1024)S(1)} collective-permute-done((f32[4608]{0:T(1024)S(1)}, f32[4608]{0:T(1024)S(1)}, u32[]{:S(2)}, u32[]{:S(2)}) %collective-permute-start.9) | collective-permute-done | bytes 18464 | tf_op jit(solution)/shard_map/ppermute | solution.py:151
  36.8 0.7 %reshape.96.packed_ref = f32[2,48,48]{2,1,0:T(8,128)} reshape(f32[4608]{0:T(1024)S(1)} %add_add_fusion) | data formatting | bytes 36864 | tf_op jit(solution)/shard_map/reshape | solution.py:329
  37.5 5.8 %shard_map.68 = (f32[72,8,128]{2,1,0:T(8,128)}, f32[36,2,36]{2,1,0:T(2,128)}) custom-call(f32[2,48,48]{2,1,0:T(8,128)} %reshape.96.packed_ref, f32[96,8,128]{2,1,0:T(8,128)} %bitcast.34), custom_call_target="tpu_custom_call" | custom-call | tf_op jit(solution)/shard_map/pallas_call | solution.py:262
  (75 shorter events, 3.8 us)
Async XLA Ops:
  0.6 6.3 %copy-start.2 = (f32[2,12,8,128]{3,2,1,0:T(8,128)S(1)}, f32[2,12,8,128]{3,2,1,0:T(8,128)}, u32[]{:S(2)}) copy-start(f32[2,12,8,128]{3,2,1,0:T(8,128)} %param.5) | copy-start | bytes 294916
  0.6 6.3 %copy-start.1 = (f32[2,12,8,128]{3,2,1,0:T(8,128)S(1)}, f32[2,12,8,128]{3,2,1,0:T(8,128)}, u32[]{:S(2)}) copy-start(f32[2,12,8,128]{3,2,1,0:T(8,128)} %param.6) | copy-start | bytes 294916
  0.7 6.3 %copy-start.4 = (f32[8]{0:T(128)S(1)}, f32[8]{0:T(128)}, u32[]{:S(2)}) copy-start(f32[8]{0:T(128)} %param.8) | copy-start | bytes 100
  0.7 6.3 %copy-start.3 = (s32[2]{0:T(128)S(1)}, s32[2]{0:T(128)}, u32[]{:S(2)}) copy-start(s32[2]{0:T(128)} %param.9) | copy-start | bytes 28
  3.7 4.9 %collective-permute-start.1 = (f32[12544]{0:T(1024)S(1)}, f32[12544]{0:T(1024)S(1)}, u32[]{:S(2)}, u32[]{:S(2)}) collective-permute-start(f32[12544]{0:T(1024)S(1)} %select_n.100), channel_id=1, source_target_pairs={{0,8},{8,0},{16,24},{24,16},{1,9},{9,1},{17,25},{25,17},{2,10},{10... | collective-permute-start | bytes 150536 | tf_op jit(solution)/shard_map/ppermute | solution.py:119
  4.2 4.9 %collective-permute-start = (f32[12544]{0:T(1024)S(1)}, f32[12544]{0:T(1024)S(1)}, u32[]{:S(2)}, u32[]{:S(2)}) collective-permute-start(f32[12544]{0:T(1024)S(1)} %select_n.98), channel_id=1, source_target_pairs={{0,24},{8,16},{16,8},{24,0},{1,25},{9,17},{17,9},{25,1},{2,26},{10... | collective-permute-start | bytes 150536 | tf_op jit(solution)/shard_map/ppermute | solution.py:122
  9.9 5.9 %collective-permute-start.3 = (f32[1176]{0:T(1024)S(1)}, f32[1176]{0:T(1024)S(1)}, u32[]{:S(2)}, u32[]{:S(2)}) collective-permute-start(f32[1176]{0:T(1024)S(1)} %reshape.89), channel_id=1, source_target_pairs={{0,1},{1,0},{2,3},{3,2},{4,5},{5,4},{6,7},{7,6},{8,9},{9,8},{10,11... | collective-permute-start | bytes 14120 | tf_op jit(solution)/shard_map/ppermute | solution.py:119
  11.3 6.3 %collective-permute-start.2 = (f32[1176]{0:T(1024)S(1)}, f32[1176]{0:T(1024)S(1)}, u32[]{:S(2)}, u32[]{:S(2)}) collective-permute-start(f32[1176]{0:T(1024)S(1)} %reshape.88), channel_id=1, source_target_pairs={{0,7},{1,2},{2,1},{3,4},{4,3},{5,6},{6,5},{7,0},{8,15},{9,10},{10,... | collective-permute-start | bytes 14120 | tf_op jit(solution)/shard_map/ppermute | solution.py:122
  20.8 16.7 %copy-start = (f32[2,48,8,128]{3,2,1,0:T(8,128)}, f32[2,48,8,128]{3,2,1,0:T(8,128)S(1)}, u32[]{:S(2)}) copy-start(f32[2,48,8,128]{3,2,1,0:T(8,128)S(1)} %pad_maximum_fusion.7) | copy-start | bytes 1179652
  22.1 3.4 %collective-permute-start.6 = (f32[4608]{0:T(1024)S(1)}, f32[4608]{0:T(1024)S(1)}, u32[]{:S(2)}, u32[]{:S(2)}) collective-permute-start(f32[4608]{0:T(1024)S(1)} %reshape.95), channel_id=1, source_target_pairs={{0,24},{8,16},{16,8},{24,0},{1,25},{9,17},{17,9},{25,1},{2,26},{10... | collective-permute-start | bytes 55304 | tf_op jit(solution)/shard_map/ppermute | solution.py:151
  22.3 3.8 %collective-permute-start.5 = (f32[4608]{0:T(1024)S(1)}, f32[4608]{0:T(1024)S(1)}, u32[]{:S(2)}, u32[]{:S(2)}) collective-permute-start(f32[4608]{0:T(1024)S(1)} %reshape.95), channel_id=1, source_target_pairs={{0,16},{8,24},{16,0},{24,8},{1,17},{9,25},{17,1},{25,9},{2,18},{10... | collective-permute-start | bytes 55304 | tf_op jit(solution)/shard_map/ppermute | solution.py:151
  23.8 2.4 %collective-permute-start.4 = (f32[4608]{0:T(1024)S(1)}, f32[4608]{0:T(1024)S(1)}, u32[]{:S(2)}, u32[]{:S(2)}) collective-permute-start(f32[4608]{0:T(1024)S(1)} %reshape.95), channel_id=1, source_target_pairs={{0,8},{8,0},{16,24},{24,16},{1,9},{9,1},{17,25},{25,17},{2,10},{10... | collective-permute-start | bytes 55304 | tf_op jit(solution)/shard_map/ppermute | solution.py:151
  26.1 3.8 %collective-permute-start.7 = (f32[4608]{0:T(1024)S(1)}, f32[4608]{0:T(1024)S(1)}, u32[]{:S(2)}, u32[]{:S(2)}) collective-permute-start(f32[4608]{0:T(1024)S(1)} %add_add_fusion.1), channel_id=1, source_target_pairs={{0,1},{1,0},{2,3},{3,2},{4,5},{5,4},{6,7},{7,6},{8,9},{9,8},{10,11... | collective-permute-start | bytes 55304 | tf_op jit(solution)/shard_map/ppermute | solution.py:151
  30.0 5.6 %collective-permute-start.10 = (f32[4608]{0:T(1024)S(1)}, f32[4608]{0:T(1024)S(1)}, u32[]{:S(2)}, u32[]{:S(2)}) collective-permute-start(f32[4608]{0:T(1024)S(1)} %add.137), channel_id=1, source_target_pairs={{0,6},{1,7},{2,4},{3,5},{4,2},{5,3},{6,0},{7,1},{8,14},{9,15},{10,... | collective-permute-start | bytes 55304 | tf_op jit(solution)/shard_map/ppermute | solution.py:151
  32.1 4.7 %collective-permute-start.9 = (f32[4608]{0:T(1024)S(1)}, f32[4608]{0:T(1024)S(1)}, u32[]{:S(2)}, u32[]{:S(2)}) collective-permute-start(f32[4608]{0:T(1024)S(1)} %add.137), channel_id=1, source_target_pairs={{0,4},{1,5},{2,6},{3,7},{4,0},{5,1},{6,2},{7,3},{8,12},{9,13},{10,... | collective-permute-start | bytes 55304 | tf_op jit(solution)/shard_map/ppermute | solution.py:151
  32.1 4.7 %collective-permute-start.8 = (f32[4608]{0:T(1024)S(1)}, f32[4608]{0:T(1024)S(1)}, u32[]{:S(2)}, u32[]{:S(2)}) collective-permute-start(f32[4608]{0:T(1024)S(1)} %add.137), channel_id=1, source_target_pairs={{0,2},{1,3},{2,0},{3,1},{4,6},{5,7},{6,4},{7,5},{8,10},{9,11},{10,... | collective-permute-start | bytes 55304 | tf_op jit(solution)/shard_map/ppermute | solution.py:151
